TPU v7x, 512 devices: a whole 4x4x16 slice. The times are simulated.
512 devices in a mesh: ctx: 32 (over x, z_hi, core), head: 16 (over z_lo, y).
Axes of the slice: x: 4, y: 4, z: 16 (z_hi: 4, z_lo: 4; z = z_hi * 4 + z_lo), core: 2. Of those that a mesh axis runs over, the one named last changes fastest.
Arguments:
- queries: bfloat16 [16384, 64, 128], P('ctx', 'head'), may hold values from -18 to 18
- key_rows: bfloat16 [4, 16384, 128], P(None, 'ctx'), may hold values from -18 to 18
- value_rows: bfloat16 [4, 16384, 128], P(None, 'ctx'), may hold values from -6 to 6
- out_grad: bfloat16 [16384, 64, 128], P('ctx', 'head'), may hold values from -36 to 36
- selected: int32 [256, 4, 16], P('ctx'), may hold values from 0 to 255, as said below
- live_slots: int32 [256, 4, 16], P('ctx'), may hold values from 0 to 1, as said below
Outputs:
- query_grad: bfloat16 [16384, 64, 128], P('ctx', 'head')
- key_grad: float32 [4, 16384, 128], P(None, 'ctx')
- value_grad: float32 [4, 16384, 128], P(None, 'ctx')
Inputs may be any that keep to these rules, and one draw needn't show every extreme that they name: `selected`: slot 0 of query block b holds b with live_slots 1. Used slots hold distinct blocks x with x <= b and x >= (b // 8 - 6) * 8; used slots come before unused ones, and unused slots hold b. The number of used slots varies between query blocks. `live_slots`: slot 0 is always 1.
All inputs are finite; a program needn't handle non-finite values.
Results may differ from a plain program's by a relative error of at most 0.017.
Values may be sent and summed in bfloat16 or wider, within the bound.
No kernel may reach another device: no remote copies, remote signals or barrier semaphores. Data moves between devices by JAX's collectives and lax.ppermute only.
A program may use at most 64 MiB of HBM per device.

v0:
```python
import jax
import jax.numpy as jnp
from jax import lax
from jax.sharding import PartitionSpec as P

HPG = 16
BLOCK = 64
REACH = 6


def shifted_2(value, axis, steps):
    count = lax.axis_size(axis)
    leading, last = (max(0, -steps), min(count, count - steps))
    return lax.ppermute(value, axis, [(source, source + steps) for source in range(leading, last)])


def visible_mask(chosen, live_mask, block_id, width):
    causal = jnp.arange(width)[:, None] >= jnp.arange(width)[None, :]
    earlier = (chosen < block_id)[None, :, None]
    allowed = (live_mask == 1)[None, :, None] & (earlier | causal[:, None, :])
    return allowed.reshape(width, -1)


def tile_grads(q_pair, do_pair, k_sel, v_sel, allowed, inv_root):
    scores = (
        jnp.einsum("bqhd,bnd->bhqn", q_pair, k_sel, preferred_element_type=jnp.float32) * inv_root
    )
    scores = jnp.where(allowed[:, None], scores, -1e30)
    row_max = jnp.max(scores, axis=-1, keepdims=True)
    shifted = jnp.exp(scores - row_max)
    weights = shifted / jnp.sum(shifted, axis=-1, keepdims=True)
    weights_b = weights.astype(jnp.bfloat16)
    output = jnp.einsum("bhqn,bnd->bqhd", weights_b, v_sel, preferred_element_type=jnp.float32)
    row_delta = jnp.sum(do_pair.astype(jnp.float32) * output, axis=-1)
    prob_grad = jnp.einsum("bqhd,bnd->bhqn", do_pair, v_sel, preferred_element_type=jnp.float32)
    score_grad = weights * (prob_grad - jnp.transpose(row_delta, (0, 2, 1))[..., None])
    score_b = score_grad.astype(jnp.bfloat16)
    query_part = (
        jnp.einsum("bhqn,bnd->bqhd", score_b, k_sel, preferred_element_type=jnp.float32) * inv_root
    )
    key_part = (
        jnp.einsum("bhqn,bqhd->bnd", score_b, q_pair, preferred_element_type=jnp.float32) * inv_root
    )
    value_part = jnp.einsum(
        "bhqn,bqhd->bnd", weights_b, do_pair, preferred_element_type=jnp.float32
    )
    return (query_part.astype(jnp.bfloat16), key_part, value_part)


def per_device(queries, key_rows, value_rows, out_grad, selected, live_slots):
    tokens_here, heads_here, width = queries.shape
    groups = key_rows.shape[0]
    blocks_here = tokens_here // BLOCK
    members = HPG // heads_here
    reach_span = REACH + 1
    inv_root = width ** (-0.5)
    ctx_index = lax.axis_index("ctx")
    group_index = lax.axis_index("head") // members
    own_tiles = jnp.stack(
        [
            lax.dynamic_index_in_dim(key_rows, group_index, 0, keepdims=False),
            lax.dynamic_index_in_dim(value_rows, group_index, 0, keepdims=False),
        ]
    )
    fetched = [own_tiles]
    moving = own_tiles
    for offset in range(REACH):
        moving = shifted_2(moving, "ctx", 1)
        fetched.append(moving)
    tile_store = jnp.stack(fetched)
    key_tiles = tile_store[:, 0].reshape(reach_span * blocks_here, BLOCK, width)
    value_tiles = tile_store[:, 1].reshape(reach_span * blocks_here, BLOCK, width)
    chosen = lax.dynamic_index_in_dim(selected, group_index, 1, keepdims=False)
    live_mask = lax.dynamic_index_in_dim(live_slots, group_index, 1, keepdims=False)
    block_ids = ctx_index * blocks_here + jnp.arange(blocks_here, dtype=jnp.int32)
    slot_index = (ctx_index - chosen // blocks_here) * blocks_here + chosen % blocks_here
    pair_count = blocks_here // 2

    def accumulate(running, inputs):
        q_pair, do_pair, slot_pair, chosen_pair, live_pair, block_pair = inputs
        k_sel = key_tiles[slot_pair].reshape(2, -1, width)
        v_sel = value_tiles[slot_pair].reshape(2, -1, width)
        allowed = jax.vmap(visible_mask, in_axes=(0, 0, 0, None))(
            chosen_pair, live_pair, block_pair, BLOCK
        )
        query_part, key_part, value_part = tile_grads(
            q_pair, do_pair, k_sel, v_sel, allowed, inv_root
        )
        stacked = jnp.stack([key_part, value_part]).reshape(2, -1, BLOCK, width)
        running = running.at[:, slot_pair.reshape(-1)].add(stacked)
        return (running, query_part)

    initial = jnp.zeros((2, reach_span * blocks_here, BLOCK, width), jnp.float32)
    inputs = (
        queries.reshape(pair_count, 2, BLOCK, heads_here, width),
        out_grad.reshape(pair_count, 2, BLOCK, heads_here, width),
        slot_index.reshape(pair_count, 2, -1),
        chosen.reshape(pair_count, 2, -1),
        live_mask.reshape(pair_count, 2, -1),
        block_ids.reshape(pair_count, 2),
    )
    grads, query_parts = lax.scan(accumulate, initial, inputs)
    parts = grads.reshape(2, reach_span, tokens_here, width)
    running = parts[:, REACH]
    for offset in range(REACH - 1, -1, -1):
        running = (
            shifted_2(running.astype(jnp.bfloat16), "ctx", -1).astype(running.dtype)
            + parts[:, offset]
        )
    spread = jnp.where(
        (jnp.arange(groups) == group_index)[None, :, None, None], running[:, None], 0.0
    )
    summed = lax.psum(spread.astype(jnp.bfloat16), "head").astype(jnp.float32)
    query_grad = query_parts.reshape(tokens_here, heads_here, width)
    return (query_grad, summed[0], summed[1])


def solution(mesh):
    return jax.shard_map(
        per_device,
        mesh=mesh,
        in_specs=(
            P("ctx", "head", None),
            P(None, "ctx", None),
            P(None, "ctx", None),
            P("ctx", "head", None),
            P("ctx", None, None),
            P("ctx", None, None),
        ),
        out_specs=(P("ctx", "head", None), P(None, "ctx", None), P(None, "ctx", None)),
        check_vma=False,
    )
```

profile of v0, /device:TPU:6, one launch (start us, length us, event | category | flops | bytes accessed | tf_op | source)
XLA Modules:
  0.0 463.3 jit_solution(13202527245153477320)
XLA Ops:
  7.2 1.0 constant_dynamic-slice_fusion.6
  8.3 1.9 collective-permute-start
  10.2 14.9 %collective-permute-done = bf16[2,512,128]{2,1,0:T(8,128)(2,1)S(1)} collective-permute-done((bf16[2,512,128]{2,1,0:T(8,128)(2,1)S(1)}, bf16[2,512,128]{2,1,0:T(8,128)(2,1)S(1)}, u32[]{:S(2)}, u32[]{:S(2)}) %collective-permute-start) | collective-permute-done | bytes 262176 | tf_op jit(solution)/shard_map/ppermute | solution.py:14
  25.0 1.9 collective-permute-start.1
  27.0 13.4 %collective-permute-done.1 = bf16[2,512,128]{2,1,0:T(8,128)(2,1)S(1)} collective-permute-done((bf16[2,512,128]{2,1,0:T(8,128)(2,1)S(1)}, bf16[2,512,128]{2,1,0:T(8,128)(2,1)S(1)}, u32[]{:S(2)}, u32[]{:S(2)}) %collective-permute-start.1) | collective-permute-done | bytes 262176 | tf_op jit(solution)/shard_map/ppermute | solution.py:14
  40.4 1.9 collective-permute-start.2
  42.3 0.8 constant_dynamic-slice_fusion.8
  43.1 12.5 %collective-permute-done.2 = bf16[2,512,128]{2,1,0:T(8,128)(2,1)S(1)} collective-permute-done((bf16[2,512,128]{2,1,0:T(8,128)(2,1)S(1)}, bf16[2,512,128]{2,1,0:T(8,128)(2,1)S(1)}, u32[]{:S(2)}, u32[]{:S(2)}) %collective-permute-start.2) | collective-permute-done | bytes 262176 | tf_op jit(solution)/shard_map/ppermute | solution.py:14
  55.6 1.9 collective-permute-start.3
  57.6 19.2 %collective-permute-done.3 = bf16[2,512,128]{2,1,0:T(8,128)(2,1)S(1)} collective-permute-done((bf16[2,512,128]{2,1,0:T(8,128)(2,1)S(1)}, bf16[2,512,128]{2,1,0:T(8,128)(2,1)S(1)}, u32[]{:S(2)}, u32[]{:S(2)}) %collective-permute-start.3) | collective-permute-done | bytes 262176 | tf_op jit(solution)/shard_map/ppermute | solution.py:14
  76.8 1.9 collective-permute-start.4
  78.8 16.3 %collective-permute-done.4 = bf16[2,512,128]{2,1,0:T(8,128)(2,1)S(1)} collective-permute-done((bf16[2,512,128]{2,1,0:T(8,128)(2,1)S(1)}, bf16[2,512,128]{2,1,0:T(8,128)(2,1)S(1)}, u32[]{:S(2)}, u32[]{:S(2)}) %collective-permute-start.4) | collective-permute-done | bytes 262176 | tf_op jit(solution)/shard_map/ppermute | solution.py:14
  95.1 1.9 collective-permute-start.5
  97.1 13.1 %collective-permute-done.5 = bf16[2,512,128]{2,1,0:T(8,128)(2,1)S(1)} collective-permute-done((bf16[2,512,128]{2,1,0:T(8,128)(2,1)S(1)}, bf16[2,512,128]{2,1,0:T(8,128)(2,1)S(1)}, u32[]{:S(2)}, u32[]{:S(2)}) %collective-permute-start.5) | collective-permute-done | bytes 262176 | tf_op jit(solution)/shard_map/ppermute | solution.py:14
  110.3 1.4 fusion.38
  111.6 2.3 broadcast_in_dim.56
  113.9 70.2 %while.12 = (s32[]{:T(128)}, f32[2,56,64,128]{3,2,1,0:T(8,128)}, bf16[4,2,64,4,128]{4,3,2,1,0:T(4,128)(2,1)}, s32[4,2,16]{2,1,0:T(2,128)S(1)}, s32[4,2,16]{2,1,0...) while((s32[]{:T(128)}, f32[2,56,64,128]{3,2,1,0:T(8,128)}, ...), condition=%wide.region_5.6_spmd, body=%wide.region_0.5_spmd.sunk | while | flops 812455680 | bytes 31499264 | solution.py:102
  114.1 0.6 fusion.74
  115.4 1.1 constant_dynamic-slice_fusion.12
  116.5 1.8 gather_fusion.1
  118.3 1.8 gather_fusion
  120.2 0.9 fusion.77
  124.2 0.8 copy_dynamic-update-slice_fusion.2
  125.0 6.4 %scatter_fusion = f32[2,56,64,128]{3,2,1,0:T(8,128)} fusion(f32[2,56,64,128]{3,2,1,0:T(8,128)} %get-tuple-element.208, s32[32]{0:T(128)S(1)} %copy-done, f32[32,2,64,128]{3,2,1,0:T(8,128)S(1)} %maximum_bitcast_fusion.2), kind=kCustom, calls=%fused_computation.2.clone.1 | custom fusion | flops 524288 | bytes 6291584 | tf_op jit(solution)/shard_map/while/body/eval_jaxpr/scatter-add | solution.py:90
  131.6 0.6 fusion.74
  132.9 1.1 constant_dynamic-slice_fusion.12
  134.0 1.8 gather_fusion.1
  135.9 1.8 gather_fusion
  137.7 0.9 fusion.77
  141.7 0.8 copy_dynamic-update-slice_fusion.2
  142.5 6.6 %scatter_fusion = f32[2,56,64,128]{3,2,1,0:T(8,128)} fusion(f32[2,56,64,128]{3,2,1,0:T(8,128)} %get-tuple-element.208, s32[32]{0:T(128)S(1)} %copy-done, f32[32,2,64,128]{3,2,1,0:T(8,128)S(1)} %maximum_bitcast_fusion.2), kind=kCustom, calls=%fused_computation.2.clone.1 | custom fusion | flops 524288 | bytes 6291584 | tf_op jit(solution)/shard_map/while/body/eval_jaxpr/scatter-add | solution.py:90
  149.2 0.6 fusion.74
  150.6 1.1 constant_dynamic-slice_fusion.12
  151.7 1.8 gather_fusion.1
  153.5 1.8 gather_fusion
  155.3 0.9 fusion.77
  159.3 0.8 copy_dynamic-update-slice_fusion.2
  160.1 6.4 %scatter_fusion = f32[2,56,64,128]{3,2,1,0:T(8,128)} fusion(f32[2,56,64,128]{3,2,1,0:T(8,128)} %get-tuple-element.208, s32[32]{0:T(128)S(1)} %copy-done, f32[32,2,64,128]{3,2,1,0:T(8,128)S(1)} %maximum_bitcast_fusion.2), kind=kCustom, calls=%fused_computation.2.clone.1 | custom fusion | flops 524288 | bytes 6291584 | tf_op jit(solution)/shard_map/while/body/eval_jaxpr/scatter-add | solution.py:90
  166.7 0.6 fusion.74
  168.1 1.1 constant_dynamic-slice_fusion.12
  169.1 1.8 gather_fusion.1
  171.0 1.8 gather_fusion
  172.8 0.9 fusion.77
  176.0 0.6 fusion.82
  176.8 0.8 copy_dynamic-update-slice_fusion.2
  177.6 6.5 %scatter_fusion = f32[2,56,64,128]{3,2,1,0:T(8,128)} fusion(f32[2,56,64,128]{3,2,1,0:T(8,128)} %get-tuple-element.208, s32[32]{0:T(128)S(1)} %copy-done, f32[32,2,64,128]{3,2,1,0:T(8,128)S(1)} %maximum_bitcast_fusion.2), kind=kCustom, calls=%fused_computation.2.clone.1 | custom fusion | flops 524288 | bytes 6291584 | tf_op jit(solution)/shard_map/while/body/eval_jaxpr/scatter-add | solution.py:90
  184.1 1.1 fusion.34
  185.1 1.9 collective-permute-start.6
  187.1 2.1 fusion.37
  189.1 10.1 %collective-permute-done.6 = bf16[2,512,128]{2,1,0:T(8,128)(2,1)S(1)} collective-permute-done((bf16[2,512,128]{2,1,0:T(8,128)(2,1)S(1)}, bf16[2,512,128]{2,1,0:T(8,128)(2,1)S(1)}, u32[]{:S(2)}, u32[]{:S(2)}) %collective-permute-start.6) | collective-permute-done | bytes 262176 | tf_op jit(solution)/shard_map/ppermute | solution.py:14
  199.3 8.6 %collective-permute-start.7 = (bf16[2,512,128]{2,1,0:T(8,128)(2,1)S(1)}, bf16[2,512,128]{2,1,0:T(8,128)(2,1)S(1)}, u32[]{:S(2)}, u32[]{:S(2)}) collective-permute-start(bf16[2,512,128]{2,1,0:T(8,128)(2,1)S(1)} %fusion.33), channel_id=1, source_target_pairs={{16,0},{32,16},{48,32},{64,48},{80,64},{96,80},{112,96},{128,112},... | collective-permute-start | bytes 786440 | tf_op jit(solution)/shard_map/ppermute | solution.py:14
  207.9 7.4 %collective-permute-done.7 = bf16[2,512,128]{2,1,0:T(8,128)(2,1)S(1)} collective-permute-done((bf16[2,512,128]{2,1,0:T(8,128)(2,1)S(1)}, bf16[2,512,128]{2,1,0:T(8,128)(2,1)S(1)}, u32[]{:S(2)}, u32[]{:S(2)}) %collective-permute-start.7) | collective-permute-done | bytes 262176 | tf_op jit(solution)/shard_map/ppermute | solution.py:14
  215.4 8.8 %collective-permute-start.8 = (bf16[2,512,128]{2,1,0:T(8,128)(2,1)S(1)}, bf16[2,512,128]{2,1,0:T(8,128)(2,1)S(1)}, u32[]{:S(2)}, u32[]{:S(2)}) collective-permute-start(bf16[2,512,128]{2,1,0:T(8,128)(2,1)S(1)} %fusion.31), channel_id=1, source_target_pairs={{16,0},{32,16},{48,32},{64,48},{80,64},{96,80},{112,96},{128,112},... | collective-permute-start | bytes 786440 | tf_op jit(solution)/shard_map/ppermute | solution.py:14
  224.1 6.1 %collective-permute-done.8 = bf16[2,512,128]{2,1,0:T(8,128)(2,1)S(1)} collective-permute-done((bf16[2,512,128]{2,1,0:T(8,128)(2,1)S(1)}, bf16[2,512,128]{2,1,0:T(8,128)(2,1)S(1)}, u32[]{:S(2)}, u32[]{:S(2)}) %collective-permute-start.8) | collective-permute-done | bytes 262176 | tf_op jit(solution)/shard_map/ppermute | solution.py:14
  230.3 8.7 %collective-permute-start.9 = (bf16[2,512,128]{2,1,0:T(8,128)(2,1)S(1)}, bf16[2,512,128]{2,1,0:T(8,128)(2,1)S(1)}, u32[]{:S(2)}, u32[]{:S(2)}) collective-permute-start(bf16[2,512,128]{2,1,0:T(8,128)(2,1)S(1)} %fusion.29), channel_id=1, source_target_pairs={{16,0},{32,16},{48,32},{64,48},{80,64},{96,80},{112,96},{128,112},... | collective-permute-start | bytes 786440 | tf_op jit(solution)/shard_map/ppermute | solution.py:14
  239.0 3.9 collective-permute-done.9
  243.0 8.7 %collective-permute-start.10 = (bf16[2,512,128]{2,1,0:T(8,128)(2,1)S(1)}, bf16[2,512,128]{2,1,0:T(8,128)(2,1)S(1)}, u32[]{:S(2)}, u32[]{:S(2)}) collective-permute-start(bf16[2,512,128]{2,1,0:T(8,128)(2,1)S(1)} %fusion.27), channel_id=1, source_target_pairs={{16,0},{32,16},{48,32},{64,48},{80,64},{96,80},{112,96},{128,112},... | collective-permute-start | bytes 786440 | tf_op jit(solution)/shard_map/ppermute | solution.py:14
  251.7 5.3 %collective-permute-done.10 = bf16[2,512,128]{2,1,0:T(8,128)(2,1)S(1)} collective-permute-done((bf16[2,512,128]{2,1,0:T(8,128)(2,1)S(1)}, bf16[2,512,128]{2,1,0:T(8,128)(2,1)S(1)}, u32[]{:S(2)}, u32[]{:S(2)}) %collective-permute-start.10) | collective-permute-done | bytes 262176 | tf_op jit(solution)/shard_map/ppermute | solution.py:14
  257.1 8.6 %collective-permute-start.11 = (bf16[2,512,128]{2,1,0:T(8,128)(2,1)S(1)}, bf16[2,512,128]{2,1,0:T(8,128)(2,1)S(1)}, u32[]{:S(2)}, u32[]{:S(2)}) collective-permute-start(bf16[2,512,128]{2,1,0:T(8,128)(2,1)S(1)} %fusion.25), channel_id=1, source_target_pairs={{16,0},{32,16},{48,32},{64,48},{80,64},{96,80},{112,96},{128,112},... | collective-permute-start | bytes 786440 | tf_op jit(solution)/shard_map/ppermute | solution.py:14
  265.8 6.0 %collective-permute-done.11 = bf16[2,512,128]{2,1,0:T(8,128)(2,1)S(1)} collective-permute-done((bf16[2,512,128]{2,1,0:T(8,128)(2,1)S(1)}, bf16[2,512,128]{2,1,0:T(8,128)(2,1)S(1)}, u32[]{:S(2)}, u32[]{:S(2)}) %collective-permute-start.11) | collective-permute-done | bytes 262176 | tf_op jit(solution)/shard_map/ppermute | solution.py:14
  271.9 1.2 select_convert_fusion
  273.1 180.6 %all-reduce.2.cloned.1.call-done = bf16[2,4,512,128]{3,2,1,0:T(8,128)(2,1)} async-done(((bf16[2,4,512,128]{3,2,1,0:T(8,128)(2,1)}), bf16[2,4,512,128]{3,2,1,0:T(8,128)(2,1)}) %all-reduce.2.cloned.1.call-update) | async-done | bytes 1048592 | tf_op jit(solution)/shard_map/psum | solution.py:113
  453.6 1.4 convert_element_type.71
  455.0 1.5 slice_bitcast_fusion
  (131 shorter events, 16.2 us)
Async XLA Ops:
  7.2 446.5 %all-reduce.2.cloned.1.call-start = ((), (), s32[]{:S(2)}) async-start(), calls=%async_computation | async-start | bytes 2097152 | tf_op jit(solution)/shard_map/psum | solution.py:113
  8.3 16.8 %collective-permute-start = (bf16[2,512,128]{2,1,0:T(8,128)(2,1)S(1)}, bf16[2,512,128]{2,1,0:T(8,128)(2,1)S(1)}, u32[]{:S(2)}, u32[]{:S(2)}) collective-permute-start(bf16[2,512,128]{2,1,0:T(8,128)(2,1)S(1)} %pad_maximum_fusion), channel_id=1, source_target_pairs={{0,16},{16,32},{32,48},{48,64},{64,80},{80,96},{96,112},{112,128},... | collective-permute-start | bytes 786440 | tf_op jit(solution)/shard_map/ppermute | solution.py:14
  25.0 15.4 %collective-permute-start.1 = (bf16[2,512,128]{2,1,0:T(8,128)(2,1)S(1)}, bf16[2,512,128]{2,1,0:T(8,128)(2,1)S(1)}, u32[]{:S(2)}, u32[]{:S(2)}) collective-permute-start(bf16[2,512,128]{2,1,0:T(8,128)(2,1)S(1)} %collective-permute-done), channel_id=1, source_target_pairs={{0,16},{16,32},{32,48},{48,64},{64,80},{80,96},{96,112},{112,128},... | collective-permute-start | bytes 786440 | tf_op jit(solution)/shard_map/ppermute | solution.py:14
  40.4 15.2 %collective-permute-start.2 = (bf16[2,512,128]{2,1,0:T(8,128)(2,1)S(1)}, bf16[2,512,128]{2,1,0:T(8,128)(2,1)S(1)}, u32[]{:S(2)}, u32[]{:S(2)}) collective-permute-start(bf16[2,512,128]{2,1,0:T(8,128)(2,1)S(1)} %collective-permute-done.1), channel_id=1, source_target_pairs={{0,16},{16,32},{32,48},{48,64},{64,80},{80,96},{96,112},{112,128},... | collective-permute-start | bytes 786440 | tf_op jit(solution)/shard_map/ppermute | solution.py:14
  55.6 21.2 %collective-permute-start.3 = (bf16[2,512,128]{2,1,0:T(8,128)(2,1)S(1)}, bf16[2,512,128]{2,1,0:T(8,128)(2,1)S(1)}, u32[]{:S(2)}, u32[]{:S(2)}) collective-permute-start(bf16[2,512,128]{2,1,0:T(8,128)(2,1)S(1)} %collective-permute-done.2), channel_id=1, source_target_pairs={{0,16},{16,32},{32,48},{48,64},{64,80},{80,96},{96,112},{112,128},... | collective-permute-start | bytes 786440 | tf_op jit(solution)/shard_map/ppermute | solution.py:14
  76.8 18.4 %collective-permute-start.4 = (bf16[2,512,128]{2,1,0:T(8,128)(2,1)S(1)}, bf16[2,512,128]{2,1,0:T(8,128)(2,1)S(1)}, u32[]{:S(2)}, u32[]{:S(2)}) collective-permute-start(bf16[2,512,128]{2,1,0:T(8,128)(2,1)S(1)} %collective-permute-done.3), channel_id=1, source_target_pairs={{0,16},{16,32},{32,48},{48,64},{64,80},{80,96},{96,112},{112,128},... | collective-permute-start | bytes 786440 | tf_op jit(solution)/shard_map/ppermute | solution.py:14
  95.1 15.1 %collective-permute-start.5 = (bf16[2,512,128]{2,1,0:T(8,128)(2,1)S(1)}, bf16[2,512,128]{2,1,0:T(8,128)(2,1)S(1)}, u32[]{:S(2)}, u32[]{:S(2)}) collective-permute-start(bf16[2,512,128]{2,1,0:T(8,128)(2,1)S(1)} %collective-permute-done.4), channel_id=1, source_target_pairs={{0,16},{16,32},{32,48},{48,64},{64,80},{80,96},{96,112},{112,128},... | collective-permute-start | bytes 786440 | tf_op jit(solution)/shard_map/ppermute | solution.py:14
  113.9 6.3 %copy-start.1 = (s32[4,2]{1,0:T(4,128)}, s32[4,2]{1,0:T(4,128)S(1)}, u32[]{:S(2)}) copy-start(s32[4,2]{1,0:T(4,128)S(1)} %get-tuple-element.225) | copy-start | bytes 100 | tf_op jit(solution)/shard_map/while
  123.9 1.0 copy-start
  125.0 6.4 %copy-start.2 = (s32[4,2]{1,0:T(4,128)S(1)}, s32[4,2]{1,0:T(4,128)}, u32[]{:S(2)}) copy-start(s32[4,2]{1,0:T(4,128)} %copy-done.1) | copy-start | bytes 100 | tf_op jit(solution)/shard_map/while
  131.4 6.3 %copy-start.1 = (s32[4,2]{1,0:T(4,128)}, s32[4,2]{1,0:T(4,128)S(1)}, u32[]{:S(2)}) copy-start(s32[4,2]{1,0:T(4,128)S(1)} %get-tuple-element.225) | copy-start | bytes 100 | tf_op jit(solution)/shard_map/while
  141.4 1.0 copy-start
  142.5 6.6 %copy-start.2 = (s32[4,2]{1,0:T(4,128)S(1)}, s32[4,2]{1,0:T(4,128)}, u32[]{:S(2)}) copy-start(s32[4,2]{1,0:T(4,128)} %copy-done.1) | copy-start | bytes 100 | tf_op jit(solution)/shard_map/while
  149.0 6.3 %copy-start.1 = (s32[4,2]{1,0:T(4,128)}, s32[4,2]{1,0:T(4,128)S(1)}, u32[]{:S(2)}) copy-start(s32[4,2]{1,0:T(4,128)S(1)} %get-tuple-element.225) | copy-start | bytes 100 | tf_op jit(solution)/shard_map/while
  159.1 1.0 copy-start
  160.1 6.4 %copy-start.2 = (s32[4,2]{1,0:T(4,128)S(1)}, s32[4,2]{1,0:T(4,128)}, u32[]{:S(2)}) copy-start(s32[4,2]{1,0:T(4,128)} %copy-done.1) | copy-start | bytes 100 | tf_op jit(solution)/shard_map/while
  166.5 6.3 %copy-start.1 = (s32[4,2]{1,0:T(4,128)}, s32[4,2]{1,0:T(4,128)S(1)}, u32[]{:S(2)}) copy-start(s32[4,2]{1,0:T(4,128)S(1)} %get-tuple-element.225) | copy-start | bytes 100 | tf_op jit(solution)/shard_map/while
  176.6 1.0 copy-start
  177.6 6.5 %copy-start.2 = (s32[4,2]{1,0:T(4,128)S(1)}, s32[4,2]{1,0:T(4,128)}, u32[]{:S(2)}) copy-start(s32[4,2]{1,0:T(4,128)} %copy-done.1) | copy-start | bytes 100 | tf_op jit(solution)/shard_map/while
  185.1 14.1 %collective-permute-start.6 = (bf16[2,512,128]{2,1,0:T(8,128)(2,1)S(1)}, bf16[2,512,128]{2,1,0:T(8,128)(2,1)S(1)}, u32[]{:S(2)}, u32[]{:S(2)}) collective-permute-start(bf16[2,512,128]{2,1,0:T(8,128)(2,1)S(1)} %fusion.34), channel_id=1, source_target_pairs={{16,0},{32,16},{48,32},{64,48},{80,64},{96,80},{112,96},{128,112},... | collective-permute-start | bytes 786440 | tf_op jit(solution)/shard_map/ppermute | solution.py:14
  199.3 16.0 %collective-permute-start.7 = (bf16[2,512,128]{2,1,0:T(8,128)(2,1)S(1)}, bf16[2,512,128]{2,1,0:T(8,128)(2,1)S(1)}, u32[]{:S(2)}, u32[]{:S(2)}) collective-permute-start(bf16[2,512,128]{2,1,0:T(8,128)(2,1)S(1)} %fusion.33), channel_id=1, source_target_pairs={{16,0},{32,16},{48,32},{64,48},{80,64},{96,80},{112,96},{128,112},... | collective-permute-start | bytes 786440 | tf_op jit(solution)/shard_map/ppermute | solution.py:14
  215.4 14.9 %collective-permute-start.8 = (bf16[2,512,128]{2,1,0:T(8,128)(2,1)S(1)}, bf16[2,512,128]{2,1,0:T(8,128)(2,1)S(1)}, u32[]{:S(2)}, u32[]{:S(2)}) collective-permute-start(bf16[2,512,128]{2,1,0:T(8,128)(2,1)S(1)} %fusion.31), channel_id=1, source_target_pairs={{16,0},{32,16},{48,32},{64,48},{80,64},{96,80},{112,96},{128,112},... | collective-permute-start | bytes 786440 | tf_op jit(solution)/shard_map/ppermute | solution.py:14
  230.3 12.6 %collective-permute-start.9 = (bf16[2,512,128]{2,1,0:T(8,128)(2,1)S(1)}, bf16[2,512,128]{2,1,0:T(8,128)(2,1)S(1)}, u32[]{:S(2)}, u32[]{:S(2)}) collective-permute-start(bf16[2,512,128]{2,1,0:T(8,128)(2,1)S(1)} %fusion.29), channel_id=1, source_target_pairs={{16,0},{32,16},{48,32},{64,48},{80,64},{96,80},{112,96},{128,112},... | collective-permute-start | bytes 786440 | tf_op jit(solution)/shard_map/ppermute | solution.py:14
  243.0 14.1 %collective-permute-start.10 = (bf16[2,512,128]{2,1,0:T(8,128)(2,1)S(1)}, bf16[2,512,128]{2,1,0:T(8,128)(2,1)S(1)}, u32[]{:S(2)}, u32[]{:S(2)}) collective-permute-start(bf16[2,512,128]{2,1,0:T(8,128)(2,1)S(1)} %fusion.27), channel_id=1, source_target_pairs={{16,0},{32,16},{48,32},{64,48},{80,64},{96,80},{112,96},{128,112},... | collective-permute-start | bytes 786440 | tf_op jit(solution)/shard_map/ppermute | solution.py:14
  257.1 14.7 %collective-permute-start.11 = (bf16[2,512,128]{2,1,0:T(8,128)(2,1)S(1)}, bf16[2,512,128]{2,1,0:T(8,128)(2,1)S(1)}, u32[]{:S(2)}, u32[]{:S(2)}) collective-permute-start(bf16[2,512,128]{2,1,0:T(8,128)(2,1)S(1)} %fusion.25), channel_id=1, source_target_pairs={{16,0},{32,16},{48,32},{64,48},{80,64},{96,80},{112,96},{128,112},... | collective-permute-start | bytes 786440 | tf_op jit(solution)/shard_map/ppermute | solution.py:14
Sparse Core Ops, SparseCore 0:
  273.2 180.3 all-reduce.1
where the time goes:
time: 465 us; the launch traced here: 463 us
  waiting for transfers between devices  309 us (66%)
  starting transfers between devices  56.9 us (12%)
  local copies, waits for them, and re-layouts  35.1 us (8%)
  other arithmetic  34.1 us (7%)
  between operations  14.3 us (3%)
  matrix products  13.7 us (3%)
    psum x1, waiting for transfers between devices, per_device(): summed = lax.psum(spread.astype(jnp.bfloat16), 'head').astype(jnp.float32)  181 us
    ppermute x12, waiting for transfers between devices, shifted_2(): lax.ppermute(value, axis, [(source, source + steps) for source in range(l...  128 us
    ppermute x12, starting transfers between devices, shifted_2(): lax.ppermute(value, axis, [(source, source + steps) for source in range(l...  56.8 us
    scatter-add x4, other arithmetic, accumulate(): running = running.at[:, slot_pair.reshape(-1)].add(stacked)  25.8 us
  transfers between devices with their start and end apart: 13, of which 13 were waited for; matrix products, arithmetic and copies ran while one was open for 1% of the time, Pallas kernels for 0%

commit v1 on v0

--- a/solution.py
+++ b/solution.py
@@ -1,6 +1,8 @@
 import jax
 import jax.numpy as jnp
+import numpy as np
 from jax import lax
+from jax.sharding import Mesh
 from jax.sharding import PartitionSpec as P
 
 HPG = 16
@@ -51,23 +53,27 @@
     tokens_here, heads_here, width = queries.shape
     groups = key_rows.shape[0]
     blocks_here = tokens_here // BLOCK
-    members = HPG // heads_here
     reach_span = REACH + 1
     inv_root = width ** (-0.5)
     ctx_index = lax.axis_index("ctx")
-    group_index = lax.axis_index("head") // members
+    group_index = lax.axis_index("grp")
+    part_index = lax.axis_index("sub")
+    parts_count = lax.axis_size("sub")
+    quarter = tokens_here // parts_count
     own_tiles = jnp.stack(
         [
             lax.dynamic_index_in_dim(key_rows, group_index, 0, keepdims=False),
             lax.dynamic_index_in_dim(value_rows, group_index, 0, keepdims=False),
         ]
     )
-    fetched = [own_tiles]
-    moving = own_tiles
+    own_part = lax.dynamic_slice_in_dim(own_tiles, part_index * quarter, quarter, axis=1)
+    fetched = []
+    moving = own_part
     for offset in range(REACH):
         moving = shifted_2(moving, "ctx", 1)
         fetched.append(moving)
-    tile_store = jnp.stack(fetched)
+    gathered = lax.all_gather(jnp.stack(fetched), "sub", axis=2, tiled=True)
+    tile_store = jnp.concatenate([own_tiles[None], gathered], axis=0)
     key_tiles = tile_store[:, 0].reshape(reach_span * blocks_here, BLOCK, width)
     value_tiles = tile_store[:, 1].reshape(reach_span * blocks_here, BLOCK, width)
     chosen = lax.dynamic_index_in_dim(selected, group_index, 1, keepdims=False)
@@ -100,33 +106,41 @@
         block_ids.reshape(pair_count, 2),
     )
     grads, query_parts = lax.scan(accumulate, initial, inputs)
-    parts = grads.reshape(2, reach_span, tokens_here, width)
+    grads = grads.reshape(2, reach_span, tokens_here, width)
+    parts = lax.psum_scatter(
+        grads.astype(jnp.bfloat16), "sub", scatter_dimension=2, tiled=True
+    ).astype(jnp.float32)
     running = parts[:, REACH]
     for offset in range(REACH - 1, -1, -1):
         running = (
             shifted_2(running.astype(jnp.bfloat16), "ctx", -1).astype(running.dtype)
             + parts[:, offset]
         )
-    spread = jnp.where(
-        (jnp.arange(groups) == group_index)[None, :, None, None], running[:, None], 0.0
-    )
-    summed = lax.psum(spread.astype(jnp.bfloat16), "head").astype(jnp.float32)
+    summed = lax.all_gather(running.astype(jnp.bfloat16), ("grp", "sub"), axis=1, tiled=True)
+    summed = summed.astype(jnp.float32).reshape(2, groups, tokens_here, width)
     query_grad = query_parts.reshape(tokens_here, heads_here, width)
     return (query_grad, summed[0], summed[1])
 
 
 def solution(mesh):
+    ctx_count, head_count = mesh.devices.shape
+    groups = 4
+    split = Mesh(
+        np.asarray(mesh.devices).reshape(ctx_count, groups, head_count // groups),
+        ("ctx", "grp", "sub"),
+    )
+    heads = ("grp", "sub")
     return jax.shard_map(
         per_device,
-        mesh=mesh,
+        mesh=split,
         in_specs=(
-            P("ctx", "head", None),
+            P("ctx", heads, None),
             P(None, "ctx", None),
             P(None, "ctx", None),
-            P("ctx", "head", None),
+            P("ctx", heads, None),
             P("ctx", None, None),
             P("ctx", None, None),
         ),
-        out_specs=(P("ctx", "head", None), P(None, "ctx", None), P(None, "ctx", None)),
+        out_specs=(P("ctx", heads, None), P(None, "ctx", None), P(None, "ctx", None)),
         check_vma=False,
     )

time: 465 us -> 385 us (0.83)
  waiting for transfers between devices: 309 us -> 217 us
  starting transfers between devices: 56.9 us -> 62.6 us
    psum x1 -> x0, waiting for transfers between devices: 181 us -> none  [per_device(): summed = lax.psum(spread.astype(jnp.bfloat16), 'head').astype(jnp.float32)]
    all_gather x0 -> x2, waiting for transfers between devices: none -> 113 us  [the longest x1 82.9 us: per_device(): lax.all_gather(running.astype(jnp.bfloat16), ('grp', 'sub'), axis=1, tile...]
    ppermute x12, waiting for transfers between devices: 128 us -> 68.8 us  [shifted_2(): lax.ppermute(value, axis, [(source, source + steps) for source in range(l...]
    reduce_scatter x0 -> x1, waiting for transfers between devices: none -> 35.5 us  [per_device(): lax.psum_scatter(grads.astype(jnp.bfloat16), 'sub', scatter_dimension=2,...]
    ppermute x12, starting transfers between devices: 56.8 us -> 62.4 us  [shifted_2(): lax.ppermute(value, axis, [(source, source + steps) for source in range(l...]
  transfers between devices with their start and end apart: 13 -> 15, of which waited for: 13 -> 15; matrix products, arithmetic and copies ran while one was open for 1% -> 1% of each run, Pallas kernels for 0% -> 0%
where the time goes in v1:
time: 385 us; the launch traced here: 384 us
  waiting for transfers between devices  217 us (56%)
  starting transfers between devices  62.6 us (16%)
  other arithmetic  38.4 us (10%)
  local copies, waits for them, and re-layouts  37.2 us (10%)
  between operations  14 us (4%)
  matrix products  13.7 us (4%)
    all_gather x1, waiting for transfers between devices, per_device(): lax.all_gather(running.astype(jnp.bfloat16), ('grp', 'sub'), axis=1, tile...  82.9 us
    ppermute x12, waiting for transfers between devices, shifted_2(): lax.ppermute(value, axis, [(source, source + steps) for source in range(l...  68.8 us
    ppermute x12, starting transfers between devices, shifted_2(): lax.ppermute(value, axis, [(source, source + steps) for source in range(l...  62.4 us
    reduce_scatter x1, waiting for transfers between devices, per_device(): lax.psum_scatter(grads.astype(jnp.bfloat16), 'sub', scatter_dimension=2,...  35.5 us
    all_gather x1, waiting for transfers between devices, per_device(): gathered = lax.all_gather(jnp.stack(fetched), 'sub', axis=2, tiled=True)  30.1 us
    scatter-add x4, other arithmetic, accumulate(): running = running.at[:, slot_pair.reshape(-1)].add(stacked)  25.7 us
  transfers between devices with their start and end apart: 15, of which 15 were waited for; matrix products, arithmetic and copies ran while one was open for 1% of the time, Pallas kernels for 0%

profile of v1, /device:TPU:6, one launch (start us, length us, event | category | flops | bytes accessed | tf_op | source)
XLA Modules:
  0.0 383.6 jit_solution(13902312137235017498)
XLA Ops:
  7.2 1.0 constant_dynamic-slice_fusion.6
  8.2 1.9 collective-permute-start
  10.2 12.8 %collective-permute-done = bf16[2,128,128]{2,1,0:T(8,128)(2,1)S(1)} collective-permute-done((bf16[2,128,128]{2,1,0:T(8,128)(2,1)S(1)}, bf16[2,128,128]{2,1,0:T(8,128)(2,1)S(1)}, u32[]{:S(2)}, u32[]{:S(2)}) %collective-permute-start) | collective-permute-done | bytes 65568 | tf_op jit(solution)/shard_map/ppermute | solution.py:16
  22.9 1.9 collective-permute-start.1
  24.8 8.6 %collective-permute-done.1 = bf16[2,128,128]{2,1,0:T(8,128)(2,1)S(1)} collective-permute-done((bf16[2,128,128]{2,1,0:T(8,128)(2,1)S(1)}, bf16[2,128,128]{2,1,0:T(8,128)(2,1)S(1)}, u32[]{:S(2)}, u32[]{:S(2)}) %collective-permute-start.1) | collective-permute-done | bytes 65568 | tf_op jit(solution)/shard_map/ppermute | solution.py:16
  33.4 1.9 collective-permute-start.2
  35.4 8.4 %collective-permute-done.2 = bf16[2,128,128]{2,1,0:T(8,128)(2,1)S(1)} collective-permute-done((bf16[2,128,128]{2,1,0:T(8,128)(2,1)S(1)}, bf16[2,128,128]{2,1,0:T(8,128)(2,1)S(1)}, u32[]{:S(2)}, u32[]{:S(2)}) %collective-permute-start.2) | collective-permute-done | bytes 65568 | tf_op jit(solution)/shard_map/ppermute | solution.py:16
  43.8 1.9 collective-permute-start.3
  45.7 8.4 %collective-permute-done.3 = bf16[2,128,128]{2,1,0:T(8,128)(2,1)S(1)} collective-permute-done((bf16[2,128,128]{2,1,0:T(8,128)(2,1)S(1)}, bf16[2,128,128]{2,1,0:T(8,128)(2,1)S(1)}, u32[]{:S(2)}, u32[]{:S(2)}) %collective-permute-start.3) | collective-permute-done | bytes 65568 | tf_op jit(solution)/shard_map/ppermute | solution.py:16
  54.2 1.9 collective-permute-start.4
  56.1 8.4 %collective-permute-done.4 = bf16[2,128,128]{2,1,0:T(8,128)(2,1)S(1)} collective-permute-done((bf16[2,128,128]{2,1,0:T(8,128)(2,1)S(1)}, bf16[2,128,128]{2,1,0:T(8,128)(2,1)S(1)}, u32[]{:S(2)}, u32[]{:S(2)}) %collective-permute-start.4) | collective-permute-done | bytes 65568 | tf_op jit(solution)/shard_map/ppermute | solution.py:16
  64.6 1.9 collective-permute-start.5
  66.5 8.4 %collective-permute-done.5 = bf16[2,128,128]{2,1,0:T(8,128)(2,1)S(1)} collective-permute-done((bf16[2,128,128]{2,1,0:T(8,128)(2,1)S(1)}, bf16[2,128,128]{2,1,0:T(8,128)(2,1)S(1)}, u32[]{:S(2)}, u32[]{:S(2)}) %collective-permute-start.5) | collective-permute-done | bytes 65568 | tf_op jit(solution)/shard_map/ppermute | solution.py:16
  75.0 0.7 copy-done
  76.3 0.7 constant_dynamic-slice_fusion.8
  77.2 30.1 %all-gather.3.cloned.1.call-done = bf16[6,2,512,128]{3,2,1,0:T(8,128)(2,1)} async-done(((bf16[6,2,128,128]{3,2,1,0:T(8,128)(2,1)}), bf16[6,2,512,128]{3,2,1,0:T(8,128)(2,1)}) %all-gather.3.cloned.1.call-update) | async-done | bytes 1572880 | tf_op jit(solution)/shard_map/all_gather | solution.py:75
  107.2 2.8 pad_maximum_fusion
  110.0 2.3 broadcast_in_dim.21
  112.2 72.4 %while.12 = (s32[]{:T(128)}, f32[2,56,64,128]{3,2,1,0:T(8,128)}, bf16[4,2,64,4,128]{4,3,2,1,0:T(4,128)(2,1)}, s32[4,2,16]{2,1,0:T(2,128)S(1)}, s32[4,2,16]{2,1,0...) while((s32[]{:T(128)}, f32[2,56,64,128]{3,2,1,0:T(8,128)}, ...), condition=%wide.region_5.6_spmd, body=%wide.region_0.5_spmd.sunk | while | flops 812455680 | bytes 31498952 | solution.py:108
  112.2 0.6 fusion.76
  114.4 1.1 constant_dynamic-slice_fusion.12
  115.5 1.8 gather_fusion.1
  117.3 1.8 gather_fusion
  119.1 0.9 fusion.78
  123.1 0.8 copy_dynamic-update-slice_fusion.2
  123.9 6.3 %scatter_fusion = f32[2,56,64,128]{3,2,1,0:T(8,128)} fusion(f32[2,56,64,128]{3,2,1,0:T(8,128)} %get-tuple-element.202, s32[32]{0:T(128)S(1)} %copy-done.1, f32[32,2,64,128]{3,2,1,0:T(8,128)S(1)} %maximum_bitcast_fusion.2), kind=kCustom, calls=%fused_computation.2.clone.1 | custom fusion | flops 524288 | bytes 6291584 | tf_op jit(solution)/shard_map/while/body/eval_jaxpr/scatter-add | solution.py:96
  132.3 1.1 constant_dynamic-slice_fusion.12
  133.4 1.8 gather_fusion.1
  135.2 1.8 gather_fusion
  137.1 0.9 fusion.78
  141.1 0.8 copy_dynamic-update-slice_fusion.2
  141.8 6.3 %scatter_fusion = f32[2,56,64,128]{3,2,1,0:T(8,128)} fusion(f32[2,56,64,128]{3,2,1,0:T(8,128)} %get-tuple-element.202, s32[32]{0:T(128)S(1)} %copy-done.1, f32[32,2,64,128]{3,2,1,0:T(8,128)S(1)} %maximum_bitcast_fusion.2), kind=kCustom, calls=%fused_computation.2.clone.1 | custom fusion | flops 524288 | bytes 6291584 | tf_op jit(solution)/shard_map/while/body/eval_jaxpr/scatter-add | solution.py:96
  150.3 1.1 constant_dynamic-slice_fusion.12
  151.4 1.8 gather_fusion.1
  153.2 1.8 gather_fusion
  155.1 0.9 fusion.78
  159.1 0.8 copy_dynamic-update-slice_fusion.2
  159.8 6.4 %scatter_fusion = f32[2,56,64,128]{3,2,1,0:T(8,128)} fusion(f32[2,56,64,128]{3,2,1,0:T(8,128)} %get-tuple-element.202, s32[32]{0:T(128)S(1)} %copy-done.1, f32[32,2,64,128]{3,2,1,0:T(8,128)S(1)} %maximum_bitcast_fusion.2), kind=kCustom, calls=%fused_computation.2.clone.1 | custom fusion | flops 524288 | bytes 6291584 | tf_op jit(solution)/shard_map/while/body/eval_jaxpr/scatter-add | solution.py:96
  168.4 1.1 constant_dynamic-slice_fusion.12
  169.5 1.8 gather_fusion.1
  171.3 1.8 gather_fusion
  173.1 0.9 fusion.78
  177.1 0.8 copy_dynamic-update-slice_fusion.2
  177.9 6.7 %scatter_fusion = f32[2,56,64,128]{3,2,1,0:T(8,128)} fusion(f32[2,56,64,128]{3,2,1,0:T(8,128)} %get-tuple-element.202, s32[32]{0:T(128)S(1)} %copy-done.1, f32[32,2,64,128]{3,2,1,0:T(8,128)S(1)} %maximum_bitcast_fusion.2), kind=kCustom, calls=%fused_computation.2.clone.1 | custom fusion | flops 524288 | bytes 6291584 | tf_op jit(solution)/shard_map/while/body/eval_jaxpr/scatter-add | solution.py:96
  184.6 2.4 convert_element_type.67
  187.1 1.4 copy.24
  188.5 35.5 %reduce-scatter.2.cloned.1.call-done = bf16[2,7,128,128]{3,2,0,1:T(8,128)(2,1)} async-done(((bf16[2,7,512,128]{3,2,0,1:T(8,128)(2,1)}), bf16[2,7,128,128]{3,2,0,1:T(8,128)(2,1)}) %reduce-scatter.2.cloned.1.call-update) | async-done | bytes 458768 | tf_op jit(solution)/shard_map/reduce_scatter | solution.py:110
  224.1 0.8 slice_bitcast_fusion.6
  224.9 8.1 %collective-permute-start.6 = (bf16[2,128,128]{2,1,0:T(8,128)(2,1)S(1)}, bf16[2,128,128]{2,1,0:T(8,128)(2,1)S(1)}, u32[]{:S(2)}, u32[]{:S(2)}) collective-permute-start(bf16[2,128,128]{2,1,0:T(8,128)(2,1)S(1)} %slice_bitcast_fusion.6), channel_id=1, source_target_pairs={{16,0},{32,16},{48,32},{64,48},{80,64},{96,80},{112,96},{128,112},... | collective-permute-start | bytes 196616 | tf_op jit(solution)/shard_map/ppermute | solution.py:16
  233.1 1.1 convert_element_type.71
  234.2 2.8 collective-permute-done.6
  237.0 8.6 %collective-permute-start.7 = (bf16[2,128,128]{2,1,0:T(8,128)(2,1)S(1)}, bf16[2,128,128]{2,1,0:T(8,128)(2,1)S(1)}, u32[]{:S(2)}, u32[]{:S(2)}) collective-permute-start(bf16[2,128,128]{2,1,0:T(8,128)(2,1)S(1)} %fusion.36), channel_id=1, source_target_pairs={{16,0},{32,16},{48,32},{64,48},{80,64},{96,80},{112,96},{128,112},... | collective-permute-start | bytes 196616 | tf_op jit(solution)/shard_map/ppermute | solution.py:16
  245.6 2.8 collective-permute-done.7
  248.4 8.6 %collective-permute-start.8 = (bf16[2,128,128]{2,1,0:T(8,128)(2,1)S(1)}, bf16[2,128,128]{2,1,0:T(8,128)(2,1)S(1)}, u32[]{:S(2)}, u32[]{:S(2)}) collective-permute-start(bf16[2,128,128]{2,1,0:T(8,128)(2,1)S(1)} %fusion.34), channel_id=1, source_target_pairs={{16,0},{32,16},{48,32},{64,48},{80,64},{96,80},{112,96},{128,112},... | collective-permute-start | bytes 196616 | tf_op jit(solution)/shard_map/ppermute | solution.py:16
  257.0 2.4 collective-permute-done.8
  259.4 8.6 %collective-permute-start.9 = (bf16[2,128,128]{2,1,0:T(8,128)(2,1)S(1)}, bf16[2,128,128]{2,1,0:T(8,128)(2,1)S(1)}, u32[]{:S(2)}, u32[]{:S(2)}) collective-permute-start(bf16[2,128,128]{2,1,0:T(8,128)(2,1)S(1)} %fusion.32), channel_id=1, source_target_pairs={{16,0},{32,16},{48,32},{64,48},{80,64},{96,80},{112,96},{128,112},... | collective-permute-start | bytes 196616 | tf_op jit(solution)/shard_map/ppermute | solution.py:16
  268.0 1.9 collective-permute-done.9
  269.9 8.6 %collective-permute-start.10 = (bf16[2,128,128]{2,1,0:T(8,128)(2,1)S(1)}, bf16[2,128,128]{2,1,0:T(8,128)(2,1)S(1)}, u32[]{:S(2)}, u32[]{:S(2)}) collective-permute-start(bf16[2,128,128]{2,1,0:T(8,128)(2,1)S(1)} %fusion.30), channel_id=1, source_target_pairs={{16,0},{32,16},{48,32},{64,48},{80,64},{96,80},{112,96},{128,112},... | collective-permute-start | bytes 196616 | tf_op jit(solution)/shard_map/ppermute | solution.py:16
  278.5 1.9 collective-permute-done.10
  280.4 8.5 %collective-permute-start.11 = (bf16[2,128,128]{2,1,0:T(8,128)(2,1)S(1)}, bf16[2,128,128]{2,1,0:T(8,128)(2,1)S(1)}, u32[]{:S(2)}, u32[]{:S(2)}) collective-permute-start(bf16[2,128,128]{2,1,0:T(8,128)(2,1)S(1)} %fusion.28), channel_id=1, source_target_pairs={{16,0},{32,16},{48,32},{64,48},{80,64},{96,80},{112,96},{128,112},... | collective-permute-start | bytes 196616 | tf_op jit(solution)/shard_map/ppermute | solution.py:16
  288.9 1.9 collective-permute-done.11
  290.8 0.6 fusion.26
  291.5 82.9 %all-gather.5.cloned.1.call-done = bf16[2,2048,128]{2,1,0:T(8,128)(2,1)} async-done(((bf16[2,128,128]{2,1,0:T(8,128)(2,1)}), bf16[2,2048,128]{2,1,0:T(8,128)(2,1)}) %all-gather.5.cloned.1.call-update) | async-done | bytes 1048592 | tf_op jit(solution)/shard_map/all_gather | solution.py:119
  374.4 2.7 fusion.40
  (122 shorter events, 21.0 us)
Async XLA Ops:
  7.2 100.1 %all-gather.3.cloned.1.call-start = ((), (), s32[]{:S(2)}) async-start(), calls=%async_computation.1 | async-start | bytes 1966080 | tf_op jit(solution)/shard_map/all_gather | solution.py:75
  8.2 14.7 %collective-permute-start = (bf16[2,128,128]{2,1,0:T(8,128)(2,1)S(1)}, bf16[2,128,128]{2,1,0:T(8,128)(2,1)S(1)}, u32[]{:S(2)}, u32[]{:S(2)}) collective-permute-start(bf16[2,128,128]{2,1,0:T(8,128)(2,1)S(1)} %fusion.37), channel_id=1, source_target_pairs={{0,16},{16,32},{32,48},{48,64},{64,80},{80,96},{96,112},{112,128},... | collective-permute-start | bytes 196616 | tf_op jit(solution)/shard_map/ppermute | solution.py:16
  22.9 10.5 %collective-permute-start.1 = (bf16[2,128,128]{2,1,0:T(8,128)(2,1)S(1)}, bf16[2,128,128]{2,1,0:T(8,128)(2,1)S(1)}, u32[]{:S(2)}, u32[]{:S(2)}) collective-permute-start(bf16[2,128,128]{2,1,0:T(8,128)(2,1)S(1)} %collective-permute-done), channel_id=1, source_target_pairs={{0,16},{16,32},{32,48},{48,64},{64,80},{80,96},{96,112},{112,128},... | collective-permute-start | bytes 196616 | tf_op jit(solution)/shard_map/ppermute | solution.py:16
  33.4 10.4 %collective-permute-start.2 = (bf16[2,128,128]{2,1,0:T(8,128)(2,1)S(1)}, bf16[2,128,128]{2,1,0:T(8,128)(2,1)S(1)}, u32[]{:S(2)}, u32[]{:S(2)}) collective-permute-start(bf16[2,128,128]{2,1,0:T(8,128)(2,1)S(1)} %collective-permute-done.1), channel_id=1, source_target_pairs={{0,16},{16,32},{32,48},{48,64},{64,80},{80,96},{96,112},{112,128},... | collective-permute-start | bytes 196616 | tf_op jit(solution)/shard_map/ppermute | solution.py:16
  43.8 10.4 %collective-permute-start.3 = (bf16[2,128,128]{2,1,0:T(8,128)(2,1)S(1)}, bf16[2,128,128]{2,1,0:T(8,128)(2,1)S(1)}, u32[]{:S(2)}, u32[]{:S(2)}) collective-permute-start(bf16[2,128,128]{2,1,0:T(8,128)(2,1)S(1)} %collective-permute-done.2), channel_id=1, source_target_pairs={{0,16},{16,32},{32,48},{48,64},{64,80},{80,96},{96,112},{112,128},... | collective-permute-start | bytes 196616 | tf_op jit(solution)/shard_map/ppermute | solution.py:16
  54.2 10.4 %collective-permute-start.4 = (bf16[2,128,128]{2,1,0:T(8,128)(2,1)S(1)}, bf16[2,128,128]{2,1,0:T(8,128)(2,1)S(1)}, u32[]{:S(2)}, u32[]{:S(2)}) collective-permute-start(bf16[2,128,128]{2,1,0:T(8,128)(2,1)S(1)} %collective-permute-done.3), channel_id=1, source_target_pairs={{0,16},{16,32},{32,48},{48,64},{64,80},{80,96},{96,112},{112,128},... | collective-permute-start | bytes 196616 | tf_op jit(solution)/shard_map/ppermute | solution.py:16
  64.6 10.4 %collective-permute-start.5 = (bf16[2,128,128]{2,1,0:T(8,128)(2,1)S(1)}, bf16[2,128,128]{2,1,0:T(8,128)(2,1)S(1)}, u32[]{:S(2)}, u32[]{:S(2)}) collective-permute-start(bf16[2,128,128]{2,1,0:T(8,128)(2,1)S(1)} %collective-permute-done.4), channel_id=1, source_target_pairs={{0,16},{16,32},{32,48},{48,64},{64,80},{80,96},{96,112},{112,128},... | collective-permute-start | bytes 196616 | tf_op jit(solution)/shard_map/ppermute | solution.py:16
  75.0 0.7 copy-start
  75.7 148.3 %reduce-scatter.2.cloned.1.call-start = ((), (), s32[]{:S(2)}) async-start(), calls=%async_computation.2 | async-start | bytes 2293760 | tf_op jit(solution)/shard_map/reduce_scatter | solution.py:110
  122.9 1.0 copy-start.1
  140.8 1.0 copy-start.1
  158.8 1.0 copy-start.1
  176.9 1.0 copy-start.1
  188.5 185.9 %all-gather.5.cloned.1.call-start = ((), (), s32[]{:S(2)}) async-start(), calls=%async_computation.3 | async-start | bytes 1114112 | tf_op jit(solution)/shard_map/all_gather | solution.py:119
  224.9 12.0 %collective-permute-start.6 = (bf16[2,128,128]{2,1,0:T(8,128)(2,1)S(1)}, bf16[2,128,128]{2,1,0:T(8,128)(2,1)S(1)}, u32[]{:S(2)}, u32[]{:S(2)}) collective-permute-start(bf16[2,128,128]{2,1,0:T(8,128)(2,1)S(1)} %slice_bitcast_fusion.6), channel_id=1, source_target_pairs={{16,0},{32,16},{48,32},{64,48},{80,64},{96,80},{112,96},{128,112},... | collective-permute-start | bytes 196616 | tf_op jit(solution)/shard_map/ppermute | solution.py:16
  237.0 11.4 %collective-permute-start.7 = (bf16[2,128,128]{2,1,0:T(8,128)(2,1)S(1)}, bf16[2,128,128]{2,1,0:T(8,128)(2,1)S(1)}, u32[]{:S(2)}, u32[]{:S(2)}) collective-permute-start(bf16[2,128,128]{2,1,0:T(8,128)(2,1)S(1)} %fusion.36), channel_id=1, source_target_pairs={{16,0},{32,16},{48,32},{64,48},{80,64},{96,80},{112,96},{128,112},... | collective-permute-start | bytes 196616 | tf_op jit(solution)/shard_map/ppermute | solution.py:16
  248.4 11.0 %collective-permute-start.8 = (bf16[2,128,128]{2,1,0:T(8,128)(2,1)S(1)}, bf16[2,128,128]{2,1,0:T(8,128)(2,1)S(1)}, u32[]{:S(2)}, u32[]{:S(2)}) collective-permute-start(bf16[2,128,128]{2,1,0:T(8,128)(2,1)S(1)} %fusion.34), channel_id=1, source_target_pairs={{16,0},{32,16},{48,32},{64,48},{80,64},{96,80},{112,96},{128,112},... | collective-permute-start | bytes 196616 | tf_op jit(solution)/shard_map/ppermute | solution.py:16
  259.4 10.5 %collective-permute-start.9 = (bf16[2,128,128]{2,1,0:T(8,128)(2,1)S(1)}, bf16[2,128,128]{2,1,0:T(8,128)(2,1)S(1)}, u32[]{:S(2)}, u32[]{:S(2)}) collective-permute-start(bf16[2,128,128]{2,1,0:T(8,128)(2,1)S(1)} %fusion.32), channel_id=1, source_target_pairs={{16,0},{32,16},{48,32},{64,48},{80,64},{96,80},{112,96},{128,112},... | collective-permute-start | bytes 196616 | tf_op jit(solution)/shard_map/ppermute | solution.py:16
  269.9 10.5 %collective-permute-start.10 = (bf16[2,128,128]{2,1,0:T(8,128)(2,1)S(1)}, bf16[2,128,128]{2,1,0:T(8,128)(2,1)S(1)}, u32[]{:S(2)}, u32[]{:S(2)}) collective-permute-start(bf16[2,128,128]{2,1,0:T(8,128)(2,1)S(1)} %fusion.30), channel_id=1, source_target_pairs={{16,0},{32,16},{48,32},{64,48},{80,64},{96,80},{112,96},{128,112},... | collective-permute-start | bytes 196616 | tf_op jit(solution)/shard_map/ppermute | solution.py:16
  280.4 10.4 %collective-permute-start.11 = (bf16[2,128,128]{2,1,0:T(8,128)(2,1)S(1)}, bf16[2,128,128]{2,1,0:T(8,128)(2,1)S(1)}, u32[]{:S(2)}, u32[]{:S(2)}) collective-permute-start(bf16[2,128,128]{2,1,0:T(8,128)(2,1)S(1)} %fusion.28), channel_id=1, source_target_pairs={{16,0},{32,16},{48,32},{64,48},{80,64},{96,80},{112,96},{128,112},... | collective-permute-start | bytes 196616 | tf_op jit(solution)/shard_map/ppermute | solution.py:16
Sparse Core Ops, SparseCore 0:
  75.9 31.3 all-gather.2
  188.6 35.4 reduce-scatter.1
  291.6 82.7 all-gather.4

commit v2 on v1

--- a/solution.py
+++ b/solution.py
@@ -14,6 +14,11 @@
     count = lax.axis_size(axis)
     leading, last = (max(0, -steps), min(count, count - steps))
     return lax.ppermute(value, axis, [(source, source + steps) for source in range(leading, last)])
+
+
+def cycled(value, axis, steps):
+    count = lax.axis_size(axis)
+    return lax.ppermute(value, axis, [(source, (source + steps) % count) for source in range(count)])
 
 
 def visible_mask(chosen, live_mask, block_id, width):
@@ -66,20 +71,20 @@
             lax.dynamic_index_in_dim(value_rows, group_index, 0, keepdims=False),
         ]
     )
-    own_part = lax.dynamic_slice_in_dim(own_tiles, part_index * quarter, quarter, axis=1)
-    fetched = []
-    moving = own_part
-    for offset in range(REACH):
-        moving = shifted_2(moving, "ctx", 1)
-        fetched.append(moving)
-    gathered = lax.all_gather(jnp.stack(fetched), "sub", axis=2, tiled=True)
-    tile_store = jnp.concatenate([own_tiles[None], gathered], axis=0)
+    rolled = jnp.roll(own_tiles, -part_index * quarter, axis=1)
+    own_part = rolled[:, :quarter]
+    fetched = jnp.stack([shifted_2(own_part, "ctx", offset) for offset in range(1, reach_span)])
+    pieces = [fetched] + [cycled(fetched, "sub", -step) for step in range(1, parts_count)]
+    tile_store = jnp.concatenate([rolled[None], jnp.concatenate(pieces, axis=2)], axis=0)
     key_tiles = tile_store[:, 0].reshape(reach_span * blocks_here, BLOCK, width)
     value_tiles = tile_store[:, 1].reshape(reach_span * blocks_here, BLOCK, width)
     chosen = lax.dynamic_index_in_dim(selected, group_index, 1, keepdims=False)
     live_mask = lax.dynamic_index_in_dim(live_slots, group_index, 1, keepdims=False)
     block_ids = ctx_index * blocks_here + jnp.arange(blocks_here, dtype=jnp.int32)
-    slot_index = (ctx_index - chosen // blocks_here) * blocks_here + chosen % blocks_here
+    local_block = chosen % blocks_here
+    per_part = blocks_here // parts_count
+    rolled_block = (local_block // per_part - part_index) % parts_count * per_part + local_block % per_part
+    slot_index = (ctx_index - chosen // blocks_here) * blocks_here + rolled_block
     pair_count = blocks_here // 2
 
     def accumulate(running, inputs):
@@ -107,17 +112,24 @@
     )
     grads, query_parts = lax.scan(accumulate, initial, inputs)
     grads = grads.reshape(2, reach_span, tokens_here, width)
-    parts = lax.psum_scatter(
-        grads.astype(jnp.bfloat16), "sub", scatter_dimension=2, tiled=True
-    ).astype(jnp.float32)
-    running = parts[:, REACH]
-    for offset in range(REACH - 1, -1, -1):
-        running = (
-            shifted_2(running.astype(jnp.bfloat16), "ctx", -1).astype(running.dtype)
-            + parts[:, offset]
-        )
-    summed = lax.all_gather(running.astype(jnp.bfloat16), ("grp", "sub"), axis=1, tiled=True)
-    summed = summed.astype(jnp.float32).reshape(2, groups, tokens_here, width)
+    sent = grads.astype(jnp.bfloat16)
+    parts = grads[:, :, :quarter]
+    for step in range(1, parts_count):
+        piece = sent[:, :, step * quarter:(step + 1) * quarter]
+        parts = parts + cycled(piece, "sub", step).astype(jnp.float32)
+    running = parts[:, 0]
+    for offset in range(1, reach_span):
+        running = running + shifted_2(
+            parts[:, offset].astype(jnp.bfloat16), "ctx", -offset
+        ).astype(jnp.float32)
+    mine = running.astype(jnp.bfloat16)
+    by_part = jnp.stack([mine] + [cycled(mine, "sub", -step) for step in range(1, parts_count)])
+    by_group = jnp.stack([by_part] + [cycled(by_part, "grp", -step) for step in range(1, groups)])
+    part_order = (jnp.arange(parts_count) - part_index) % parts_count
+    group_order = (jnp.arange(groups) - group_index) % groups
+    ordered = jnp.take(jnp.take(by_group, group_order, axis=0), part_order, axis=1)
+    summed = jnp.transpose(ordered, (2, 0, 1, 3, 4)).reshape(2, groups, tokens_here, width)
+    summed = summed.astype(jnp.float32)
     query_grad = query_parts.reshape(tokens_here, heads_here, width)
     return (query_grad, summed[0], summed[1])
 

time: 385 us -> 270 us (0.70)
  waiting for transfers between devices: 217 us -> 53.3 us
  starting transfers between devices: 62.6 us -> 123 us
  between operations: 14 us -> 1.11 us
    all_gather x2 -> x0, waiting for transfers between devices: 113 us -> none  [the longest x1 82.9 us: per_device(): lax.all_gather(running.astype(jnp.bfloat16), ('grp', 'sub'), axis=1, tile...]
    ppermute x0 -> x12, starting transfers between devices: none -> 46.1 us  [cycled(): lax.ppermute(value, axis, [(source, (source + steps) % count) for source...]
    ppermute x12, waiting for transfers between devices: 68.8 us -> 24.8 us  [shifted_2(): lax.ppermute(value, axis, [(source, source + steps) for source in range(l...]
    reduce_scatter x1 -> x0, waiting for transfers between devices: 35.5 us -> none  [per_device(): lax.psum_scatter(grads.astype(jnp.bfloat16), 'sub', scatter_dimension=2,...]
    ppermute x0 -> x12, waiting for transfers between devices: none -> 28.5 us  [cycled(): lax.ppermute(value, axis, [(source, (source + steps) % count) for source...]
    ppermute x12, starting transfers between devices: 62.4 us -> 77 us  [shifted_2(): lax.ppermute(value, axis, [(source, source + steps) for source in range(l...]
    convert_element_type x8 -> x2, other arithmetic: 4.27 us -> 0.28 us  [the longest x1 0.21 us: per_device(): summed = summed.astype(jnp.float32)]
  transfers between devices with their start and end apart: 15 -> 24, of which waited for: 15 -> 12; matrix products, arithmetic and copies ran while one was open for 1% -> 1% of each run, Pallas kernels for 0% -> 0%
where the time goes in v2:
time: 270 us; the launch traced here: 265 us
  starting transfers between devices  123 us (46%)
  waiting for transfers between devices  53.3 us (20%)
  local copies, waits for them, and re-layouts  38.9 us (14%)
  other arithmetic  35 us (13%)
  matrix products  13.7 us (5%)
    ppermute x12, starting transfers between devices, shifted_2(): lax.ppermute(value, axis, [(source, source + steps) for source in range(l...  77 us
    ppermute x12, starting transfers between devices, cycled(): lax.ppermute(value, axis, [(source, (source + steps) % count) for source...  46.1 us
    ppermute x12, waiting for transfers between devices, cycled(): lax.ppermute(value, axis, [(source, (source + steps) % count) for source...  28.5 us
    scatter-add x4, other arithmetic, accumulate(): running = running.at[:, slot_pair.reshape(-1)].add(stacked)  26.1 us
    ppermute x12, waiting for transfers between devices, shifted_2(): lax.ppermute(value, axis, [(source, source + steps) for source in range(l...  24.8 us
    gather x4, local copies, waits for them, and re-layouts, accumulate(): k_sel = key_tiles[slot_pair].reshape(2, -1, width)  7.31 us
    gather x4, local copies, waits for them, and re-layouts, accumulate(): v_sel = value_tiles[slot_pair].reshape(2, -1, width)  7.31 us
  transfers between devices with their start and end apart: 24, of which 12 were waited for; matrix products, arithmetic and copies ran while one was open for 1% of the time, Pallas kernels for 0%

profile of v2, /device:TPU:6, one launch (start us, length us, event | category | flops | bytes accessed | tf_op | source)
XLA Modules:
  0.0 265.4 jit_solution(14604304620797563282)
XLA Ops:
  0.7 1.0 constant_dynamic-slice_fusion.6
  2.1 12.7 %collective-permute-start.5 = (bf16[2,128,128]{2,1,0:T(8,128)(2,1)S(1)}, bf16[2,128,128]{2,1,0:T(8,128)(2,1)S(1)}, u32[]{:S(2)}, u32[]{:S(2)}) collective-permute-start(bf16[2,128,128]{2,1,0:T(8,128)(2,1)S(1)} %slice.80), channel_id=1, source_target_pairs={{0,96},{16,112},{32,128},{48,144},{64,160},{80,176},{96,192},{112,... | collective-permute-start | bytes 196616 | tf_op jit(solution)/shard_map/ppermute | solution.py:16
  14.9 3.7 %collective-permute-start.4 = (bf16[2,128,128]{2,1,0:T(8,128)(2,1)S(1)}, bf16[2,128,128]{2,1,0:T(8,128)(2,1)S(1)}, u32[]{:S(2)}, u32[]{:S(2)}) collective-permute-start(bf16[2,128,128]{2,1,0:T(8,128)(2,1)S(1)} %slice.80), channel_id=1, source_target_pairs={{0,80},{16,96},{32,112},{48,128},{64,144},{80,160},{96,176},{112,1... | collective-permute-start | bytes 196616 | tf_op jit(solution)/shard_map/ppermute | solution.py:16
  18.6 1.9 collective-permute-start.3
  20.5 3.4 %collective-permute-start.2 = (bf16[2,128,128]{2,1,0:T(8,128)(2,1)S(1)}, bf16[2,128,128]{2,1,0:T(8,128)(2,1)S(1)}, u32[]{:S(2)}, u32[]{:S(2)}) collective-permute-start(bf16[2,128,128]{2,1,0:T(8,128)(2,1)S(1)} %slice.80), channel_id=1, source_target_pairs={{0,48},{16,64},{32,80},{48,96},{64,112},{80,128},{96,144},{112,160... | collective-permute-start | bytes 196616 | tf_op jit(solution)/shard_map/ppermute | solution.py:16
  23.9 1.9 collective-permute-start
  26.6 11.9 %collective-permute-done = bf16[2,128,128]{2,1,0:T(8,128)(2,1)S(1)} collective-permute-done((bf16[2,128,128]{2,1,0:T(8,128)(2,1)S(1)}, bf16[2,128,128]{2,1,0:T(8,128)(2,1)S(1)}, u32[]{:S(2)}, u32[]{:S(2)}) %collective-permute-start) | collective-permute-done | bytes 65568 | tf_op jit(solution)/shard_map/ppermute | solution.py:16
  38.5 1.9 collective-permute-start.1
  40.4 10.5 %collective-permute-done.1 = bf16[2,128,128]{2,1,0:T(8,128)(2,1)S(1)} collective-permute-done((bf16[2,128,128]{2,1,0:T(8,128)(2,1)S(1)}, bf16[2,128,128]{2,1,0:T(8,128)(2,1)S(1)}, u32[]{:S(2)}, u32[]{:S(2)}) %collective-permute-start.1) | collective-permute-done | bytes 65568 | tf_op jit(solution)/shard_map/ppermute | solution.py:16
  51.1 3.5 %collective-permute-start.8 = (bf16[6,2,128,128]{3,2,1,0:T(8,128)(2,1)S(1)}, bf16[6,2,128,128]{3,2,1,0:T(8,128)(2,1)S(1)}, u32[]{:S(2)}, u32[]{:S(2)}) collective-permute-start(bf16[6,2,128,128]{3,2,1,0:T(8,128)(2,1)S(1)} %bitcast_dynamic-update-slice_fusion), channel_id=1, source_target_pairs={{0,1},{1,2},{2,3},{3,0},{4,5},{5,6},{6,7},{7,4},{8,9},{9,10},{10,1... | collective-permute-start | bytes 1179656 | tf_op jit(solution)/shard_map/ppermute | solution.py:21
  54.6 4.8 %collective-permute-start.7 = (bf16[6,2,128,128]{3,2,1,0:T(8,128)(2,1)S(1)}, bf16[6,2,128,128]{3,2,1,0:T(8,128)(2,1)S(1)}, u32[]{:S(2)}, u32[]{:S(2)}) collective-permute-start(bf16[6,2,128,128]{3,2,1,0:T(8,128)(2,1)S(1)} %bitcast_dynamic-update-slice_fusion), channel_id=1, source_target_pairs={{0,2},{1,3},{2,0},{3,1},{4,6},{5,7},{6,4},{7,5},{8,10},{9,11},{10,... | collective-permute-start | bytes 1179656 | tf_op jit(solution)/shard_map/ppermute | solution.py:21
  59.4 3.3 %collective-permute-start.6 = (bf16[6,2,128,128]{3,2,1,0:T(8,128)(2,1)S(1)}, bf16[6,2,128,128]{3,2,1,0:T(8,128)(2,1)S(1)}, u32[]{:S(2)}, u32[]{:S(2)}) collective-permute-start(bf16[6,2,128,128]{3,2,1,0:T(8,128)(2,1)S(1)} %bitcast_dynamic-update-slice_fusion), channel_id=1, source_target_pairs={{0,3},{1,0},{2,1},{3,2},{4,7},{5,4},{6,5},{7,6},{8,11},{9,8},{10,9... | collective-permute-start | bytes 1179656 | tf_op jit(solution)/shard_map/ppermute | solution.py:21
  63.8 3.6 %collective-permute-done.7 = bf16[6,2,128,128]{3,2,1,0:T(8,128)(2,1)S(1)} collective-permute-done((bf16[6,2,128,128]{3,2,1,0:T(8,128)(2,1)S(1)}, bf16[6,2,128,128]{3,2,1,0:T(8,128)(2,1)S(1)}, u32[]{:S(2)}, u32[]{:S(2)}) %collective-permute-start.7) | collective-permute-done | bytes 393248 | tf_op jit(solution)/shard_map/ppermute | solution.py:21
  67.4 1.6 collective-permute-done.6
  69.2 1.4 fusion.51
  70.6 2.3 broadcast_in_dim.55
  72.8 72.9 %while.12 = (s32[]{:T(128)}, f32[2,56,64,128]{3,2,1,0:T(8,128)}, bf16[4,2,64,4,128]{4,3,2,1,0:T(4,128)(2,1)}, s32[4,2,16]{2,1,0:T(2,128)S(1)}, s32[4,2,16]{2,1,0...) while((s32[]{:T(128)}, f32[2,56,64,128]{3,2,1,0:T(8,128)}, ...), condition=%wide.region_5.6_spmd, body=%wide.region_0.5_spmd.sunk | while | flops 812455680 | bytes 31498952 | solution.py:113
  75.1 1.1 constant_dynamic-slice_fusion.12
  76.1 1.8 gather_fusion.1
  78.0 1.8 gather_fusion
  79.8 0.9 fusion.94
  84.5 6.4 %scatter_fusion = f32[2,56,64,128]{3,2,1,0:T(8,128)} fusion(f32[2,56,64,128]{3,2,1,0:T(8,128)} %get-tuple-element.228, s32[32]{0:T(128)S(1)} %copy-done, f32[32,2,64,128]{3,2,1,0:T(8,128)S(1)} %maximum_bitcast_fusion.2), kind=kCustom, calls=%fused_computation.4.clone.1 | custom fusion | flops 524288 | bytes 6291584 | tf_op jit(solution)/shard_map/while/body/eval_jaxpr/scatter-add | solution.py:101
  93.1 1.1 constant_dynamic-slice_fusion.12
  94.2 1.8 gather_fusion.1
  96.0 1.8 gather_fusion
  97.9 0.9 fusion.94
  102.6 6.6 %scatter_fusion = f32[2,56,64,128]{3,2,1,0:T(8,128)} fusion(f32[2,56,64,128]{3,2,1,0:T(8,128)} %get-tuple-element.228, s32[32]{0:T(128)S(1)} %copy-done, f32[32,2,64,128]{3,2,1,0:T(8,128)S(1)} %maximum_bitcast_fusion.2), kind=kCustom, calls=%fused_computation.4.clone.1 | custom fusion | flops 524288 | bytes 6291584 | tf_op jit(solution)/shard_map/while/body/eval_jaxpr/scatter-add | solution.py:101
  111.4 1.1 constant_dynamic-slice_fusion.12
  112.4 1.8 gather_fusion.1
  114.3 1.8 gather_fusion
  116.1 0.9 fusion.94
  120.8 6.6 %scatter_fusion = f32[2,56,64,128]{3,2,1,0:T(8,128)} fusion(f32[2,56,64,128]{3,2,1,0:T(8,128)} %get-tuple-element.228, s32[32]{0:T(128)S(1)} %copy-done, f32[32,2,64,128]{3,2,1,0:T(8,128)S(1)} %maximum_bitcast_fusion.2), kind=kCustom, calls=%fused_computation.4.clone.1 | custom fusion | flops 524288 | bytes 6291584 | tf_op jit(solution)/shard_map/while/body/eval_jaxpr/scatter-add | solution.py:101
  129.6 1.1 constant_dynamic-slice_fusion.12
  130.7 1.8 gather_fusion.1
  132.5 1.8 gather_fusion
  134.3 0.9 fusion.94
  138.3 0.8 copy_dynamic-update-slice_fusion.2
  139.1 6.6 %scatter_fusion = f32[2,56,64,128]{3,2,1,0:T(8,128)} fusion(f32[2,56,64,128]{3,2,1,0:T(8,128)} %get-tuple-element.228, s32[32]{0:T(128)S(1)} %copy-done, f32[32,2,64,128]{3,2,1,0:T(8,128)S(1)} %maximum_bitcast_fusion.2), kind=kCustom, calls=%fused_computation.4.clone.1 | custom fusion | flops 524288 | bytes 6291584 | tf_op jit(solution)/shard_map/while/body/eval_jaxpr/scatter-add | solution.py:101
  145.7 2.0 fusion.50
  147.7 4.7 %collective-permute-start.9 = (bf16[2,7,128,128]{3,2,0,1:T(8,128)(2,1)S(1)}, bf16[2,7,128,128]{3,2,0,1:T(8,128)(2,1)S(1)}, u32[]{:S(2)}, u32[]{:S(2)}) collective-permute-start(bf16[2,7,128,128]{3,2,0,1:T(8,128)(2,1)S(1)} %get-tuple-element.117), channel_id=1, source_target_pairs={{0,1},{1,2},{2,3},{3,0},{4,5},{5,6},{6,7},{7,4},{8,9},{9,10},{10,1... | collective-permute-start | bytes 1376264 | tf_op jit(solution)/shard_map/ppermute | solution.py:21
  152.4 2.3 collective-permute-start.11
  154.8 4.0 %collective-permute-start.10 = (bf16[2,7,128,128]{3,2,0,1:T(8,128)(2,1)S(1)}, bf16[2,7,128,128]{3,2,0,1:T(8,128)(2,1)S(1)}, u32[]{:S(2)}, u32[]{:S(2)}) collective-permute-start(bf16[2,7,128,128]{3,2,0,1:T(8,128)(2,1)S(1)} %get-tuple-element.119), channel_id=1, source_target_pairs={{0,2},{1,3},{2,0},{3,1},{4,6},{5,7},{6,4},{7,5},{8,10},{9,11},{10,... | collective-permute-start | bytes 1376264 | tf_op jit(solution)/shard_map/ppermute | solution.py:21
  158.8 2.1 collective-permute-done.9
  160.9 1.9 collective-permute-done.11
  162.8 3.8 %collective-permute-done.10 = bf16[2,7,128,128]{3,2,0,1:T(8,128)(2,1)S(1)} collective-permute-done((bf16[2,7,128,128]{3,2,0,1:T(8,128)(2,1)S(1)}, bf16[2,7,128,128]{3,2,0,1:T(8,128)(2,1)S(1)}, u32[]{:S(2)}, u32[]{:S(2)}) %collective-permute-start.10) | collective-permute-done | bytes 458784 | tf_op jit(solution)/shard_map/ppermute | solution.py:21
  166.6 1.4 fusion.46
  168.1 1.9 collective-permute-start.12
  170.0 9.8 %collective-permute-start.17 = (bf16[2,128,128]{2,1,0:T(8,128)(2,1)S(1)}, bf16[2,128,128]{2,1,0:T(8,128)(2,1)S(1)}, u32[]{:S(2)}, u32[]{:S(2)}) collective-permute-start(bf16[2,128,128]{2,1,0:T(8,128)(2,1)S(1)} %get-tuple-element.123), channel_id=1, source_target_pairs={{96,0},{112,16},{128,32},{144,48},{160,64},{176,80},{192,96},{208,... | collective-permute-start | bytes 196616 | tf_op jit(solution)/shard_map/ppermute | solution.py:16
  179.9 7.5 %collective-permute-start.16 = (bf16[2,128,128]{2,1,0:T(8,128)(2,1)S(1)}, bf16[2,128,128]{2,1,0:T(8,128)(2,1)S(1)}, u32[]{:S(2)}, u32[]{:S(2)}) collective-permute-start(bf16[2,128,128]{2,1,0:T(8,128)(2,1)S(1)} %get-tuple-element.124), channel_id=1, source_target_pairs={{80,0},{96,16},{112,32},{128,48},{144,64},{160,80},{176,96},{192,1... | collective-permute-start | bytes 196616 | tf_op jit(solution)/shard_map/ppermute | solution.py:16
  187.4 14.0 %collective-permute-start.15 = (bf16[2,128,128]{2,1,0:T(8,128)(2,1)S(1)}, bf16[2,128,128]{2,1,0:T(8,128)(2,1)S(1)}, u32[]{:S(2)}, u32[]{:S(2)}) collective-permute-start(bf16[2,128,128]{2,1,0:T(8,128)(2,1)S(1)} %get-tuple-element.125), channel_id=1, source_target_pairs={{64,0},{80,16},{96,32},{112,48},{128,64},{144,80},{160,96},{176,11... | collective-permute-start | bytes 196616 | tf_op jit(solution)/shard_map/ppermute | solution.py:16
  201.4 9.4 %collective-permute-start.14 = (bf16[2,128,128]{2,1,0:T(8,128)(2,1)S(1)}, bf16[2,128,128]{2,1,0:T(8,128)(2,1)S(1)}, u32[]{:S(2)}, u32[]{:S(2)}) collective-permute-start(bf16[2,128,128]{2,1,0:T(8,128)(2,1)S(1)} %get-tuple-element.126), channel_id=1, source_target_pairs={{48,0},{64,16},{80,32},{96,48},{112,64},{128,80},{144,96},{160,112... | collective-permute-start | bytes 196616 | tf_op jit(solution)/shard_map/ppermute | solution.py:16
  210.8 8.8 %collective-permute-start.13 = (bf16[2,128,128]{2,1,0:T(8,128)(2,1)S(1)}, bf16[2,128,128]{2,1,0:T(8,128)(2,1)S(1)}, u32[]{:S(2)}, u32[]{:S(2)}) collective-permute-start(bf16[2,128,128]{2,1,0:T(8,128)(2,1)S(1)} %get-tuple-element.127), channel_id=1, source_target_pairs={{32,0},{48,16},{64,32},{80,48},{96,64},{112,80},{128,96},{144,112}... | collective-permute-start | bytes 196616 | tf_op jit(solution)/shard_map/ppermute | solution.py:16
  219.7 2.3 collective-permute-done.13
  222.1 5.7 %collective-permute-start.20 = (bf16[2,128,128]{2,1,0:T(8,128)(2,1)S(1)}, bf16[2,128,128]{2,1,0:T(8,128)(2,1)S(1)}, u32[]{:S(2)}, u32[]{:S(2)}) collective-permute-start(bf16[2,128,128]{2,1,0:T(8,128)(2,1)S(1)} %fusion.34), channel_id=1, source_target_pairs={{0,1},{1,2},{2,3},{3,0},{4,5},{5,6},{6,7},{7,4},{8,9},{9,10},{10,1... | collective-permute-start | bytes 196616 | tf_op jit(solution)/shard_map/ppermute | solution.py:21
  227.8 5.6 %collective-permute-start.19 = (bf16[2,128,128]{2,1,0:T(8,128)(2,1)S(1)}, bf16[2,128,128]{2,1,0:T(8,128)(2,1)S(1)}, u32[]{:S(2)}, u32[]{:S(2)}) collective-permute-start(bf16[2,128,128]{2,1,0:T(8,128)(2,1)S(1)} %fusion.34), channel_id=1, source_target_pairs={{0,2},{1,3},{2,0},{3,1},{4,6},{5,7},{6,4},{7,5},{8,10},{9,11},{10,... | collective-permute-start | bytes 196616 | tf_op jit(solution)/shard_map/ppermute | solution.py:21
  233.5 1.9 collective-permute-start.18
  235.7 3.9 %collective-permute-done.18 = bf16[2,128,128]{2,1,0:T(8,128)(2,1)S(1)} collective-permute-done((bf16[2,128,128]{2,1,0:T(8,128)(2,1)S(1)}, bf16[2,128,128]{2,1,0:T(8,128)(2,1)S(1)}, u32[]{:S(2)}, u32[]{:S(2)}) %collective-permute-start.18) | collective-permute-done | bytes 65568 | tf_op jit(solution)/shard_map/ppermute | solution.py:21
  239.7 4.3 %collective-permute-start.22 = (bf16[4,2,128,128]{3,2,1,0:T(8,128)(2,1)S(1)}, bf16[4,2,128,128]{3,2,1,0:T(8,128)(2,1)S(1)}, u32[]{:S(2)}, u32[]{:S(2)}) collective-permute-start(bf16[4,2,128,128]{3,2,1,0:T(8,128)(2,1)S(1)} %get-tuple-element.129), channel_id=1, source_target_pairs={{0,8},{4,12},{8,0},{12,4},{1,9},{5,13},{9,1},{13,5},{2,10},{6,14},... | collective-permute-start | bytes 786440 | tf_op jit(solution)/shard_map/ppermute | solution.py:21
  244.0 1.9 collective-permute-start.21
  246.0 3.9 %collective-permute-start.23 = (bf16[4,2,128,128]{3,2,1,0:T(8,128)(2,1)S(1)}, bf16[4,2,128,128]{3,2,1,0:T(8,128)(2,1)S(1)}, u32[]{:S(2)}, u32[]{:S(2)}) collective-permute-start(bf16[4,2,128,128]{3,2,1,0:T(8,128)(2,1)S(1)} %get-tuple-element.129), channel_id=1, source_target_pairs={{0,4},{4,8},{8,12},{12,0},{1,5},{5,9},{9,13},{13,1},{2,6},{6,10},{... | collective-permute-start | bytes 786440 | tf_op jit(solution)/shard_map/ppermute | solution.py:21
  249.9 9.7 %collective-permute-done.22 = bf16[4,2,128,128]{3,2,1,0:T(8,128)(2,1)S(1)} collective-permute-done((bf16[4,2,128,128]{3,2,1,0:T(8,128)(2,1)S(1)}, bf16[4,2,128,128]{3,2,1,0:T(8,128)(2,1)S(1)}, u32[]{:S(2)}, u32[]{:S(2)}) %collective-permute-start.22) | collective-permute-done | bytes 262176 | tf_op jit(solution)/shard_map/ppermute | solution.py:21
  259.7 1.4 collective-permute-done.21
  263.4 1.0 copy.42
  264.4 1.0 copy.41
  (144 shorter events, 28.4 us)
Async XLA Ops:
  2.1 48.9 %collective-permute-start.5 = (bf16[2,128,128]{2,1,0:T(8,128)(2,1)S(1)}, bf16[2,128,128]{2,1,0:T(8,128)(2,1)S(1)}, u32[]{:S(2)}, u32[]{:S(2)}) collective-permute-start(bf16[2,128,128]{2,1,0:T(8,128)(2,1)S(1)} %slice.80), channel_id=1, source_target_pairs={{0,96},{16,112},{32,128},{48,144},{64,160},{80,176},{96,192},{112,... | collective-permute-start | bytes 196616 | tf_op jit(solution)/shard_map/ppermute | solution.py:16
  14.9 36.2 %collective-permute-start.4 = (bf16[2,128,128]{2,1,0:T(8,128)(2,1)S(1)}, bf16[2,128,128]{2,1,0:T(8,128)(2,1)S(1)}, u32[]{:S(2)}, u32[]{:S(2)}) collective-permute-start(bf16[2,128,128]{2,1,0:T(8,128)(2,1)S(1)} %slice.80), channel_id=1, source_target_pairs={{0,80},{16,96},{32,112},{48,128},{64,144},{80,160},{96,176},{112,1... | collective-permute-start | bytes 196616 | tf_op jit(solution)/shard_map/ppermute | solution.py:16
  18.6 32.4 %collective-permute-start.3 = (bf16[2,128,128]{2,1,0:T(8,128)(2,1)S(1)}, bf16[2,128,128]{2,1,0:T(8,128)(2,1)S(1)}, u32[]{:S(2)}, u32[]{:S(2)}) collective-permute-start(bf16[2,128,128]{2,1,0:T(8,128)(2,1)S(1)} %slice.80), channel_id=1, source_target_pairs={{0,64},{16,80},{32,96},{48,112},{64,128},{80,144},{96,160},{112,17... | collective-permute-start | bytes 196616 | tf_op jit(solution)/shard_map/ppermute | solution.py:16
  20.5 30.4 %collective-permute-start.2 = (bf16[2,128,128]{2,1,0:T(8,128)(2,1)S(1)}, bf16[2,128,128]{2,1,0:T(8,128)(2,1)S(1)}, u32[]{:S(2)}, u32[]{:S(2)}) collective-permute-start(bf16[2,128,128]{2,1,0:T(8,128)(2,1)S(1)} %slice.80), channel_id=1, source_target_pairs={{0,48},{16,64},{32,80},{48,96},{64,112},{80,128},{96,144},{112,160... | collective-permute-start | bytes 196616 | tf_op jit(solution)/shard_map/ppermute | solution.py:16
  23.9 14.6 %collective-permute-start = (bf16[2,128,128]{2,1,0:T(8,128)(2,1)S(1)}, bf16[2,128,128]{2,1,0:T(8,128)(2,1)S(1)}, u32[]{:S(2)}, u32[]{:S(2)}) collective-permute-start(bf16[2,128,128]{2,1,0:T(8,128)(2,1)S(1)} %slice.80), channel_id=1, source_target_pairs={{0,16},{16,32},{32,48},{48,64},{64,80},{80,96},{96,112},{112,128},... | collective-permute-start | bytes 196616 | tf_op jit(solution)/shard_map/ppermute | solution.py:16
  38.5 12.5 %collective-permute-start.1 = (bf16[2,128,128]{2,1,0:T(8,128)(2,1)S(1)}, bf16[2,128,128]{2,1,0:T(8,128)(2,1)S(1)}, u32[]{:S(2)}, u32[]{:S(2)}) collective-permute-start(bf16[2,128,128]{2,1,0:T(8,128)(2,1)S(1)} %slice.80), channel_id=1, source_target_pairs={{0,32},{16,48},{32,64},{48,80},{64,96},{80,112},{96,128},{112,144}... | collective-permute-start | bytes 196616 | tf_op jit(solution)/shard_map/ppermute | solution.py:16
  51.1 12.7 %collective-permute-start.8 = (bf16[6,2,128,128]{3,2,1,0:T(8,128)(2,1)S(1)}, bf16[6,2,128,128]{3,2,1,0:T(8,128)(2,1)S(1)}, u32[]{:S(2)}, u32[]{:S(2)}) collective-permute-start(bf16[6,2,128,128]{3,2,1,0:T(8,128)(2,1)S(1)} %bitcast_dynamic-update-slice_fusion), channel_id=1, source_target_pairs={{0,1},{1,2},{2,3},{3,0},{4,5},{5,6},{6,7},{7,4},{8,9},{9,10},{10,1... | collective-permute-start | bytes 1179656 | tf_op jit(solution)/shard_map/ppermute | solution.py:21
  54.6 12.8 %collective-permute-start.7 = (bf16[6,2,128,128]{3,2,1,0:T(8,128)(2,1)S(1)}, bf16[6,2,128,128]{3,2,1,0:T(8,128)(2,1)S(1)}, u32[]{:S(2)}, u32[]{:S(2)}) collective-permute-start(bf16[6,2,128,128]{3,2,1,0:T(8,128)(2,1)S(1)} %bitcast_dynamic-update-slice_fusion), channel_id=1, source_target_pairs={{0,2},{1,3},{2,0},{3,1},{4,6},{5,7},{6,4},{7,5},{8,10},{9,11},{10,... | collective-permute-start | bytes 1179656 | tf_op jit(solution)/shard_map/ppermute | solution.py:21
  59.4 9.7 %collective-permute-start.6 = (bf16[6,2,128,128]{3,2,1,0:T(8,128)(2,1)S(1)}, bf16[6,2,128,128]{3,2,1,0:T(8,128)(2,1)S(1)}, u32[]{:S(2)}, u32[]{:S(2)}) collective-permute-start(bf16[6,2,128,128]{3,2,1,0:T(8,128)(2,1)S(1)} %bitcast_dynamic-update-slice_fusion), channel_id=1, source_target_pairs={{0,3},{1,0},{2,1},{3,2},{4,7},{5,4},{6,5},{7,6},{8,11},{9,8},{10,9... | collective-permute-start | bytes 1179656 | tf_op jit(solution)/shard_map/ppermute | solution.py:21
  83.5 1.0 copy-start
  101.6 1.0 copy-start
  119.8 1.0 copy-start
  138.1 1.0 copy-start
  147.7 13.2 %collective-permute-start.9 = (bf16[2,7,128,128]{3,2,0,1:T(8,128)(2,1)S(1)}, bf16[2,7,128,128]{3,2,0,1:T(8,128)(2,1)S(1)}, u32[]{:S(2)}, u32[]{:S(2)}) collective-permute-start(bf16[2,7,128,128]{3,2,0,1:T(8,128)(2,1)S(1)} %get-tuple-element.117), channel_id=1, source_target_pairs={{0,1},{1,2},{2,3},{3,0},{4,5},{5,6},{6,7},{7,4},{8,9},{9,10},{10,1... | collective-permute-start | bytes 1376264 | tf_op jit(solution)/shard_map/ppermute | solution.py:21
  152.4 10.4 %collective-permute-start.11 = (bf16[2,7,128,128]{3,2,0,1:T(8,128)(2,1)S(1)}, bf16[2,7,128,128]{3,2,0,1:T(8,128)(2,1)S(1)}, u32[]{:S(2)}, u32[]{:S(2)}) collective-permute-start(bf16[2,7,128,128]{3,2,0,1:T(8,128)(2,1)S(1)} %get-tuple-element.118), channel_id=1, source_target_pairs={{0,3},{1,0},{2,1},{3,2},{4,7},{5,4},{6,5},{7,6},{8,11},{9,8},{10,9... | collective-permute-start | bytes 1376264 | tf_op jit(solution)/shard_map/ppermute | solution.py:21
  154.8 11.9 %collective-permute-start.10 = (bf16[2,7,128,128]{3,2,0,1:T(8,128)(2,1)S(1)}, bf16[2,7,128,128]{3,2,0,1:T(8,128)(2,1)S(1)}, u32[]{:S(2)}, u32[]{:S(2)}) collective-permute-start(bf16[2,7,128,128]{3,2,0,1:T(8,128)(2,1)S(1)} %get-tuple-element.119), channel_id=1, source_target_pairs={{0,2},{1,3},{2,0},{3,1},{4,6},{5,7},{6,4},{7,5},{8,10},{9,11},{10,... | collective-permute-start | bytes 1376264 | tf_op jit(solution)/shard_map/ppermute | solution.py:21
  168.1 42.7 %collective-permute-start.12 = (bf16[2,128,128]{2,1,0:T(8,128)(2,1)S(1)}, bf16[2,128,128]{2,1,0:T(8,128)(2,1)S(1)}, u32[]{:S(2)}, u32[]{:S(2)}) collective-permute-start(bf16[2,128,128]{2,1,0:T(8,128)(2,1)S(1)} %get-tuple-element.122), channel_id=1, source_target_pairs={{16,0},{32,16},{48,32},{64,48},{80,64},{96,80},{112,96},{128,112},... | collective-permute-start | bytes 196616 | tf_op jit(solution)/shard_map/ppermute | solution.py:16
  170.0 49.6 %collective-permute-start.17 = (bf16[2,128,128]{2,1,0:T(8,128)(2,1)S(1)}, bf16[2,128,128]{2,1,0:T(8,128)(2,1)S(1)}, u32[]{:S(2)}, u32[]{:S(2)}) collective-permute-start(bf16[2,128,128]{2,1,0:T(8,128)(2,1)S(1)} %get-tuple-element.123), channel_id=1, source_target_pairs={{96,0},{112,16},{128,32},{144,48},{160,64},{176,80},{192,96},{208,... | collective-permute-start | bytes 196616 | tf_op jit(solution)/shard_map/ppermute | solution.py:16
  179.9 39.8 %collective-permute-start.16 = (bf16[2,128,128]{2,1,0:T(8,128)(2,1)S(1)}, bf16[2,128,128]{2,1,0:T(8,128)(2,1)S(1)}, u32[]{:S(2)}, u32[]{:S(2)}) collective-permute-start(bf16[2,128,128]{2,1,0:T(8,128)(2,1)S(1)} %get-tuple-element.124), channel_id=1, source_target_pairs={{80,0},{96,16},{112,32},{128,48},{144,64},{160,80},{176,96},{192,1... | collective-permute-start | bytes 196616 | tf_op jit(solution)/shard_map/ppermute | solution.py:16
  187.4 32.3 %collective-permute-start.15 = (bf16[2,128,128]{2,1,0:T(8,128)(2,1)S(1)}, bf16[2,128,128]{2,1,0:T(8,128)(2,1)S(1)}, u32[]{:S(2)}, u32[]{:S(2)}) collective-permute-start(bf16[2,128,128]{2,1,0:T(8,128)(2,1)S(1)} %get-tuple-element.125), channel_id=1, source_target_pairs={{64,0},{80,16},{96,32},{112,48},{128,64},{144,80},{160,96},{176,11... | collective-permute-start | bytes 196616 | tf_op jit(solution)/shard_map/ppermute | solution.py:16
  201.4 18.3 %collective-permute-start.14 = (bf16[2,128,128]{2,1,0:T(8,128)(2,1)S(1)}, bf16[2,128,128]{2,1,0:T(8,128)(2,1)S(1)}, u32[]{:S(2)}, u32[]{:S(2)}) collective-permute-start(bf16[2,128,128]{2,1,0:T(8,128)(2,1)S(1)} %get-tuple-element.126), channel_id=1, source_target_pairs={{48,0},{64,16},{80,32},{96,48},{112,64},{128,80},{144,96},{160,112... | collective-permute-start | bytes 196616 | tf_op jit(solution)/shard_map/ppermute | solution.py:16
  210.8 11.2 %collective-permute-start.13 = (bf16[2,128,128]{2,1,0:T(8,128)(2,1)S(1)}, bf16[2,128,128]{2,1,0:T(8,128)(2,1)S(1)}, u32[]{:S(2)}, u32[]{:S(2)}) collective-permute-start(bf16[2,128,128]{2,1,0:T(8,128)(2,1)S(1)} %get-tuple-element.127), channel_id=1, source_target_pairs={{32,0},{48,16},{64,32},{80,48},{96,64},{112,80},{128,96},{144,112}... | collective-permute-start | bytes 196616 | tf_op jit(solution)/shard_map/ppermute | solution.py:16
  222.1 13.3 %collective-permute-start.20 = (bf16[2,128,128]{2,1,0:T(8,128)(2,1)S(1)}, bf16[2,128,128]{2,1,0:T(8,128)(2,1)S(1)}, u32[]{:S(2)}, u32[]{:S(2)}) collective-permute-start(bf16[2,128,128]{2,1,0:T(8,128)(2,1)S(1)} %fusion.34), channel_id=1, source_target_pairs={{0,1},{1,2},{2,3},{3,0},{4,5},{5,6},{6,7},{7,4},{8,9},{9,10},{10,1... | collective-permute-start | bytes 196616 | tf_op jit(solution)/shard_map/ppermute | solution.py:21
  227.8 7.9 %collective-permute-start.19 = (bf16[2,128,128]{2,1,0:T(8,128)(2,1)S(1)}, bf16[2,128,128]{2,1,0:T(8,128)(2,1)S(1)}, u32[]{:S(2)}, u32[]{:S(2)}) collective-permute-start(bf16[2,128,128]{2,1,0:T(8,128)(2,1)S(1)} %fusion.34), channel_id=1, source_target_pairs={{0,2},{1,3},{2,0},{3,1},{4,6},{5,7},{6,4},{7,5},{8,10},{9,11},{10,... | collective-permute-start | bytes 196616 | tf_op jit(solution)/shard_map/ppermute | solution.py:21
  233.5 6.2 %collective-permute-start.18 = (bf16[2,128,128]{2,1,0:T(8,128)(2,1)S(1)}, bf16[2,128,128]{2,1,0:T(8,128)(2,1)S(1)}, u32[]{:S(2)}, u32[]{:S(2)}) collective-permute-start(bf16[2,128,128]{2,1,0:T(8,128)(2,1)S(1)} %fusion.34), channel_id=1, source_target_pairs={{0,3},{1,0},{2,1},{3,2},{4,7},{5,4},{6,5},{7,6},{8,11},{9,8},{10,9... | collective-permute-start | bytes 196616 | tf_op jit(solution)/shard_map/ppermute | solution.py:21
  239.7 20.0 %collective-permute-start.22 = (bf16[4,2,128,128]{3,2,1,0:T(8,128)(2,1)S(1)}, bf16[4,2,128,128]{3,2,1,0:T(8,128)(2,1)S(1)}, u32[]{:S(2)}, u32[]{:S(2)}) collective-permute-start(bf16[4,2,128,128]{3,2,1,0:T(8,128)(2,1)S(1)} %get-tuple-element.129), channel_id=1, source_target_pairs={{0,8},{4,12},{8,0},{12,4},{1,9},{5,13},{9,1},{13,5},{2,10},{6,14},... | collective-permute-start | bytes 786440 | tf_op jit(solution)/shard_map/ppermute | solution.py:21
  244.0 17.1 %collective-permute-start.21 = (bf16[4,2,128,128]{3,2,1,0:T(8,128)(2,1)S(1)}, bf16[4,2,128,128]{3,2,1,0:T(8,128)(2,1)S(1)}, u32[]{:S(2)}, u32[]{:S(2)}) collective-permute-start(bf16[4,2,128,128]{3,2,1,0:T(8,128)(2,1)S(1)} %get-tuple-element.129), channel_id=1, source_target_pairs={{0,12},{4,0},{8,4},{12,8},{1,13},{5,1},{9,5},{13,9},{2,14},{6,2},{... | collective-permute-start | bytes 786440 | tf_op jit(solution)/shard_map/ppermute | solution.py:21
  246.0 15.1 %collective-permute-start.23 = (bf16[4,2,128,128]{3,2,1,0:T(8,128)(2,1)S(1)}, bf16[4,2,128,128]{3,2,1,0:T(8,128)(2,1)S(1)}, u32[]{:S(2)}, u32[]{:S(2)}) collective-permute-start(bf16[4,2,128,128]{3,2,1,0:T(8,128)(2,1)S(1)} %get-tuple-element.129), channel_id=1, source_target_pairs={{0,4},{4,8},{8,12},{12,0},{1,5},{5,9},{9,13},{13,1},{2,6},{6,10},{... | collective-permute-start | bytes 786440 | tf_op jit(solution)/shard_map/ppermute | solution.py:21

commit v3 on v2

--- a/solution.py
+++ b/solution.py
@@ -1,7 +1,11 @@
+import functools
+
 import jax
 import jax.numpy as jnp
 import numpy as np
 from jax import lax
+from jax.experimental import pallas as pl
+from jax.experimental.pallas import tpu as pltpu
 from jax.sharding import Mesh
 from jax.sharding import PartitionSpec as P
 
@@ -21,37 +25,106 @@
     return lax.ppermute(value, axis, [(source, (source + steps) % count) for source in range(count)])
 
 
-def visible_mask(chosen, live_mask, block_id, width):
-    causal = jnp.arange(width)[:, None] >= jnp.arange(width)[None, :]
-    earlier = (chosen < block_id)[None, :, None]
-    allowed = (live_mask == 1)[None, :, None] & (earlier | causal[:, None, :])
-    return allowed.reshape(width, -1)
-
-
-def tile_grads(q_pair, do_pair, k_sel, v_sel, allowed, inv_root):
-    scores = (
-        jnp.einsum("bqhd,bnd->bhqn", q_pair, k_sel, preferred_element_type=jnp.float32) * inv_root
-    )
-    scores = jnp.where(allowed[:, None], scores, -1e30)
-    row_max = jnp.max(scores, axis=-1, keepdims=True)
+def block_kernel(slots_ref, q_ref, do_ref, code_ref, k_ref, v_ref, dq_ref, dk_ref, dv_ref,
+                 k_sel, v_sel, *, inv_root, heads_here):
+    step = pl.program_id(0)
+    slots = k_sel.shape[0] // BLOCK
+
+    @pl.when(step == 0)
+    def _():
+        dk_ref[...] = jnp.zeros_like(dk_ref)
+        dv_ref[...] = jnp.zeros_like(dv_ref)
+
+    for slot in range(slots):
+        start = pl.multiple_of(slots_ref[step, slot] * BLOCK, BLOCK)
+        k_sel[slot * BLOCK:(slot + 1) * BLOCK, :] = k_ref[pl.ds(start, BLOCK), :]
+        v_sel[slot * BLOCK:(slot + 1) * BLOCK, :] = v_ref[pl.ds(start, BLOCK), :]
+    q = q_ref[...]
+    do = do_ref[...]
+    keys = k_sel[...]
+    values = v_sel[...]
+    rows, cols = q.shape[0], keys.shape[0]
+    scores = lax.dot_general(
+        q, keys, (((1,), (1,)), ((), ())), preferred_element_type=jnp.float32
+    ) * inv_root
+    code = code_ref[...]
+    query_pos = lax.broadcasted_iota(jnp.int32, (rows, cols), 0) // heads_here
+    key_pos = lax.broadcasted_iota(jnp.int32, (rows, cols), 1) % BLOCK
+    allowed = (code == 2) | ((code == 1) & (query_pos >= key_pos))
+    scores = jnp.where(allowed, scores, -1e30)
+    row_max = jnp.max(scores, axis=1, keepdims=True)
     shifted = jnp.exp(scores - row_max)
-    weights = shifted / jnp.sum(shifted, axis=-1, keepdims=True)
+    weights = shifted / jnp.sum(shifted, axis=1, keepdims=True)
     weights_b = weights.astype(jnp.bfloat16)
-    output = jnp.einsum("bhqn,bnd->bqhd", weights_b, v_sel, preferred_element_type=jnp.float32)
-    row_delta = jnp.sum(do_pair.astype(jnp.float32) * output, axis=-1)
-    prob_grad = jnp.einsum("bqhd,bnd->bhqn", do_pair, v_sel, preferred_element_type=jnp.float32)
-    score_grad = weights * (prob_grad - jnp.transpose(row_delta, (0, 2, 1))[..., None])
-    score_b = score_grad.astype(jnp.bfloat16)
-    query_part = (
-        jnp.einsum("bhqn,bnd->bqhd", score_b, k_sel, preferred_element_type=jnp.float32) * inv_root
-    )
-    key_part = (
-        jnp.einsum("bhqn,bqhd->bnd", score_b, q_pair, preferred_element_type=jnp.float32) * inv_root
-    )
-    value_part = jnp.einsum(
-        "bhqn,bqhd->bnd", weights_b, do_pair, preferred_element_type=jnp.float32
-    )
-    return (query_part.astype(jnp.bfloat16), key_part, value_part)
+    output = jnp.dot(weights_b, values, preferred_element_type=jnp.float32)
+    row_delta = jnp.sum(do.astype(jnp.float32) * output, axis=1, keepdims=True)
+    prob_grad = lax.dot_general(
+        do, values, (((1,), (1,)), ((), ())), preferred_element_type=jnp.float32
+    )
+    score_b = (weights * (prob_grad - row_delta)).astype(jnp.bfloat16)
+    query_part = jnp.dot(score_b, keys, preferred_element_type=jnp.float32) * inv_root
+    dq_ref[...] = query_part.astype(jnp.bfloat16)
+    key_part = lax.dot_general(
+        score_b, q, (((0,), (0,)), ((), ())), preferred_element_type=jnp.float32
+    ) * inv_root
+    value_part = lax.dot_general(
+        weights_b, do, (((0,), (0,)), ((), ())), preferred_element_type=jnp.float32
+    )
+    for slot in range(slots):
+        start = pl.multiple_of(slots_ref[step, slot] * BLOCK, BLOCK)
+        dk_ref[pl.ds(start, BLOCK), :] += key_part[slot * BLOCK:(slot + 1) * BLOCK]
+        dv_ref[pl.ds(start, BLOCK), :] += value_part[slot * BLOCK:(slot + 1) * BLOCK]
+
+
+def local_grads(queries, out_grad, key_tiles, value_tiles, slot_index, code, inv_root,
+                interpret=False):
+    tokens_here, heads_here, width = queries.shape
+    blocks_here, slots = slot_index.shape
+    rows = BLOCK * heads_here
+    store = key_tiles.shape[0] * BLOCK
+    cols = slots * BLOCK
+    code_cols = jnp.repeat(code.astype(jnp.int32), BLOCK, axis=1).reshape(blocks_here, 1, cols)
+    kernel = functools.partial(block_kernel, inv_root=inv_root, heads_here=heads_here)
+    whole = lambda step, slots_ref: (0, 0)
+    per_block = lambda step, slots_ref: (step, 0)
+    query_grad, key_grad, value_grad = pl.pallas_call(
+        kernel,
+        grid_spec=pltpu.PrefetchScalarGridSpec(
+            num_scalar_prefetch=1,
+            grid=(blocks_here,),
+            in_specs=[
+                pl.BlockSpec((rows, width), per_block),
+                pl.BlockSpec((rows, width), per_block),
+                pl.BlockSpec((None, 1, cols), lambda step, slots_ref: (step, 0, 0)),
+                pl.BlockSpec((store, width), whole),
+                pl.BlockSpec((store, width), whole),
+            ],
+            out_specs=[
+                pl.BlockSpec((rows, width), per_block),
+                pl.BlockSpec((store, width), whole),
+                pl.BlockSpec((store, width), whole),
+            ],
+            scratch_shapes=[
+                pltpu.VMEM((cols, width), jnp.bfloat16),
+                pltpu.VMEM((cols, width), jnp.bfloat16),
+            ],
+        ),
+        out_shape=[
+            jax.ShapeDtypeStruct((tokens_here * heads_here, width), jnp.bfloat16),
+            jax.ShapeDtypeStruct((store, width), jnp.float32),
+            jax.ShapeDtypeStruct((store, width), jnp.float32),
+        ],
+        compiler_params=pltpu.CompilerParams(dimension_semantics=("arbitrary",)),
+        interpret=interpret,
+    )(
+        slot_index.astype(jnp.int32),
+        queries.reshape(tokens_here * heads_here, width),
+        out_grad.reshape(tokens_here * heads_here, width),
+        code_cols,
+        key_tiles.reshape(store, width),
+        value_tiles.reshape(store, width),
+    )
+    return query_grad.reshape(tokens_here, heads_here, width), key_grad, value_grad
 
 
 def per_device(queries, key_rows, value_rows, out_grad, selected, live_slots):
@@ -85,33 +158,12 @@
     per_part = blocks_here // parts_count
     rolled_block = (local_block // per_part - part_index) % parts_count * per_part + local_block % per_part
     slot_index = (ctx_index - chosen // blocks_here) * blocks_here + rolled_block
-    pair_count = blocks_here // 2
-
-    def accumulate(running, inputs):
-        q_pair, do_pair, slot_pair, chosen_pair, live_pair, block_pair = inputs
-        k_sel = key_tiles[slot_pair].reshape(2, -1, width)
-        v_sel = value_tiles[slot_pair].reshape(2, -1, width)
-        allowed = jax.vmap(visible_mask, in_axes=(0, 0, 0, None))(
-            chosen_pair, live_pair, block_pair, BLOCK
-        )
-        query_part, key_part, value_part = tile_grads(
-            q_pair, do_pair, k_sel, v_sel, allowed, inv_root
-        )
-        stacked = jnp.stack([key_part, value_part]).reshape(2, -1, BLOCK, width)
-        running = running.at[:, slot_pair.reshape(-1)].add(stacked)
-        return (running, query_part)
-
-    initial = jnp.zeros((2, reach_span * blocks_here, BLOCK, width), jnp.float32)
-    inputs = (
-        queries.reshape(pair_count, 2, BLOCK, heads_here, width),
-        out_grad.reshape(pair_count, 2, BLOCK, heads_here, width),
-        slot_index.reshape(pair_count, 2, -1),
-        chosen.reshape(pair_count, 2, -1),
-        live_mask.reshape(pair_count, 2, -1),
-        block_ids.reshape(pair_count, 2),
-    )
-    grads, query_parts = lax.scan(accumulate, initial, inputs)
-    grads = grads.reshape(2, reach_span, tokens_here, width)
+    slot_index = jnp.clip(slot_index, 0, reach_span * blocks_here - 1)
+    code = jnp.where(live_mask == 1, jnp.where(chosen < block_ids[:, None], 2, 1), 0)
+    query_grad, key_grad, value_grad = local_grads(
+        queries, out_grad, key_tiles, value_tiles, slot_index, code, inv_root
+    )
+    grads = jnp.stack([key_grad, value_grad]).reshape(2, reach_span, tokens_here, width)
     sent = grads.astype(jnp.bfloat16)
     parts = grads[:, :, :quarter]
     for step in range(1, parts_count):
@@ -130,7 +182,6 @@
     ordered = jnp.take(jnp.take(by_group, group_order, axis=0), part_order, axis=1)
     summed = jnp.transpose(ordered, (2, 0, 1, 3, 4)).reshape(2, groups, tokens_here, width)
     summed = summed.astype(jnp.float32)
-    query_grad = query_parts.reshape(tokens_here, heads_here, width)
     return (query_grad, summed[0], summed[1])
 
 

time: 270 us -> 214 us (0.79)
  the two profiles are of different devices: /device:TPU:6 before, /device:TPU:63 now
where the time goes in v3:
time: 214 us; the launch traced here: 213 us
  starting transfers between devices  99.4 us (46%)
  waiting for transfers between devices  82.8 us (39%)
  Pallas kernels  16.9 us (8%)
  local copies, waits for them, and re-layouts  7.9 us (4%)
  other arithmetic  5.12 us (2%)
    ppermute x12, starting transfers between devices, shifted_2(): lax.ppermute(value, axis, [(source, source + steps) for source in range(l...  58.8 us
    ppermute x12, waiting for transfers between devices, cycled(): lax.ppermute(value, axis, [(source, (source + steps) % count) for source...  55.2 us
    ppermute x12, starting transfers between devices, cycled(): lax.ppermute(value, axis, [(source, (source + steps) % count) for source...  40.6 us
    ppermute x12, waiting for transfers between devices, shifted_2(): lax.ppermute(value, axis, [(source, source + steps) for source in range(l...  27.6 us
    pallas_call x1, Pallas kernels, local_grads(): pl.pallas_call(kernel, grid_spec=pltpu.PrefetchScalarGridSpec(num_scalar_...  16.9 us
  transfers between devices with their start and end apart: 24, of which 16 were waited for; matrix products, arithmetic and copies ran while one was open for 1% of the time, Pallas kernels for 0%

profile of v3, /device:TPU:63, one launch (start us, length us, event | category | flops | bytes accessed | tf_op | source)
XLA Modules:
  0.0 213.3 jit_solution(15972626057007193927)
XLA Ops:
  0.7 1.0 constant_dynamic-slice_fusion
  1.7 0.5 fusion.6
  2.1 9.4 %collective-permute-start = (bf16[2,128,128]{2,1,0:T(8,128)(2,1)S(1)}, bf16[2,128,128]{2,1,0:T(8,128)(2,1)S(1)}, u32[]{:S(2)}, u32[]{:S(2)}) collective-permute-start(bf16[2,128,128]{2,1,0:T(8,128)(2,1)S(1)} %slice.76), channel_id=1, source_target_pairs={{0,16},{16,32},{32,48},{48,64},{64,80},{80,96},{96,112},{112,128},... | collective-permute-start | bytes 196616 | tf_op jit(solution)/shard_map/ppermute | solution.py:20
  11.5 7.9 %collective-permute-start.1 = (bf16[2,128,128]{2,1,0:T(8,128)(2,1)S(1)}, bf16[2,128,128]{2,1,0:T(8,128)(2,1)S(1)}, u32[]{:S(2)}, u32[]{:S(2)}) collective-permute-start(bf16[2,128,128]{2,1,0:T(8,128)(2,1)S(1)} %slice.76), channel_id=1, source_target_pairs={{0,32},{16,48},{32,64},{48,80},{64,96},{80,112},{96,128},{112,144}... | collective-permute-start | bytes 196616 | tf_op jit(solution)/shard_map/ppermute | solution.py:20
  19.5 4.0 %collective-permute-start.2 = (bf16[2,128,128]{2,1,0:T(8,128)(2,1)S(1)}, bf16[2,128,128]{2,1,0:T(8,128)(2,1)S(1)}, u32[]{:S(2)}, u32[]{:S(2)}) collective-permute-start(bf16[2,128,128]{2,1,0:T(8,128)(2,1)S(1)} %slice.76), channel_id=1, source_target_pairs={{0,48},{16,64},{32,80},{48,96},{64,112},{80,128},{96,144},{112,160... | collective-permute-start | bytes 196616 | tf_op jit(solution)/shard_map/ppermute | solution.py:20
  23.5 1.9 collective-permute-start.3
  25.4 1.9 collective-permute-start.4
  27.3 0.8 constant_dynamic-slice_fusion.2
  28.1 0.0 collective-permute-done
  28.1 1.9 collective-permute-start.5
  30.1 7.5 %collective-permute-done.2 = bf16[2,128,128]{2,1,0:T(8,128)(2,1)S(1)} collective-permute-done((bf16[2,128,128]{2,1,0:T(8,128)(2,1)S(1)}, bf16[2,128,128]{2,1,0:T(8,128)(2,1)S(1)}, u32[]{:S(2)}, u32[]{:S(2)}) %collective-permute-start.2) | collective-permute-done | bytes 65568 | tf_op jit(solution)/shard_map/ppermute | solution.py:20
  37.6 3.7 %collective-permute-done.3 = bf16[2,128,128]{2,1,0:T(8,128)(2,1)S(1)} collective-permute-done((bf16[2,128,128]{2,1,0:T(8,128)(2,1)S(1)}, bf16[2,128,128]{2,1,0:T(8,128)(2,1)S(1)}, u32[]{:S(2)}, u32[]{:S(2)}) %collective-permute-start.3) | collective-permute-done | bytes 65568 | tf_op jit(solution)/shard_map/ppermute | solution.py:20
  41.3 8.6 %collective-permute-done.4 = bf16[2,128,128]{2,1,0:T(8,128)(2,1)S(1)} collective-permute-done((bf16[2,128,128]{2,1,0:T(8,128)(2,1)S(1)}, bf16[2,128,128]{2,1,0:T(8,128)(2,1)S(1)}, u32[]{:S(2)}, u32[]{:S(2)}) %collective-permute-start.4) | collective-permute-done | bytes 65568 | tf_op jit(solution)/shard_map/ppermute | solution.py:20
  49.9 0.4 collective-permute-done.5
  50.4 1.9 collective-permute-start.8
  52.3 4.1 %collective-permute-start.7 = (bf16[6,2,128,128]{3,2,1,0:T(8,128)(2,1)S(1)}, bf16[6,2,128,128]{3,2,1,0:T(8,128)(2,1)S(1)}, u32[]{:S(2)}, u32[]{:S(2)}) collective-permute-start(bf16[6,2,128,128]{3,2,1,0:T(8,128)(2,1)S(1)} %bitcast_dynamic-update-slice_fusion), channel_id=1, source_target_pairs={{0,2},{1,3},{2,0},{3,1},{4,6},{5,7},{6,4},{7,5},{8,10},{9,11},{10,... | collective-permute-start | bytes 1179656 | tf_op jit(solution)/shard_map/ppermute | solution.py:25
  56.4 1.9 collective-permute-start.6
  58.4 0.6 select_select_fusion
  59.0 0.1 broadcast_in_dim.31
  59.1 0.7 reshape_reshape.3.code_ref
  59.8 0.5 fusion.38
  60.3 1.9 collective-permute-done.8
  62.2 3.2 %collective-permute-done.7 = bf16[6,2,128,128]{3,2,1,0:T(8,128)(2,1)S(1)} collective-permute-done((bf16[6,2,128,128]{3,2,1,0:T(8,128)(2,1)S(1)}, bf16[6,2,128,128]{3,2,1,0:T(8,128)(2,1)S(1)}, u32[]{:S(2)}, u32[]{:S(2)}) %collective-permute-start.7) | collective-permute-done | bytes 393248 | tf_op jit(solution)/shard_map/ppermute | solution.py:25
  65.4 9.7 %collective-permute-done.6 = bf16[6,2,128,128]{3,2,1,0:T(8,128)(2,1)S(1)} collective-permute-done((bf16[6,2,128,128]{3,2,1,0:T(8,128)(2,1)S(1)}, bf16[6,2,128,128]{3,2,1,0:T(8,128)(2,1)S(1)}, u32[]{:S(2)}, u32[]{:S(2)}) %collective-permute-start.6) | collective-permute-done | bytes 393248 | tf_op jit(solution)/shard_map/ppermute | solution.py:25
  75.2 0.1 maximum_maximum_fusion
  75.3 1.4 fusion.37
  76.7 16.9 %shard_map.85 = (bf16[2048,128]{1,0:T(8,128)(2,1)}, f32[3584,128]{1,0:T(8,128)}, f32[3584,128]{1,0:T(8,128)}) custom-call(s32[8,16]{1,0:T(8,128)} %get-tuple-element.27.slots_ref, bf16[2048,128]{1,0:T(8,128)(2,1)} %bitcast.92, bf16[2048,128]{1,0:T(8,128)(2,1)} %bitcast.93, s32[8,1,1024]{2,1,0:T(1,128)} %reshape_reshape.3.code_ref, ...), custom_call_target="tpu_custom_call" | custom-call | tf_op jit(solution)/shard_map/pallas_call | solution.py:90
  93.6 2.5 %fusion = bf16[2,7,512,128]{3,2,1,0:T(8,128)(2,1)S(1)} fusion(f32[1,7,512,128]{3,2,1,0:T(8,128)} %bitcast.86, f32[1,7,512,128]{3,2,1,0:T(8,128)} %bitcast.84), kind=kLoop, calls=%fused_computation.5 | loop fusion | flops 917504 | bytes 5505024 | tf_op jit(solution)/shard_map/convert_element_type | solution.py:167
  96.1 0.1 fusion.36
  96.2 2.1 collective-permute-start.11
  98.2 4.2 %collective-permute-start.10 = (bf16[2,7,128,128]{3,2,1,0:T(8,128)(2,1)S(1)}, bf16[2,7,128,128]{3,2,1,0:T(8,128)(2,1)S(1)}, u32[]{:S(2)}, u32[]{:S(2)}) collective-permute-start(bf16[2,7,128,128]{3,2,1,0:T(8,128)(2,1)S(1)} %get-tuple-element.15), channel_id=1, source_target_pairs={{0,2},{1,3},{2,0},{3,1},{4,6},{5,7},{6,4},{7,5},{8,10},{9,11},{10,... | collective-permute-start | bytes 1376264 | tf_op jit(solution)/shard_map/ppermute | solution.py:25
  102.4 4.0 %collective-permute-start.9 = (bf16[2,7,128,128]{3,2,1,0:T(8,128)(2,1)S(1)}, bf16[2,7,128,128]{3,2,1,0:T(8,128)(2,1)S(1)}, u32[]{:S(2)}, u32[]{:S(2)}) collective-permute-start(bf16[2,7,128,128]{3,2,1,0:T(8,128)(2,1)S(1)} %get-tuple-element.13), channel_id=1, source_target_pairs={{0,1},{1,2},{2,3},{3,0},{4,5},{5,6},{6,7},{7,4},{8,9},{9,10},{10,1... | collective-permute-start | bytes 1376264 | tf_op jit(solution)/shard_map/ppermute | solution.py:25
  106.4 4.7 %collective-permute-done.11 = bf16[2,7,128,128]{3,2,1,0:T(8,128)(2,1)S(1)} collective-permute-done((bf16[2,7,128,128]{3,2,1,0:T(8,128)(2,1)S(1)}, bf16[2,7,128,128]{3,2,1,0:T(8,128)(2,1)S(1)}, u32[]{:S(2)}, u32[]{:S(2)}) %collective-permute-start.11) | collective-permute-done | bytes 458784 | tf_op jit(solution)/shard_map/ppermute | solution.py:25
  111.1 9.7 %collective-permute-done.10 = bf16[2,7,128,128]{3,2,1,0:T(8,128)(2,1)S(1)} collective-permute-done((bf16[2,7,128,128]{3,2,1,0:T(8,128)(2,1)S(1)}, bf16[2,7,128,128]{3,2,1,0:T(8,128)(2,1)S(1)}, u32[]{:S(2)}, u32[]{:S(2)}) %collective-permute-start.10) | collective-permute-done | bytes 458784 | tf_op jit(solution)/shard_map/ppermute | solution.py:25
  120.8 2.4 %collective-permute-done.9 = bf16[2,7,128,128]{3,2,1,0:T(8,128)(2,1)S(1)} collective-permute-done((bf16[2,7,128,128]{3,2,1,0:T(8,128)(2,1)S(1)}, bf16[2,7,128,128]{3,2,1,0:T(8,128)(2,1)S(1)}, u32[]{:S(2)}, u32[]{:S(2)}) %collective-permute-start.9) | collective-permute-done | bytes 458784 | tf_op jit(solution)/shard_map/ppermute | solution.py:25
  123.2 0.3 fusion.33
  123.5 7.4 %collective-permute-start.17 = (bf16[2,128,128]{2,1,0:T(8,128)(2,1)S(1)}, bf16[2,128,128]{2,1,0:T(8,128)(2,1)S(1)}, u32[]{:S(2)}, u32[]{:S(2)}) collective-permute-start(bf16[2,128,128]{2,1,0:T(8,128)(2,1)S(1)} %get-tuple-element.22), channel_id=1, source_target_pairs={{96,0},{112,16},{128,32},{144,48},{160,64},{176,80},{192,96},{208,... | collective-permute-start | bytes 196616 | tf_op jit(solution)/shard_map/ppermute | solution.py:20
  130.8 6.3 %collective-permute-start.16 = (bf16[2,128,128]{2,1,0:T(8,128)(2,1)S(1)}, bf16[2,128,128]{2,1,0:T(8,128)(2,1)S(1)}, u32[]{:S(2)}, u32[]{:S(2)}) collective-permute-start(bf16[2,128,128]{2,1,0:T(8,128)(2,1)S(1)} %get-tuple-element.23), channel_id=1, source_target_pairs={{80,0},{96,16},{112,32},{128,48},{144,64},{160,80},{176,96},{192,1... | collective-permute-start | bytes 196616 | tf_op jit(solution)/shard_map/ppermute | solution.py:20
  137.2 6.8 %collective-permute-start.15 = (bf16[2,128,128]{2,1,0:T(8,128)(2,1)S(1)}, bf16[2,128,128]{2,1,0:T(8,128)(2,1)S(1)}, u32[]{:S(2)}, u32[]{:S(2)}) collective-permute-start(bf16[2,128,128]{2,1,0:T(8,128)(2,1)S(1)} %get-tuple-element.19), channel_id=1, source_target_pairs={{64,0},{80,16},{96,32},{112,48},{128,64},{144,80},{160,96},{176,11... | collective-permute-start | bytes 196616 | tf_op jit(solution)/shard_map/ppermute | solution.py:20
  144.0 1.9 collective-permute-start.14
  145.9 2.5 %collective-permute-start.13 = (bf16[2,128,128]{2,1,0:T(8,128)(2,1)S(1)}, bf16[2,128,128]{2,1,0:T(8,128)(2,1)S(1)}, u32[]{:S(2)}, u32[]{:S(2)}) collective-permute-start(bf16[2,128,128]{2,1,0:T(8,128)(2,1)S(1)} %get-tuple-element.21), channel_id=1, source_target_pairs={{32,0},{48,16},{64,32},{80,48},{96,64},{112,80},{128,96},{144,112}... | collective-permute-start | bytes 196616 | tf_op jit(solution)/shard_map/ppermute | solution.py:20
  148.4 6.8 %collective-permute-start.12 = (bf16[2,128,128]{2,1,0:T(8,128)(2,1)S(1)}, bf16[2,128,128]{2,1,0:T(8,128)(2,1)S(1)}, u32[]{:S(2)}, u32[]{:S(2)}) collective-permute-start(bf16[2,128,128]{2,1,0:T(8,128)(2,1)S(1)} %get-tuple-element.18), channel_id=1, source_target_pairs={{16,0},{32,16},{48,32},{64,48},{80,64},{96,80},{112,96},{128,112},... | collective-permute-start | bytes 196616 | tf_op jit(solution)/shard_map/ppermute | solution.py:20
  155.3 0.0 collective-permute-done.15
  155.3 3.9 %collective-permute-done.14 = bf16[2,128,128]{2,1,0:T(8,128)(2,1)S(1)} collective-permute-done((bf16[2,128,128]{2,1,0:T(8,128)(2,1)S(1)}, bf16[2,128,128]{2,1,0:T(8,128)(2,1)S(1)}, u32[]{:S(2)}, u32[]{:S(2)}) %collective-permute-start.14) | collective-permute-done | bytes 65568 | tf_op jit(solution)/shard_map/ppermute | solution.py:20
  159.2 3.5 %collective-permute-done.12 = bf16[2,128,128]{2,1,0:T(8,128)(2,1)S(1)} collective-permute-done((bf16[2,128,128]{2,1,0:T(8,128)(2,1)S(1)}, bf16[2,128,128]{2,1,0:T(8,128)(2,1)S(1)}, u32[]{:S(2)}, u32[]{:S(2)}) %collective-permute-start.12) | collective-permute-done | bytes 65568 | tf_op jit(solution)/shard_map/ppermute | solution.py:20
  162.7 0.1 fusion.14
  162.7 3.3 %collective-permute-start.20 = (bf16[2,128,128]{2,1,0:T(8,128)(2,1)S(1)}, bf16[2,128,128]{2,1,0:T(8,128)(2,1)S(1)}, u32[]{:S(2)}, u32[]{:S(2)}) collective-permute-start(bf16[2,128,128]{2,1,0:T(8,128)(2,1)S(1)} %fusion.14), channel_id=1, source_target_pairs={{0,1},{1,2},{2,3},{3,0},{4,5},{5,6},{6,7},{7,4},{8,9},{9,10},{10,1... | collective-permute-start | bytes 196616 | tf_op jit(solution)/shard_map/ppermute | solution.py:25
  166.0 3.5 %collective-permute-start.19 = (bf16[2,128,128]{2,1,0:T(8,128)(2,1)S(1)}, bf16[2,128,128]{2,1,0:T(8,128)(2,1)S(1)}, u32[]{:S(2)}, u32[]{:S(2)}) collective-permute-start(bf16[2,128,128]{2,1,0:T(8,128)(2,1)S(1)} %fusion.14), channel_id=1, source_target_pairs={{0,2},{1,3},{2,0},{3,1},{4,6},{5,7},{6,4},{7,5},{8,10},{9,11},{10,... | collective-permute-start | bytes 196616 | tf_op jit(solution)/shard_map/ppermute | solution.py:25
  169.5 2.2 %collective-permute-start.18 = (bf16[2,128,128]{2,1,0:T(8,128)(2,1)S(1)}, bf16[2,128,128]{2,1,0:T(8,128)(2,1)S(1)}, u32[]{:S(2)}, u32[]{:S(2)}) collective-permute-start(bf16[2,128,128]{2,1,0:T(8,128)(2,1)S(1)} %fusion.14), channel_id=1, source_target_pairs={{0,3},{1,0},{2,1},{3,2},{4,7},{5,4},{6,5},{7,6},{8,11},{9,8},{10,9... | collective-permute-start | bytes 196616 | tf_op jit(solution)/shard_map/ppermute | solution.py:25
  171.7 1.5 collective-permute-done.19
  173.2 3.3 %collective-permute-done.18 = bf16[2,128,128]{2,1,0:T(8,128)(2,1)S(1)} collective-permute-done((bf16[2,128,128]{2,1,0:T(8,128)(2,1)S(1)}, bf16[2,128,128]{2,1,0:T(8,128)(2,1)S(1)}, u32[]{:S(2)}, u32[]{:S(2)}) %collective-permute-start.18) | collective-permute-done | bytes 65568 | tf_op jit(solution)/shard_map/ppermute | solution.py:25
  176.6 6.8 %collective-permute-start.23 = (bf16[4,2,128,128]{3,2,1,0:T(8,128)(2,1)S(1)}, bf16[4,2,128,128]{3,2,1,0:T(8,128)(2,1)S(1)}, u32[]{:S(2)}, u32[]{:S(2)}) collective-permute-start(bf16[4,2,128,128]{3,2,1,0:T(8,128)(2,1)S(1)} %get-tuple-element.25), channel_id=1, source_target_pairs={{0,4},{4,8},{8,12},{12,0},{1,5},{5,9},{9,13},{13,1},{2,6},{6,10},{... | collective-permute-start | bytes 786440 | tf_op jit(solution)/shard_map/ppermute | solution.py:25
  183.4 3.8 %collective-permute-start.22 = (bf16[4,2,128,128]{3,2,1,0:T(8,128)(2,1)S(1)}, bf16[4,2,128,128]{3,2,1,0:T(8,128)(2,1)S(1)}, u32[]{:S(2)}, u32[]{:S(2)}) collective-permute-start(bf16[4,2,128,128]{3,2,1,0:T(8,128)(2,1)S(1)} %get-tuple-element.25), channel_id=1, source_target_pairs={{0,8},{4,12},{8,0},{12,4},{1,9},{5,13},{9,1},{13,5},{2,10},{6,14},... | collective-permute-start | bytes 786440 | tf_op jit(solution)/shard_map/ppermute | solution.py:25
  187.2 2.9 %collective-permute-start.21 = (bf16[4,2,128,128]{3,2,1,0:T(8,128)(2,1)S(1)}, bf16[4,2,128,128]{3,2,1,0:T(8,128)(2,1)S(1)}, u32[]{:S(2)}, u32[]{:S(2)}) collective-permute-start(bf16[4,2,128,128]{3,2,1,0:T(8,128)(2,1)S(1)} %get-tuple-element.25), channel_id=1, source_target_pairs={{0,12},{4,0},{8,4},{12,8},{1,13},{5,1},{9,5},{13,9},{2,14},{6,2},{... | collective-permute-start | bytes 786440 | tf_op jit(solution)/shard_map/ppermute | solution.py:25
  190.1 15.7 %collective-permute-done.22 = bf16[4,2,128,128]{3,2,1,0:T(8,128)(2,1)S(1)} collective-permute-done((bf16[4,2,128,128]{3,2,1,0:T(8,128)(2,1)S(1)}, bf16[4,2,128,128]{3,2,1,0:T(8,128)(2,1)S(1)}, u32[]{:S(2)}, u32[]{:S(2)}) %collective-permute-start.22) | collective-permute-done | bytes 262176 | tf_op jit(solution)/shard_map/ppermute | solution.py:25
  205.9 3.0 %collective-permute-done.21 = bf16[4,2,128,128]{3,2,1,0:T(8,128)(2,1)S(1)} collective-permute-done((bf16[4,2,128,128]{3,2,1,0:T(8,128)(2,1)S(1)}, bf16[4,2,128,128]{3,2,1,0:T(8,128)(2,1)S(1)}, u32[]{:S(2)}, u32[]{:S(2)}) %collective-permute-start.21) | collective-permute-done | bytes 262176 | tf_op jit(solution)/shard_map/ppermute | solution.py:25
  208.9 0.1 pad_maximum_fusion.1
  209.1 0.7 gather_fusion
  209.8 0.2 broadcast_select_fusion
  210.0 0.7 gather_fusion.1
  210.7 0.2 convert_bitcast_fusion
  211.0 0.2 fusion.35
  211.2 1.0 copy.17
  212.2 1.0 copy.18
  (25 shorter events, 0.2 us)
Async XLA Ops:
  2.1 26.0 %collective-permute-start = (bf16[2,128,128]{2,1,0:T(8,128)(2,1)S(1)}, bf16[2,128,128]{2,1,0:T(8,128)(2,1)S(1)}, u32[]{:S(2)}, u32[]{:S(2)}) collective-permute-start(bf16[2,128,128]{2,1,0:T(8,128)(2,1)S(1)} %slice.76), channel_id=1, source_target_pairs={{0,16},{16,32},{32,48},{48,64},{64,80},{80,96},{96,112},{112,128},... | collective-permute-start | bytes 196616 | tf_op jit(solution)/shard_map/ppermute | solution.py:20
  11.5 18.5 %collective-permute-start.1 = (bf16[2,128,128]{2,1,0:T(8,128)(2,1)S(1)}, bf16[2,128,128]{2,1,0:T(8,128)(2,1)S(1)}, u32[]{:S(2)}, u32[]{:S(2)}) collective-permute-start(bf16[2,128,128]{2,1,0:T(8,128)(2,1)S(1)} %slice.76), channel_id=1, source_target_pairs={{0,32},{16,48},{32,64},{48,80},{64,96},{80,112},{96,128},{112,144}... | collective-permute-start | bytes 196616 | tf_op jit(solution)/shard_map/ppermute | solution.py:20
  19.5 18.1 %collective-permute-start.2 = (bf16[2,128,128]{2,1,0:T(8,128)(2,1)S(1)}, bf16[2,128,128]{2,1,0:T(8,128)(2,1)S(1)}, u32[]{:S(2)}, u32[]{:S(2)}) collective-permute-start(bf16[2,128,128]{2,1,0:T(8,128)(2,1)S(1)} %slice.76), channel_id=1, source_target_pairs={{0,48},{16,64},{32,80},{48,96},{64,112},{80,128},{96,144},{112,160... | collective-permute-start | bytes 196616 | tf_op jit(solution)/shard_map/ppermute | solution.py:20
  23.5 17.8 %collective-permute-start.3 = (bf16[2,128,128]{2,1,0:T(8,128)(2,1)S(1)}, bf16[2,128,128]{2,1,0:T(8,128)(2,1)S(1)}, u32[]{:S(2)}, u32[]{:S(2)}) collective-permute-start(bf16[2,128,128]{2,1,0:T(8,128)(2,1)S(1)} %slice.76), channel_id=1, source_target_pairs={{0,64},{16,80},{32,96},{48,112},{64,128},{80,144},{96,160},{112,17... | collective-permute-start | bytes 196616 | tf_op jit(solution)/shard_map/ppermute | solution.py:20
  25.4 24.5 %collective-permute-start.4 = (bf16[2,128,128]{2,1,0:T(8,128)(2,1)S(1)}, bf16[2,128,128]{2,1,0:T(8,128)(2,1)S(1)}, u32[]{:S(2)}, u32[]{:S(2)}) collective-permute-start(bf16[2,128,128]{2,1,0:T(8,128)(2,1)S(1)} %slice.76), channel_id=1, source_target_pairs={{0,80},{16,96},{32,112},{48,128},{64,144},{80,160},{96,176},{112,1... | collective-permute-start | bytes 196616 | tf_op jit(solution)/shard_map/ppermute | solution.py:20
  28.1 22.2 %collective-permute-start.5 = (bf16[2,128,128]{2,1,0:T(8,128)(2,1)S(1)}, bf16[2,128,128]{2,1,0:T(8,128)(2,1)S(1)}, u32[]{:S(2)}, u32[]{:S(2)}) collective-permute-start(bf16[2,128,128]{2,1,0:T(8,128)(2,1)S(1)} %slice.76), channel_id=1, source_target_pairs={{0,96},{16,112},{32,128},{48,144},{64,160},{80,176},{96,192},{112,... | collective-permute-start | bytes 196616 | tf_op jit(solution)/shard_map/ppermute | solution.py:20
  50.4 11.8 %collective-permute-start.8 = (bf16[6,2,128,128]{3,2,1,0:T(8,128)(2,1)S(1)}, bf16[6,2,128,128]{3,2,1,0:T(8,128)(2,1)S(1)}, u32[]{:S(2)}, u32[]{:S(2)}) collective-permute-start(bf16[6,2,128,128]{3,2,1,0:T(8,128)(2,1)S(1)} %bitcast_dynamic-update-slice_fusion), channel_id=1, source_target_pairs={{0,1},{1,2},{2,3},{3,0},{4,5},{5,6},{6,7},{7,4},{8,9},{9,10},{10,1... | collective-permute-start | bytes 1179656 | tf_op jit(solution)/shard_map/ppermute | solution.py:25
  52.3 13.1 %collective-permute-start.7 = (bf16[6,2,128,128]{3,2,1,0:T(8,128)(2,1)S(1)}, bf16[6,2,128,128]{3,2,1,0:T(8,128)(2,1)S(1)}, u32[]{:S(2)}, u32[]{:S(2)}) collective-permute-start(bf16[6,2,128,128]{3,2,1,0:T(8,128)(2,1)S(1)} %bitcast_dynamic-update-slice_fusion), channel_id=1, source_target_pairs={{0,2},{1,3},{2,0},{3,1},{4,6},{5,7},{6,4},{7,5},{8,10},{9,11},{10,... | collective-permute-start | bytes 1179656 | tf_op jit(solution)/shard_map/ppermute | solution.py:25
  56.4 18.7 %collective-permute-start.6 = (bf16[6,2,128,128]{3,2,1,0:T(8,128)(2,1)S(1)}, bf16[6,2,128,128]{3,2,1,0:T(8,128)(2,1)S(1)}, u32[]{:S(2)}, u32[]{:S(2)}) collective-permute-start(bf16[6,2,128,128]{3,2,1,0:T(8,128)(2,1)S(1)} %bitcast_dynamic-update-slice_fusion), channel_id=1, source_target_pairs={{0,3},{1,0},{2,1},{3,2},{4,7},{5,4},{6,5},{7,6},{8,11},{9,8},{10,9... | collective-permute-start | bytes 1179656 | tf_op jit(solution)/shard_map/ppermute | solution.py:25
  93.6 29.6 %copy-start.1 = (f32[3584,128]{1,0:T(8,128)S(1)}, f32[3584,128]{1,0:T(8,128)}, u32[]{:S(2)}) copy-start(f32[3584,128]{1,0:T(8,128)} %get-tuple-element.8) | copy-start | bytes 5505028
  96.1 27.1 %copy-start = (f32[3584,128]{1,0:T(8,128)S(1)}, f32[3584,128]{1,0:T(8,128)}, u32[]{:S(2)}) copy-start(f32[3584,128]{1,0:T(8,128)} %get-tuple-element.7) | copy-start | bytes 5505028
  96.2 14.9 %collective-permute-start.11 = (bf16[2,7,128,128]{3,2,1,0:T(8,128)(2,1)S(1)}, bf16[2,7,128,128]{3,2,1,0:T(8,128)(2,1)S(1)}, u32[]{:S(2)}, u32[]{:S(2)}) collective-permute-start(bf16[2,7,128,128]{3,2,1,0:T(8,128)(2,1)S(1)} %get-tuple-element.14), channel_id=1, source_target_pairs={{0,3},{1,0},{2,1},{3,2},{4,7},{5,4},{6,5},{7,6},{8,11},{9,8},{10,9... | collective-permute-start | bytes 1376264 | tf_op jit(solution)/shard_map/ppermute | solution.py:25
  98.2 22.6 %collective-permute-start.10 = (bf16[2,7,128,128]{3,2,1,0:T(8,128)(2,1)S(1)}, bf16[2,7,128,128]{3,2,1,0:T(8,128)(2,1)S(1)}, u32[]{:S(2)}, u32[]{:S(2)}) collective-permute-start(bf16[2,7,128,128]{3,2,1,0:T(8,128)(2,1)S(1)} %get-tuple-element.15), channel_id=1, source_target_pairs={{0,2},{1,3},{2,0},{3,1},{4,6},{5,7},{6,4},{7,5},{8,10},{9,11},{10,... | collective-permute-start | bytes 1376264 | tf_op jit(solution)/shard_map/ppermute | solution.py:25
  102.4 20.7 %collective-permute-start.9 = (bf16[2,7,128,128]{3,2,1,0:T(8,128)(2,1)S(1)}, bf16[2,7,128,128]{3,2,1,0:T(8,128)(2,1)S(1)}, u32[]{:S(2)}, u32[]{:S(2)}) collective-permute-start(bf16[2,7,128,128]{3,2,1,0:T(8,128)(2,1)S(1)} %get-tuple-element.13), channel_id=1, source_target_pairs={{0,1},{1,2},{2,3},{3,0},{4,5},{5,6},{6,7},{7,4},{8,9},{9,10},{10,1... | collective-permute-start | bytes 1376264 | tf_op jit(solution)/shard_map/ppermute | solution.py:25
  123.5 24.9 %collective-permute-start.17 = (bf16[2,128,128]{2,1,0:T(8,128)(2,1)S(1)}, bf16[2,128,128]{2,1,0:T(8,128)(2,1)S(1)}, u32[]{:S(2)}, u32[]{:S(2)}) collective-permute-start(bf16[2,128,128]{2,1,0:T(8,128)(2,1)S(1)} %get-tuple-element.22), channel_id=1, source_target_pairs={{96,0},{112,16},{128,32},{144,48},{160,64},{176,80},{192,96},{208,... | collective-permute-start | bytes 196616 | tf_op jit(solution)/shard_map/ppermute | solution.py:20
  130.8 24.4 %collective-permute-start.16 = (bf16[2,128,128]{2,1,0:T(8,128)(2,1)S(1)}, bf16[2,128,128]{2,1,0:T(8,128)(2,1)S(1)}, u32[]{:S(2)}, u32[]{:S(2)}) collective-permute-start(bf16[2,128,128]{2,1,0:T(8,128)(2,1)S(1)} %get-tuple-element.23), channel_id=1, source_target_pairs={{80,0},{96,16},{112,32},{128,48},{144,64},{160,80},{176,96},{192,1... | collective-permute-start | bytes 196616 | tf_op jit(solution)/shard_map/ppermute | solution.py:20
  137.2 18.1 %collective-permute-start.15 = (bf16[2,128,128]{2,1,0:T(8,128)(2,1)S(1)}, bf16[2,128,128]{2,1,0:T(8,128)(2,1)S(1)}, u32[]{:S(2)}, u32[]{:S(2)}) collective-permute-start(bf16[2,128,128]{2,1,0:T(8,128)(2,1)S(1)} %get-tuple-element.19), channel_id=1, source_target_pairs={{64,0},{80,16},{96,32},{112,48},{128,64},{144,80},{160,96},{176,11... | collective-permute-start | bytes 196616 | tf_op jit(solution)/shard_map/ppermute | solution.py:20
  144.0 15.2 %collective-permute-start.14 = (bf16[2,128,128]{2,1,0:T(8,128)(2,1)S(1)}, bf16[2,128,128]{2,1,0:T(8,128)(2,1)S(1)}, u32[]{:S(2)}, u32[]{:S(2)}) collective-permute-start(bf16[2,128,128]{2,1,0:T(8,128)(2,1)S(1)} %get-tuple-element.20), channel_id=1, source_target_pairs={{48,0},{64,16},{80,32},{96,48},{112,64},{128,80},{144,96},{160,112... | collective-permute-start | bytes 196616 | tf_op jit(solution)/shard_map/ppermute | solution.py:20
  145.9 13.3 %collective-permute-start.13 = (bf16[2,128,128]{2,1,0:T(8,128)(2,1)S(1)}, bf16[2,128,128]{2,1,0:T(8,128)(2,1)S(1)}, u32[]{:S(2)}, u32[]{:S(2)}) collective-permute-start(bf16[2,128,128]{2,1,0:T(8,128)(2,1)S(1)} %get-tuple-element.21), channel_id=1, source_target_pairs={{32,0},{48,16},{64,32},{80,48},{96,64},{112,80},{128,96},{144,112}... | collective-permute-start | bytes 196616 | tf_op jit(solution)/shard_map/ppermute | solution.py:20
  148.4 14.3 %collective-permute-start.12 = (bf16[2,128,128]{2,1,0:T(8,128)(2,1)S(1)}, bf16[2,128,128]{2,1,0:T(8,128)(2,1)S(1)}, u32[]{:S(2)}, u32[]{:S(2)}) collective-permute-start(bf16[2,128,128]{2,1,0:T(8,128)(2,1)S(1)} %get-tuple-element.18), channel_id=1, source_target_pairs={{16,0},{32,16},{48,32},{64,48},{80,64},{96,80},{112,96},{128,112},... | collective-permute-start | bytes 196616 | tf_op jit(solution)/shard_map/ppermute | solution.py:20
  162.7 9.0 %collective-permute-start.20 = (bf16[2,128,128]{2,1,0:T(8,128)(2,1)S(1)}, bf16[2,128,128]{2,1,0:T(8,128)(2,1)S(1)}, u32[]{:S(2)}, u32[]{:S(2)}) collective-permute-start(bf16[2,128,128]{2,1,0:T(8,128)(2,1)S(1)} %fusion.14), channel_id=1, source_target_pairs={{0,1},{1,2},{2,3},{3,0},{4,5},{5,6},{6,7},{7,4},{8,9},{9,10},{10,1... | collective-permute-start | bytes 196616 | tf_op jit(solution)/shard_map/ppermute | solution.py:25
  166.0 7.1 %collective-permute-start.19 = (bf16[2,128,128]{2,1,0:T(8,128)(2,1)S(1)}, bf16[2,128,128]{2,1,0:T(8,128)(2,1)S(1)}, u32[]{:S(2)}, u32[]{:S(2)}) collective-permute-start(bf16[2,128,128]{2,1,0:T(8,128)(2,1)S(1)} %fusion.14), channel_id=1, source_target_pairs={{0,2},{1,3},{2,0},{3,1},{4,6},{5,7},{6,4},{7,5},{8,10},{9,11},{10,... | collective-permute-start | bytes 196616 | tf_op jit(solution)/shard_map/ppermute | solution.py:25
  169.5 7.0 %collective-permute-start.18 = (bf16[2,128,128]{2,1,0:T(8,128)(2,1)S(1)}, bf16[2,128,128]{2,1,0:T(8,128)(2,1)S(1)}, u32[]{:S(2)}, u32[]{:S(2)}) collective-permute-start(bf16[2,128,128]{2,1,0:T(8,128)(2,1)S(1)} %fusion.14), channel_id=1, source_target_pairs={{0,3},{1,0},{2,1},{3,2},{4,7},{5,4},{6,5},{7,6},{8,11},{9,8},{10,9... | collective-permute-start | bytes 196616 | tf_op jit(solution)/shard_map/ppermute | solution.py:25
  176.6 13.6 %collective-permute-start.23 = (bf16[4,2,128,128]{3,2,1,0:T(8,128)(2,1)S(1)}, bf16[4,2,128,128]{3,2,1,0:T(8,128)(2,1)S(1)}, u32[]{:S(2)}, u32[]{:S(2)}) collective-permute-start(bf16[4,2,128,128]{3,2,1,0:T(8,128)(2,1)S(1)} %get-tuple-element.25), channel_id=1, source_target_pairs={{0,4},{4,8},{8,12},{12,0},{1,5},{5,9},{9,13},{13,1},{2,6},{6,10},{... | collective-permute-start | bytes 786440 | tf_op jit(solution)/shard_map/ppermute | solution.py:25
  183.4 22.5 %collective-permute-start.22 = (bf16[4,2,128,128]{3,2,1,0:T(8,128)(2,1)S(1)}, bf16[4,2,128,128]{3,2,1,0:T(8,128)(2,1)S(1)}, u32[]{:S(2)}, u32[]{:S(2)}) collective-permute-start(bf16[4,2,128,128]{3,2,1,0:T(8,128)(2,1)S(1)} %get-tuple-element.25), channel_id=1, source_target_pairs={{0,8},{4,12},{8,0},{12,4},{1,9},{5,13},{9,1},{13,5},{2,10},{6,14},... | collective-permute-start | bytes 786440 | tf_op jit(solution)/shard_map/ppermute | solution.py:25
  187.2 21.7 %collective-permute-start.21 = (bf16[4,2,128,128]{3,2,1,0:T(8,128)(2,1)S(1)}, bf16[4,2,128,128]{3,2,1,0:T(8,128)(2,1)S(1)}, u32[]{:S(2)}, u32[]{:S(2)}) collective-permute-start(bf16[4,2,128,128]{3,2,1,0:T(8,128)(2,1)S(1)} %get-tuple-element.25), channel_id=1, source_target_pairs={{0,12},{4,0},{8,4},{12,8},{1,13},{5,1},{9,5},{13,9},{2,14},{6,2},{... | collective-permute-start | bytes 786440 | tf_op jit(solution)/shard_map/ppermute | solution.py:25

commit v4 on v3

--- a/solution.py
+++ b/solution.py
@@ -54,7 +54,7 @@
     scores = jnp.where(allowed, scores, -1e30)
     row_max = jnp.max(scores, axis=1, keepdims=True)
     shifted = jnp.exp(scores - row_max)
-    weights = shifted / jnp.sum(shifted, axis=1, keepdims=True)
+    weights = shifted * (1.0 / jnp.sum(shifted, axis=1, keepdims=True))
     weights_b = weights.astype(jnp.bfloat16)
     output = jnp.dot(weights_b, values, preferred_element_type=jnp.float32)
     row_delta = jnp.sum(do.astype(jnp.float32) * output, axis=1, keepdims=True)
@@ -175,11 +175,12 @@
             parts[:, offset].astype(jnp.bfloat16), "ctx", -offset
         ).astype(jnp.float32)
     mine = running.astype(jnp.bfloat16)
-    by_part = jnp.stack([mine] + [cycled(mine, "sub", -step) for step in range(1, parts_count)])
-    by_group = jnp.stack([by_part] + [cycled(by_part, "grp", -step) for step in range(1, groups)])
+    by_group = jnp.stack([mine] + [cycled(mine, "grp", -step) for step in range(1, groups)])
+    by_part = jnp.stack([by_group] + [cycled(by_group, "sub", -step) for step in range(1, parts_count)])
     part_order = (jnp.arange(parts_count) - part_index) % parts_count
     group_order = (jnp.arange(groups) - group_index) % groups
-    ordered = jnp.take(jnp.take(by_group, group_order, axis=0), part_order, axis=1)
+    ordered = jnp.take(jnp.take(by_part, part_order, axis=0), group_order, axis=1)
+    ordered = jnp.transpose(ordered, (1, 0, 2, 3, 4))
     summed = jnp.transpose(ordered, (2, 0, 1, 3, 4)).reshape(2, groups, tokens_here, width)
     summed = summed.astype(jnp.float32)
     return (query_grad, summed[0], summed[1])

time: 214 us -> 205 us (0.958)
  the two profiles are of different devices: /device:TPU:63 before, /device:TPU:6 now
where the time goes in v4:
time: 205 us; the launch traced here: 204 us
  starting transfers between devices  98.1 us (48%)
  waiting for transfers between devices  76.1 us (37%)
  Pallas kernels  16.9 us (8%)
  local copies, waits for them, and re-layouts  7.06 us (3%)
  other arithmetic  5.12 us (2%)
    ppermute x12, starting transfers between devices, shifted_2(): lax.ppermute(value, axis, [(source, source + steps) for source in range(l...  56.6 us
    ppermute x12, waiting for transfers between devices, cycled(): lax.ppermute(value, axis, [(source, (source + steps) % count) for source...  43.7 us
    ppermute x12, starting transfers between devices, cycled(): lax.ppermute(value, axis, [(source, (source + steps) % count) for source...  41.6 us
    ppermute x12, waiting for transfers between devices, shifted_2(): lax.ppermute(value, axis, [(source, source + steps) for source in range(l...  32.4 us
    pallas_call x1, Pallas kernels, local_grads(): pl.pallas_call(kernel, grid_spec=pltpu.PrefetchScalarGridSpec(num_scalar_...  16.9 us
  transfers between devices with their start and end apart: 24, of which 14 were waited for; matrix products, arithmetic and copies ran while one was open for 1% of the time, Pallas kernels for 0%

profile of v4, /device:TPU:6, one launch (start us, length us, event | category | flops | bytes accessed | tf_op | source)
XLA Modules:
  0.0 204.4 jit_solution(9722955639330474640)
XLA Ops:
  0.7 1.0 constant_dynamic-slice_fusion
  1.7 0.5 fusion.6
  2.1 1.9 collective-permute-start
  4.1 9.1 %collective-permute-start.1 = (bf16[2,128,128]{2,1,0:T(8,128)(2,1)S(1)}, bf16[2,128,128]{2,1,0:T(8,128)(2,1)S(1)}, u32[]{:S(2)}, u32[]{:S(2)}) collective-permute-start(bf16[2,128,128]{2,1,0:T(8,128)(2,1)S(1)} %slice.76), channel_id=1, source_target_pairs={{0,32},{16,48},{32,64},{48,80},{64,96},{80,112},{96,128},{112,144}... | collective-permute-start | bytes 196616 | tf_op jit(solution)/shard_map/ppermute | solution.py:20
  13.2 10.9 %collective-permute-start.2 = (bf16[2,128,128]{2,1,0:T(8,128)(2,1)S(1)}, bf16[2,128,128]{2,1,0:T(8,128)(2,1)S(1)}, u32[]{:S(2)}, u32[]{:S(2)}) collective-permute-start(bf16[2,128,128]{2,1,0:T(8,128)(2,1)S(1)} %slice.76), channel_id=1, source_target_pairs={{0,48},{16,64},{32,80},{48,96},{64,112},{80,128},{96,144},{112,160... | collective-permute-start | bytes 196616 | tf_op jit(solution)/shard_map/ppermute | solution.py:20
  24.1 1.9 collective-permute-start.3
  26.0 1.9 collective-permute-start.4
  28.0 0.8 constant_dynamic-slice_fusion.2
  28.7 0.0 collective-permute-done
  28.7 1.9 collective-permute-start.5
  30.7 0.0 collective-permute-done.1
  30.7 0.0 collective-permute-done.2
  30.7 9.2 %collective-permute-done.3 = bf16[2,128,128]{2,1,0:T(8,128)(2,1)S(1)} collective-permute-done((bf16[2,128,128]{2,1,0:T(8,128)(2,1)S(1)}, bf16[2,128,128]{2,1,0:T(8,128)(2,1)S(1)}, u32[]{:S(2)}, u32[]{:S(2)}) %collective-permute-start.3) | collective-permute-done | bytes 65568 | tf_op jit(solution)/shard_map/ppermute | solution.py:20
  39.9 12.5 %collective-permute-done.4 = bf16[2,128,128]{2,1,0:T(8,128)(2,1)S(1)} collective-permute-done((bf16[2,128,128]{2,1,0:T(8,128)(2,1)S(1)}, bf16[2,128,128]{2,1,0:T(8,128)(2,1)S(1)}, u32[]{:S(2)}, u32[]{:S(2)}) %collective-permute-start.4) | collective-permute-done | bytes 65568 | tf_op jit(solution)/shard_map/ppermute | solution.py:20
  52.4 0.9 collective-permute-done.5
  53.4 3.5 %collective-permute-start.8 = (bf16[6,2,128,128]{3,2,1,0:T(8,128)(2,1)S(1)}, bf16[6,2,128,128]{3,2,1,0:T(8,128)(2,1)S(1)}, u32[]{:S(2)}, u32[]{:S(2)}) collective-permute-start(bf16[6,2,128,128]{3,2,1,0:T(8,128)(2,1)S(1)} %bitcast_dynamic-update-slice_fusion), channel_id=1, source_target_pairs={{0,1},{1,2},{2,3},{3,0},{4,5},{5,6},{6,7},{7,4},{8,9},{9,10},{10,1... | collective-permute-start | bytes 1179656 | tf_op jit(solution)/shard_map/ppermute | solution.py:25
  56.9 4.8 %collective-permute-start.7 = (bf16[6,2,128,128]{3,2,1,0:T(8,128)(2,1)S(1)}, bf16[6,2,128,128]{3,2,1,0:T(8,128)(2,1)S(1)}, u32[]{:S(2)}, u32[]{:S(2)}) collective-permute-start(bf16[6,2,128,128]{3,2,1,0:T(8,128)(2,1)S(1)} %bitcast_dynamic-update-slice_fusion), channel_id=1, source_target_pairs={{0,2},{1,3},{2,0},{3,1},{4,6},{5,7},{6,4},{7,5},{8,10},{9,11},{10,... | collective-permute-start | bytes 1179656 | tf_op jit(solution)/shard_map/ppermute | solution.py:25
  61.7 3.3 %collective-permute-start.6 = (bf16[6,2,128,128]{3,2,1,0:T(8,128)(2,1)S(1)}, bf16[6,2,128,128]{3,2,1,0:T(8,128)(2,1)S(1)}, u32[]{:S(2)}, u32[]{:S(2)}) collective-permute-start(bf16[6,2,128,128]{3,2,1,0:T(8,128)(2,1)S(1)} %bitcast_dynamic-update-slice_fusion), channel_id=1, source_target_pairs={{0,3},{1,0},{2,1},{3,2},{4,7},{5,4},{6,5},{7,6},{8,11},{9,8},{10,9... | collective-permute-start | bytes 1179656 | tf_op jit(solution)/shard_map/ppermute | solution.py:25
  65.0 0.6 select_select_fusion
  65.6 0.1 broadcast_in_dim.31
  65.7 0.7 reshape_reshape.3.code_ref
  66.4 0.5 fusion.38
  66.8 1.1 collective-permute-done.8
  68.0 9.6 %collective-permute-done.7 = bf16[6,2,128,128]{3,2,1,0:T(8,128)(2,1)S(1)} collective-permute-done((bf16[6,2,128,128]{3,2,1,0:T(8,128)(2,1)S(1)}, bf16[6,2,128,128]{3,2,1,0:T(8,128)(2,1)S(1)}, u32[]{:S(2)}, u32[]{:S(2)}) %collective-permute-start.7) | collective-permute-done | bytes 393248 | tf_op jit(solution)/shard_map/ppermute | solution.py:25
  77.6 1.4 collective-permute-done.6
  78.9 0.1 maximum_maximum_fusion
  79.1 1.4 fusion.37
  80.4 16.9 %shard_map.85 = (bf16[2048,128]{1,0:T(8,128)(2,1)}, f32[3584,128]{1,0:T(8,128)}, f32[3584,128]{1,0:T(8,128)}) custom-call(s32[8,16]{1,0:T(8,128)} %get-tuple-element.27.slots_ref, bf16[2048,128]{1,0:T(8,128)(2,1)} %bitcast.92, bf16[2048,128]{1,0:T(8,128)(2,1)} %bitcast.93, s32[8,1,1024]{2,1,0:T(1,128)} %reshape_reshape.3.code_ref, ...), custom_call_target="tpu_custom_call" | custom-call | tf_op jit(solution)/shard_map/pallas_call | solution.py:90
  97.4 2.5 %fusion = bf16[2,7,512,128]{3,2,1,0:T(8,128)(2,1)S(1)} fusion(f32[1,7,512,128]{3,2,1,0:T(8,128)} %bitcast.86, f32[1,7,512,128]{3,2,1,0:T(8,128)} %bitcast.84), kind=kLoop, calls=%fused_computation.5 | loop fusion | flops 917504 | bytes 5505024 | tf_op jit(solution)/shard_map/convert_element_type | solution.py:167
  99.9 0.1 fusion.36
  100.0 4.7 %collective-permute-start.11 = (bf16[2,7,128,128]{3,2,1,0:T(8,128)(2,1)S(1)}, bf16[2,7,128,128]{3,2,1,0:T(8,128)(2,1)S(1)}, u32[]{:S(2)}, u32[]{:S(2)}) collective-permute-start(bf16[2,7,128,128]{3,2,1,0:T(8,128)(2,1)S(1)} %get-tuple-element.14), channel_id=1, source_target_pairs={{0,3},{1,0},{2,1},{3,2},{4,7},{5,4},{6,5},{7,6},{8,11},{9,8},{10,9... | collective-permute-start | bytes 1376264 | tf_op jit(solution)/shard_map/ppermute | solution.py:25
  104.6 3.8 %collective-permute-start.10 = (bf16[2,7,128,128]{3,2,1,0:T(8,128)(2,1)S(1)}, bf16[2,7,128,128]{3,2,1,0:T(8,128)(2,1)S(1)}, u32[]{:S(2)}, u32[]{:S(2)}) collective-permute-start(bf16[2,7,128,128]{3,2,1,0:T(8,128)(2,1)S(1)} %get-tuple-element.15), channel_id=1, source_target_pairs={{0,2},{1,3},{2,0},{3,1},{4,6},{5,7},{6,4},{7,5},{8,10},{9,11},{10,... | collective-permute-start | bytes 1376264 | tf_op jit(solution)/shard_map/ppermute | solution.py:25
  108.5 1.9 collective-permute-start.9
  110.4 14.0 %collective-permute-done.11 = bf16[2,7,128,128]{3,2,1,0:T(8,128)(2,1)S(1)} collective-permute-done((bf16[2,7,128,128]{3,2,1,0:T(8,128)(2,1)S(1)}, bf16[2,7,128,128]{3,2,1,0:T(8,128)(2,1)S(1)}, u32[]{:S(2)}, u32[]{:S(2)}) %collective-permute-start.11) | collective-permute-done | bytes 458784 | tf_op jit(solution)/shard_map/ppermute | solution.py:25
  124.5 0.0 collective-permute-done.10
  124.5 5.6 %collective-permute-done.9 = bf16[2,7,128,128]{3,2,1,0:T(8,128)(2,1)S(1)} collective-permute-done((bf16[2,7,128,128]{3,2,1,0:T(8,128)(2,1)S(1)}, bf16[2,7,128,128]{3,2,1,0:T(8,128)(2,1)S(1)}, u32[]{:S(2)}, u32[]{:S(2)}) %collective-permute-start.9) | collective-permute-done | bytes 458784 | tf_op jit(solution)/shard_map/ppermute | solution.py:25
  130.1 0.3 fusion.33
  130.4 1.9 collective-permute-start.17
  132.3 8.0 %collective-permute-start.16 = (bf16[2,128,128]{2,1,0:T(8,128)(2,1)S(1)}, bf16[2,128,128]{2,1,0:T(8,128)(2,1)S(1)}, u32[]{:S(2)}, u32[]{:S(2)}) collective-permute-start(bf16[2,128,128]{2,1,0:T(8,128)(2,1)S(1)} %get-tuple-element.23), channel_id=1, source_target_pairs={{80,0},{96,16},{112,32},{128,48},{144,64},{160,80},{176,96},{192,1... | collective-permute-start | bytes 196616 | tf_op jit(solution)/shard_map/ppermute | solution.py:20
  140.3 1.9 collective-permute-start.15
  142.2 12.2 %collective-permute-start.14 = (bf16[2,128,128]{2,1,0:T(8,128)(2,1)S(1)}, bf16[2,128,128]{2,1,0:T(8,128)(2,1)S(1)}, u32[]{:S(2)}, u32[]{:S(2)}) collective-permute-start(bf16[2,128,128]{2,1,0:T(8,128)(2,1)S(1)} %get-tuple-element.20), channel_id=1, source_target_pairs={{48,0},{64,16},{80,32},{96,48},{112,64},{128,80},{144,96},{160,112... | collective-permute-start | bytes 196616 | tf_op jit(solution)/shard_map/ppermute | solution.py:20
  154.4 2.9 %collective-permute-start.13 = (bf16[2,128,128]{2,1,0:T(8,128)(2,1)S(1)}, bf16[2,128,128]{2,1,0:T(8,128)(2,1)S(1)}, u32[]{:S(2)}, u32[]{:S(2)}) collective-permute-start(bf16[2,128,128]{2,1,0:T(8,128)(2,1)S(1)} %get-tuple-element.21), channel_id=1, source_target_pairs={{32,0},{48,16},{64,32},{80,48},{96,64},{112,80},{128,96},{144,112}... | collective-permute-start | bytes 196616 | tf_op jit(solution)/shard_map/ppermute | solution.py:20
  157.4 0.0 collective-permute-done.17
  157.4 1.9 collective-permute-start.12
  159.3 0.0 collective-permute-done.15
  159.3 1.5 collective-permute-done.14
  160.8 8.3 %collective-permute-done.13 = bf16[2,128,128]{2,1,0:T(8,128)(2,1)S(1)} collective-permute-done((bf16[2,128,128]{2,1,0:T(8,128)(2,1)S(1)}, bf16[2,128,128]{2,1,0:T(8,128)(2,1)S(1)}, u32[]{:S(2)}, u32[]{:S(2)}) %collective-permute-start.13) | collective-permute-done | bytes 65568 | tf_op jit(solution)/shard_map/ppermute | solution.py:20
  169.1 0.1 fusion.14
  169.2 1.9 collective-permute-start.20
  171.1 1.9 collective-permute-start.19
  173.0 5.7 %collective-permute-start.18 = (bf16[2,128,128]{2,1,0:T(8,128)(2,1)S(1)}, bf16[2,128,128]{2,1,0:T(8,128)(2,1)S(1)}, u32[]{:S(2)}, u32[]{:S(2)}) collective-permute-start(bf16[2,128,128]{2,1,0:T(8,128)(2,1)S(1)} %fusion.14), channel_id=1, source_target_pairs={{0,12},{4,0},{8,4},{12,8},{1,13},{5,1},{9,5},{13,9},{2,14},{6,2},{... | collective-permute-start | bytes 196616 | tf_op jit(solution)/shard_map/ppermute | solution.py:25
  178.8 1.6 collective-permute-done.19
  180.4 1.4 collective-permute-done.18
  181.8 3.5 %collective-permute-start.23 = (bf16[4,2,128,128]{3,2,1,0:T(8,128)(2,1)S(1)}, bf16[4,2,128,128]{3,2,1,0:T(8,128)(2,1)S(1)}, u32[]{:S(2)}, u32[]{:S(2)}) collective-permute-start(bf16[4,2,128,128]{3,2,1,0:T(8,128)(2,1)S(1)} %get-tuple-element.25), channel_id=1, source_target_pairs={{0,1},{1,2},{2,3},{3,0},{4,5},{5,6},{6,7},{7,4},{8,9},{9,10},{10,1... | collective-permute-start | bytes 786440 | tf_op jit(solution)/shard_map/ppermute | solution.py:25
  185.3 3.0 %collective-permute-start.22 = (bf16[4,2,128,128]{3,2,1,0:T(8,128)(2,1)S(1)}, bf16[4,2,128,128]{3,2,1,0:T(8,128)(2,1)S(1)}, u32[]{:S(2)}, u32[]{:S(2)}) collective-permute-start(bf16[4,2,128,128]{3,2,1,0:T(8,128)(2,1)S(1)} %get-tuple-element.25), channel_id=1, source_target_pairs={{0,2},{1,3},{2,0},{3,1},{4,6},{5,7},{6,4},{7,5},{8,10},{9,11},{10,... | collective-permute-start | bytes 786440 | tf_op jit(solution)/shard_map/ppermute | solution.py:25
  188.3 3.6 %collective-permute-start.21 = (bf16[4,2,128,128]{3,2,1,0:T(8,128)(2,1)S(1)}, bf16[4,2,128,128]{3,2,1,0:T(8,128)(2,1)S(1)}, u32[]{:S(2)}, u32[]{:S(2)}) collective-permute-start(bf16[4,2,128,128]{3,2,1,0:T(8,128)(2,1)S(1)} %get-tuple-element.25), channel_id=1, source_target_pairs={{0,3},{1,0},{2,1},{3,2},{4,7},{5,4},{6,5},{7,6},{8,11},{9,8},{10,9... | collective-permute-start | bytes 786440 | tf_op jit(solution)/shard_map/ppermute | solution.py:25
  191.9 6.5 %collective-permute-done.23 = bf16[4,2,128,128]{3,2,1,0:T(8,128)(2,1)S(1)} collective-permute-done((bf16[4,2,128,128]{3,2,1,0:T(8,128)(2,1)S(1)}, bf16[4,2,128,128]{3,2,1,0:T(8,128)(2,1)S(1)}, u32[]{:S(2)}, u32[]{:S(2)}) %collective-permute-start.23) | collective-permute-done | bytes 262176 | tf_op jit(solution)/shard_map/ppermute | solution.py:25
  198.4 2.5 %collective-permute-done.21 = bf16[4,2,128,128]{3,2,1,0:T(8,128)(2,1)S(1)} collective-permute-done((bf16[4,2,128,128]{3,2,1,0:T(8,128)(2,1)S(1)}, bf16[4,2,128,128]{3,2,1,0:T(8,128)(2,1)S(1)}, u32[]{:S(2)}, u32[]{:S(2)}) %collective-permute-start.21) | collective-permute-done | bytes 262176 | tf_op jit(solution)/shard_map/ppermute | solution.py:25
  200.9 0.1 pad_maximum_fusion.1
  201.0 0.7 gather_fusion
  201.8 0.2 broadcast_select_fusion
  201.9 0.7 gather_fusion.1
  202.7 0.2 convert_bitcast_fusion
  202.9 1.5 fusion.35
  (23 shorter events, 0.2 us)
Async XLA Ops:
  2.1 26.6 %collective-permute-start = (bf16[2,128,128]{2,1,0:T(8,128)(2,1)S(1)}, bf16[2,128,128]{2,1,0:T(8,128)(2,1)S(1)}, u32[]{:S(2)}, u32[]{:S(2)}) collective-permute-start(bf16[2,128,128]{2,1,0:T(8,128)(2,1)S(1)} %slice.76), channel_id=1, source_target_pairs={{0,16},{16,32},{32,48},{48,64},{64,80},{80,96},{96,112},{112,128},... | collective-permute-start | bytes 196616 | tf_op jit(solution)/shard_map/ppermute | solution.py:20
  4.1 26.6 %collective-permute-start.1 = (bf16[2,128,128]{2,1,0:T(8,128)(2,1)S(1)}, bf16[2,128,128]{2,1,0:T(8,128)(2,1)S(1)}, u32[]{:S(2)}, u32[]{:S(2)}) collective-permute-start(bf16[2,128,128]{2,1,0:T(8,128)(2,1)S(1)} %slice.76), channel_id=1, source_target_pairs={{0,32},{16,48},{32,64},{48,80},{64,96},{80,112},{96,128},{112,144}... | collective-permute-start | bytes 196616 | tf_op jit(solution)/shard_map/ppermute | solution.py:20
  13.2 17.5 %collective-permute-start.2 = (bf16[2,128,128]{2,1,0:T(8,128)(2,1)S(1)}, bf16[2,128,128]{2,1,0:T(8,128)(2,1)S(1)}, u32[]{:S(2)}, u32[]{:S(2)}) collective-permute-start(bf16[2,128,128]{2,1,0:T(8,128)(2,1)S(1)} %slice.76), channel_id=1, source_target_pairs={{0,48},{16,64},{32,80},{48,96},{64,112},{80,128},{96,144},{112,160... | collective-permute-start | bytes 196616 | tf_op jit(solution)/shard_map/ppermute | solution.py:20
  24.1 15.8 %collective-permute-start.3 = (bf16[2,128,128]{2,1,0:T(8,128)(2,1)S(1)}, bf16[2,128,128]{2,1,0:T(8,128)(2,1)S(1)}, u32[]{:S(2)}, u32[]{:S(2)}) collective-permute-start(bf16[2,128,128]{2,1,0:T(8,128)(2,1)S(1)} %slice.76), channel_id=1, source_target_pairs={{0,64},{16,80},{32,96},{48,112},{64,128},{80,144},{96,160},{112,17... | collective-permute-start | bytes 196616 | tf_op jit(solution)/shard_map/ppermute | solution.py:20
  26.0 26.4 %collective-permute-start.4 = (bf16[2,128,128]{2,1,0:T(8,128)(2,1)S(1)}, bf16[2,128,128]{2,1,0:T(8,128)(2,1)S(1)}, u32[]{:S(2)}, u32[]{:S(2)}) collective-permute-start(bf16[2,128,128]{2,1,0:T(8,128)(2,1)S(1)} %slice.76), channel_id=1, source_target_pairs={{0,80},{16,96},{32,112},{48,128},{64,144},{80,160},{96,176},{112,1... | collective-permute-start | bytes 196616 | tf_op jit(solution)/shard_map/ppermute | solution.py:20
  28.7 24.6 %collective-permute-start.5 = (bf16[2,128,128]{2,1,0:T(8,128)(2,1)S(1)}, bf16[2,128,128]{2,1,0:T(8,128)(2,1)S(1)}, u32[]{:S(2)}, u32[]{:S(2)}) collective-permute-start(bf16[2,128,128]{2,1,0:T(8,128)(2,1)S(1)} %slice.76), channel_id=1, source_target_pairs={{0,96},{16,112},{32,128},{48,144},{64,160},{80,176},{96,192},{112,... | collective-permute-start | bytes 196616 | tf_op jit(solution)/shard_map/ppermute | solution.py:20
  53.4 14.6 %collective-permute-start.8 = (bf16[6,2,128,128]{3,2,1,0:T(8,128)(2,1)S(1)}, bf16[6,2,128,128]{3,2,1,0:T(8,128)(2,1)S(1)}, u32[]{:S(2)}, u32[]{:S(2)}) collective-permute-start(bf16[6,2,128,128]{3,2,1,0:T(8,128)(2,1)S(1)} %bitcast_dynamic-update-slice_fusion), channel_id=1, source_target_pairs={{0,1},{1,2},{2,3},{3,0},{4,5},{5,6},{6,7},{7,4},{8,9},{9,10},{10,1... | collective-permute-start | bytes 1179656 | tf_op jit(solution)/shard_map/ppermute | solution.py:25
  56.9 20.7 %collective-permute-start.7 = (bf16[6,2,128,128]{3,2,1,0:T(8,128)(2,1)S(1)}, bf16[6,2,128,128]{3,2,1,0:T(8,128)(2,1)S(1)}, u32[]{:S(2)}, u32[]{:S(2)}) collective-permute-start(bf16[6,2,128,128]{3,2,1,0:T(8,128)(2,1)S(1)} %bitcast_dynamic-update-slice_fusion), channel_id=1, source_target_pairs={{0,2},{1,3},{2,0},{3,1},{4,6},{5,7},{6,4},{7,5},{8,10},{9,11},{10,... | collective-permute-start | bytes 1179656 | tf_op jit(solution)/shard_map/ppermute | solution.py:25
  61.7 17.3 %collective-permute-start.6 = (bf16[6,2,128,128]{3,2,1,0:T(8,128)(2,1)S(1)}, bf16[6,2,128,128]{3,2,1,0:T(8,128)(2,1)S(1)}, u32[]{:S(2)}, u32[]{:S(2)}) collective-permute-start(bf16[6,2,128,128]{3,2,1,0:T(8,128)(2,1)S(1)} %bitcast_dynamic-update-slice_fusion), channel_id=1, source_target_pairs={{0,3},{1,0},{2,1},{3,2},{4,7},{5,4},{6,5},{7,6},{8,11},{9,8},{10,9... | collective-permute-start | bytes 1179656 | tf_op jit(solution)/shard_map/ppermute | solution.py:25
  97.4 32.7 %copy-start.1 = (f32[3584,128]{1,0:T(8,128)S(1)}, f32[3584,128]{1,0:T(8,128)}, u32[]{:S(2)}) copy-start(f32[3584,128]{1,0:T(8,128)} %get-tuple-element.8) | copy-start | bytes 5505028
  99.9 30.2 %copy-start = (f32[3584,128]{1,0:T(8,128)S(1)}, f32[3584,128]{1,0:T(8,128)}, u32[]{:S(2)}) copy-start(f32[3584,128]{1,0:T(8,128)} %get-tuple-element.7) | copy-start | bytes 5505028
  100.0 24.5 %collective-permute-start.11 = (bf16[2,7,128,128]{3,2,1,0:T(8,128)(2,1)S(1)}, bf16[2,7,128,128]{3,2,1,0:T(8,128)(2,1)S(1)}, u32[]{:S(2)}, u32[]{:S(2)}) collective-permute-start(bf16[2,7,128,128]{3,2,1,0:T(8,128)(2,1)S(1)} %get-tuple-element.14), channel_id=1, source_target_pairs={{0,3},{1,0},{2,1},{3,2},{4,7},{5,4},{6,5},{7,6},{8,11},{9,8},{10,9... | collective-permute-start | bytes 1376264 | tf_op jit(solution)/shard_map/ppermute | solution.py:25
  104.6 19.8 %collective-permute-start.10 = (bf16[2,7,128,128]{3,2,1,0:T(8,128)(2,1)S(1)}, bf16[2,7,128,128]{3,2,1,0:T(8,128)(2,1)S(1)}, u32[]{:S(2)}, u32[]{:S(2)}) collective-permute-start(bf16[2,7,128,128]{3,2,1,0:T(8,128)(2,1)S(1)} %get-tuple-element.15), channel_id=1, source_target_pairs={{0,2},{1,3},{2,0},{3,1},{4,6},{5,7},{6,4},{7,5},{8,10},{9,11},{10,... | collective-permute-start | bytes 1376264 | tf_op jit(solution)/shard_map/ppermute | solution.py:25
  108.5 21.6 %collective-permute-start.9 = (bf16[2,7,128,128]{3,2,1,0:T(8,128)(2,1)S(1)}, bf16[2,7,128,128]{3,2,1,0:T(8,128)(2,1)S(1)}, u32[]{:S(2)}, u32[]{:S(2)}) collective-permute-start(bf16[2,7,128,128]{3,2,1,0:T(8,128)(2,1)S(1)} %get-tuple-element.13), channel_id=1, source_target_pairs={{0,1},{1,2},{2,3},{3,0},{4,5},{5,6},{6,7},{7,4},{8,9},{9,10},{10,1... | collective-permute-start | bytes 1376264 | tf_op jit(solution)/shard_map/ppermute | solution.py:25
  130.4 27.0 %collective-permute-start.17 = (bf16[2,128,128]{2,1,0:T(8,128)(2,1)S(1)}, bf16[2,128,128]{2,1,0:T(8,128)(2,1)S(1)}, u32[]{:S(2)}, u32[]{:S(2)}) collective-permute-start(bf16[2,128,128]{2,1,0:T(8,128)(2,1)S(1)} %get-tuple-element.22), channel_id=1, source_target_pairs={{96,0},{112,16},{128,32},{144,48},{160,64},{176,80},{192,96},{208,... | collective-permute-start | bytes 196616 | tf_op jit(solution)/shard_map/ppermute | solution.py:20
  132.3 27.0 %collective-permute-start.16 = (bf16[2,128,128]{2,1,0:T(8,128)(2,1)S(1)}, bf16[2,128,128]{2,1,0:T(8,128)(2,1)S(1)}, u32[]{:S(2)}, u32[]{:S(2)}) collective-permute-start(bf16[2,128,128]{2,1,0:T(8,128)(2,1)S(1)} %get-tuple-element.23), channel_id=1, source_target_pairs={{80,0},{96,16},{112,32},{128,48},{144,64},{160,80},{176,96},{192,1... | collective-permute-start | bytes 196616 | tf_op jit(solution)/shard_map/ppermute | solution.py:20
  140.3 19.0 %collective-permute-start.15 = (bf16[2,128,128]{2,1,0:T(8,128)(2,1)S(1)}, bf16[2,128,128]{2,1,0:T(8,128)(2,1)S(1)}, u32[]{:S(2)}, u32[]{:S(2)}) collective-permute-start(bf16[2,128,128]{2,1,0:T(8,128)(2,1)S(1)} %get-tuple-element.19), channel_id=1, source_target_pairs={{64,0},{80,16},{96,32},{112,48},{128,64},{144,80},{160,96},{176,11... | collective-permute-start | bytes 196616 | tf_op jit(solution)/shard_map/ppermute | solution.py:20
  142.2 18.6 %collective-permute-start.14 = (bf16[2,128,128]{2,1,0:T(8,128)(2,1)S(1)}, bf16[2,128,128]{2,1,0:T(8,128)(2,1)S(1)}, u32[]{:S(2)}, u32[]{:S(2)}) collective-permute-start(bf16[2,128,128]{2,1,0:T(8,128)(2,1)S(1)} %get-tuple-element.20), channel_id=1, source_target_pairs={{48,0},{64,16},{80,32},{96,48},{112,64},{128,80},{144,96},{160,112... | collective-permute-start | bytes 196616 | tf_op jit(solution)/shard_map/ppermute | solution.py:20
  154.4 14.7 %collective-permute-start.13 = (bf16[2,128,128]{2,1,0:T(8,128)(2,1)S(1)}, bf16[2,128,128]{2,1,0:T(8,128)(2,1)S(1)}, u32[]{:S(2)}, u32[]{:S(2)}) collective-permute-start(bf16[2,128,128]{2,1,0:T(8,128)(2,1)S(1)} %get-tuple-element.21), channel_id=1, source_target_pairs={{32,0},{48,16},{64,32},{80,48},{96,64},{112,80},{128,96},{144,112}... | collective-permute-start | bytes 196616 | tf_op jit(solution)/shard_map/ppermute | solution.py:20
  157.4 11.7 %collective-permute-start.12 = (bf16[2,128,128]{2,1,0:T(8,128)(2,1)S(1)}, bf16[2,128,128]{2,1,0:T(8,128)(2,1)S(1)}, u32[]{:S(2)}, u32[]{:S(2)}) collective-permute-start(bf16[2,128,128]{2,1,0:T(8,128)(2,1)S(1)} %get-tuple-element.18), channel_id=1, source_target_pairs={{16,0},{32,16},{48,32},{64,48},{80,64},{96,80},{112,96},{128,112},... | collective-permute-start | bytes 196616 | tf_op jit(solution)/shard_map/ppermute | solution.py:20
  169.2 9.6 %collective-permute-start.20 = (bf16[2,128,128]{2,1,0:T(8,128)(2,1)S(1)}, bf16[2,128,128]{2,1,0:T(8,128)(2,1)S(1)}, u32[]{:S(2)}, u32[]{:S(2)}) collective-permute-start(bf16[2,128,128]{2,1,0:T(8,128)(2,1)S(1)} %fusion.14), channel_id=1, source_target_pairs={{0,4},{4,8},{8,12},{12,0},{1,5},{5,9},{9,13},{13,1},{2,6},{6,10},{... | collective-permute-start | bytes 196616 | tf_op jit(solution)/shard_map/ppermute | solution.py:25
  171.1 9.2 %collective-permute-start.19 = (bf16[2,128,128]{2,1,0:T(8,128)(2,1)S(1)}, bf16[2,128,128]{2,1,0:T(8,128)(2,1)S(1)}, u32[]{:S(2)}, u32[]{:S(2)}) collective-permute-start(bf16[2,128,128]{2,1,0:T(8,128)(2,1)S(1)} %fusion.14), channel_id=1, source_target_pairs={{0,8},{4,12},{8,0},{12,4},{1,9},{5,13},{9,1},{13,5},{2,10},{6,14},... | collective-permute-start | bytes 196616 | tf_op jit(solution)/shard_map/ppermute | solution.py:25
  173.0 8.7 %collective-permute-start.18 = (bf16[2,128,128]{2,1,0:T(8,128)(2,1)S(1)}, bf16[2,128,128]{2,1,0:T(8,128)(2,1)S(1)}, u32[]{:S(2)}, u32[]{:S(2)}) collective-permute-start(bf16[2,128,128]{2,1,0:T(8,128)(2,1)S(1)} %fusion.14), channel_id=1, source_target_pairs={{0,12},{4,0},{8,4},{12,8},{1,13},{5,1},{9,5},{13,9},{2,14},{6,2},{... | collective-permute-start | bytes 196616 | tf_op jit(solution)/shard_map/ppermute | solution.py:25
  181.8 16.6 %collective-permute-start.23 = (bf16[4,2,128,128]{3,2,1,0:T(8,128)(2,1)S(1)}, bf16[4,2,128,128]{3,2,1,0:T(8,128)(2,1)S(1)}, u32[]{:S(2)}, u32[]{:S(2)}) collective-permute-start(bf16[4,2,128,128]{3,2,1,0:T(8,128)(2,1)S(1)} %get-tuple-element.25), channel_id=1, source_target_pairs={{0,1},{1,2},{2,3},{3,0},{4,5},{5,6},{6,7},{7,4},{8,9},{9,10},{10,1... | collective-permute-start | bytes 786440 | tf_op jit(solution)/shard_map/ppermute | solution.py:25
  185.3 13.1 %collective-permute-start.22 = (bf16[4,2,128,128]{3,2,1,0:T(8,128)(2,1)S(1)}, bf16[4,2,128,128]{3,2,1,0:T(8,128)(2,1)S(1)}, u32[]{:S(2)}, u32[]{:S(2)}) collective-permute-start(bf16[4,2,128,128]{3,2,1,0:T(8,128)(2,1)S(1)} %get-tuple-element.25), channel_id=1, source_target_pairs={{0,2},{1,3},{2,0},{3,1},{4,6},{5,7},{6,4},{7,5},{8,10},{9,11},{10,... | collective-permute-start | bytes 786440 | tf_op jit(solution)/shard_map/ppermute | solution.py:25
  188.3 12.6 %collective-permute-start.21 = (bf16[4,2,128,128]{3,2,1,0:T(8,128)(2,1)S(1)}, bf16[4,2,128,128]{3,2,1,0:T(8,128)(2,1)S(1)}, u32[]{:S(2)}, u32[]{:S(2)}) collective-permute-start(bf16[4,2,128,128]{3,2,1,0:T(8,128)(2,1)S(1)} %get-tuple-element.25), channel_id=1, source_target_pairs={{0,3},{1,0},{2,1},{3,2},{4,7},{5,4},{6,5},{7,6},{8,11},{9,8},{10,9... | collective-permute-start | bytes 786440 | tf_op jit(solution)/shard_map/ppermute | solution.py:25

commit v5 on v4

--- a/solution.py
+++ b/solution.py
@@ -165,15 +165,18 @@
     )
     grads = jnp.stack([key_grad, value_grad]).reshape(2, reach_span, tokens_here, width)
     sent = grads.astype(jnp.bfloat16)
-    parts = grads[:, :, :quarter]
-    for step in range(1, parts_count):
-        piece = sent[:, :, step * quarter:(step + 1) * quarter]
-        parts = parts + cycled(piece, "sub", step).astype(jnp.float32)
-    running = parts[:, 0]
-    for offset in range(1, reach_span):
-        running = running + shifted_2(
-            parts[:, offset].astype(jnp.bfloat16), "ctx", -offset
-        ).astype(jnp.float32)
+    split = REACH // 2 + 1
+    running = None
+    for lo, hi in ((split, reach_span), (0, split)):
+        part = grads[:, lo:hi, :quarter]
+        for step in range(1, parts_count):
+            piece = sent[:, lo:hi, step * quarter:(step + 1) * quarter]
+            part = part + cycled(piece, "sub", step).astype(jnp.float32)
+        for offset in range(lo, hi):
+            term = part[:, offset - lo]
+            if offset:
+                term = shifted_2(term.astype(jnp.bfloat16), "ctx", -offset).astype(jnp.float32)
+            running = term if running is None else running + term
     mine = running.astype(jnp.bfloat16)
     by_group = jnp.stack([mine] + [cycled(mine, "grp", -step) for step in range(1, groups)])
     by_part = jnp.stack([by_group] + [cycled(by_group, "sub", -step) for step in range(1, parts_count)])

time: 205 us -> 202 us (0.985)
  waiting for transfers between devices: 76.1 us -> 64.3 us
  starting transfers between devices: 98.1 us -> 107 us
    ppermute x12 -> x15, waiting for transfers between devices: 43.7 us -> 32.2 us  [cycled(): lax.ppermute(value, axis, [(source, (source + steps) % count) for source...]
    ppermute x12 -> x15, starting transfers between devices: 41.6 us -> 50.1 us  [cycled(): lax.ppermute(value, axis, [(source, (source + steps) % count) for source...]
    convert_element_type x1 -> x0, other arithmetic: 2.48 us -> none  [per_device(): sent = grads.astype(jnp.bfloat16)]
  transfers between devices with their start and end apart: 24 -> 27, of which waited for: 14 -> 12; matrix products, arithmetic and copies ran while one was open for 1% -> 2% of each run, Pallas kernels for 0% -> 0%
where the time goes in v5:
time: 202 us; the launch traced here: 200 us
  starting transfers between devices  107 us (53%)
  waiting for transfers between devices  64.3 us (32%)
  Pallas kernels  16.9 us (8%)
  local copies, waits for them, and re-layouts  6.96 us (3%)
  other arithmetic  4.34 us (2%)
    ppermute x12, starting transfers between devices, shifted_2(): lax.ppermute(value, axis, [(source, source + steps) for source in range(l...  56.6 us
    ppermute x15, starting transfers between devices, cycled(): lax.ppermute(value, axis, [(source, (source + steps) % count) for source...  50.1 us
    ppermute x15, waiting for transfers between devices, cycled(): lax.ppermute(value, axis, [(source, (source + steps) % count) for source...  32.2 us
    ppermute x12, waiting for transfers between devices, shifted_2(): lax.ppermute(value, axis, [(source, source + steps) for source in range(l...  32 us
    pallas_call x1, Pallas kernels, local_grads(): pl.pallas_call(kernel, grid_spec=pltpu.PrefetchScalarGridSpec(num_scalar_...  16.9 us
  transfers between devices with their start and end apart: 27, of which 12 were waited for; matrix products, arithmetic and copies ran while one was open for 2% of the time, Pallas kernels for 0%

profile of v5, /device:TPU:6, one launch (start us, length us, event | category | flops | bytes accessed | tf_op | source)
XLA Modules:
  0.0 200.4 jit_solution(388046336505507474)
XLA Ops:
  0.7 1.0 constant_dynamic-slice_fusion
  1.7 0.5 fusion.8
  2.1 1.9 collective-permute-start
  4.1 9.1 %collective-permute-start.1 = (bf16[2,128,128]{2,1,0:T(8,128)(2,1)S(1)}, bf16[2,128,128]{2,1,0:T(8,128)(2,1)S(1)}, u32[]{:S(2)}, u32[]{:S(2)}) collective-permute-start(bf16[2,128,128]{2,1,0:T(8,128)(2,1)S(1)} %slice.92), channel_id=1, source_target_pairs={{0,32},{16,48},{32,64},{48,80},{64,96},{80,112},{96,128},{112,144}... | collective-permute-start | bytes 196616 | tf_op jit(solution)/shard_map/ppermute | solution.py:20
  13.2 10.9 %collective-permute-start.2 = (bf16[2,128,128]{2,1,0:T(8,128)(2,1)S(1)}, bf16[2,128,128]{2,1,0:T(8,128)(2,1)S(1)}, u32[]{:S(2)}, u32[]{:S(2)}) collective-permute-start(bf16[2,128,128]{2,1,0:T(8,128)(2,1)S(1)} %slice.92), channel_id=1, source_target_pairs={{0,48},{16,64},{32,80},{48,96},{64,112},{80,128},{96,144},{112,160... | collective-permute-start | bytes 196616 | tf_op jit(solution)/shard_map/ppermute | solution.py:20
  24.1 1.9 collective-permute-start.3
  26.0 1.9 collective-permute-start.4
  28.0 0.8 constant_dynamic-slice_fusion.2
  28.7 0.0 collective-permute-done
  28.7 1.9 collective-permute-start.5
  30.7 0.0 collective-permute-done.1
  30.7 0.0 collective-permute-done.2
  30.7 9.2 %collective-permute-done.3 = bf16[2,128,128]{2,1,0:T(8,128)(2,1)S(1)} collective-permute-done((bf16[2,128,128]{2,1,0:T(8,128)(2,1)S(1)}, bf16[2,128,128]{2,1,0:T(8,128)(2,1)S(1)}, u32[]{:S(2)}, u32[]{:S(2)}) %collective-permute-start.3) | collective-permute-done | bytes 65568 | tf_op jit(solution)/shard_map/ppermute | solution.py:20
  39.9 12.5 %collective-permute-done.4 = bf16[2,128,128]{2,1,0:T(8,128)(2,1)S(1)} collective-permute-done((bf16[2,128,128]{2,1,0:T(8,128)(2,1)S(1)}, bf16[2,128,128]{2,1,0:T(8,128)(2,1)S(1)}, u32[]{:S(2)}, u32[]{:S(2)}) %collective-permute-start.4) | collective-permute-done | bytes 65568 | tf_op jit(solution)/shard_map/ppermute | solution.py:20
  52.4 0.9 collective-permute-done.5
  53.4 4.9 %collective-permute-start.6 = (bf16[6,2,128,128]{3,2,1,0:T(8,128)(2,1)S(1)}, bf16[6,2,128,128]{3,2,1,0:T(8,128)(2,1)S(1)}, u32[]{:S(2)}, u32[]{:S(2)}) collective-permute-start(bf16[6,2,128,128]{3,2,1,0:T(8,128)(2,1)S(1)} %bitcast_dynamic-update-slice_fusion), channel_id=1, source_target_pairs={{0,3},{1,0},{2,1},{3,2},{4,7},{5,4},{6,5},{7,6},{8,11},{9,8},{10,9... | collective-permute-start | bytes 1179656 | tf_op jit(solution)/shard_map/ppermute | solution.py:25
  58.3 2.5 %collective-permute-start.7 = (bf16[6,2,128,128]{3,2,1,0:T(8,128)(2,1)S(1)}, bf16[6,2,128,128]{3,2,1,0:T(8,128)(2,1)S(1)}, u32[]{:S(2)}, u32[]{:S(2)}) collective-permute-start(bf16[6,2,128,128]{3,2,1,0:T(8,128)(2,1)S(1)} %bitcast_dynamic-update-slice_fusion), channel_id=1, source_target_pairs={{0,2},{1,3},{2,0},{3,1},{4,6},{5,7},{6,4},{7,5},{8,10},{9,11},{10,... | collective-permute-start | bytes 1179656 | tf_op jit(solution)/shard_map/ppermute | solution.py:25
  60.8 2.9 %collective-permute-start.8 = (bf16[6,2,128,128]{3,2,1,0:T(8,128)(2,1)S(1)}, bf16[6,2,128,128]{3,2,1,0:T(8,128)(2,1)S(1)}, u32[]{:S(2)}, u32[]{:S(2)}) collective-permute-start(bf16[6,2,128,128]{3,2,1,0:T(8,128)(2,1)S(1)} %bitcast_dynamic-update-slice_fusion), channel_id=1, source_target_pairs={{0,1},{1,2},{2,3},{3,0},{4,5},{5,6},{6,7},{7,4},{8,9},{9,10},{10,1... | collective-permute-start | bytes 1179656 | tf_op jit(solution)/shard_map/ppermute | solution.py:25
  63.7 0.6 select_select_fusion
  64.4 0.1 broadcast_in_dim.31
  64.4 0.7 reshape_reshape.3.code_ref
  65.1 0.5 fusion.39
  65.6 10.1 %collective-permute-done.6 = bf16[6,2,128,128]{3,2,1,0:T(8,128)(2,1)S(1)} collective-permute-done((bf16[6,2,128,128]{3,2,1,0:T(8,128)(2,1)S(1)}, bf16[6,2,128,128]{3,2,1,0:T(8,128)(2,1)S(1)}, u32[]{:S(2)}, u32[]{:S(2)}) %collective-permute-start.6) | collective-permute-done | bytes 393248 | tf_op jit(solution)/shard_map/ppermute | solution.py:25
  75.7 5.6 %collective-permute-done.8 = bf16[6,2,128,128]{3,2,1,0:T(8,128)(2,1)S(1)} collective-permute-done((bf16[6,2,128,128]{3,2,1,0:T(8,128)(2,1)S(1)}, bf16[6,2,128,128]{3,2,1,0:T(8,128)(2,1)S(1)}, u32[]{:S(2)}, u32[]{:S(2)}) %collective-permute-start.8) | collective-permute-done | bytes 393248 | tf_op jit(solution)/shard_map/ppermute | solution.py:25
  81.3 0.1 maximum_maximum_fusion
  81.4 1.4 fusion.38
  82.8 16.9 %shard_map.85 = (bf16[2048,128]{1,0:T(8,128)(2,1)}, f32[3584,128]{1,0:T(8,128)}, f32[3584,128]{1,0:T(8,128)}) custom-call(s32[8,16]{1,0:T(8,128)} %get-tuple-element.30.slots_ref, bf16[2048,128]{1,0:T(8,128)(2,1)} %bitcast.86, bf16[2048,128]{1,0:T(8,128)(2,1)} %bitcast.87, s32[8,1,1024]{2,1,0:T(1,128)} %reshape_reshape.3.code_ref, ...), custom_call_target="tpu_custom_call" | custom-call | tf_op jit(solution)/shard_map/pallas_call | solution.py:90
  99.7 1.6 fusion.36
  101.4 2.5 %collective-permute-start.10 = (bf16[2,3,128,128]{3,2,0,1:T(8,128)(2,1)S(1)}, bf16[2,3,128,128]{3,2,0,1:T(8,128)(2,1)S(1)}, u32[]{:S(2)}, u32[]{:S(2)}) collective-permute-start(bf16[2,3,128,128]{3,2,0,1:T(8,128)(2,1)S(1)} %get-tuple-element.15), channel_id=1, source_target_pairs={{0,2},{1,3},{2,0},{3,1},{4,6},{5,7},{6,4},{7,5},{8,10},{9,11},{10,... | collective-permute-start | bytes 589832 | tf_op jit(solution)/shard_map/ppermute | solution.py:25
  103.9 3.1 %collective-permute-start.11 = (bf16[2,3,128,128]{3,2,0,1:T(8,128)(2,1)S(1)}, bf16[2,3,128,128]{3,2,0,1:T(8,128)(2,1)S(1)}, u32[]{:S(2)}, u32[]{:S(2)}) collective-permute-start(bf16[2,3,128,128]{3,2,0,1:T(8,128)(2,1)S(1)} %get-tuple-element.14), channel_id=1, source_target_pairs={{0,3},{1,0},{2,1},{3,2},{4,7},{5,4},{6,5},{7,6},{8,11},{9,8},{10,9... | collective-permute-start | bytes 589832 | tf_op jit(solution)/shard_map/ppermute | solution.py:25
  107.0 2.7 %collective-permute-start.9 = (bf16[2,3,128,128]{3,2,0,1:T(8,128)(2,1)S(1)}, bf16[2,3,128,128]{3,2,0,1:T(8,128)(2,1)S(1)}, u32[]{:S(2)}, u32[]{:S(2)}) collective-permute-start(bf16[2,3,128,128]{3,2,0,1:T(8,128)(2,1)S(1)} %get-tuple-element.13), channel_id=1, source_target_pairs={{0,1},{1,2},{2,3},{3,0},{4,5},{5,6},{6,7},{7,4},{8,9},{9,10},{10,1... | collective-permute-start | bytes 589832 | tf_op jit(solution)/shard_map/ppermute | solution.py:25
  109.8 0.2 fusion.37
  109.9 2.7 %collective-permute-start.15 = (bf16[2,4,128,128]{3,2,0,1:T(8,128)(2,1)S(1)}, bf16[2,4,128,128]{3,2,0,1:T(8,128)(2,1)S(1)}, u32[]{:S(2)}, u32[]{:S(2)}) collective-permute-start(bf16[2,4,128,128]{3,2,0,1:T(8,128)(2,1)S(1)} %get-tuple-element.16), channel_id=1, source_target_pairs={{0,1},{1,2},{2,3},{3,0},{4,5},{5,6},{6,7},{7,4},{8,9},{9,10},{10,1... | collective-permute-start | bytes 786440 | tf_op jit(solution)/shard_map/ppermute | solution.py:25
  112.7 4.9 %collective-permute-start.16 = (bf16[2,4,128,128]{3,2,0,1:T(8,128)(2,1)S(1)}, bf16[2,4,128,128]{3,2,0,1:T(8,128)(2,1)S(1)}, u32[]{:S(2)}, u32[]{:S(2)}) collective-permute-start(bf16[2,4,128,128]{3,2,0,1:T(8,128)(2,1)S(1)} %get-tuple-element.18), channel_id=1, source_target_pairs={{0,2},{1,3},{2,0},{3,1},{4,6},{5,7},{6,4},{7,5},{8,10},{9,11},{10,... | collective-permute-start | bytes 786440 | tf_op jit(solution)/shard_map/ppermute | solution.py:25
  117.7 3.6 %collective-permute-start.17 = (bf16[2,4,128,128]{3,2,0,1:T(8,128)(2,1)S(1)}, bf16[2,4,128,128]{3,2,0,1:T(8,128)(2,1)S(1)}, u32[]{:S(2)}, u32[]{:S(2)}) collective-permute-start(bf16[2,4,128,128]{3,2,0,1:T(8,128)(2,1)S(1)} %get-tuple-element.17), channel_id=1, source_target_pairs={{0,3},{1,0},{2,1},{3,2},{4,7},{5,4},{6,5},{7,6},{8,11},{9,8},{10,9... | collective-permute-start | bytes 786440 | tf_op jit(solution)/shard_map/ppermute | solution.py:25
  121.2 0.0 collective-permute-done.11
  121.2 0.1 fusion.6
  121.4 7.0 %collective-permute-start.12 = (bf16[2,128,128]{2,1,0:T(8,128)(2,1)S(1)}, bf16[2,128,128]{2,1,0:T(8,128)(2,1)S(1)}, u32[]{:S(2)}, u32[]{:S(2)}) collective-permute-start(bf16[2,128,128]{2,1,0:T(8,128)(2,1)S(1)} %get-tuple-element.26), channel_id=1, source_target_pairs={{64,0},{80,16},{96,32},{112,48},{128,64},{144,80},{160,96},{176,11... | collective-permute-start | bytes 196616 | tf_op jit(solution)/shard_map/ppermute | solution.py:20
  128.4 1.9 collective-permute-start.13
  130.3 1.9 collective-permute-start.14
  132.3 0.1 fusion.33
  132.4 8.4 %collective-permute-start.18 = (bf16[2,128,128]{2,1,0:T(8,128)(2,1)S(1)}, bf16[2,128,128]{2,1,0:T(8,128)(2,1)S(1)}, u32[]{:S(2)}, u32[]{:S(2)}) collective-permute-start(bf16[2,128,128]{2,1,0:T(8,128)(2,1)S(1)} %get-tuple-element.23), channel_id=1, source_target_pairs={{16,0},{32,16},{48,32},{64,48},{80,64},{96,80},{112,96},{128,112},... | collective-permute-start | bytes 196616 | tf_op jit(solution)/shard_map/ppermute | solution.py:20
  140.8 7.6 %collective-permute-start.19 = (bf16[2,128,128]{2,1,0:T(8,128)(2,1)S(1)}, bf16[2,128,128]{2,1,0:T(8,128)(2,1)S(1)}, u32[]{:S(2)}, u32[]{:S(2)}) collective-permute-start(bf16[2,128,128]{2,1,0:T(8,128)(2,1)S(1)} %get-tuple-element.25), channel_id=1, source_target_pairs={{32,0},{48,16},{64,32},{80,48},{96,64},{112,80},{128,96},{144,112}... | collective-permute-start | bytes 196616 | tf_op jit(solution)/shard_map/ppermute | solution.py:20
  148.4 2.1 %collective-permute-start.20 = (bf16[2,128,128]{2,1,0:T(8,128)(2,1)S(1)}, bf16[2,128,128]{2,1,0:T(8,128)(2,1)S(1)}, u32[]{:S(2)}, u32[]{:S(2)}) collective-permute-start(bf16[2,128,128]{2,1,0:T(8,128)(2,1)S(1)} %get-tuple-element.24), channel_id=1, source_target_pairs={{48,0},{64,16},{80,32},{96,48},{112,64},{128,80},{144,96},{160,112... | collective-permute-start | bytes 196616 | tf_op jit(solution)/shard_map/ppermute | solution.py:20
  150.6 4.6 %collective-permute-done.19 = bf16[2,128,128]{2,1,0:T(8,128)(2,1)S(1)} collective-permute-done((bf16[2,128,128]{2,1,0:T(8,128)(2,1)S(1)}, bf16[2,128,128]{2,1,0:T(8,128)(2,1)S(1)}, u32[]{:S(2)}, u32[]{:S(2)}) %collective-permute-start.19) | collective-permute-done | bytes 65568 | tf_op jit(solution)/shard_map/ppermute | solution.py:20
  155.1 4.8 %collective-permute-done.20 = bf16[2,128,128]{2,1,0:T(8,128)(2,1)S(1)} collective-permute-done((bf16[2,128,128]{2,1,0:T(8,128)(2,1)S(1)}, bf16[2,128,128]{2,1,0:T(8,128)(2,1)S(1)}, u32[]{:S(2)}, u32[]{:S(2)}) %collective-permute-start.20) | collective-permute-done | bytes 65568 | tf_op jit(solution)/shard_map/ppermute | solution.py:20
  160.0 0.1 fusion.14
  160.0 7.2 %collective-permute-start.21 = (bf16[2,128,128]{2,1,0:T(8,128)(2,1)S(1)}, bf16[2,128,128]{2,1,0:T(8,128)(2,1)S(1)}, u32[]{:S(2)}, u32[]{:S(2)}) collective-permute-start(bf16[2,128,128]{2,1,0:T(8,128)(2,1)S(1)} %fusion.14), channel_id=1, source_target_pairs={{0,12},{4,0},{8,4},{12,8},{1,13},{5,1},{9,5},{13,9},{2,14},{6,2},{... | collective-permute-start | bytes 196616 | tf_op jit(solution)/shard_map/ppermute | solution.py:25
  167.3 1.9 collective-permute-start.22
  169.2 2.5 %collective-permute-start.23 = (bf16[2,128,128]{2,1,0:T(8,128)(2,1)S(1)}, bf16[2,128,128]{2,1,0:T(8,128)(2,1)S(1)}, u32[]{:S(2)}, u32[]{:S(2)}) collective-permute-start(bf16[2,128,128]{2,1,0:T(8,128)(2,1)S(1)} %fusion.14), channel_id=1, source_target_pairs={{0,4},{4,8},{8,12},{12,0},{1,5},{5,9},{9,13},{13,1},{2,6},{6,10},{... | collective-permute-start | bytes 196616 | tf_op jit(solution)/shard_map/ppermute | solution.py:25
  171.7 2.9 %collective-permute-done.22 = bf16[2,128,128]{2,1,0:T(8,128)(2,1)S(1)} collective-permute-done((bf16[2,128,128]{2,1,0:T(8,128)(2,1)S(1)}, bf16[2,128,128]{2,1,0:T(8,128)(2,1)S(1)}, u32[]{:S(2)}, u32[]{:S(2)}) %collective-permute-start.22) | collective-permute-done | bytes 65568 | tf_op jit(solution)/shard_map/ppermute | solution.py:25
  174.6 2.8 %collective-permute-done.23 = bf16[2,128,128]{2,1,0:T(8,128)(2,1)S(1)} collective-permute-done((bf16[2,128,128]{2,1,0:T(8,128)(2,1)S(1)}, bf16[2,128,128]{2,1,0:T(8,128)(2,1)S(1)}, u32[]{:S(2)}, u32[]{:S(2)}) %collective-permute-start.23) | collective-permute-done | bytes 65568 | tf_op jit(solution)/shard_map/ppermute | solution.py:25
  177.5 1.9 collective-permute-start.24
  179.5 4.7 %collective-permute-start.25 = (bf16[4,2,128,128]{3,2,1,0:T(8,128)(2,1)S(1)}, bf16[4,2,128,128]{3,2,1,0:T(8,128)(2,1)S(1)}, u32[]{:S(2)}, u32[]{:S(2)}) collective-permute-start(bf16[4,2,128,128]{3,2,1,0:T(8,128)(2,1)S(1)} %get-tuple-element.22), channel_id=1, source_target_pairs={{0,2},{1,3},{2,0},{3,1},{4,6},{5,7},{6,4},{7,5},{8,10},{9,11},{10,... | collective-permute-start | bytes 786440 | tf_op jit(solution)/shard_map/ppermute | solution.py:25
  184.1 1.9 collective-permute-start.26
  186.1 2.4 %collective-permute-done.24 = bf16[4,2,128,128]{3,2,1,0:T(8,128)(2,1)S(1)} collective-permute-done((bf16[4,2,128,128]{3,2,1,0:T(8,128)(2,1)S(1)}, bf16[4,2,128,128]{3,2,1,0:T(8,128)(2,1)S(1)}, u32[]{:S(2)}, u32[]{:S(2)}) %collective-permute-start.24) | collective-permute-done | bytes 262176 | tf_op jit(solution)/shard_map/ppermute | solution.py:25
  188.6 3.4 %collective-permute-done.25 = bf16[4,2,128,128]{3,2,1,0:T(8,128)(2,1)S(1)} collective-permute-done((bf16[4,2,128,128]{3,2,1,0:T(8,128)(2,1)S(1)}, bf16[4,2,128,128]{3,2,1,0:T(8,128)(2,1)S(1)}, u32[]{:S(2)}, u32[]{:S(2)}) %collective-permute-start.25) | collective-permute-done | bytes 262176 | tf_op jit(solution)/shard_map/ppermute | solution.py:25
  192.0 4.9 %collective-permute-done.26 = bf16[4,2,128,128]{3,2,1,0:T(8,128)(2,1)S(1)} collective-permute-done((bf16[4,2,128,128]{3,2,1,0:T(8,128)(2,1)S(1)}, bf16[4,2,128,128]{3,2,1,0:T(8,128)(2,1)S(1)}, u32[]{:S(2)}, u32[]{:S(2)}) %collective-permute-start.26) | collective-permute-done | bytes 262176 | tf_op jit(solution)/shard_map/ppermute | solution.py:25
  196.9 0.1 pad_maximum_fusion.1
  197.0 0.7 gather_fusion
  197.8 0.2 broadcast_select_fusion
  198.0 0.7 gather_fusion.1
  198.7 0.2 convert_bitcast_fusion
  198.9 1.5 fusion.35
  (31 shorter events, 0.3 us)
Async XLA Ops:
  2.1 26.6 %collective-permute-start = (bf16[2,128,128]{2,1,0:T(8,128)(2,1)S(1)}, bf16[2,128,128]{2,1,0:T(8,128)(2,1)S(1)}, u32[]{:S(2)}, u32[]{:S(2)}) collective-permute-start(bf16[2,128,128]{2,1,0:T(8,128)(2,1)S(1)} %slice.92), channel_id=1, source_target_pairs={{0,16},{16,32},{32,48},{48,64},{64,80},{80,96},{96,112},{112,128},... | collective-permute-start | bytes 196616 | tf_op jit(solution)/shard_map/ppermute | solution.py:20
  4.1 26.6 %collective-permute-start.1 = (bf16[2,128,128]{2,1,0:T(8,128)(2,1)S(1)}, bf16[2,128,128]{2,1,0:T(8,128)(2,1)S(1)}, u32[]{:S(2)}, u32[]{:S(2)}) collective-permute-start(bf16[2,128,128]{2,1,0:T(8,128)(2,1)S(1)} %slice.92), channel_id=1, source_target_pairs={{0,32},{16,48},{32,64},{48,80},{64,96},{80,112},{96,128},{112,144}... | collective-permute-start | bytes 196616 | tf_op jit(solution)/shard_map/ppermute | solution.py:20
  13.2 17.5 %collective-permute-start.2 = (bf16[2,128,128]{2,1,0:T(8,128)(2,1)S(1)}, bf16[2,128,128]{2,1,0:T(8,128)(2,1)S(1)}, u32[]{:S(2)}, u32[]{:S(2)}) collective-permute-start(bf16[2,128,128]{2,1,0:T(8,128)(2,1)S(1)} %slice.92), channel_id=1, source_target_pairs={{0,48},{16,64},{32,80},{48,96},{64,112},{80,128},{96,144},{112,160... | collective-permute-start | bytes 196616 | tf_op jit(solution)/shard_map/ppermute | solution.py:20
  24.1 15.8 %collective-permute-start.3 = (bf16[2,128,128]{2,1,0:T(8,128)(2,1)S(1)}, bf16[2,128,128]{2,1,0:T(8,128)(2,1)S(1)}, u32[]{:S(2)}, u32[]{:S(2)}) collective-permute-start(bf16[2,128,128]{2,1,0:T(8,128)(2,1)S(1)} %slice.92), channel_id=1, source_target_pairs={{0,64},{16,80},{32,96},{48,112},{64,128},{80,144},{96,160},{112,17... | collective-permute-start | bytes 196616 | tf_op jit(solution)/shard_map/ppermute | solution.py:20
  26.0 26.4 %collective-permute-start.4 = (bf16[2,128,128]{2,1,0:T(8,128)(2,1)S(1)}, bf16[2,128,128]{2,1,0:T(8,128)(2,1)S(1)}, u32[]{:S(2)}, u32[]{:S(2)}) collective-permute-start(bf16[2,128,128]{2,1,0:T(8,128)(2,1)S(1)} %slice.92), channel_id=1, source_target_pairs={{0,80},{16,96},{32,112},{48,128},{64,144},{80,160},{96,176},{112,1... | collective-permute-start | bytes 196616 | tf_op jit(solution)/shard_map/ppermute | solution.py:20
  28.7 24.6 %collective-permute-start.5 = (bf16[2,128,128]{2,1,0:T(8,128)(2,1)S(1)}, bf16[2,128,128]{2,1,0:T(8,128)(2,1)S(1)}, u32[]{:S(2)}, u32[]{:S(2)}) collective-permute-start(bf16[2,128,128]{2,1,0:T(8,128)(2,1)S(1)} %slice.92), channel_id=1, source_target_pairs={{0,96},{16,112},{32,128},{48,144},{64,160},{80,176},{96,192},{112,... | collective-permute-start | bytes 196616 | tf_op jit(solution)/shard_map/ppermute | solution.py:20
  53.4 22.3 %collective-permute-start.6 = (bf16[6,2,128,128]{3,2,1,0:T(8,128)(2,1)S(1)}, bf16[6,2,128,128]{3,2,1,0:T(8,128)(2,1)S(1)}, u32[]{:S(2)}, u32[]{:S(2)}) collective-permute-start(bf16[6,2,128,128]{3,2,1,0:T(8,128)(2,1)S(1)} %bitcast_dynamic-update-slice_fusion), channel_id=1, source_target_pairs={{0,3},{1,0},{2,1},{3,2},{4,7},{5,4},{6,5},{7,6},{8,11},{9,8},{10,9... | collective-permute-start | bytes 1179656 | tf_op jit(solution)/shard_map/ppermute | solution.py:25
  58.3 17.4 %collective-permute-start.7 = (bf16[6,2,128,128]{3,2,1,0:T(8,128)(2,1)S(1)}, bf16[6,2,128,128]{3,2,1,0:T(8,128)(2,1)S(1)}, u32[]{:S(2)}, u32[]{:S(2)}) collective-permute-start(bf16[6,2,128,128]{3,2,1,0:T(8,128)(2,1)S(1)} %bitcast_dynamic-update-slice_fusion), channel_id=1, source_target_pairs={{0,2},{1,3},{2,0},{3,1},{4,6},{5,7},{6,4},{7,5},{8,10},{9,11},{10,... | collective-permute-start | bytes 1179656 | tf_op jit(solution)/shard_map/ppermute | solution.py:25
  60.8 20.5 %collective-permute-start.8 = (bf16[6,2,128,128]{3,2,1,0:T(8,128)(2,1)S(1)}, bf16[6,2,128,128]{3,2,1,0:T(8,128)(2,1)S(1)}, u32[]{:S(2)}, u32[]{:S(2)}) collective-permute-start(bf16[6,2,128,128]{3,2,1,0:T(8,128)(2,1)S(1)} %bitcast_dynamic-update-slice_fusion), channel_id=1, source_target_pairs={{0,1},{1,2},{2,3},{3,0},{4,5},{5,6},{6,7},{7,4},{8,9},{9,10},{10,1... | collective-permute-start | bytes 1179656 | tf_op jit(solution)/shard_map/ppermute | solution.py:25
  99.7 10.0 %copy-start = (f32[3584,128]{1,0:T(8,128)S(1)}, f32[3584,128]{1,0:T(8,128)}, u32[]{:S(2)}) copy-start(f32[3584,128]{1,0:T(8,128)} %get-tuple-element.7) | copy-start | bytes 5505028
  99.7 10.0 %copy-start.1 = (f32[3584,128]{1,0:T(8,128)S(1)}, f32[3584,128]{1,0:T(8,128)}, u32[]{:S(2)}) copy-start(f32[3584,128]{1,0:T(8,128)} %get-tuple-element.8) | copy-start | bytes 5505028
  101.4 16.3 %collective-permute-start.10 = (bf16[2,3,128,128]{3,2,0,1:T(8,128)(2,1)S(1)}, bf16[2,3,128,128]{3,2,0,1:T(8,128)(2,1)S(1)}, u32[]{:S(2)}, u32[]{:S(2)}) collective-permute-start(bf16[2,3,128,128]{3,2,0,1:T(8,128)(2,1)S(1)} %get-tuple-element.15), channel_id=1, source_target_pairs={{0,2},{1,3},{2,0},{3,1},{4,6},{5,7},{6,4},{7,5},{8,10},{9,11},{10,... | collective-permute-start | bytes 589832 | tf_op jit(solution)/shard_map/ppermute | solution.py:25
  103.9 17.3 %collective-permute-start.11 = (bf16[2,3,128,128]{3,2,0,1:T(8,128)(2,1)S(1)}, bf16[2,3,128,128]{3,2,0,1:T(8,128)(2,1)S(1)}, u32[]{:S(2)}, u32[]{:S(2)}) collective-permute-start(bf16[2,3,128,128]{3,2,0,1:T(8,128)(2,1)S(1)} %get-tuple-element.14), channel_id=1, source_target_pairs={{0,3},{1,0},{2,1},{3,2},{4,7},{5,4},{6,5},{7,6},{8,11},{9,8},{10,9... | collective-permute-start | bytes 589832 | tf_op jit(solution)/shard_map/ppermute | solution.py:25
  107.0 14.2 %collective-permute-start.9 = (bf16[2,3,128,128]{3,2,0,1:T(8,128)(2,1)S(1)}, bf16[2,3,128,128]{3,2,0,1:T(8,128)(2,1)S(1)}, u32[]{:S(2)}, u32[]{:S(2)}) collective-permute-start(bf16[2,3,128,128]{3,2,0,1:T(8,128)(2,1)S(1)} %get-tuple-element.13), channel_id=1, source_target_pairs={{0,1},{1,2},{2,3},{3,0},{4,5},{5,6},{6,7},{7,4},{8,9},{9,10},{10,1... | collective-permute-start | bytes 589832 | tf_op jit(solution)/shard_map/ppermute | solution.py:25
  109.9 20.4 %collective-permute-start.15 = (bf16[2,4,128,128]{3,2,0,1:T(8,128)(2,1)S(1)}, bf16[2,4,128,128]{3,2,0,1:T(8,128)(2,1)S(1)}, u32[]{:S(2)}, u32[]{:S(2)}) collective-permute-start(bf16[2,4,128,128]{3,2,0,1:T(8,128)(2,1)S(1)} %get-tuple-element.16), channel_id=1, source_target_pairs={{0,1},{1,2},{2,3},{3,0},{4,5},{5,6},{6,7},{7,4},{8,9},{9,10},{10,1... | collective-permute-start | bytes 786440 | tf_op jit(solution)/shard_map/ppermute | solution.py:25
  112.7 19.6 %collective-permute-start.16 = (bf16[2,4,128,128]{3,2,0,1:T(8,128)(2,1)S(1)}, bf16[2,4,128,128]{3,2,0,1:T(8,128)(2,1)S(1)}, u32[]{:S(2)}, u32[]{:S(2)}) collective-permute-start(bf16[2,4,128,128]{3,2,0,1:T(8,128)(2,1)S(1)} %get-tuple-element.18), channel_id=1, source_target_pairs={{0,2},{1,3},{2,0},{3,1},{4,6},{5,7},{6,4},{7,5},{8,10},{9,11},{10,... | collective-permute-start | bytes 786440 | tf_op jit(solution)/shard_map/ppermute | solution.py:25
  117.7 14.6 %collective-permute-start.17 = (bf16[2,4,128,128]{3,2,0,1:T(8,128)(2,1)S(1)}, bf16[2,4,128,128]{3,2,0,1:T(8,128)(2,1)S(1)}, u32[]{:S(2)}, u32[]{:S(2)}) collective-permute-start(bf16[2,4,128,128]{3,2,0,1:T(8,128)(2,1)S(1)} %get-tuple-element.17), channel_id=1, source_target_pairs={{0,3},{1,0},{2,1},{3,2},{4,7},{5,4},{6,5},{7,6},{8,11},{9,8},{10,9... | collective-permute-start | bytes 786440 | tf_op jit(solution)/shard_map/ppermute | solution.py:25
  121.4 27.0 %collective-permute-start.12 = (bf16[2,128,128]{2,1,0:T(8,128)(2,1)S(1)}, bf16[2,128,128]{2,1,0:T(8,128)(2,1)S(1)}, u32[]{:S(2)}, u32[]{:S(2)}) collective-permute-start(bf16[2,128,128]{2,1,0:T(8,128)(2,1)S(1)} %get-tuple-element.26), channel_id=1, source_target_pairs={{64,0},{80,16},{96,32},{112,48},{128,64},{144,80},{160,96},{176,11... | collective-permute-start | bytes 196616 | tf_op jit(solution)/shard_map/ppermute | solution.py:20
  128.4 22.1 %collective-permute-start.13 = (bf16[2,128,128]{2,1,0:T(8,128)(2,1)S(1)}, bf16[2,128,128]{2,1,0:T(8,128)(2,1)S(1)}, u32[]{:S(2)}, u32[]{:S(2)}) collective-permute-start(bf16[2,128,128]{2,1,0:T(8,128)(2,1)S(1)} %get-tuple-element.28), channel_id=1, source_target_pairs={{80,0},{96,16},{112,32},{128,48},{144,64},{160,80},{176,96},{192,1... | collective-permute-start | bytes 196616 | tf_op jit(solution)/shard_map/ppermute | solution.py:20
  130.3 20.2 %collective-permute-start.14 = (bf16[2,128,128]{2,1,0:T(8,128)(2,1)S(1)}, bf16[2,128,128]{2,1,0:T(8,128)(2,1)S(1)}, u32[]{:S(2)}, u32[]{:S(2)}) collective-permute-start(bf16[2,128,128]{2,1,0:T(8,128)(2,1)S(1)} %get-tuple-element.27), channel_id=1, source_target_pairs={{96,0},{112,16},{128,32},{144,48},{160,64},{176,80},{192,96},{208,... | collective-permute-start | bytes 196616 | tf_op jit(solution)/shard_map/ppermute | solution.py:20
  132.4 18.1 %collective-permute-start.18 = (bf16[2,128,128]{2,1,0:T(8,128)(2,1)S(1)}, bf16[2,128,128]{2,1,0:T(8,128)(2,1)S(1)}, u32[]{:S(2)}, u32[]{:S(2)}) collective-permute-start(bf16[2,128,128]{2,1,0:T(8,128)(2,1)S(1)} %get-tuple-element.23), channel_id=1, source_target_pairs={{16,0},{32,16},{48,32},{64,48},{80,64},{96,80},{112,96},{128,112},... | collective-permute-start | bytes 196616 | tf_op jit(solution)/shard_map/ppermute | solution.py:20
  140.8 14.3 %collective-permute-start.19 = (bf16[2,128,128]{2,1,0:T(8,128)(2,1)S(1)}, bf16[2,128,128]{2,1,0:T(8,128)(2,1)S(1)}, u32[]{:S(2)}, u32[]{:S(2)}) collective-permute-start(bf16[2,128,128]{2,1,0:T(8,128)(2,1)S(1)} %get-tuple-element.25), channel_id=1, source_target_pairs={{32,0},{48,16},{64,32},{80,48},{96,64},{112,80},{128,96},{144,112}... | collective-permute-start | bytes 196616 | tf_op jit(solution)/shard_map/ppermute | solution.py:20
  148.4 11.6 %collective-permute-start.20 = (bf16[2,128,128]{2,1,0:T(8,128)(2,1)S(1)}, bf16[2,128,128]{2,1,0:T(8,128)(2,1)S(1)}, u32[]{:S(2)}, u32[]{:S(2)}) collective-permute-start(bf16[2,128,128]{2,1,0:T(8,128)(2,1)S(1)} %get-tuple-element.24), channel_id=1, source_target_pairs={{48,0},{64,16},{80,32},{96,48},{112,64},{128,80},{144,96},{160,112... | collective-permute-start | bytes 196616 | tf_op jit(solution)/shard_map/ppermute | solution.py:20
  160.0 11.7 %collective-permute-start.21 = (bf16[2,128,128]{2,1,0:T(8,128)(2,1)S(1)}, bf16[2,128,128]{2,1,0:T(8,128)(2,1)S(1)}, u32[]{:S(2)}, u32[]{:S(2)}) collective-permute-start(bf16[2,128,128]{2,1,0:T(8,128)(2,1)S(1)} %fusion.14), channel_id=1, source_target_pairs={{0,12},{4,0},{8,4},{12,8},{1,13},{5,1},{9,5},{13,9},{2,14},{6,2},{... | collective-permute-start | bytes 196616 | tf_op jit(solution)/shard_map/ppermute | solution.py:25
  167.3 7.4 %collective-permute-start.22 = (bf16[2,128,128]{2,1,0:T(8,128)(2,1)S(1)}, bf16[2,128,128]{2,1,0:T(8,128)(2,1)S(1)}, u32[]{:S(2)}, u32[]{:S(2)}) collective-permute-start(bf16[2,128,128]{2,1,0:T(8,128)(2,1)S(1)} %fusion.14), channel_id=1, source_target_pairs={{0,8},{4,12},{8,0},{12,4},{1,9},{5,13},{9,1},{13,5},{2,10},{6,14},... | collective-permute-start | bytes 196616 | tf_op jit(solution)/shard_map/ppermute | solution.py:25
  169.2 8.3 %collective-permute-start.23 = (bf16[2,128,128]{2,1,0:T(8,128)(2,1)S(1)}, bf16[2,128,128]{2,1,0:T(8,128)(2,1)S(1)}, u32[]{:S(2)}, u32[]{:S(2)}) collective-permute-start(bf16[2,128,128]{2,1,0:T(8,128)(2,1)S(1)} %fusion.14), channel_id=1, source_target_pairs={{0,4},{4,8},{8,12},{12,0},{1,5},{5,9},{9,13},{13,1},{2,6},{6,10},{... | collective-permute-start | bytes 196616 | tf_op jit(solution)/shard_map/ppermute | solution.py:25
  177.5 11.0 %collective-permute-start.24 = (bf16[4,2,128,128]{3,2,1,0:T(8,128)(2,1)S(1)}, bf16[4,2,128,128]{3,2,1,0:T(8,128)(2,1)S(1)}, u32[]{:S(2)}, u32[]{:S(2)}) collective-permute-start(bf16[4,2,128,128]{3,2,1,0:T(8,128)(2,1)S(1)} %get-tuple-element.22), channel_id=1, source_target_pairs={{0,3},{1,0},{2,1},{3,2},{4,7},{5,4},{6,5},{7,6},{8,11},{9,8},{10,9... | collective-permute-start | bytes 786440 | tf_op jit(solution)/shard_map/ppermute | solution.py:25
  179.5 12.5 %collective-permute-start.25 = (bf16[4,2,128,128]{3,2,1,0:T(8,128)(2,1)S(1)}, bf16[4,2,128,128]{3,2,1,0:T(8,128)(2,1)S(1)}, u32[]{:S(2)}, u32[]{:S(2)}) collective-permute-start(bf16[4,2,128,128]{3,2,1,0:T(8,128)(2,1)S(1)} %get-tuple-element.22), channel_id=1, source_target_pairs={{0,2},{1,3},{2,0},{3,1},{4,6},{5,7},{6,4},{7,5},{8,10},{9,11},{10,... | collective-permute-start | bytes 786440 | tf_op jit(solution)/shard_map/ppermute | solution.py:25
  184.1 12.8 %collective-permute-start.26 = (bf16[4,2,128,128]{3,2,1,0:T(8,128)(2,1)S(1)}, bf16[4,2,128,128]{3,2,1,0:T(8,128)(2,1)S(1)}, u32[]{:S(2)}, u32[]{:S(2)}) collective-permute-start(bf16[4,2,128,128]{3,2,1,0:T(8,128)(2,1)S(1)} %get-tuple-element.22), channel_id=1, source_target_pairs={{0,1},{1,2},{2,3},{3,0},{4,5},{5,6},{6,7},{7,4},{8,9},{9,10},{10,1... | collective-permute-start | bytes 786440 | tf_op jit(solution)/shard_map/ppermute | solution.py:25

commit v6 on v5

--- a/solution.py
+++ b/solution.py
@@ -47,10 +47,8 @@
     scores = lax.dot_general(
         q, keys, (((1,), (1,)), ((), ())), preferred_element_type=jnp.float32
     ) * inv_root
-    code = code_ref[...]
-    query_pos = lax.broadcasted_iota(jnp.int32, (rows, cols), 0) // heads_here
-    key_pos = lax.broadcasted_iota(jnp.int32, (rows, cols), 1) % BLOCK
-    allowed = (code == 2) | ((code == 1) & (query_pos >= key_pos))
+    query_pos = lax.broadcasted_iota(jnp.int32, (rows, 1), 0) // heads_here
+    allowed = query_pos >= code_ref[...]
     scores = jnp.where(allowed, scores, -1e30)
     row_max = jnp.max(scores, axis=1, keepdims=True)
     shifted = jnp.exp(scores - row_max)
@@ -83,7 +81,10 @@
     rows = BLOCK * heads_here
     store = key_tiles.shape[0] * BLOCK
     cols = slots * BLOCK
-    code_cols = jnp.repeat(code.astype(jnp.int32), BLOCK, axis=1).reshape(blocks_here, 1, cols)
+    key_pos = jnp.tile(jnp.arange(BLOCK, dtype=jnp.int32), slots)[None, :]
+    code_cols = jnp.repeat(code.astype(jnp.int32), BLOCK, axis=1)
+    code_cols = jnp.where(code_cols == 2, 0, jnp.where(code_cols == 1, key_pos, BLOCK))
+    code_cols = code_cols.reshape(blocks_here, 1, cols)
     kernel = functools.partial(block_kernel, inv_root=inv_root, heads_here=heads_here)
     whole = lambda step, slots_ref: (0, 0)
     per_block = lambda step, slots_ref: (step, 0)
@@ -182,8 +183,9 @@
     by_part = jnp.stack([by_group] + [cycled(by_group, "sub", -step) for step in range(1, parts_count)])
     part_order = (jnp.arange(parts_count) - part_index) % parts_count
     group_order = (jnp.arange(groups) - group_index) % groups
-    ordered = jnp.take(jnp.take(by_part, part_order, axis=0), group_order, axis=1)
-    ordered = jnp.transpose(ordered, (1, 0, 2, 3, 4))
+    flat_order = (part_order[None, :] * groups + group_order[:, None]).reshape(-1)
+    ordered = jnp.take(by_part.reshape((parts_count * groups,) + mine.shape), flat_order, axis=0)
+    ordered = ordered.reshape((groups, parts_count) + mine.shape)
     summed = jnp.transpose(ordered, (2, 0, 1, 3, 4)).reshape(2, groups, tokens_here, width)
     summed = summed.astype(jnp.float32)
     return (query_grad, summed[0], summed[1])

time: 202 us -> 198 us (0.980)
  waiting for transfers between devices: 64.3 us -> 60.7 us
where the time goes in v6:
time: 198 us; the launch traced here: 197 us
  starting transfers between devices  108 us (55%)
  waiting for transfers between devices  60.7 us (31%)
  Pallas kernels  15.8 us (8%)
  local copies, waits for them, and re-layouts  6.01 us (3%)
  other arithmetic  5.05 us (3%)
    ppermute x12, starting transfers between devices, shifted_2(): lax.ppermute(value, axis, [(source, source + steps) for source in range(l...  56.5 us
    ppermute x15, starting transfers between devices, cycled(): lax.ppermute(value, axis, [(source, (source + steps) % count) for source...  51.5 us
    ppermute x12, waiting for transfers between devices, shifted_2(): lax.ppermute(value, axis, [(source, source + steps) for source in range(l...  30.4 us
    ppermute x15, waiting for transfers between devices, cycled(): lax.ppermute(value, axis, [(source, (source + steps) % count) for source...  30.3 us
    pallas_call x1, Pallas kernels, local_grads(): pl.pallas_call(kernel, grid_spec=pltpu.PrefetchScalarGridSpec(num_scalar_...  15.8 us
  transfers between devices with their start and end apart: 27, of which 12 were waited for; matrix products, arithmetic and copies ran while one was open for 2% of the time, Pallas kernels for 0%

profile of v6, /device:TPU:6, one launch (start us, length us, event | category | flops | bytes accessed | tf_op | source)
XLA Modules:
  0.0 196.8 jit_solution(2899548972877397451)
XLA Ops:
  0.7 1.0 constant_dynamic-slice_fusion
  1.7 0.5 fusion.8
  2.1 1.9 collective-permute-start
  4.1 9.1 %collective-permute-start.1 = (bf16[2,128,128]{2,1,0:T(8,128)(2,1)S(1)}, bf16[2,128,128]{2,1,0:T(8,128)(2,1)S(1)}, u32[]{:S(2)}, u32[]{:S(2)}) collective-permute-start(bf16[2,128,128]{2,1,0:T(8,128)(2,1)S(1)} %slice.90), channel_id=1, source_target_pairs={{0,32},{16,48},{32,64},{48,80},{64,96},{80,112},{96,128},{112,144}... | collective-permute-start | bytes 196616 | tf_op jit(solution)/shard_map/ppermute | solution.py:20
  13.2 10.9 %collective-permute-start.2 = (bf16[2,128,128]{2,1,0:T(8,128)(2,1)S(1)}, bf16[2,128,128]{2,1,0:T(8,128)(2,1)S(1)}, u32[]{:S(2)}, u32[]{:S(2)}) collective-permute-start(bf16[2,128,128]{2,1,0:T(8,128)(2,1)S(1)} %slice.90), channel_id=1, source_target_pairs={{0,48},{16,64},{32,80},{48,96},{64,112},{80,128},{96,144},{112,160... | collective-permute-start | bytes 196616 | tf_op jit(solution)/shard_map/ppermute | solution.py:20
  24.1 1.9 collective-permute-start.3
  26.0 1.9 collective-permute-start.4
  28.0 0.8 constant_dynamic-slice_fusion.2
  28.7 0.1 fusion.23
  28.8 0.6 fusion.18.slots_ref
  29.4 1.9 collective-permute-start.5
  31.4 8.5 %collective-permute-done.3 = bf16[2,128,128]{2,1,0:T(8,128)(2,1)S(1)} collective-permute-done((bf16[2,128,128]{2,1,0:T(8,128)(2,1)S(1)}, bf16[2,128,128]{2,1,0:T(8,128)(2,1)S(1)}, u32[]{:S(2)}, u32[]{:S(2)}) %collective-permute-start.3) | collective-permute-done | bytes 65568 | tf_op jit(solution)/shard_map/ppermute | solution.py:20
  39.9 12.5 %collective-permute-done.4 = bf16[2,128,128]{2,1,0:T(8,128)(2,1)S(1)} collective-permute-done((bf16[2,128,128]{2,1,0:T(8,128)(2,1)S(1)}, bf16[2,128,128]{2,1,0:T(8,128)(2,1)S(1)}, u32[]{:S(2)}, u32[]{:S(2)}) %collective-permute-start.4) | collective-permute-done | bytes 65568 | tf_op jit(solution)/shard_map/ppermute | solution.py:20
  52.4 0.9 collective-permute-done.5
  53.4 4.9 %collective-permute-start.6 = (bf16[6,2,128,128]{3,2,1,0:T(8,128)(2,1)S(1)}, bf16[6,2,128,128]{3,2,1,0:T(8,128)(2,1)S(1)}, u32[]{:S(2)}, u32[]{:S(2)}) collective-permute-start(bf16[6,2,128,128]{3,2,1,0:T(8,128)(2,1)S(1)} %bitcast_dynamic-update-slice_fusion), channel_id=1, source_target_pairs={{0,3},{1,0},{2,1},{3,2},{4,7},{5,4},{6,5},{7,6},{8,11},{9,8},{10,9... | collective-permute-start | bytes 1179656 | tf_op jit(solution)/shard_map/ppermute | solution.py:25
  58.3 2.5 %collective-permute-start.7 = (bf16[6,2,128,128]{3,2,1,0:T(8,128)(2,1)S(1)}, bf16[6,2,128,128]{3,2,1,0:T(8,128)(2,1)S(1)}, u32[]{:S(2)}, u32[]{:S(2)}) collective-permute-start(bf16[6,2,128,128]{3,2,1,0:T(8,128)(2,1)S(1)} %bitcast_dynamic-update-slice_fusion), channel_id=1, source_target_pairs={{0,2},{1,3},{2,0},{3,1},{4,6},{5,7},{6,4},{7,5},{8,10},{9,11},{10,... | collective-permute-start | bytes 1179656 | tf_op jit(solution)/shard_map/ppermute | solution.py:25
  60.8 2.9 %collective-permute-start.8 = (bf16[6,2,128,128]{3,2,1,0:T(8,128)(2,1)S(1)}, bf16[6,2,128,128]{3,2,1,0:T(8,128)(2,1)S(1)}, u32[]{:S(2)}, u32[]{:S(2)}) collective-permute-start(bf16[6,2,128,128]{3,2,1,0:T(8,128)(2,1)S(1)} %bitcast_dynamic-update-slice_fusion), channel_id=1, source_target_pairs={{0,1},{1,2},{2,3},{3,0},{4,5},{5,6},{6,7},{7,4},{8,9},{9,10},{10,1... | collective-permute-start | bytes 1179656 | tf_op jit(solution)/shard_map/ppermute | solution.py:25
  63.7 0.1 broadcast_in_dim.45
  63.8 0.1 eq.53
  63.9 0.1 broadcast_in_dim.47
  64.0 0.1 eq.54
  64.2 0.5 fusion.39
  64.7 0.7 select_select_fusion.code_ref
  65.3 10.3 %collective-permute-done.6 = bf16[6,2,128,128]{3,2,1,0:T(8,128)(2,1)S(1)} collective-permute-done((bf16[6,2,128,128]{3,2,1,0:T(8,128)(2,1)S(1)}, bf16[6,2,128,128]{3,2,1,0:T(8,128)(2,1)S(1)}, u32[]{:S(2)}, u32[]{:S(2)}) %collective-permute-start.6) | collective-permute-done | bytes 393248 | tf_op jit(solution)/shard_map/ppermute | solution.py:25
  75.7 5.6 %collective-permute-done.8 = bf16[6,2,128,128]{3,2,1,0:T(8,128)(2,1)S(1)} collective-permute-done((bf16[6,2,128,128]{3,2,1,0:T(8,128)(2,1)S(1)}, bf16[6,2,128,128]{3,2,1,0:T(8,128)(2,1)S(1)}, u32[]{:S(2)}, u32[]{:S(2)}) %collective-permute-start.8) | collective-permute-done | bytes 393248 | tf_op jit(solution)/shard_map/ppermute | solution.py:25
  81.3 0.1 maximum_maximum_fusion
  81.4 1.4 fusion.38
  82.8 15.8 %shard_map.85 = (bf16[2048,128]{1,0:T(8,128)(2,1)}, f32[3584,128]{1,0:T(8,128)}, f32[3584,128]{1,0:T(8,128)}) custom-call(s32[8,16]{1,0:T(8,128)} %fusion.18.slots_ref, bf16[2048,128]{1,0:T(8,128)(2,1)} %bitcast.89, bf16[2048,128]{1,0:T(8,128)(2,1)} %bitcast.90, s32[8,1,1024]{2,1,0:T(1,128)} %select_select_fusion.code_ref, bf16[3584,128]{1,0:T(8,128)(2,1)} %bitcast.86, ...), custom_call_target="tpu_custom_call" | custom-call | tf_op jit(solution)/shard_map/pallas_call | solution.py:91
  98.6 1.6 fusion.36
  100.3 2.5 %collective-permute-start.10 = (bf16[2,3,128,128]{3,2,0,1:T(8,128)(2,1)S(1)}, bf16[2,3,128,128]{3,2,0,1:T(8,128)(2,1)S(1)}, u32[]{:S(2)}, u32[]{:S(2)}) collective-permute-start(bf16[2,3,128,128]{3,2,0,1:T(8,128)(2,1)S(1)} %get-tuple-element.18), channel_id=1, source_target_pairs={{0,2},{1,3},{2,0},{3,1},{4,6},{5,7},{6,4},{7,5},{8,10},{9,11},{10,... | collective-permute-start | bytes 589832 | tf_op jit(solution)/shard_map/ppermute | solution.py:25
  102.8 3.1 %collective-permute-start.11 = (bf16[2,3,128,128]{3,2,0,1:T(8,128)(2,1)S(1)}, bf16[2,3,128,128]{3,2,0,1:T(8,128)(2,1)S(1)}, u32[]{:S(2)}, u32[]{:S(2)}) collective-permute-start(bf16[2,3,128,128]{3,2,0,1:T(8,128)(2,1)S(1)} %get-tuple-element.17), channel_id=1, source_target_pairs={{0,3},{1,0},{2,1},{3,2},{4,7},{5,4},{6,5},{7,6},{8,11},{9,8},{10,9... | collective-permute-start | bytes 589832 | tf_op jit(solution)/shard_map/ppermute | solution.py:25
  105.9 2.7 %collective-permute-start.9 = (bf16[2,3,128,128]{3,2,0,1:T(8,128)(2,1)S(1)}, bf16[2,3,128,128]{3,2,0,1:T(8,128)(2,1)S(1)}, u32[]{:S(2)}, u32[]{:S(2)}) collective-permute-start(bf16[2,3,128,128]{3,2,0,1:T(8,128)(2,1)S(1)} %get-tuple-element.16), channel_id=1, source_target_pairs={{0,1},{1,2},{2,3},{3,0},{4,5},{5,6},{6,7},{7,4},{8,9},{9,10},{10,1... | collective-permute-start | bytes 589832 | tf_op jit(solution)/shard_map/ppermute | solution.py:25
  108.7 0.2 fusion.37
  108.9 2.8 %collective-permute-start.15 = (bf16[2,4,128,128]{3,2,0,1:T(8,128)(2,1)S(1)}, bf16[2,4,128,128]{3,2,0,1:T(8,128)(2,1)S(1)}, u32[]{:S(2)}, u32[]{:S(2)}) collective-permute-start(bf16[2,4,128,128]{3,2,0,1:T(8,128)(2,1)S(1)} %get-tuple-element.19), channel_id=1, source_target_pairs={{0,1},{1,2},{2,3},{3,0},{4,5},{5,6},{6,7},{7,4},{8,9},{9,10},{10,1... | collective-permute-start | bytes 786440 | tf_op jit(solution)/shard_map/ppermute | solution.py:25
  111.6 5.0 %collective-permute-start.16 = (bf16[2,4,128,128]{3,2,0,1:T(8,128)(2,1)S(1)}, bf16[2,4,128,128]{3,2,0,1:T(8,128)(2,1)S(1)}, u32[]{:S(2)}, u32[]{:S(2)}) collective-permute-start(bf16[2,4,128,128]{3,2,0,1:T(8,128)(2,1)S(1)} %get-tuple-element.21), channel_id=1, source_target_pairs={{0,2},{1,3},{2,0},{3,1},{4,6},{5,7},{6,4},{7,5},{8,10},{9,11},{10,... | collective-permute-start | bytes 786440 | tf_op jit(solution)/shard_map/ppermute | solution.py:25
  116.6 3.6 %collective-permute-start.17 = (bf16[2,4,128,128]{3,2,0,1:T(8,128)(2,1)S(1)}, bf16[2,4,128,128]{3,2,0,1:T(8,128)(2,1)S(1)}, u32[]{:S(2)}, u32[]{:S(2)}) collective-permute-start(bf16[2,4,128,128]{3,2,0,1:T(8,128)(2,1)S(1)} %get-tuple-element.20), channel_id=1, source_target_pairs={{0,3},{1,0},{2,1},{3,2},{4,7},{5,4},{6,5},{7,6},{8,11},{9,8},{10,9... | collective-permute-start | bytes 786440 | tf_op jit(solution)/shard_map/ppermute | solution.py:25
  120.2 0.1 fusion.6
  120.3 7.5 %collective-permute-start.12 = (bf16[2,128,128]{2,1,0:T(8,128)(2,1)S(1)}, bf16[2,128,128]{2,1,0:T(8,128)(2,1)S(1)}, u32[]{:S(2)}, u32[]{:S(2)}) collective-permute-start(bf16[2,128,128]{2,1,0:T(8,128)(2,1)S(1)} %get-tuple-element.29), channel_id=1, source_target_pairs={{64,0},{80,16},{96,32},{112,48},{128,64},{144,80},{160,96},{176,11... | collective-permute-start | bytes 196616 | tf_op jit(solution)/shard_map/ppermute | solution.py:20
  127.8 1.9 collective-permute-start.13
  129.7 1.9 collective-permute-start.14
  131.7 0.1 fusion.33
  131.9 8.0 %collective-permute-start.18 = (bf16[2,128,128]{2,1,0:T(8,128)(2,1)S(1)}, bf16[2,128,128]{2,1,0:T(8,128)(2,1)S(1)}, u32[]{:S(2)}, u32[]{:S(2)}) collective-permute-start(bf16[2,128,128]{2,1,0:T(8,128)(2,1)S(1)} %get-tuple-element.26), channel_id=1, source_target_pairs={{16,0},{32,16},{48,32},{64,48},{80,64},{96,80},{112,96},{128,112},... | collective-permute-start | bytes 196616 | tf_op jit(solution)/shard_map/ppermute | solution.py:20
  139.9 7.6 %collective-permute-start.19 = (bf16[2,128,128]{2,1,0:T(8,128)(2,1)S(1)}, bf16[2,128,128]{2,1,0:T(8,128)(2,1)S(1)}, u32[]{:S(2)}, u32[]{:S(2)}) collective-permute-start(bf16[2,128,128]{2,1,0:T(8,128)(2,1)S(1)} %get-tuple-element.28), channel_id=1, source_target_pairs={{32,0},{48,16},{64,32},{80,48},{96,64},{112,80},{128,96},{144,112}... | collective-permute-start | bytes 196616 | tf_op jit(solution)/shard_map/ppermute | solution.py:20
  147.5 1.9 collective-permute-start.20
  149.4 0.1 broadcast_add_fusion
  149.5 0.1 add.175
  149.6 2.8 %collective-permute-done.19 = bf16[2,128,128]{2,1,0:T(8,128)(2,1)S(1)} collective-permute-done((bf16[2,128,128]{2,1,0:T(8,128)(2,1)S(1)}, bf16[2,128,128]{2,1,0:T(8,128)(2,1)S(1)}, u32[]{:S(2)}, u32[]{:S(2)}) %collective-permute-start.19) | collective-permute-done | bytes 65568 | tf_op jit(solution)/shard_map/ppermute | solution.py:20
  152.4 5.7 %collective-permute-done.20 = bf16[2,128,128]{2,1,0:T(8,128)(2,1)S(1)} collective-permute-done((bf16[2,128,128]{2,1,0:T(8,128)(2,1)S(1)}, bf16[2,128,128]{2,1,0:T(8,128)(2,1)S(1)}, u32[]{:S(2)}, u32[]{:S(2)}) %collective-permute-start.20) | collective-permute-done | bytes 65568 | tf_op jit(solution)/shard_map/ppermute | solution.py:20
  158.1 7.0 %collective-permute-start.21 = (bf16[2,128,128]{2,1,0:T(8,128)(2,1)S(1)}, bf16[2,128,128]{2,1,0:T(8,128)(2,1)S(1)}, u32[]{:S(2)}, u32[]{:S(2)}) collective-permute-start(bf16[2,128,128]{2,1,0:T(8,128)(2,1)S(1)} %fusion.14), channel_id=1, source_target_pairs={{0,12},{4,0},{8,4},{12,8},{1,13},{5,1},{9,5},{13,9},{2,14},{6,2},{... | collective-permute-start | bytes 196616 | tf_op jit(solution)/shard_map/ppermute | solution.py:25
  165.1 4.5 %collective-permute-start.22 = (bf16[2,128,128]{2,1,0:T(8,128)(2,1)S(1)}, bf16[2,128,128]{2,1,0:T(8,128)(2,1)S(1)}, u32[]{:S(2)}, u32[]{:S(2)}) collective-permute-start(bf16[2,128,128]{2,1,0:T(8,128)(2,1)S(1)} %fusion.14), channel_id=1, source_target_pairs={{0,8},{4,12},{8,0},{12,4},{1,9},{5,13},{9,1},{13,5},{2,10},{6,14},... | collective-permute-start | bytes 196616 | tf_op jit(solution)/shard_map/ppermute | solution.py:25
  169.6 1.9 collective-permute-start.23
  171.6 1.3 collective-permute-done.22
  172.9 4.7 %collective-permute-done.23 = bf16[2,128,128]{2,1,0:T(8,128)(2,1)S(1)} collective-permute-done((bf16[2,128,128]{2,1,0:T(8,128)(2,1)S(1)}, bf16[2,128,128]{2,1,0:T(8,128)(2,1)S(1)}, u32[]{:S(2)}, u32[]{:S(2)}) %collective-permute-start.23) | collective-permute-done | bytes 65568 | tf_op jit(solution)/shard_map/ppermute | solution.py:25
  177.6 2.0 %collective-permute-start.24 = (bf16[4,2,128,128]{3,2,1,0:T(8,128)(2,1)S(1)}, bf16[4,2,128,128]{3,2,1,0:T(8,128)(2,1)S(1)}, u32[]{:S(2)}, u32[]{:S(2)}) collective-permute-start(bf16[4,2,128,128]{3,2,1,0:T(8,128)(2,1)S(1)} %get-tuple-element.25), channel_id=1, source_target_pairs={{0,3},{1,0},{2,1},{3,2},{4,7},{5,4},{6,5},{7,6},{8,11},{9,8},{10,9... | collective-permute-start | bytes 786440 | tf_op jit(solution)/shard_map/ppermute | solution.py:25
  179.7 4.2 %collective-permute-start.25 = (bf16[4,2,128,128]{3,2,1,0:T(8,128)(2,1)S(1)}, bf16[4,2,128,128]{3,2,1,0:T(8,128)(2,1)S(1)}, u32[]{:S(2)}, u32[]{:S(2)}) collective-permute-start(bf16[4,2,128,128]{3,2,1,0:T(8,128)(2,1)S(1)} %get-tuple-element.25), channel_id=1, source_target_pairs={{0,2},{1,3},{2,0},{3,1},{4,6},{5,7},{6,4},{7,5},{8,10},{9,11},{10,... | collective-permute-start | bytes 786440 | tf_op jit(solution)/shard_map/ppermute | solution.py:25
  183.8 1.9 collective-permute-start.26
  185.8 0.1 compare_and_fusion
  185.8 1.4 collective-permute-done.24
  187.3 4.6 %collective-permute-done.25 = bf16[4,2,128,128]{3,2,1,0:T(8,128)(2,1)S(1)} collective-permute-done((bf16[4,2,128,128]{3,2,1,0:T(8,128)(2,1)S(1)}, bf16[4,2,128,128]{3,2,1,0:T(8,128)(2,1)S(1)}, u32[]{:S(2)}, u32[]{:S(2)}) %collective-permute-start.25) | collective-permute-done | bytes 262176 | tf_op jit(solution)/shard_map/ppermute | solution.py:25
  191.9 2.3 %collective-permute-done.26 = bf16[4,2,128,128]{3,2,1,0:T(8,128)(2,1)S(1)} collective-permute-done((bf16[4,2,128,128]{3,2,1,0:T(8,128)(2,1)S(1)}, bf16[4,2,128,128]{3,2,1,0:T(8,128)(2,1)S(1)}, u32[]{:S(2)}, u32[]{:S(2)}) %collective-permute-start.26) | collective-permute-done | bytes 262176 | tf_op jit(solution)/shard_map/ppermute | solution.py:25
  194.2 0.1 pad_maximum_fusion.1
  194.3 0.7 gather_fusion
  195.2 0.2 convert_bitcast_fusion
  195.4 1.5 fusion.35
  (38 shorter events, 0.4 us)
Async XLA Ops:
  2.1 27.3 %collective-permute-start = (bf16[2,128,128]{2,1,0:T(8,128)(2,1)S(1)}, bf16[2,128,128]{2,1,0:T(8,128)(2,1)S(1)}, u32[]{:S(2)}, u32[]{:S(2)}) collective-permute-start(bf16[2,128,128]{2,1,0:T(8,128)(2,1)S(1)} %slice.90), channel_id=1, source_target_pairs={{0,16},{16,32},{32,48},{48,64},{64,80},{80,96},{96,112},{112,128},... | collective-permute-start | bytes 196616 | tf_op jit(solution)/shard_map/ppermute | solution.py:20
  4.1 27.3 %collective-permute-start.1 = (bf16[2,128,128]{2,1,0:T(8,128)(2,1)S(1)}, bf16[2,128,128]{2,1,0:T(8,128)(2,1)S(1)}, u32[]{:S(2)}, u32[]{:S(2)}) collective-permute-start(bf16[2,128,128]{2,1,0:T(8,128)(2,1)S(1)} %slice.90), channel_id=1, source_target_pairs={{0,32},{16,48},{32,64},{48,80},{64,96},{80,112},{96,128},{112,144}... | collective-permute-start | bytes 196616 | tf_op jit(solution)/shard_map/ppermute | solution.py:20
  13.2 18.2 %collective-permute-start.2 = (bf16[2,128,128]{2,1,0:T(8,128)(2,1)S(1)}, bf16[2,128,128]{2,1,0:T(8,128)(2,1)S(1)}, u32[]{:S(2)}, u32[]{:S(2)}) collective-permute-start(bf16[2,128,128]{2,1,0:T(8,128)(2,1)S(1)} %slice.90), channel_id=1, source_target_pairs={{0,48},{16,64},{32,80},{48,96},{64,112},{80,128},{96,144},{112,160... | collective-permute-start | bytes 196616 | tf_op jit(solution)/shard_map/ppermute | solution.py:20
  24.1 15.8 %collective-permute-start.3 = (bf16[2,128,128]{2,1,0:T(8,128)(2,1)S(1)}, bf16[2,128,128]{2,1,0:T(8,128)(2,1)S(1)}, u32[]{:S(2)}, u32[]{:S(2)}) collective-permute-start(bf16[2,128,128]{2,1,0:T(8,128)(2,1)S(1)} %slice.90), channel_id=1, source_target_pairs={{0,64},{16,80},{32,96},{48,112},{64,128},{80,144},{96,160},{112,17... | collective-permute-start | bytes 196616 | tf_op jit(solution)/shard_map/ppermute | solution.py:20
  26.0 26.4 %collective-permute-start.4 = (bf16[2,128,128]{2,1,0:T(8,128)(2,1)S(1)}, bf16[2,128,128]{2,1,0:T(8,128)(2,1)S(1)}, u32[]{:S(2)}, u32[]{:S(2)}) collective-permute-start(bf16[2,128,128]{2,1,0:T(8,128)(2,1)S(1)} %slice.90), channel_id=1, source_target_pairs={{0,80},{16,96},{32,112},{48,128},{64,144},{80,160},{96,176},{112,1... | collective-permute-start | bytes 196616 | tf_op jit(solution)/shard_map/ppermute | solution.py:20
  29.4 23.9 %collective-permute-start.5 = (bf16[2,128,128]{2,1,0:T(8,128)(2,1)S(1)}, bf16[2,128,128]{2,1,0:T(8,128)(2,1)S(1)}, u32[]{:S(2)}, u32[]{:S(2)}) collective-permute-start(bf16[2,128,128]{2,1,0:T(8,128)(2,1)S(1)} %slice.90), channel_id=1, source_target_pairs={{0,96},{16,112},{32,128},{48,144},{64,160},{80,176},{96,192},{112,... | collective-permute-start | bytes 196616 | tf_op jit(solution)/shard_map/ppermute | solution.py:20
  53.4 22.3 %collective-permute-start.6 = (bf16[6,2,128,128]{3,2,1,0:T(8,128)(2,1)S(1)}, bf16[6,2,128,128]{3,2,1,0:T(8,128)(2,1)S(1)}, u32[]{:S(2)}, u32[]{:S(2)}) collective-permute-start(bf16[6,2,128,128]{3,2,1,0:T(8,128)(2,1)S(1)} %bitcast_dynamic-update-slice_fusion), channel_id=1, source_target_pairs={{0,3},{1,0},{2,1},{3,2},{4,7},{5,4},{6,5},{7,6},{8,11},{9,8},{10,9... | collective-permute-start | bytes 1179656 | tf_op jit(solution)/shard_map/ppermute | solution.py:25
  58.3 17.4 %collective-permute-start.7 = (bf16[6,2,128,128]{3,2,1,0:T(8,128)(2,1)S(1)}, bf16[6,2,128,128]{3,2,1,0:T(8,128)(2,1)S(1)}, u32[]{:S(2)}, u32[]{:S(2)}) collective-permute-start(bf16[6,2,128,128]{3,2,1,0:T(8,128)(2,1)S(1)} %bitcast_dynamic-update-slice_fusion), channel_id=1, source_target_pairs={{0,2},{1,3},{2,0},{3,1},{4,6},{5,7},{6,4},{7,5},{8,10},{9,11},{10,... | collective-permute-start | bytes 1179656 | tf_op jit(solution)/shard_map/ppermute | solution.py:25
  60.8 20.5 %collective-permute-start.8 = (bf16[6,2,128,128]{3,2,1,0:T(8,128)(2,1)S(1)}, bf16[6,2,128,128]{3,2,1,0:T(8,128)(2,1)S(1)}, u32[]{:S(2)}, u32[]{:S(2)}) collective-permute-start(bf16[6,2,128,128]{3,2,1,0:T(8,128)(2,1)S(1)} %bitcast_dynamic-update-slice_fusion), channel_id=1, source_target_pairs={{0,1},{1,2},{2,3},{3,0},{4,5},{5,6},{6,7},{7,4},{8,9},{9,10},{10,1... | collective-permute-start | bytes 1179656 | tf_op jit(solution)/shard_map/ppermute | solution.py:25
  98.6 10.1 %copy-start = (f32[3584,128]{1,0:T(8,128)S(1)}, f32[3584,128]{1,0:T(8,128)}, u32[]{:S(2)}) copy-start(f32[3584,128]{1,0:T(8,128)} %get-tuple-element.7) | copy-start | bytes 5505028
  98.6 10.1 %copy-start.1 = (f32[3584,128]{1,0:T(8,128)S(1)}, f32[3584,128]{1,0:T(8,128)}, u32[]{:S(2)}) copy-start(f32[3584,128]{1,0:T(8,128)} %get-tuple-element.8) | copy-start | bytes 5505028
  100.3 16.3 %collective-permute-start.10 = (bf16[2,3,128,128]{3,2,0,1:T(8,128)(2,1)S(1)}, bf16[2,3,128,128]{3,2,0,1:T(8,128)(2,1)S(1)}, u32[]{:S(2)}, u32[]{:S(2)}) collective-permute-start(bf16[2,3,128,128]{3,2,0,1:T(8,128)(2,1)S(1)} %get-tuple-element.18), channel_id=1, source_target_pairs={{0,2},{1,3},{2,0},{3,1},{4,6},{5,7},{6,4},{7,5},{8,10},{9,11},{10,... | collective-permute-start | bytes 589832 | tf_op jit(solution)/shard_map/ppermute | solution.py:25
  102.8 17.3 %collective-permute-start.11 = (bf16[2,3,128,128]{3,2,0,1:T(8,128)(2,1)S(1)}, bf16[2,3,128,128]{3,2,0,1:T(8,128)(2,1)S(1)}, u32[]{:S(2)}, u32[]{:S(2)}) collective-permute-start(bf16[2,3,128,128]{3,2,0,1:T(8,128)(2,1)S(1)} %get-tuple-element.17), channel_id=1, source_target_pairs={{0,3},{1,0},{2,1},{3,2},{4,7},{5,4},{6,5},{7,6},{8,11},{9,8},{10,9... | collective-permute-start | bytes 589832 | tf_op jit(solution)/shard_map/ppermute | solution.py:25
  105.9 14.2 %collective-permute-start.9 = (bf16[2,3,128,128]{3,2,0,1:T(8,128)(2,1)S(1)}, bf16[2,3,128,128]{3,2,0,1:T(8,128)(2,1)S(1)}, u32[]{:S(2)}, u32[]{:S(2)}) collective-permute-start(bf16[2,3,128,128]{3,2,0,1:T(8,128)(2,1)S(1)} %get-tuple-element.16), channel_id=1, source_target_pairs={{0,1},{1,2},{2,3},{3,0},{4,5},{5,6},{6,7},{7,4},{8,9},{9,10},{10,1... | collective-permute-start | bytes 589832 | tf_op jit(solution)/shard_map/ppermute | solution.py:25
  108.9 20.9 %collective-permute-start.15 = (bf16[2,4,128,128]{3,2,0,1:T(8,128)(2,1)S(1)}, bf16[2,4,128,128]{3,2,0,1:T(8,128)(2,1)S(1)}, u32[]{:S(2)}, u32[]{:S(2)}) collective-permute-start(bf16[2,4,128,128]{3,2,0,1:T(8,128)(2,1)S(1)} %get-tuple-element.19), channel_id=1, source_target_pairs={{0,1},{1,2},{2,3},{3,0},{4,5},{5,6},{6,7},{7,4},{8,9},{9,10},{10,1... | collective-permute-start | bytes 786440 | tf_op jit(solution)/shard_map/ppermute | solution.py:25
  111.6 20.1 %collective-permute-start.16 = (bf16[2,4,128,128]{3,2,0,1:T(8,128)(2,1)S(1)}, bf16[2,4,128,128]{3,2,0,1:T(8,128)(2,1)S(1)}, u32[]{:S(2)}, u32[]{:S(2)}) collective-permute-start(bf16[2,4,128,128]{3,2,0,1:T(8,128)(2,1)S(1)} %get-tuple-element.21), channel_id=1, source_target_pairs={{0,2},{1,3},{2,0},{3,1},{4,6},{5,7},{6,4},{7,5},{8,10},{9,11},{10,... | collective-permute-start | bytes 786440 | tf_op jit(solution)/shard_map/ppermute | solution.py:25
  116.6 15.1 %collective-permute-start.17 = (bf16[2,4,128,128]{3,2,0,1:T(8,128)(2,1)S(1)}, bf16[2,4,128,128]{3,2,0,1:T(8,128)(2,1)S(1)}, u32[]{:S(2)}, u32[]{:S(2)}) collective-permute-start(bf16[2,4,128,128]{3,2,0,1:T(8,128)(2,1)S(1)} %get-tuple-element.20), channel_id=1, source_target_pairs={{0,3},{1,0},{2,1},{3,2},{4,7},{5,4},{6,5},{7,6},{8,11},{9,8},{10,9... | collective-permute-start | bytes 786440 | tf_op jit(solution)/shard_map/ppermute | solution.py:25
  120.3 27.2 %collective-permute-start.12 = (bf16[2,128,128]{2,1,0:T(8,128)(2,1)S(1)}, bf16[2,128,128]{2,1,0:T(8,128)(2,1)S(1)}, u32[]{:S(2)}, u32[]{:S(2)}) collective-permute-start(bf16[2,128,128]{2,1,0:T(8,128)(2,1)S(1)} %get-tuple-element.29), channel_id=1, source_target_pairs={{64,0},{80,16},{96,32},{112,48},{128,64},{144,80},{160,96},{176,11... | collective-permute-start | bytes 196616 | tf_op jit(solution)/shard_map/ppermute | solution.py:20
  127.8 21.7 %collective-permute-start.13 = (bf16[2,128,128]{2,1,0:T(8,128)(2,1)S(1)}, bf16[2,128,128]{2,1,0:T(8,128)(2,1)S(1)}, u32[]{:S(2)}, u32[]{:S(2)}) collective-permute-start(bf16[2,128,128]{2,1,0:T(8,128)(2,1)S(1)} %get-tuple-element.31), channel_id=1, source_target_pairs={{80,0},{96,16},{112,32},{128,48},{144,64},{160,80},{176,96},{192,1... | collective-permute-start | bytes 196616 | tf_op jit(solution)/shard_map/ppermute | solution.py:20
  129.7 19.8 %collective-permute-start.14 = (bf16[2,128,128]{2,1,0:T(8,128)(2,1)S(1)}, bf16[2,128,128]{2,1,0:T(8,128)(2,1)S(1)}, u32[]{:S(2)}, u32[]{:S(2)}) collective-permute-start(bf16[2,128,128]{2,1,0:T(8,128)(2,1)S(1)} %get-tuple-element.30), channel_id=1, source_target_pairs={{96,0},{112,16},{128,32},{144,48},{160,64},{176,80},{192,96},{208,... | collective-permute-start | bytes 196616 | tf_op jit(solution)/shard_map/ppermute | solution.py:20
  131.9 17.7 %collective-permute-start.18 = (bf16[2,128,128]{2,1,0:T(8,128)(2,1)S(1)}, bf16[2,128,128]{2,1,0:T(8,128)(2,1)S(1)}, u32[]{:S(2)}, u32[]{:S(2)}) collective-permute-start(bf16[2,128,128]{2,1,0:T(8,128)(2,1)S(1)} %get-tuple-element.26), channel_id=1, source_target_pairs={{16,0},{32,16},{48,32},{64,48},{80,64},{96,80},{112,96},{128,112},... | collective-permute-start | bytes 196616 | tf_op jit(solution)/shard_map/ppermute | solution.py:20
  139.9 12.5 %collective-permute-start.19 = (bf16[2,128,128]{2,1,0:T(8,128)(2,1)S(1)}, bf16[2,128,128]{2,1,0:T(8,128)(2,1)S(1)}, u32[]{:S(2)}, u32[]{:S(2)}) collective-permute-start(bf16[2,128,128]{2,1,0:T(8,128)(2,1)S(1)} %get-tuple-element.28), channel_id=1, source_target_pairs={{32,0},{48,16},{64,32},{80,48},{96,64},{112,80},{128,96},{144,112}... | collective-permute-start | bytes 196616 | tf_op jit(solution)/shard_map/ppermute | solution.py:20
  147.5 10.6 %collective-permute-start.20 = (bf16[2,128,128]{2,1,0:T(8,128)(2,1)S(1)}, bf16[2,128,128]{2,1,0:T(8,128)(2,1)S(1)}, u32[]{:S(2)}, u32[]{:S(2)}) collective-permute-start(bf16[2,128,128]{2,1,0:T(8,128)(2,1)S(1)} %get-tuple-element.27), channel_id=1, source_target_pairs={{48,0},{64,16},{80,32},{96,48},{112,64},{128,80},{144,96},{160,112... | collective-permute-start | bytes 196616 | tf_op jit(solution)/shard_map/ppermute | solution.py:20
  158.1 13.4 %collective-permute-start.21 = (bf16[2,128,128]{2,1,0:T(8,128)(2,1)S(1)}, bf16[2,128,128]{2,1,0:T(8,128)(2,1)S(1)}, u32[]{:S(2)}, u32[]{:S(2)}) collective-permute-start(bf16[2,128,128]{2,1,0:T(8,128)(2,1)S(1)} %fusion.14), channel_id=1, source_target_pairs={{0,12},{4,0},{8,4},{12,8},{1,13},{5,1},{9,5},{13,9},{2,14},{6,2},{... | collective-permute-start | bytes 196616 | tf_op jit(solution)/shard_map/ppermute | solution.py:25
  165.1 7.8 %collective-permute-start.22 = (bf16[2,128,128]{2,1,0:T(8,128)(2,1)S(1)}, bf16[2,128,128]{2,1,0:T(8,128)(2,1)S(1)}, u32[]{:S(2)}, u32[]{:S(2)}) collective-permute-start(bf16[2,128,128]{2,1,0:T(8,128)(2,1)S(1)} %fusion.14), channel_id=1, source_target_pairs={{0,8},{4,12},{8,0},{12,4},{1,9},{5,13},{9,1},{13,5},{2,10},{6,14},... | collective-permute-start | bytes 196616 | tf_op jit(solution)/shard_map/ppermute | solution.py:25
  169.6 8.0 %collective-permute-start.23 = (bf16[2,128,128]{2,1,0:T(8,128)(2,1)S(1)}, bf16[2,128,128]{2,1,0:T(8,128)(2,1)S(1)}, u32[]{:S(2)}, u32[]{:S(2)}) collective-permute-start(bf16[2,128,128]{2,1,0:T(8,128)(2,1)S(1)} %fusion.14), channel_id=1, source_target_pairs={{0,4},{4,8},{8,12},{12,0},{1,5},{5,9},{9,13},{13,1},{2,6},{6,10},{... | collective-permute-start | bytes 196616 | tf_op jit(solution)/shard_map/ppermute | solution.py:25
  177.6 9.6 %collective-permute-start.24 = (bf16[4,2,128,128]{3,2,1,0:T(8,128)(2,1)S(1)}, bf16[4,2,128,128]{3,2,1,0:T(8,128)(2,1)S(1)}, u32[]{:S(2)}, u32[]{:S(2)}) collective-permute-start(bf16[4,2,128,128]{3,2,1,0:T(8,128)(2,1)S(1)} %get-tuple-element.25), channel_id=1, source_target_pairs={{0,3},{1,0},{2,1},{3,2},{4,7},{5,4},{6,5},{7,6},{8,11},{9,8},{10,9... | collective-permute-start | bytes 786440 | tf_op jit(solution)/shard_map/ppermute | solution.py:25
  179.7 12.2 %collective-permute-start.25 = (bf16[4,2,128,128]{3,2,1,0:T(8,128)(2,1)S(1)}, bf16[4,2,128,128]{3,2,1,0:T(8,128)(2,1)S(1)}, u32[]{:S(2)}, u32[]{:S(2)}) collective-permute-start(bf16[4,2,128,128]{3,2,1,0:T(8,128)(2,1)S(1)} %get-tuple-element.25), channel_id=1, source_target_pairs={{0,2},{1,3},{2,0},{3,1},{4,6},{5,7},{6,4},{7,5},{8,10},{9,11},{10,... | collective-permute-start | bytes 786440 | tf_op jit(solution)/shard_map/ppermute | solution.py:25
  183.8 10.4 %collective-permute-start.26 = (bf16[4,2,128,128]{3,2,1,0:T(8,128)(2,1)S(1)}, bf16[4,2,128,128]{3,2,1,0:T(8,128)(2,1)S(1)}, u32[]{:S(2)}, u32[]{:S(2)}) collective-permute-start(bf16[4,2,128,128]{3,2,1,0:T(8,128)(2,1)S(1)} %get-tuple-element.25), channel_id=1, source_target_pairs={{0,1},{1,2},{2,3},{3,0},{4,5},{5,6},{6,7},{7,4},{8,9},{9,10},{10,1... | collective-permute-start | bytes 786440 | tf_op jit(solution)/shard_map/ppermute | solution.py:25

commit v7 on v6

--- a/solution.py
+++ b/solution.py
@@ -14,15 +14,29 @@
 REACH = 6
 
 
-def shifted_2(value, axis, steps):
-    count = lax.axis_size(axis)
-    leading, last = (max(0, -steps), min(count, count - steps))
-    return lax.ppermute(value, axis, [(source, source + steps) for source in range(leading, last)])
-
-
 def cycled(value, axis, steps):
     count = lax.axis_size(axis)
     return lax.ppermute(value, axis, [(source, (source + steps) % count) for source in range(count)])
+
+
+def chip_pairs(count, step):
+    nearer = [(target - (2 * step - 1), target) for target in range(0, count, 2)]
+    farther = [(target - (2 * step + 1), target) for target in range(1, count, 2)]
+    return [(source, target) for source, target in nearer + farther if source >= 0]
+
+
+def chip_fetch(value, axis, step):
+    return lax.ppermute(value, axis, chip_pairs(lax.axis_size(axis), step))
+
+
+def chip_return(value, axis, step):
+    pairs = chip_pairs(lax.axis_size(axis), step)
+    return lax.ppermute(value, axis, [(target, source) for source, target in pairs])
+
+
+def swap_cores(value, axis):
+    count = lax.axis_size(axis)
+    return lax.ppermute(value, axis, [(source, source ^ 1) for source in range(count)])
 
 
 def block_kernel(slots_ref, q_ref, do_ref, code_ref, k_ref, v_ref, dq_ref, dk_ref, dv_ref,
@@ -147,7 +161,19 @@
     )
     rolled = jnp.roll(own_tiles, -part_index * quarter, axis=1)
     own_part = rolled[:, :quarter]
-    fetched = jnp.stack([shifted_2(own_part, "ctx", offset) for offset in range(1, reach_span)])
+    even = ctx_index % 2 == 0
+    took = [chip_fetch(own_part, "ctx", step) for step in range(1, 4)]
+    other = swap_cores(jnp.stack([own_part] + took), "ctx")
+    fetched = jnp.stack(
+        [
+            jnp.where(even, took[0], other[0]),
+            other[1],
+            jnp.where(even, took[1], took[0]),
+            other[2],
+            jnp.where(even, took[2], took[1]),
+            other[3],
+        ]
+    )
     pieces = [fetched] + [cycled(fetched, "sub", -step) for step in range(1, parts_count)]
     tile_store = jnp.concatenate([rolled[None], jnp.concatenate(pieces, axis=2)], axis=0)
     key_tiles = tile_store[:, 0].reshape(reach_span * blocks_here, BLOCK, width)
@@ -166,18 +192,29 @@
     )
     grads = jnp.stack([key_grad, value_grad]).reshape(2, reach_span, tokens_here, width)
     sent = grads.astype(jnp.bfloat16)
-    split = REACH // 2 + 1
-    running = None
-    for lo, hi in ((split, reach_span), (0, split)):
-        part = grads[:, lo:hi, :quarter]
+
+    def reduce_parts(offsets):
+        part = jnp.stack([grads[:, offset, :quarter] for offset in offsets], axis=1)
         for step in range(1, parts_count):
-            piece = sent[:, lo:hi, step * quarter:(step + 1) * quarter]
+            piece = jnp.stack(
+                [sent[:, offset, step * quarter:(step + 1) * quarter] for offset in offsets], axis=1
+            )
             part = part + cycled(piece, "sub", step).astype(jnp.float32)
-        for offset in range(lo, hi):
-            term = part[:, offset - lo]
-            if offset:
-                term = shifted_2(term.astype(jnp.bfloat16), "ctx", -offset).astype(jnp.float32)
-            running = term if running is None else running + term
+        return dict(zip(offsets, [part[:, index] for index in range(len(offsets))]))
+
+    shared = reduce_parts((1, 2, 4, 6))
+    other = swap_cores(
+        jnp.stack([shared[1], shared[2], shared[4], shared[6]]).astype(jnp.bfloat16), "ctx"
+    ).astype(jnp.float32)
+    kept = reduce_parts((0, 3, 5))
+    running = kept[0] + jnp.where(even, other[0], 0.0)
+    outgoing = [
+        jnp.where(even, shared[1] + other[1], kept[3] + other[1]),
+        jnp.where(even, kept[3] + other[2], kept[5] + other[2]),
+        jnp.where(even, kept[5] + other[3], other[3]),
+    ]
+    for step, term in enumerate(outgoing, start=1):
+        running = running + chip_return(term.astype(jnp.bfloat16), "ctx", step).astype(jnp.float32)
     mine = running.astype(jnp.bfloat16)
     by_group = jnp.stack([mine] + [cycled(mine, "grp", -step) for step in range(1, groups)])
     by_part = jnp.stack([by_group] + [cycled(by_group, "sub", -step) for step in range(1, parts_count)])

time: 198 us -> 177 us (0.89)
  waiting for transfers between devices: 60.7 us -> 46.3 us
  starting transfers between devices: 108 us -> 99.6 us
    ppermute x12 -> x8, starting transfers between devices: 56.5 us -> 43.7 us  [the longest x3 21 us: chip_fetch(): return lax.ppermute(value, axis, chip_pairs(lax.axis_size(axis), step))]
    ppermute x12 -> x8, waiting for transfers between devices: 30.4 us -> 19.8 us  [the longest x3 11.5 us: chip_return(): lax.ppermute(value, axis, [(target, source) for source, target in pairs])]
    ppermute x15, starting transfers between devices: 51.5 us -> 55.9 us  [cycled(): lax.ppermute(value, axis, [(source, (source + steps) % count) for source...]
    ppermute x15, waiting for transfers between devices: 30.3 us -> 26.5 us  [cycled(): lax.ppermute(value, axis, [(source, (source + steps) % count) for source...]
    convert_element_type x0 -> x3, other arithmetic: none -> 2.35 us  [the longest x1 2.26 us: per_device(): sent = grads.astype(jnp.bfloat16)]
  transfers between devices with their start and end apart: 27 -> 23, of which waited for: 12 -> 16; matrix products, arithmetic and copies ran while one was open for 2% -> 2% of each run, Pallas kernels for 0% -> 0%
where the time goes in v7:
time: 177 us; the launch traced here: 175 us
  starting transfers between devices  99.6 us (56%)
  waiting for transfers between devices  46.3 us (26%)
  Pallas kernels  15.8 us (9%)
  local copies, waits for them, and re-layouts  6.11 us (3%)
  other arithmetic  6.05 us (3%)
    ppermute x15, starting transfers between devices, cycled(): lax.ppermute(value, axis, [(source, (source + steps) % count) for source...  55.9 us
    ppermute x15, waiting for transfers between devices, cycled(): lax.ppermute(value, axis, [(source, (source + steps) % count) for source...  26.5 us
    ppermute x3, starting transfers between devices, chip_fetch(): return lax.ppermute(value, axis, chip_pairs(lax.axis_size(axis), step))  21 us
    ppermute x3, starting transfers between devices, chip_return(): lax.ppermute(value, axis, [(target, source) for source, target in pairs])  17.9 us
    pallas_call x1, Pallas kernels, local_grads(): pl.pallas_call(kernel, grid_spec=pltpu.PrefetchScalarGridSpec(num_scalar_...  15.8 us
    ppermute x3, waiting for transfers between devices, chip_return(): lax.ppermute(value, axis, [(target, source) for source, target in pairs])  11.5 us
    ppermute x3, waiting for transfers between devices, chip_fetch(): return lax.ppermute(value, axis, chip_pairs(lax.axis_size(axis), step))  6.82 us
    ppermute x2, starting transfers between devices, swap_cores(): lax.ppermute(value, axis, [(source, source ^ 1) for source in range(count)])  4.7 us
  transfers between devices with their start and end apart: 23, of which 16 were waited for; matrix products, arithmetic and copies ran while one was open for 2% of the time, Pallas kernels for 0%

profile of v7, /device:TPU:6, one launch (start us, length us, event | category | flops | bytes accessed | tf_op | source)
XLA Modules:
  0.0 175.0 jit_solution(7010606299559011190)
XLA Ops:
  0.7 1.0 constant_dynamic-slice_fusion
  1.7 0.5 fusion.6
  2.2 15.2 %collective-permute-start.1 = (bf16[2,128,128]{2,1,0:T(8,128)(2,1)S(1)}, bf16[2,128,128]{2,1,0:T(8,128)(2,1)S(1)}, u32[]{:S(2)}, u32[]{:S(2)}) collective-permute-start(bf16[2,128,128]{2,1,0:T(8,128)(2,1)S(1)} %get-tuple-element.50), channel_id=1, source_target_pairs={{16,64},{48,96},{80,128},{112,160},{144,192},{176,224},{208,256},{... | collective-permute-start | bytes 196616 | tf_op jit(solution)/shard_map/ppermute | solution.py:29
  17.3 1.9 %collective-permute-start.2 = (bf16[2,128,128]{2,1,0:T(8,128)(2,1)S(1)}, bf16[2,128,128]{2,1,0:T(8,128)(2,1)S(1)}, u32[]{:S(2)}, u32[]{:S(2)}) collective-permute-start(bf16[2,128,128]{2,1,0:T(8,128)(2,1)S(1)} %get-tuple-element.50), channel_id=1, source_target_pairs={{16,96},{48,128},{80,160},{112,192},{144,224},{176,256},{208,288},... | collective-permute-start | bytes 196616 | tf_op jit(solution)/shard_map/ppermute | solution.py:29
  19.3 3.9 %collective-permute-start = (bf16[2,128,128]{2,1,0:T(8,128)(2,1)S(1)}, bf16[2,128,128]{2,1,0:T(8,128)(2,1)S(1)}, u32[]{:S(2)}, u32[]{:S(2)}) collective-permute-start(bf16[2,128,128]{2,1,0:T(8,128)(2,1)S(1)} %get-tuple-element.50), channel_id=1, source_target_pairs={{16,32},{48,64},{80,96},{112,128},{144,160},{176,192},{208,224},{2... | collective-permute-start | bytes 196616 | tf_op jit(solution)/shard_map/ppermute | solution.py:29
  23.2 0.8 constant_dynamic-slice_fusion.2
  24.0 0.6 fusion.30.slots_ref
  24.6 6.1 %collective-permute-done.2 = bf16[2,128,128]{2,1,0:T(8,128)(2,1)S(1)} collective-permute-done((bf16[2,128,128]{2,1,0:T(8,128)(2,1)S(1)}, bf16[2,128,128]{2,1,0:T(8,128)(2,1)S(1)}, u32[]{:S(2)}, u32[]{:S(2)}) %collective-permute-start.2) | collective-permute-done | bytes 65568 | tf_op jit(solution)/shard_map/ppermute | solution.py:29
  30.7 0.7 collective-permute-done
  31.5 2.8 %collective-permute-start.3 = (bf16[4,2,128,128]{3,2,1,0:T(8,128)(2,1)S(1)}, bf16[4,2,128,128]{3,2,1,0:T(8,128)(2,1)S(1)}, u32[]{:S(2)}, u32[]{:S(2)}) collective-permute-start(bf16[4,2,128,128]{3,2,1,0:T(8,128)(2,1)S(1)} %pad_maximum_fusion.2), channel_id=1, source_target_pairs={{0,16},{16,0},{32,48},{48,32},{64,80},{80,64},{96,112},{112,96},{1... | collective-permute-start | bytes 786440 | tf_op jit(solution)/shard_map/ppermute | solution.py:39
  34.3 0.1 fusion.35
  34.3 1.0 collective-permute-done.3
  35.5 3.5 %collective-permute-start.6 = (bf16[6,2,128,128]{3,2,1,0:T(8,128)(2,1)S(1)}, bf16[6,2,128,128]{3,2,1,0:T(8,128)(2,1)S(1)}, u32[]{:S(2)}, u32[]{:S(2)}) collective-permute-start(bf16[6,2,128,128]{3,2,1,0:T(8,128)(2,1)S(1)} %slice_dynamic-update-slice_fusion), channel_id=1, source_target_pairs={{0,1},{1,2},{2,3},{3,0},{4,5},{5,6},{6,7},{7,4},{8,9},{9,10},{10,1... | collective-permute-start | bytes 1179656 | tf_op jit(solution)/shard_map/ppermute | solution.py:19
  39.0 4.8 %collective-permute-start.5 = (bf16[6,2,128,128]{3,2,1,0:T(8,128)(2,1)S(1)}, bf16[6,2,128,128]{3,2,1,0:T(8,128)(2,1)S(1)}, u32[]{:S(2)}, u32[]{:S(2)}) collective-permute-start(bf16[6,2,128,128]{3,2,1,0:T(8,128)(2,1)S(1)} %slice_dynamic-update-slice_fusion), channel_id=1, source_target_pairs={{0,2},{1,3},{2,0},{3,1},{4,6},{5,7},{6,4},{7,5},{8,10},{9,11},{10,... | collective-permute-start | bytes 1179656 | tf_op jit(solution)/shard_map/ppermute | solution.py:19
  43.9 3.3 %collective-permute-start.4 = (bf16[6,2,128,128]{3,2,1,0:T(8,128)(2,1)S(1)}, bf16[6,2,128,128]{3,2,1,0:T(8,128)(2,1)S(1)}, u32[]{:S(2)}, u32[]{:S(2)}) collective-permute-start(bf16[6,2,128,128]{3,2,1,0:T(8,128)(2,1)S(1)} %slice_dynamic-update-slice_fusion), channel_id=1, source_target_pairs={{0,3},{1,0},{2,1},{3,2},{4,7},{5,4},{6,5},{7,6},{8,11},{9,8},{10,9... | collective-permute-start | bytes 1179656 | tf_op jit(solution)/shard_map/ppermute | solution.py:19
  47.2 0.1 broadcast_in_dim.51
  47.3 0.1 eq.60
  47.4 0.1 broadcast_in_dim.49
  47.5 0.1 eq.59
  47.6 0.5 fusion.51
  48.1 0.7 select_select_fusion.code_ref
  48.8 1.3 collective-permute-done.6
  50.1 9.6 %collective-permute-done.5 = bf16[6,2,128,128]{3,2,1,0:T(8,128)(2,1)S(1)} collective-permute-done((bf16[6,2,128,128]{3,2,1,0:T(8,128)(2,1)S(1)}, bf16[6,2,128,128]{3,2,1,0:T(8,128)(2,1)S(1)}, u32[]{:S(2)}, u32[]{:S(2)}) %collective-permute-start.5) | collective-permute-done | bytes 393248 | tf_op jit(solution)/shard_map/ppermute | solution.py:19
  59.7 1.4 collective-permute-done.4
  61.1 0.1 maximum_maximum_fusion
  61.2 1.4 fusion.50
  62.6 15.8 %shard_map.85 = (bf16[2048,128]{1,0:T(8,128)(2,1)}, f32[3584,128]{1,0:T(8,128)}, f32[3584,128]{1,0:T(8,128)}) custom-call(s32[8,16]{1,0:T(8,128)} %fusion.30.slots_ref, bf16[2048,128]{1,0:T(8,128)(2,1)} %bitcast.126, bf16[2048,128]{1,0:T(8,128)(2,1)} %bitcast.127, s32[8,1,1024]{2,1,0:T(1,128)} %select_select_fusion.code_ref, bf16[3584,128]{1,0:T(8,128)(2,1)} %bitcast.121, ...), custom_call_target="tpu_custom_call" | custom-call | tf_op jit(solution)/shard_map/pallas_call | solution.py:105
  78.4 2.3 %fusion = bf16[2,7,512,128]{3,2,0,1:T(8,128)(2,1)S(1)} fusion(f32[1,7,512,128]{3,2,0,1:T(8,128)} %bitcast.115, f32[1,7,512,128]{3,2,0,1:T(8,128)} %bitcast.112), kind=kLoop, calls=%fused_computation.14 | loop fusion | flops 917504 | bytes 5505024 | tf_op jit(solution)/shard_map/convert_element_type | solution.py:194
  80.7 0.1 fusion.48
  80.8 5.3 %collective-permute-start.8 = (bf16[2,3,128,128]{3,2,0,1:T(8,128)(2,1)S(1)}, bf16[2,3,128,128]{3,2,0,1:T(8,128)(2,1)S(1)}, u32[]{:S(2)}, u32[]{:S(2)}) collective-permute-start(bf16[2,3,128,128]{3,2,0,1:T(8,128)(2,1)S(1)} %pad_maximum_fusion.9), channel_id=1, source_target_pairs={{0,2},{1,3},{2,0},{3,1},{4,6},{5,7},{6,4},{7,5},{8,10},{9,11},{10,... | collective-permute-start | bytes 589832 | tf_op jit(solution)/shard_map/ppermute | solution.py:19
  86.2 3.9 %collective-permute-start.9 = (bf16[2,3,128,128]{3,2,0,1:T(8,128)(2,1)S(1)}, bf16[2,3,128,128]{3,2,0,1:T(8,128)(2,1)S(1)}, u32[]{:S(2)}, u32[]{:S(2)}) collective-permute-start(bf16[2,3,128,128]{3,2,0,1:T(8,128)(2,1)S(1)} %pad_maximum_fusion.10), channel_id=1, source_target_pairs={{0,3},{1,0},{2,1},{3,2},{4,7},{5,4},{6,5},{7,6},{8,11},{9,8},{10,9... | collective-permute-start | bytes 589832 | tf_op jit(solution)/shard_map/ppermute | solution.py:19
  90.2 2.3 %collective-permute-start.11 = (bf16[2,4,128,128]{3,2,0,1:T(8,128)(2,1)S(1)}, bf16[2,4,128,128]{3,2,0,1:T(8,128)(2,1)S(1)}, u32[]{:S(2)}, u32[]{:S(2)}) collective-permute-start(bf16[2,4,128,128]{3,2,0,1:T(8,128)(2,1)S(1)} %pad_maximum_fusion.4), channel_id=1, source_target_pairs={{0,2},{1,3},{2,0},{3,1},{4,6},{5,7},{6,4},{7,5},{8,10},{9,11},{10,... | collective-permute-start | bytes 786440 | tf_op jit(solution)/shard_map/ppermute | solution.py:19
  92.5 4.2 %collective-permute-start.12 = (bf16[2,4,128,128]{3,2,0,1:T(8,128)(2,1)S(1)}, bf16[2,4,128,128]{3,2,0,1:T(8,128)(2,1)S(1)}, u32[]{:S(2)}, u32[]{:S(2)}) collective-permute-start(bf16[2,4,128,128]{3,2,0,1:T(8,128)(2,1)S(1)} %pad_maximum_fusion.5), channel_id=1, source_target_pairs={{0,3},{1,0},{2,1},{3,2},{4,7},{5,4},{6,5},{7,6},{8,11},{9,8},{10,9... | collective-permute-start | bytes 786440 | tf_op jit(solution)/shard_map/ppermute | solution.py:19
  96.7 1.9 %collective-permute-start.10 = (bf16[2,4,128,128]{3,2,0,1:T(8,128)(2,1)S(1)}, bf16[2,4,128,128]{3,2,0,1:T(8,128)(2,1)S(1)}, u32[]{:S(2)}, u32[]{:S(2)}) collective-permute-start(bf16[2,4,128,128]{3,2,0,1:T(8,128)(2,1)S(1)} %pad_maximum_fusion.3), channel_id=1, source_target_pairs={{0,1},{1,2},{2,3},{3,0},{4,5},{5,6},{6,7},{7,4},{8,9},{9,10},{10,1... | collective-permute-start | bytes 786440 | tf_op jit(solution)/shard_map/ppermute | solution.py:19
  98.8 2.6 %collective-permute-done.11 = bf16[2,4,128,128]{3,2,0,1:T(8,128)(2,1)S(1)} collective-permute-done((bf16[2,4,128,128]{3,2,0,1:T(8,128)(2,1)S(1)}, bf16[2,4,128,128]{3,2,0,1:T(8,128)(2,1)S(1)}, u32[]{:S(2)}, u32[]{:S(2)}) %collective-permute-start.11) | collective-permute-done | bytes 262176 | tf_op jit(solution)/shard_map/ppermute | solution.py:19
  101.4 5.2 %collective-permute-start.7 = (bf16[2,3,128,128]{3,2,0,1:T(8,128)(2,1)S(1)}, bf16[2,3,128,128]{3,2,0,1:T(8,128)(2,1)S(1)}, u32[]{:S(2)}, u32[]{:S(2)}) collective-permute-start(bf16[2,3,128,128]{3,2,0,1:T(8,128)(2,1)S(1)} %pad_maximum_fusion.8), channel_id=1, source_target_pairs={{0,1},{1,2},{2,3},{3,0},{4,5},{5,6},{6,7},{7,4},{8,9},{9,10},{10,1... | collective-permute-start | bytes 589832 | tf_op jit(solution)/shard_map/ppermute | solution.py:19
  106.6 0.2 collective-permute-done.12
  106.8 1.1 collective-permute-done.10
  107.9 0.1 fusion.45
  108.1 1.9 %collective-permute-start.13 = (bf16[4,2,128,128]{3,2,1,0:T(8,128)(2,1)S(1)}, bf16[4,2,128,128]{3,2,1,0:T(8,128)(2,1)S(1)}, u32[]{:S(2)}, u32[]{:S(2)}) collective-permute-start(bf16[4,2,128,128]{3,2,1,0:T(8,128)(2,1)S(1)} %pad_maximum_fusion.6), channel_id=1, source_target_pairs={{0,16},{16,0},{32,48},{48,32},{64,80},{80,64},{96,112},{112,96},{1... | collective-permute-start | bytes 786440 | tf_op jit(solution)/shard_map/ppermute | solution.py:39
  110.0 1.0 collective-permute-done.7
  111.0 0.1 fusion.4
  111.1 0.4 collective-permute-done.13
  111.6 6.3 %collective-permute-start.14 = (bf16[2,128,128]{2,1,0:T(8,128)(2,1)S(1)}, bf16[2,128,128]{2,1,0:T(8,128)(2,1)S(1)}, u32[]{:S(2)}, u32[]{:S(2)}) collective-permute-start(bf16[2,128,128]{2,1,0:T(8,128)(2,1)S(1)} %get-tuple-element.41), channel_id=1, source_target_pairs={{32,16},{64,48},{96,80},{128,112},{160,144},{192,176},{224,208},{2... | collective-permute-start | bytes 196616 | tf_op jit(solution)/shard_map/ppermute | solution.py:34
  117.9 4.4 %collective-permute-start.16 = (bf16[2,128,128]{2,1,0:T(8,128)(2,1)S(1)}, bf16[2,128,128]{2,1,0:T(8,128)(2,1)S(1)}, u32[]{:S(2)}, u32[]{:S(2)}) collective-permute-start(bf16[2,128,128]{2,1,0:T(8,128)(2,1)S(1)} %get-tuple-element.42), channel_id=1, source_target_pairs={{96,16},{128,48},{160,80},{192,112},{224,144},{256,176},{288,208},... | collective-permute-start | bytes 196616 | tf_op jit(solution)/shard_map/ppermute | solution.py:34
  122.3 7.3 %collective-permute-start.15 = (bf16[2,128,128]{2,1,0:T(8,128)(2,1)S(1)}, bf16[2,128,128]{2,1,0:T(8,128)(2,1)S(1)}, u32[]{:S(2)}, u32[]{:S(2)}) collective-permute-start(bf16[2,128,128]{2,1,0:T(8,128)(2,1)S(1)} %get-tuple-element.43), channel_id=1, source_target_pairs={{64,16},{96,48},{128,80},{160,112},{192,144},{224,176},{256,208},{... | collective-permute-start | bytes 196616 | tf_op jit(solution)/shard_map/ppermute | solution.py:34
  129.6 0.1 broadcast_add_fusion
  129.6 0.1 add.192
  129.7 11.5 %collective-permute-done.15 = bf16[2,128,128]{2,1,0:T(8,128)(2,1)S(1)} collective-permute-done((bf16[2,128,128]{2,1,0:T(8,128)(2,1)S(1)}, bf16[2,128,128]{2,1,0:T(8,128)(2,1)S(1)}, u32[]{:S(2)}, u32[]{:S(2)}) %collective-permute-start.15) | collective-permute-done | bytes 65568 | tf_op jit(solution)/shard_map/ppermute | solution.py:34
  141.3 1.9 %collective-permute-start.19 = (bf16[2,128,128]{2,1,0:T(8,128)(2,1)S(1)}, bf16[2,128,128]{2,1,0:T(8,128)(2,1)S(1)}, u32[]{:S(2)}, u32[]{:S(2)}) collective-permute-start(bf16[2,128,128]{2,1,0:T(8,128)(2,1)S(1)} %fusion.20), channel_id=1, source_target_pairs={{0,4},{4,8},{8,12},{12,0},{1,5},{5,9},{9,13},{13,1},{2,6},{6,10},{... | collective-permute-start | bytes 196616 | tf_op jit(solution)/shard_map/ppermute | solution.py:19
  143.2 5.0 %collective-permute-start.18 = (bf16[2,128,128]{2,1,0:T(8,128)(2,1)S(1)}, bf16[2,128,128]{2,1,0:T(8,128)(2,1)S(1)}, u32[]{:S(2)}, u32[]{:S(2)}) collective-permute-start(bf16[2,128,128]{2,1,0:T(8,128)(2,1)S(1)} %fusion.20), channel_id=1, source_target_pairs={{0,8},{4,12},{8,0},{12,4},{1,9},{5,13},{9,1},{13,5},{2,10},{6,14},... | collective-permute-start | bytes 196616 | tf_op jit(solution)/shard_map/ppermute | solution.py:19
  148.2 4.8 %collective-permute-start.17 = (bf16[2,128,128]{2,1,0:T(8,128)(2,1)S(1)}, bf16[2,128,128]{2,1,0:T(8,128)(2,1)S(1)}, u32[]{:S(2)}, u32[]{:S(2)}) collective-permute-start(bf16[2,128,128]{2,1,0:T(8,128)(2,1)S(1)} %fusion.20), channel_id=1, source_target_pairs={{0,12},{4,0},{8,4},{12,8},{1,13},{5,1},{9,5},{13,9},{2,14},{6,2},{... | collective-permute-start | bytes 196616 | tf_op jit(solution)/shard_map/ppermute | solution.py:19
  153.1 1.9 %collective-permute-done.17 = bf16[2,128,128]{2,1,0:T(8,128)(2,1)S(1)} collective-permute-done((bf16[2,128,128]{2,1,0:T(8,128)(2,1)S(1)}, bf16[2,128,128]{2,1,0:T(8,128)(2,1)S(1)}, u32[]{:S(2)}, u32[]{:S(2)}) %collective-permute-start.17) | collective-permute-done | bytes 65568 | tf_op jit(solution)/shard_map/ppermute | solution.py:19
  155.0 4.0 %collective-permute-start.21 = (bf16[4,2,128,128]{3,2,1,0:T(8,128)(2,1)S(1)}, bf16[4,2,128,128]{3,2,1,0:T(8,128)(2,1)S(1)}, u32[]{:S(2)}, u32[]{:S(2)}) collective-permute-start(bf16[4,2,128,128]{3,2,1,0:T(8,128)(2,1)S(1)} %get-tuple-element.45), channel_id=1, source_target_pairs={{0,2},{1,3},{2,0},{3,1},{4,6},{5,7},{6,4},{7,5},{8,10},{9,11},{10,... | collective-permute-start | bytes 786440 | tf_op jit(solution)/shard_map/ppermute | solution.py:19
  159.0 3.9 %collective-permute-start.20 = (bf16[4,2,128,128]{3,2,1,0:T(8,128)(2,1)S(1)}, bf16[4,2,128,128]{3,2,1,0:T(8,128)(2,1)S(1)}, u32[]{:S(2)}, u32[]{:S(2)}) collective-permute-start(bf16[4,2,128,128]{3,2,1,0:T(8,128)(2,1)S(1)} %get-tuple-element.45), channel_id=1, source_target_pairs={{0,3},{1,0},{2,1},{3,2},{4,7},{5,4},{6,5},{7,6},{8,11},{9,8},{10,9... | collective-permute-start | bytes 786440 | tf_op jit(solution)/shard_map/ppermute | solution.py:19
  162.9 2.0 %collective-permute-start.22 = (bf16[4,2,128,128]{3,2,1,0:T(8,128)(2,1)S(1)}, bf16[4,2,128,128]{3,2,1,0:T(8,128)(2,1)S(1)}, u32[]{:S(2)}, u32[]{:S(2)}) collective-permute-start(bf16[4,2,128,128]{3,2,1,0:T(8,128)(2,1)S(1)} %get-tuple-element.45), channel_id=1, source_target_pairs={{0,1},{1,2},{2,3},{3,0},{4,5},{5,6},{6,7},{7,4},{8,9},{9,10},{10,1... | collective-permute-start | bytes 786440 | tf_op jit(solution)/shard_map/ppermute | solution.py:19
  164.8 0.1 compare_and_fusion
  164.9 0.4 collective-permute-done.21
  165.3 4.8 %collective-permute-done.20 = bf16[4,2,128,128]{3,2,1,0:T(8,128)(2,1)S(1)} collective-permute-done((bf16[4,2,128,128]{3,2,1,0:T(8,128)(2,1)S(1)}, bf16[4,2,128,128]{3,2,1,0:T(8,128)(2,1)S(1)}, u32[]{:S(2)}, u32[]{:S(2)}) %collective-permute-start.20) | collective-permute-done | bytes 262176 | tf_op jit(solution)/shard_map/ppermute | solution.py:19
  170.1 2.2 %collective-permute-done.22 = bf16[4,2,128,128]{3,2,1,0:T(8,128)(2,1)S(1)} collective-permute-done((bf16[4,2,128,128]{3,2,1,0:T(8,128)(2,1)S(1)}, bf16[4,2,128,128]{3,2,1,0:T(8,128)(2,1)S(1)}, u32[]{:S(2)}, u32[]{:S(2)}) %collective-permute-start.22) | collective-permute-done | bytes 262176 | tf_op jit(solution)/shard_map/ppermute | solution.py:19
  172.4 0.1 pad_maximum_fusion.1
  172.5 0.7 gather_fusion
  173.3 0.2 convert_bitcast_fusion
  173.6 1.5 fusion.47
  (43 shorter events, 0.9 us)
Async XLA Ops:
  2.2 22.4 %collective-permute-start.1 = (bf16[2,128,128]{2,1,0:T(8,128)(2,1)S(1)}, bf16[2,128,128]{2,1,0:T(8,128)(2,1)S(1)}, u32[]{:S(2)}, u32[]{:S(2)}) collective-permute-start(bf16[2,128,128]{2,1,0:T(8,128)(2,1)S(1)} %get-tuple-element.50), channel_id=1, source_target_pairs={{16,64},{48,96},{80,128},{112,160},{144,192},{176,224},{208,256},{... | collective-permute-start | bytes 196616 | tf_op jit(solution)/shard_map/ppermute | solution.py:29
  17.3 13.4 %collective-permute-start.2 = (bf16[2,128,128]{2,1,0:T(8,128)(2,1)S(1)}, bf16[2,128,128]{2,1,0:T(8,128)(2,1)S(1)}, u32[]{:S(2)}, u32[]{:S(2)}) collective-permute-start(bf16[2,128,128]{2,1,0:T(8,128)(2,1)S(1)} %get-tuple-element.50), channel_id=1, source_target_pairs={{16,96},{48,128},{80,160},{112,192},{144,224},{176,256},{208,288},... | collective-permute-start | bytes 196616 | tf_op jit(solution)/shard_map/ppermute | solution.py:29
  19.3 12.2 %collective-permute-start = (bf16[2,128,128]{2,1,0:T(8,128)(2,1)S(1)}, bf16[2,128,128]{2,1,0:T(8,128)(2,1)S(1)}, u32[]{:S(2)}, u32[]{:S(2)}) collective-permute-start(bf16[2,128,128]{2,1,0:T(8,128)(2,1)S(1)} %get-tuple-element.50), channel_id=1, source_target_pairs={{16,32},{48,64},{80,96},{112,128},{144,160},{176,192},{208,224},{2... | collective-permute-start | bytes 196616 | tf_op jit(solution)/shard_map/ppermute | solution.py:29
  31.5 3.9 %collective-permute-start.3 = (bf16[4,2,128,128]{3,2,1,0:T(8,128)(2,1)S(1)}, bf16[4,2,128,128]{3,2,1,0:T(8,128)(2,1)S(1)}, u32[]{:S(2)}, u32[]{:S(2)}) collective-permute-start(bf16[4,2,128,128]{3,2,1,0:T(8,128)(2,1)S(1)} %pad_maximum_fusion.2), channel_id=1, source_target_pairs={{0,16},{16,0},{32,48},{48,32},{64,80},{80,64},{96,112},{112,96},{1... | collective-permute-start | bytes 786440 | tf_op jit(solution)/shard_map/ppermute | solution.py:39
  35.5 14.6 %collective-permute-start.6 = (bf16[6,2,128,128]{3,2,1,0:T(8,128)(2,1)S(1)}, bf16[6,2,128,128]{3,2,1,0:T(8,128)(2,1)S(1)}, u32[]{:S(2)}, u32[]{:S(2)}) collective-permute-start(bf16[6,2,128,128]{3,2,1,0:T(8,128)(2,1)S(1)} %slice_dynamic-update-slice_fusion), channel_id=1, source_target_pairs={{0,1},{1,2},{2,3},{3,0},{4,5},{5,6},{6,7},{7,4},{8,9},{9,10},{10,1... | collective-permute-start | bytes 1179656 | tf_op jit(solution)/shard_map/ppermute | solution.py:19
  39.0 20.7 %collective-permute-start.5 = (bf16[6,2,128,128]{3,2,1,0:T(8,128)(2,1)S(1)}, bf16[6,2,128,128]{3,2,1,0:T(8,128)(2,1)S(1)}, u32[]{:S(2)}, u32[]{:S(2)}) collective-permute-start(bf16[6,2,128,128]{3,2,1,0:T(8,128)(2,1)S(1)} %slice_dynamic-update-slice_fusion), channel_id=1, source_target_pairs={{0,2},{1,3},{2,0},{3,1},{4,6},{5,7},{6,4},{7,5},{8,10},{9,11},{10,... | collective-permute-start | bytes 1179656 | tf_op jit(solution)/shard_map/ppermute | solution.py:19
  43.9 17.2 %collective-permute-start.4 = (bf16[6,2,128,128]{3,2,1,0:T(8,128)(2,1)S(1)}, bf16[6,2,128,128]{3,2,1,0:T(8,128)(2,1)S(1)}, u32[]{:S(2)}, u32[]{:S(2)}) collective-permute-start(bf16[6,2,128,128]{3,2,1,0:T(8,128)(2,1)S(1)} %slice_dynamic-update-slice_fusion), channel_id=1, source_target_pairs={{0,3},{1,0},{2,1},{3,2},{4,7},{5,4},{6,5},{7,6},{8,11},{9,8},{10,9... | collective-permute-start | bytes 1179656 | tf_op jit(solution)/shard_map/ppermute | solution.py:19
  80.7 18.0 %copy-start = (f32[3584,128]{1,0:T(8,128)S(1)}, f32[3584,128]{1,0:T(8,128)}, u32[]{:S(2)}) copy-start(f32[3584,128]{1,0:T(8,128)} %get-tuple-element.7) | copy-start | bytes 5505028
  80.7 18.0 %copy-start.1 = (f32[3584,128]{1,0:T(8,128)S(1)}, f32[3584,128]{1,0:T(8,128)}, u32[]{:S(2)}) copy-start(f32[3584,128]{1,0:T(8,128)} %get-tuple-element.8) | copy-start | bytes 5505028
  80.8 29.2 %collective-permute-start.8 = (bf16[2,3,128,128]{3,2,0,1:T(8,128)(2,1)S(1)}, bf16[2,3,128,128]{3,2,0,1:T(8,128)(2,1)S(1)}, u32[]{:S(2)}, u32[]{:S(2)}) collective-permute-start(bf16[2,3,128,128]{3,2,0,1:T(8,128)(2,1)S(1)} %pad_maximum_fusion.9), channel_id=1, source_target_pairs={{0,2},{1,3},{2,0},{3,1},{4,6},{5,7},{6,4},{7,5},{8,10},{9,11},{10,... | collective-permute-start | bytes 589832 | tf_op jit(solution)/shard_map/ppermute | solution.py:19
  86.2 23.9 %collective-permute-start.9 = (bf16[2,3,128,128]{3,2,0,1:T(8,128)(2,1)S(1)}, bf16[2,3,128,128]{3,2,0,1:T(8,128)(2,1)S(1)}, u32[]{:S(2)}, u32[]{:S(2)}) collective-permute-start(bf16[2,3,128,128]{3,2,0,1:T(8,128)(2,1)S(1)} %pad_maximum_fusion.10), channel_id=1, source_target_pairs={{0,3},{1,0},{2,1},{3,2},{4,7},{5,4},{6,5},{7,6},{8,11},{9,8},{10,9... | collective-permute-start | bytes 589832 | tf_op jit(solution)/shard_map/ppermute | solution.py:19
  90.2 11.2 %collective-permute-start.11 = (bf16[2,4,128,128]{3,2,0,1:T(8,128)(2,1)S(1)}, bf16[2,4,128,128]{3,2,0,1:T(8,128)(2,1)S(1)}, u32[]{:S(2)}, u32[]{:S(2)}) collective-permute-start(bf16[2,4,128,128]{3,2,0,1:T(8,128)(2,1)S(1)} %pad_maximum_fusion.4), channel_id=1, source_target_pairs={{0,2},{1,3},{2,0},{3,1},{4,6},{5,7},{6,4},{7,5},{8,10},{9,11},{10,... | collective-permute-start | bytes 786440 | tf_op jit(solution)/shard_map/ppermute | solution.py:19
  92.5 14.3 %collective-permute-start.12 = (bf16[2,4,128,128]{3,2,0,1:T(8,128)(2,1)S(1)}, bf16[2,4,128,128]{3,2,0,1:T(8,128)(2,1)S(1)}, u32[]{:S(2)}, u32[]{:S(2)}) collective-permute-start(bf16[2,4,128,128]{3,2,0,1:T(8,128)(2,1)S(1)} %pad_maximum_fusion.5), channel_id=1, source_target_pairs={{0,3},{1,0},{2,1},{3,2},{4,7},{5,4},{6,5},{7,6},{8,11},{9,8},{10,9... | collective-permute-start | bytes 786440 | tf_op jit(solution)/shard_map/ppermute | solution.py:19
  96.7 11.1 %collective-permute-start.10 = (bf16[2,4,128,128]{3,2,0,1:T(8,128)(2,1)S(1)}, bf16[2,4,128,128]{3,2,0,1:T(8,128)(2,1)S(1)}, u32[]{:S(2)}, u32[]{:S(2)}) collective-permute-start(bf16[2,4,128,128]{3,2,0,1:T(8,128)(2,1)S(1)} %pad_maximum_fusion.3), channel_id=1, source_target_pairs={{0,1},{1,2},{2,3},{3,0},{4,5},{5,6},{6,7},{7,4},{8,9},{9,10},{10,1... | collective-permute-start | bytes 786440 | tf_op jit(solution)/shard_map/ppermute | solution.py:19
  101.4 9.7 %collective-permute-start.7 = (bf16[2,3,128,128]{3,2,0,1:T(8,128)(2,1)S(1)}, bf16[2,3,128,128]{3,2,0,1:T(8,128)(2,1)S(1)}, u32[]{:S(2)}, u32[]{:S(2)}) collective-permute-start(bf16[2,3,128,128]{3,2,0,1:T(8,128)(2,1)S(1)} %pad_maximum_fusion.8), channel_id=1, source_target_pairs={{0,1},{1,2},{2,3},{3,0},{4,5},{5,6},{6,7},{7,4},{8,9},{9,10},{10,1... | collective-permute-start | bytes 589832 | tf_op jit(solution)/shard_map/ppermute | solution.py:19
  108.1 3.4 %collective-permute-start.13 = (bf16[4,2,128,128]{3,2,1,0:T(8,128)(2,1)S(1)}, bf16[4,2,128,128]{3,2,1,0:T(8,128)(2,1)S(1)}, u32[]{:S(2)}, u32[]{:S(2)}) collective-permute-start(bf16[4,2,128,128]{3,2,1,0:T(8,128)(2,1)S(1)} %pad_maximum_fusion.6), channel_id=1, source_target_pairs={{0,16},{16,0},{32,48},{48,32},{64,80},{80,64},{96,112},{112,96},{1... | collective-permute-start | bytes 786440 | tf_op jit(solution)/shard_map/ppermute | solution.py:39
  111.6 18.1 %collective-permute-start.14 = (bf16[2,128,128]{2,1,0:T(8,128)(2,1)S(1)}, bf16[2,128,128]{2,1,0:T(8,128)(2,1)S(1)}, u32[]{:S(2)}, u32[]{:S(2)}) collective-permute-start(bf16[2,128,128]{2,1,0:T(8,128)(2,1)S(1)} %get-tuple-element.41), channel_id=1, source_target_pairs={{32,16},{64,48},{96,80},{128,112},{160,144},{192,176},{224,208},{2... | collective-permute-start | bytes 196616 | tf_op jit(solution)/shard_map/ppermute | solution.py:34
  117.9 11.8 %collective-permute-start.16 = (bf16[2,128,128]{2,1,0:T(8,128)(2,1)S(1)}, bf16[2,128,128]{2,1,0:T(8,128)(2,1)S(1)}, u32[]{:S(2)}, u32[]{:S(2)}) collective-permute-start(bf16[2,128,128]{2,1,0:T(8,128)(2,1)S(1)} %get-tuple-element.42), channel_id=1, source_target_pairs={{96,16},{128,48},{160,80},{192,112},{224,144},{256,176},{288,208},... | collective-permute-start | bytes 196616 | tf_op jit(solution)/shard_map/ppermute | solution.py:34
  122.3 19.0 %collective-permute-start.15 = (bf16[2,128,128]{2,1,0:T(8,128)(2,1)S(1)}, bf16[2,128,128]{2,1,0:T(8,128)(2,1)S(1)}, u32[]{:S(2)}, u32[]{:S(2)}) collective-permute-start(bf16[2,128,128]{2,1,0:T(8,128)(2,1)S(1)} %get-tuple-element.43), channel_id=1, source_target_pairs={{64,16},{96,48},{128,80},{160,112},{192,144},{224,176},{256,208},{... | collective-permute-start | bytes 196616 | tf_op jit(solution)/shard_map/ppermute | solution.py:34
  141.3 11.7 %collective-permute-start.19 = (bf16[2,128,128]{2,1,0:T(8,128)(2,1)S(1)}, bf16[2,128,128]{2,1,0:T(8,128)(2,1)S(1)}, u32[]{:S(2)}, u32[]{:S(2)}) collective-permute-start(bf16[2,128,128]{2,1,0:T(8,128)(2,1)S(1)} %fusion.20), channel_id=1, source_target_pairs={{0,4},{4,8},{8,12},{12,0},{1,5},{5,9},{9,13},{13,1},{2,6},{6,10},{... | collective-permute-start | bytes 196616 | tf_op jit(solution)/shard_map/ppermute | solution.py:19
  143.2 9.8 %collective-permute-start.18 = (bf16[2,128,128]{2,1,0:T(8,128)(2,1)S(1)}, bf16[2,128,128]{2,1,0:T(8,128)(2,1)S(1)}, u32[]{:S(2)}, u32[]{:S(2)}) collective-permute-start(bf16[2,128,128]{2,1,0:T(8,128)(2,1)S(1)} %fusion.20), channel_id=1, source_target_pairs={{0,8},{4,12},{8,0},{12,4},{1,9},{5,13},{9,1},{13,5},{2,10},{6,14},... | collective-permute-start | bytes 196616 | tf_op jit(solution)/shard_map/ppermute | solution.py:19
  148.2 6.7 %collective-permute-start.17 = (bf16[2,128,128]{2,1,0:T(8,128)(2,1)S(1)}, bf16[2,128,128]{2,1,0:T(8,128)(2,1)S(1)}, u32[]{:S(2)}, u32[]{:S(2)}) collective-permute-start(bf16[2,128,128]{2,1,0:T(8,128)(2,1)S(1)} %fusion.20), channel_id=1, source_target_pairs={{0,12},{4,0},{8,4},{12,8},{1,13},{5,1},{9,5},{13,9},{2,14},{6,2},{... | collective-permute-start | bytes 196616 | tf_op jit(solution)/shard_map/ppermute | solution.py:19
  155.0 10.4 %collective-permute-start.21 = (bf16[4,2,128,128]{3,2,1,0:T(8,128)(2,1)S(1)}, bf16[4,2,128,128]{3,2,1,0:T(8,128)(2,1)S(1)}, u32[]{:S(2)}, u32[]{:S(2)}) collective-permute-start(bf16[4,2,128,128]{3,2,1,0:T(8,128)(2,1)S(1)} %get-tuple-element.45), channel_id=1, source_target_pairs={{0,2},{1,3},{2,0},{3,1},{4,6},{5,7},{6,4},{7,5},{8,10},{9,11},{10,... | collective-permute-start | bytes 786440 | tf_op jit(solution)/shard_map/ppermute | solution.py:19
  159.0 11.2 %collective-permute-start.20 = (bf16[4,2,128,128]{3,2,1,0:T(8,128)(2,1)S(1)}, bf16[4,2,128,128]{3,2,1,0:T(8,128)(2,1)S(1)}, u32[]{:S(2)}, u32[]{:S(2)}) collective-permute-start(bf16[4,2,128,128]{3,2,1,0:T(8,128)(2,1)S(1)} %get-tuple-element.45), channel_id=1, source_target_pairs={{0,3},{1,0},{2,1},{3,2},{4,7},{5,4},{6,5},{7,6},{8,11},{9,8},{10,9... | collective-permute-start | bytes 786440 | tf_op jit(solution)/shard_map/ppermute | solution.py:19
  162.9 9.5 %collective-permute-start.22 = (bf16[4,2,128,128]{3,2,1,0:T(8,128)(2,1)S(1)}, bf16[4,2,128,128]{3,2,1,0:T(8,128)(2,1)S(1)}, u32[]{:S(2)}, u32[]{:S(2)}) collective-permute-start(bf16[4,2,128,128]{3,2,1,0:T(8,128)(2,1)S(1)} %get-tuple-element.45), channel_id=1, source_target_pairs={{0,1},{1,2},{2,3},{3,0},{4,5},{5,6},{6,7},{7,4},{8,9},{9,10},{10,1... | collective-permute-start | bytes 786440 | tf_op jit(solution)/shard_map/ppermute | solution.py:19

commit v8 on v6

--- a/solution.py
+++ b/solution.py
@@ -14,15 +14,29 @@
 REACH = 6
 
 
-def shifted_2(value, axis, steps):
-    count = lax.axis_size(axis)
-    leading, last = (max(0, -steps), min(count, count - steps))
-    return lax.ppermute(value, axis, [(source, source + steps) for source in range(leading, last)])
-
-
 def cycled(value, axis, steps):
     count = lax.axis_size(axis)
     return lax.ppermute(value, axis, [(source, (source + steps) % count) for source in range(count)])
+
+
+def chip_pairs(count, step):
+    nearer = [(target - (2 * step - 1), target) for target in range(0, count, 2)]
+    farther = [(target - (2 * step + 1), target) for target in range(1, count, 2)]
+    return [(source, target) for source, target in nearer + farther if source >= 0]
+
+
+def chip_fetch(value, axis, step):
+    return lax.ppermute(value, axis, chip_pairs(lax.axis_size(axis), step))
+
+
+def chip_return(value, axis, step):
+    pairs = chip_pairs(lax.axis_size(axis), step)
+    return lax.ppermute(value, axis, [(target, source) for source, target in pairs])
+
+
+def swap_cores(value, axis):
+    count = lax.axis_size(axis)
+    return lax.ppermute(value, axis, [(source, source ^ 1) for source in range(count)])
 
 
 def block_kernel(slots_ref, q_ref, do_ref, code_ref, k_ref, v_ref, dq_ref, dk_ref, dv_ref,
@@ -147,37 +161,48 @@
     )
     rolled = jnp.roll(own_tiles, -part_index * quarter, axis=1)
     own_part = rolled[:, :quarter]
-    fetched = jnp.stack([shifted_2(own_part, "ctx", offset) for offset in range(1, reach_span)])
-    pieces = [fetched] + [cycled(fetched, "sub", -step) for step in range(1, parts_count)]
-    tile_store = jnp.concatenate([rolled[None], jnp.concatenate(pieces, axis=2)], axis=0)
-    key_tiles = tile_store[:, 0].reshape(reach_span * blocks_here, BLOCK, width)
-    value_tiles = tile_store[:, 1].reshape(reach_span * blocks_here, BLOCK, width)
+    even = ctx_index % 2 == 0
+    took = jnp.stack([chip_fetch(own_part, "ctx", step) for step in range(1, 4)])
+    pieces = [took] + [cycled(took, "sub", -step) for step in range(1, parts_count)]
+    took = jnp.concatenate(pieces, axis=2)
+    mine = jnp.concatenate([rolled[None], took], axis=0)
+    tile_store = jnp.concatenate([mine, swap_cores(mine, "ctx")], axis=0)
+    store_span = tile_store.shape[0]
+    key_tiles = tile_store[:, 0].reshape(store_span * blocks_here, BLOCK, width)
+    value_tiles = tile_store[:, 1].reshape(store_span * blocks_here, BLOCK, width)
     chosen = lax.dynamic_index_in_dim(selected, group_index, 1, keepdims=False)
     live_mask = lax.dynamic_index_in_dim(live_slots, group_index, 1, keepdims=False)
     block_ids = ctx_index * blocks_here + jnp.arange(blocks_here, dtype=jnp.int32)
     local_block = chosen % blocks_here
     per_part = blocks_here // parts_count
     rolled_block = (local_block // per_part - part_index) % parts_count * per_part + local_block % per_part
-    slot_index = (ctx_index - chosen // blocks_here) * blocks_here + rolled_block
-    slot_index = jnp.clip(slot_index, 0, reach_span * blocks_here - 1)
+    offset = jnp.clip(ctx_index - chosen // blocks_here, 0, REACH)
+    placed = jnp.where(
+        even, jnp.array([0, 1, 5, 2, 6, 3, 7], jnp.int32)[offset], jnp.array([0, 4, 5, 1, 6, 2, 7], jnp.int32)[offset]
+    )
+    slot_index = placed * blocks_here + rolled_block
     code = jnp.where(live_mask == 1, jnp.where(chosen < block_ids[:, None], 2, 1), 0)
     query_grad, key_grad, value_grad = local_grads(
         queries, out_grad, key_tiles, value_tiles, slot_index, code, inv_root
     )
-    grads = jnp.stack([key_grad, value_grad]).reshape(2, reach_span, tokens_here, width)
-    sent = grads.astype(jnp.bfloat16)
-    split = REACH // 2 + 1
-    running = None
-    for lo, hi in ((split, reach_span), (0, split)):
-        part = grads[:, lo:hi, :quarter]
+    grads = jnp.stack([key_grad, value_grad]).reshape(2, store_span, tokens_here, width)
+    half = store_span // 2
+    back = swap_cores(grads[:, half:].astype(jnp.bfloat16), "ctx").astype(jnp.float32)
+    totals = grads[:, :half] + back
+    sent = totals.astype(jnp.bfloat16)
+
+    def reduce_parts(lo, hi):
+        part = totals[:, lo:hi, :quarter]
         for step in range(1, parts_count):
             piece = sent[:, lo:hi, step * quarter:(step + 1) * quarter]
             part = part + cycled(piece, "sub", step).astype(jnp.float32)
-        for offset in range(lo, hi):
-            term = part[:, offset - lo]
-            if offset:
-                term = shifted_2(term.astype(jnp.bfloat16), "ctx", -offset).astype(jnp.float32)
-            running = term if running is None else running + term
+        return part
+
+    fetched_parts = reduce_parts(1, half)
+    running = reduce_parts(0, 1)[:, 0]
+    for step in range(1, half):
+        term = fetched_parts[:, step - 1].astype(jnp.bfloat16)
+        running = running + chip_return(term, "ctx", step).astype(jnp.float32)
     mine = running.astype(jnp.bfloat16)
     by_group = jnp.stack([mine] + [cycled(mine, "grp", -step) for step in range(1, groups)])
     by_part = jnp.stack([by_group] + [cycled(by_group, "sub", -step) for step in range(1, parts_count)])

time: 198 us -> 168 us (0.85)
  waiting for transfers between devices: 60.7 us -> 32.8 us
  starting transfers between devices: 108 us -> 99.5 us
  local copies, waits for them, and re-layouts: 6.01 us -> 9.31 us
    ppermute x15, waiting for transfers between devices: 30.3 us -> 10.2 us  [cycled(): lax.ppermute(value, axis, [(source, (source + steps) % count) for source...]
    ppermute x12 -> x8, starting transfers between devices: 56.5 us -> 40.7 us  [the longest x3 21 us: chip_fetch(): return lax.ppermute(value, axis, chip_pairs(lax.axis_size(axis), step))]
    ppermute x12 -> x8, waiting for transfers between devices: 30.4 us -> 22.6 us  [the longest x3 10.3 us: chip_return(): lax.ppermute(value, axis, [(target, source) for source, target in pairs])]
    ppermute x15, starting transfers between devices: 51.5 us -> 58.8 us  [cycled(): lax.ppermute(value, axis, [(source, (source + steps) % count) for source...]
    gather x0 -> x2, local copies, waits for them, and re-layouts: none -> 2.45 us  [the longest x1 1.23 us: per_device(): jnp.array([0, 1, 5, 2, 6, 3, 7], jnp.int32)[offset]]
  transfers between devices with their start and end apart: 27 -> 23, of which waited for: 12 -> 12; matrix products, arithmetic and copies ran while one was open for 2% -> 4% of each run, Pallas kernels for 0% -> 0%
where the time goes in v8:
time: 168 us; the launch traced here: 165 us
  starting transfers between devices  99.5 us (59%)
  waiting for transfers between devices  32.8 us (20%)
  Pallas kernels  16.1 us (10%)
  local copies, waits for them, and re-layouts  9.31 us (6%)
  other arithmetic  6.53 us (4%)
    ppermute x15, starting transfers between devices, cycled(): lax.ppermute(value, axis, [(source, (source + steps) % count) for source...  58.8 us
    ppermute x3, starting transfers between devices, chip_fetch(): return lax.ppermute(value, axis, chip_pairs(lax.axis_size(axis), step))  21 us
    pallas_call x1, Pallas kernels, local_grads(): pl.pallas_call(kernel, grid_spec=pltpu.PrefetchScalarGridSpec(num_scalar_...  16.1 us
    ppermute x3, starting transfers between devices, chip_return(): lax.ppermute(value, axis, [(target, source) for source, target in pairs])  15.6 us
    ppermute x3, waiting for transfers between devices, chip_return(): lax.ppermute(value, axis, [(target, source) for source, target in pairs])  10.3 us
    ppermute x15, waiting for transfers between devices, cycled(): lax.ppermute(value, axis, [(source, (source + steps) % count) for source...  10.2 us
    ppermute x3, waiting for transfers between devices, chip_fetch(): return lax.ppermute(value, axis, chip_pairs(lax.axis_size(axis), step))  9.16 us
    ppermute x2, starting transfers between devices, swap_cores(): lax.ppermute(value, axis, [(source, source ^ 1) for source in range(count)])  4.1 us
  transfers between devices with their start and end apart: 23, of which 12 were waited for; matrix products, arithmetic and copies ran while one was open for 4% of the time, Pallas kernels for 0%

profile of v8, /device:TPU:6, one launch (start us, length us, event | category | flops | bytes accessed | tf_op | source)
XLA Modules:
  0.0 165.5 jit_solution(12755081923338392409)
XLA Ops:
  0.7 1.0 constant_dynamic-slice_fusion
  1.7 0.5 fusion.7
  2.2 12.2 %collective-permute-start.2 = (bf16[2,128,128]{2,1,0:T(8,128)(2,1)S(1)}, bf16[2,128,128]{2,1,0:T(8,128)(2,1)S(1)}, u32[]{:S(2)}, u32[]{:S(2)}) collective-permute-start(bf16[2,128,128]{2,1,0:T(8,128)(2,1)S(1)} %slice.84), channel_id=1, source_target_pairs={{16,96},{48,128},{80,160},{112,192},{144,224},{176,256},{208,288},... | collective-permute-start | bytes 196616 | tf_op jit(solution)/shard_map/ppermute | solution.py:29
  14.3 4.3 %collective-permute-start.1 = (bf16[2,128,128]{2,1,0:T(8,128)(2,1)S(1)}, bf16[2,128,128]{2,1,0:T(8,128)(2,1)S(1)}, u32[]{:S(2)}, u32[]{:S(2)}) collective-permute-start(bf16[2,128,128]{2,1,0:T(8,128)(2,1)S(1)} %slice.84), channel_id=1, source_target_pairs={{16,64},{48,96},{80,128},{112,160},{144,192},{176,224},{208,256},{... | collective-permute-start | bytes 196616 | tf_op jit(solution)/shard_map/ppermute | solution.py:29
  18.6 4.6 %collective-permute-start = (bf16[2,128,128]{2,1,0:T(8,128)(2,1)S(1)}, bf16[2,128,128]{2,1,0:T(8,128)(2,1)S(1)}, u32[]{:S(2)}, u32[]{:S(2)}) collective-permute-start(bf16[2,128,128]{2,1,0:T(8,128)(2,1)S(1)} %slice.84), channel_id=1, source_target_pairs={{16,32},{48,64},{80,96},{112,128},{144,160},{176,192},{208,224},{2... | collective-permute-start | bytes 196616 | tf_op jit(solution)/shard_map/ppermute | solution.py:29
  23.2 0.8 constant_dynamic-slice_fusion.2
  24.0 0.1 reshape.262
  24.1 2.6 %collective-permute-done.2 = bf16[2,128,128]{2,1,0:T(8,128)(2,1)S(1)} collective-permute-done((bf16[2,128,128]{2,1,0:T(8,128)(2,1)S(1)}, bf16[2,128,128]{2,1,0:T(8,128)(2,1)S(1)}, u32[]{:S(2)}, u32[]{:S(2)}) %collective-permute-start.2) | collective-permute-done | bytes 65568 | tf_op jit(solution)/shard_map/ppermute | solution.py:29
  26.7 3.3 %collective-permute-done.1 = bf16[2,128,128]{2,1,0:T(8,128)(2,1)S(1)} collective-permute-done((bf16[2,128,128]{2,1,0:T(8,128)(2,1)S(1)}, bf16[2,128,128]{2,1,0:T(8,128)(2,1)S(1)}, u32[]{:S(2)}, u32[]{:S(2)}) %collective-permute-start.1) | collective-permute-done | bytes 65568 | tf_op jit(solution)/shard_map/ppermute | solution.py:29
  29.9 3.3 %collective-permute-done = bf16[2,128,128]{2,1,0:T(8,128)(2,1)S(1)} collective-permute-done((bf16[2,128,128]{2,1,0:T(8,128)(2,1)S(1)}, bf16[2,128,128]{2,1,0:T(8,128)(2,1)S(1)}, u32[]{:S(2)}, u32[]{:S(2)}) %collective-permute-start) | collective-permute-done | bytes 65568 | tf_op jit(solution)/shard_map/ppermute | solution.py:29
  33.3 3.5 %collective-permute-start.5 = (bf16[3,2,128,128]{3,2,1,0:T(8,128)(2,1)S(1)}, bf16[3,2,128,128]{3,2,1,0:T(8,128)(2,1)S(1)}, u32[]{:S(2)}, u32[]{:S(2)}) collective-permute-start(bf16[3,2,128,128]{3,2,1,0:T(8,128)(2,1)S(1)} %pad_maximum_fusion.4), channel_id=1, source_target_pairs={{0,1},{1,2},{2,3},{3,0},{4,5},{5,6},{6,7},{7,4},{8,9},{9,10},{10,1... | collective-permute-start | bytes 589832 | tf_op jit(solution)/shard_map/ppermute | solution.py:19
  36.8 4.8 %collective-permute-start.4 = (bf16[3,2,128,128]{3,2,1,0:T(8,128)(2,1)S(1)}, bf16[3,2,128,128]{3,2,1,0:T(8,128)(2,1)S(1)}, u32[]{:S(2)}, u32[]{:S(2)}) collective-permute-start(bf16[3,2,128,128]{3,2,1,0:T(8,128)(2,1)S(1)} %pad_maximum_fusion.4), channel_id=1, source_target_pairs={{0,2},{1,3},{2,0},{3,1},{4,6},{5,7},{6,4},{7,5},{8,10},{9,11},{10,... | collective-permute-start | bytes 589832 | tf_op jit(solution)/shard_map/ppermute | solution.py:19
  41.6 3.3 %collective-permute-start.3 = (bf16[3,2,128,128]{3,2,1,0:T(8,128)(2,1)S(1)}, bf16[3,2,128,128]{3,2,1,0:T(8,128)(2,1)S(1)}, u32[]{:S(2)}, u32[]{:S(2)}) collective-permute-start(bf16[3,2,128,128]{3,2,1,0:T(8,128)(2,1)S(1)} %pad_maximum_fusion.4), channel_id=1, source_target_pairs={{0,3},{1,0},{2,1},{3,2},{4,7},{5,4},{6,5},{7,6},{8,11},{9,8},{10,9... | collective-permute-start | bytes 589832 | tf_op jit(solution)/shard_map/ppermute | solution.py:19
  44.9 1.2 gather_fusion
  46.1 1.2 gather_fusion.1
  47.4 0.5 fusion.39
  47.9 0.9 collective-permute-done.4
  48.7 1.3 collective-permute-done.3
  50.1 1.9 %collective-permute-start.6 = (bf16[4,2,512,128]{3,2,1,0:T(8,128)(2,1)S(1)}, bf16[4,2,512,128]{3,2,1,0:T(8,128)(2,1)S(1)}, u32[]{:S(2)}, u32[]{:S(2)}) collective-permute-start(bf16[4,2,512,128]{3,2,1,0:T(8,128)(2,1)S(1)} %maximum_maximum_fusion), channel_id=1, source_target_pairs={{0,16},{16,0},{32,48},{48,32},{64,80},{80,64},{96,112},{112,96},{1... | collective-permute-start | bytes 3145736 | tf_op jit(solution)/shard_map/ppermute | solution.py:39
  52.1 0.1 reshape.289
  52.2 0.1 fusion.25
  52.3 0.1 broadcast_in_dim.47
  52.3 0.1 eq.59
  52.4 0.1 broadcast_in_dim.49
  52.5 0.1 eq.60
  52.7 0.6 fusion.24.slots_ref
  53.3 0.7 select_select_fusion.code_ref
  54.0 0.7 collective-permute-done.6
  54.7 0.2 pad_maximum_fusion.1
  54.9 1.5 fusion.36
  56.3 16.1 %shard_map.103 = (bf16[2048,128]{1,0:T(8,128)(2,1)}, f32[4096,128]{1,0:T(8,128)}, f32[4096,128]{1,0:T(8,128)}) custom-call(s32[8,16]{1,0:T(8,128)} %fusion.24.slots_ref, bf16[2048,128]{1,0:T(8,128)(2,1)} %bitcast.85, bf16[2048,128]{1,0:T(8,128)(2,1)} %bitcast.86, s32[8,1,1024]{2,1,0:T(1,128)} %select_select_fusion.code_ref, bf16[4096,128]{1,0:T(8,128)(2,1)} %bitcast.73, ...), custom_call_target="tpu_custom_call" | custom-call | tf_op jit(solution)/shard_map/pallas_call | solution.py:105
  72.5 1.8 %fusion.2 = bf16[2,4,512,128]{3,2,1,0:T(8,128)(2,1)S(1)} fusion(f32[1,8,512,128]{3,2,1,0:T(8,128)} %bitcast.65, f32[1,8,512,128]{3,2,1,0:T(8,128)} %bitcast.60), kind=kLoop, calls=%fused_computation.8 | loop fusion | flops 524288 | bytes 5242880 | tf_op jit(solution)/shard_map/convert.4
  74.3 2.2 %collective-permute-start.7 = (bf16[2,4,512,128]{3,2,1,0:T(8,128)(2,1)S(1)}, bf16[2,4,512,128]{3,2,1,0:T(8,128)(2,1)S(1)}, u32[]{:S(2)}, u32[]{:S(2)}) collective-permute-start(bf16[2,4,512,128]{3,2,1,0:T(8,128)(2,1)S(1)} %fusion.2), channel_id=1, source_target_pairs={{0,16},{16,0},{32,48},{48,32},{64,80},{80,64},{96,112},{112,96},{1... | collective-permute-start | bytes 3145736 | tf_op jit(solution)/shard_map/ppermute | solution.py:39
  76.6 2.5 %collective-permute-done.7 = bf16[2,4,512,128]{3,2,1,0:T(8,128)(2,1)S(1)} collective-permute-done((bf16[2,4,512,128]{3,2,1,0:T(8,128)(2,1)S(1)}, bf16[2,4,512,128]{3,2,1,0:T(8,128)(2,1)S(1)}, u32[]{:S(2)}, u32[]{:S(2)}) %collective-permute-start.7) | collective-permute-done | bytes 1048608 | tf_op jit(solution)/shard_map/ppermute | solution.py:39
  79.0 0.2 fusion.38
  79.2 4.4 %collective-permute-start.11 = (bf16[2,3,128,128]{3,2,0,1:T(8,128)(2,1)S(1)}, bf16[2,3,128,128]{3,2,0,1:T(8,128)(2,1)S(1)}, u32[]{:S(2)}, u32[]{:S(2)}) collective-permute-start(bf16[2,3,128,128]{3,2,0,1:T(8,128)(2,1)S(1)} %get-tuple-element.19), channel_id=1, source_target_pairs={{0,1},{1,2},{2,3},{3,0},{4,5},{5,6},{6,7},{7,4},{8,9},{9,10},{10,1... | collective-permute-start | bytes 589832 | tf_op jit(solution)/shard_map/ppermute | solution.py:19
  83.6 3.5 %collective-permute-start.12 = (bf16[2,3,128,128]{3,2,0,1:T(8,128)(2,1)S(1)}, bf16[2,3,128,128]{3,2,0,1:T(8,128)(2,1)S(1)}, u32[]{:S(2)}, u32[]{:S(2)}) collective-permute-start(bf16[2,3,128,128]{3,2,0,1:T(8,128)(2,1)S(1)} %get-tuple-element.21), channel_id=1, source_target_pairs={{0,2},{1,3},{2,0},{3,1},{4,6},{5,7},{6,4},{7,5},{8,10},{9,11},{10,... | collective-permute-start | bytes 589832 | tf_op jit(solution)/shard_map/ppermute | solution.py:19
  87.2 3.6 %collective-permute-start.13 = (bf16[2,3,128,128]{3,2,0,1:T(8,128)(2,1)S(1)}, bf16[2,3,128,128]{3,2,0,1:T(8,128)(2,1)S(1)}, u32[]{:S(2)}, u32[]{:S(2)}) collective-permute-start(bf16[2,3,128,128]{3,2,0,1:T(8,128)(2,1)S(1)} %get-tuple-element.20), channel_id=1, source_target_pairs={{0,3},{1,0},{2,1},{3,2},{4,7},{5,4},{6,5},{7,6},{8,11},{9,8},{10,9... | collective-permute-start | bytes 589832 | tf_op jit(solution)/shard_map/ppermute | solution.py:19
  90.8 2.7 %collective-permute-start.10 = (bf16[2,1,128,128]{3,2,0,1:T(8,128)(2,1)S(1)}, bf16[2,1,128,128]{3,2,0,1:T(8,128)(2,1)S(1)}, u32[]{:S(2)}, u32[]{:S(2)}) collective-permute-start(bf16[2,1,128,128]{3,2,0,1:T(8,128)(2,1)S(1)} %get-tuple-element.17), channel_id=1, source_target_pairs={{0,3},{1,0},{2,1},{3,2},{4,7},{5,4},{6,5},{7,6},{8,11},{9,8},{10,9... | collective-permute-start | bytes 196616 | tf_op jit(solution)/shard_map/ppermute | solution.py:19
  93.5 3.5 %collective-permute-start.9 = (bf16[2,1,128,128]{3,2,0,1:T(8,128)(2,1)S(1)}, bf16[2,1,128,128]{3,2,0,1:T(8,128)(2,1)S(1)}, u32[]{:S(2)}, u32[]{:S(2)}) collective-permute-start(bf16[2,1,128,128]{3,2,0,1:T(8,128)(2,1)S(1)} %get-tuple-element.18), channel_id=1, source_target_pairs={{0,2},{1,3},{2,0},{3,1},{4,6},{5,7},{6,4},{7,5},{8,10},{9,11},{10,... | collective-permute-start | bytes 196616 | tf_op jit(solution)/shard_map/ppermute | solution.py:19
  97.1 0.2 fusion.1
  97.3 1.9 %collective-permute-start.8 = (bf16[2,1,128,128]{3,2,0,1:T(8,128)(2,1)S(1)}, bf16[2,1,128,128]{3,2,0,1:T(8,128)(2,1)S(1)}, u32[]{:S(2)}, u32[]{:S(2)}) collective-permute-start(bf16[2,1,128,128]{3,2,0,1:T(8,128)(2,1)S(1)} %get-tuple-element.16), channel_id=1, source_target_pairs={{0,1},{1,2},{2,3},{3,0},{4,5},{5,6},{6,7},{7,4},{8,9},{9,10},{10,1... | collective-permute-start | bytes 196616 | tf_op jit(solution)/shard_map/ppermute | solution.py:19
  99.3 0.1 fusion.5
  99.4 0.7 slice_bitcast_fusion.2
  100.0 5.0 %collective-permute-start.16 = (bf16[2,128,128]{2,1,0:T(8,128)(2,1)}, bf16[2,128,128]{2,1,0:T(8,128)(2,1)S(1)}, u32[]{:S(2)}, u32[]{:S(2)}) collective-permute-start(bf16[2,128,128]{2,1,0:T(8,128)(2,1)} %get-tuple-element.25), channel_id=1, source_target_pairs={{96,16},{128,48},{160,80},{192,112},{224,144},{256,176},{288,208},... | collective-permute-start | bytes 196616 | tf_op jit(solution)/shard_map/ppermute | solution.py:34
  105.1 6.4 %collective-permute-start.15 = (bf16[2,128,128]{2,1,0:T(8,128)(2,1)}, bf16[2,128,128]{2,1,0:T(8,128)(2,1)}, u32[]{:S(2)}, u32[]{:S(2)}) collective-permute-start(bf16[2,128,128]{2,1,0:T(8,128)(2,1)} %get-tuple-element.26), channel_id=1, source_target_pairs={{64,16},{96,48},{128,80},{160,112},{192,144},{224,176},{256,208},{... | collective-permute-start | bytes 196616 | tf_op jit(solution)/shard_map/ppermute | solution.py:34
  111.5 4.2 %collective-permute-start.14 = (bf16[2,128,128]{2,1,0:T(8,128)(2,1)}, bf16[2,128,128]{2,1,0:T(8,128)(2,1)}, u32[]{:S(2)}, u32[]{:S(2)}) collective-permute-start(bf16[2,128,128]{2,1,0:T(8,128)(2,1)} %get-tuple-element.24), channel_id=1, source_target_pairs={{32,16},{64,48},{96,80},{128,112},{160,144},{192,176},{224,208},{2... | collective-permute-start | bytes 196616 | tf_op jit(solution)/shard_map/ppermute | solution.py:34
  115.8 0.1 add.191
  115.9 4.7 %collective-permute-done.15 = bf16[2,128,128]{2,1,0:T(8,128)(2,1)} collective-permute-done((bf16[2,128,128]{2,1,0:T(8,128)(2,1)}, bf16[2,128,128]{2,1,0:T(8,128)(2,1)}, u32[]{:S(2)}, u32[]{:S(2)}) %collective-permute-start.15) | collective-permute-done | bytes 65568 | tf_op jit(solution)/shard_map/ppermute | solution.py:34
  120.5 5.6 %collective-permute-done.14 = bf16[2,128,128]{2,1,0:T(8,128)(2,1)} collective-permute-done((bf16[2,128,128]{2,1,0:T(8,128)(2,1)}, bf16[2,128,128]{2,1,0:T(8,128)(2,1)}, u32[]{:S(2)}, u32[]{:S(2)}) %collective-permute-start.14) | collective-permute-done | bytes 65568 | tf_op jit(solution)/shard_map/ppermute | solution.py:34
  126.1 1.0 fusion.15
  127.1 2.5 %collective-permute-start.19 = (bf16[2,128,128]{2,1,0:T(8,128)(2,1)S(1)}, bf16[2,128,128]{2,1,0:T(8,128)(2,1)S(1)}, u32[]{:S(2)}, u32[]{:S(2)}) collective-permute-start(bf16[2,128,128]{2,1,0:T(8,128)(2,1)S(1)} %fusion.15), channel_id=1, source_target_pairs={{0,4},{4,8},{8,12},{12,0},{1,5},{5,9},{9,13},{13,1},{2,6},{6,10},{... | collective-permute-start | bytes 196616 | tf_op jit(solution)/shard_map/ppermute | solution.py:19
  129.6 8.2 %collective-permute-start.18 = (bf16[2,128,128]{2,1,0:T(8,128)(2,1)S(1)}, bf16[2,128,128]{2,1,0:T(8,128)(2,1)S(1)}, u32[]{:S(2)}, u32[]{:S(2)}) collective-permute-start(bf16[2,128,128]{2,1,0:T(8,128)(2,1)S(1)} %fusion.15), channel_id=1, source_target_pairs={{0,8},{4,12},{8,0},{12,4},{1,9},{5,13},{9,1},{13,5},{2,10},{6,14},... | collective-permute-start | bytes 196616 | tf_op jit(solution)/shard_map/ppermute | solution.py:19
  137.8 4.8 %collective-permute-start.17 = (bf16[2,128,128]{2,1,0:T(8,128)(2,1)S(1)}, bf16[2,128,128]{2,1,0:T(8,128)(2,1)S(1)}, u32[]{:S(2)}, u32[]{:S(2)}) collective-permute-start(bf16[2,128,128]{2,1,0:T(8,128)(2,1)S(1)} %fusion.15), channel_id=1, source_target_pairs={{0,12},{4,0},{8,4},{12,8},{1,13},{5,1},{9,5},{13,9},{2,14},{6,2},{... | collective-permute-start | bytes 196616 | tf_op jit(solution)/shard_map/ppermute | solution.py:19
  142.6 1.9 %collective-permute-done.17 = bf16[2,128,128]{2,1,0:T(8,128)(2,1)S(1)} collective-permute-done((bf16[2,128,128]{2,1,0:T(8,128)(2,1)S(1)}, bf16[2,128,128]{2,1,0:T(8,128)(2,1)S(1)}, u32[]{:S(2)}, u32[]{:S(2)}) %collective-permute-start.17) | collective-permute-done | bytes 65568 | tf_op jit(solution)/shard_map/ppermute | solution.py:19
  144.5 3.8 %collective-permute-start.22 = (bf16[4,2,128,128]{3,2,1,0:T(8,128)(2,1)S(1)}, bf16[4,2,128,128]{3,2,1,0:T(8,128)(2,1)S(1)}, u32[]{:S(2)}, u32[]{:S(2)}) collective-permute-start(bf16[4,2,128,128]{3,2,1,0:T(8,128)(2,1)S(1)} %get-tuple-element.23), channel_id=1, source_target_pairs={{0,1},{1,2},{2,3},{3,0},{4,5},{5,6},{6,7},{7,4},{8,9},{9,10},{10,1... | collective-permute-start | bytes 786440 | tf_op jit(solution)/shard_map/ppermute | solution.py:19
  148.3 4.7 %collective-permute-start.21 = (bf16[4,2,128,128]{3,2,1,0:T(8,128)(2,1)S(1)}, bf16[4,2,128,128]{3,2,1,0:T(8,128)(2,1)S(1)}, u32[]{:S(2)}, u32[]{:S(2)}) collective-permute-start(bf16[4,2,128,128]{3,2,1,0:T(8,128)(2,1)S(1)} %get-tuple-element.23), channel_id=1, source_target_pairs={{0,2},{1,3},{2,0},{3,1},{4,6},{5,7},{6,4},{7,5},{8,10},{9,11},{10,... | collective-permute-start | bytes 786440 | tf_op jit(solution)/shard_map/ppermute | solution.py:19
  153.0 3.6 %collective-permute-start.20 = (bf16[4,2,128,128]{3,2,1,0:T(8,128)(2,1)S(1)}, bf16[4,2,128,128]{3,2,1,0:T(8,128)(2,1)S(1)}, u32[]{:S(2)}, u32[]{:S(2)}) collective-permute-start(bf16[4,2,128,128]{3,2,1,0:T(8,128)(2,1)S(1)} %get-tuple-element.23), channel_id=1, source_target_pairs={{0,3},{1,0},{2,1},{3,2},{4,7},{5,4},{6,5},{7,6},{8,11},{9,8},{10,9... | collective-permute-start | bytes 786440 | tf_op jit(solution)/shard_map/ppermute | solution.py:19
  156.7 4.8 %collective-permute-done.21 = bf16[4,2,128,128]{3,2,1,0:T(8,128)(2,1)S(1)} collective-permute-done((bf16[4,2,128,128]{3,2,1,0:T(8,128)(2,1)S(1)}, bf16[4,2,128,128]{3,2,1,0:T(8,128)(2,1)S(1)}, u32[]{:S(2)}, u32[]{:S(2)}) %collective-permute-start.21) | collective-permute-done | bytes 262176 | tf_op jit(solution)/shard_map/ppermute | solution.py:19
  161.5 1.3 collective-permute-done.20
  162.8 0.1 pad_maximum_fusion.2
  163.0 0.7 gather_fusion.2
  163.8 0.2 convert_bitcast_fusion
  164.0 1.5 fusion.35
  (37 shorter events, 0.6 us)
Async XLA Ops:
  0.6 44.2 %copy-start.1 = (s32[7]{0:T(128)S(1)}, s32[7]{0:T(128)}, u32[]{:S(2)}) copy-start(s32[7]{0:T(128)} %constant.156.clone) | copy-start | bytes 88
  2.2 24.5 %collective-permute-start.2 = (bf16[2,128,128]{2,1,0:T(8,128)(2,1)S(1)}, bf16[2,128,128]{2,1,0:T(8,128)(2,1)S(1)}, u32[]{:S(2)}, u32[]{:S(2)}) collective-permute-start(bf16[2,128,128]{2,1,0:T(8,128)(2,1)S(1)} %slice.84), channel_id=1, source_target_pairs={{16,96},{48,128},{80,160},{112,192},{144,224},{176,256},{208,288},... | collective-permute-start | bytes 196616 | tf_op jit(solution)/shard_map/ppermute | solution.py:29
  14.3 15.6 %collective-permute-start.1 = (bf16[2,128,128]{2,1,0:T(8,128)(2,1)S(1)}, bf16[2,128,128]{2,1,0:T(8,128)(2,1)S(1)}, u32[]{:S(2)}, u32[]{:S(2)}) collective-permute-start(bf16[2,128,128]{2,1,0:T(8,128)(2,1)S(1)} %slice.84), channel_id=1, source_target_pairs={{16,64},{48,96},{80,128},{112,160},{144,192},{176,224},{208,256},{... | collective-permute-start | bytes 196616 | tf_op jit(solution)/shard_map/ppermute | solution.py:29
  18.6 14.6 %collective-permute-start = (bf16[2,128,128]{2,1,0:T(8,128)(2,1)S(1)}, bf16[2,128,128]{2,1,0:T(8,128)(2,1)S(1)}, u32[]{:S(2)}, u32[]{:S(2)}) collective-permute-start(bf16[2,128,128]{2,1,0:T(8,128)(2,1)S(1)} %slice.84), channel_id=1, source_target_pairs={{16,32},{48,64},{80,96},{112,128},{144,160},{176,192},{208,224},{2... | collective-permute-start | bytes 196616 | tf_op jit(solution)/shard_map/ppermute | solution.py:29
  33.3 14.6 %collective-permute-start.5 = (bf16[3,2,128,128]{3,2,1,0:T(8,128)(2,1)S(1)}, bf16[3,2,128,128]{3,2,1,0:T(8,128)(2,1)S(1)}, u32[]{:S(2)}, u32[]{:S(2)}) collective-permute-start(bf16[3,2,128,128]{3,2,1,0:T(8,128)(2,1)S(1)} %pad_maximum_fusion.4), channel_id=1, source_target_pairs={{0,1},{1,2},{2,3},{3,0},{4,5},{5,6},{6,7},{7,4},{8,9},{9,10},{10,1... | collective-permute-start | bytes 589832 | tf_op jit(solution)/shard_map/ppermute | solution.py:19
  36.8 12.0 %collective-permute-start.4 = (bf16[3,2,128,128]{3,2,1,0:T(8,128)(2,1)S(1)}, bf16[3,2,128,128]{3,2,1,0:T(8,128)(2,1)S(1)}, u32[]{:S(2)}, u32[]{:S(2)}) collective-permute-start(bf16[3,2,128,128]{3,2,1,0:T(8,128)(2,1)S(1)} %pad_maximum_fusion.4), channel_id=1, source_target_pairs={{0,2},{1,3},{2,0},{3,1},{4,6},{5,7},{6,4},{7,5},{8,10},{9,11},{10,... | collective-permute-start | bytes 589832 | tf_op jit(solution)/shard_map/ppermute | solution.py:19
  41.6 8.5 %collective-permute-start.3 = (bf16[3,2,128,128]{3,2,1,0:T(8,128)(2,1)S(1)}, bf16[3,2,128,128]{3,2,1,0:T(8,128)(2,1)S(1)}, u32[]{:S(2)}, u32[]{:S(2)}) collective-permute-start(bf16[3,2,128,128]{3,2,1,0:T(8,128)(2,1)S(1)} %pad_maximum_fusion.4), channel_id=1, source_target_pairs={{0,3},{1,0},{2,1},{3,2},{4,7},{5,4},{6,5},{7,6},{8,11},{9,8},{10,9... | collective-permute-start | bytes 589832 | tf_op jit(solution)/shard_map/ppermute | solution.py:19
  44.9 1.2 copy-start
  50.1 4.6 %collective-permute-start.6 = (bf16[4,2,512,128]{3,2,1,0:T(8,128)(2,1)S(1)}, bf16[4,2,512,128]{3,2,1,0:T(8,128)(2,1)S(1)}, u32[]{:S(2)}, u32[]{:S(2)}) collective-permute-start(bf16[4,2,512,128]{3,2,1,0:T(8,128)(2,1)S(1)} %maximum_maximum_fusion), channel_id=1, source_target_pairs={{0,16},{16,0},{32,48},{48,32},{64,80},{80,64},{96,112},{112,96},{1... | collective-permute-start | bytes 3145736 | tf_op jit(solution)/shard_map/ppermute | solution.py:39
  72.5 6.5 %copy-start.2 = (f32[4096,128]{1,0:T(8,128)S(1)}, f32[4096,128]{1,0:T(8,128)}, u32[]{:S(2)}) copy-start(f32[4096,128]{1,0:T(8,128)} %get-tuple-element.7) | copy-start | bytes 6291460
  72.5 6.5 %copy-start.3 = (f32[4096,128]{1,0:T(8,128)S(1)}, f32[4096,128]{1,0:T(8,128)}, u32[]{:S(2)}) copy-start(f32[4096,128]{1,0:T(8,128)} %get-tuple-element.8) | copy-start | bytes 6291460
  74.3 4.7 %collective-permute-start.7 = (bf16[2,4,512,128]{3,2,1,0:T(8,128)(2,1)S(1)}, bf16[2,4,512,128]{3,2,1,0:T(8,128)(2,1)S(1)}, u32[]{:S(2)}, u32[]{:S(2)}) collective-permute-start(bf16[2,4,512,128]{3,2,1,0:T(8,128)(2,1)S(1)} %fusion.2), channel_id=1, source_target_pairs={{0,16},{16,0},{32,48},{48,32},{64,80},{80,64},{96,112},{112,96},{1... | collective-permute-start | bytes 3145736 | tf_op jit(solution)/shard_map/ppermute | solution.py:39
  79.2 18.1 %collective-permute-start.11 = (bf16[2,3,128,128]{3,2,0,1:T(8,128)(2,1)S(1)}, bf16[2,3,128,128]{3,2,0,1:T(8,128)(2,1)S(1)}, u32[]{:S(2)}, u32[]{:S(2)}) collective-permute-start(bf16[2,3,128,128]{3,2,0,1:T(8,128)(2,1)S(1)} %get-tuple-element.19), channel_id=1, source_target_pairs={{0,1},{1,2},{2,3},{3,0},{4,5},{5,6},{6,7},{7,4},{8,9},{9,10},{10,1... | collective-permute-start | bytes 589832 | tf_op jit(solution)/shard_map/ppermute | solution.py:19
  83.6 15.6 %collective-permute-start.12 = (bf16[2,3,128,128]{3,2,0,1:T(8,128)(2,1)S(1)}, bf16[2,3,128,128]{3,2,0,1:T(8,128)(2,1)S(1)}, u32[]{:S(2)}, u32[]{:S(2)}) collective-permute-start(bf16[2,3,128,128]{3,2,0,1:T(8,128)(2,1)S(1)} %get-tuple-element.21), channel_id=1, source_target_pairs={{0,2},{1,3},{2,0},{3,1},{4,6},{5,7},{6,4},{7,5},{8,10},{9,11},{10,... | collective-permute-start | bytes 589832 | tf_op jit(solution)/shard_map/ppermute | solution.py:19
  87.2 12.1 %collective-permute-start.13 = (bf16[2,3,128,128]{3,2,0,1:T(8,128)(2,1)S(1)}, bf16[2,3,128,128]{3,2,0,1:T(8,128)(2,1)S(1)}, u32[]{:S(2)}, u32[]{:S(2)}) collective-permute-start(bf16[2,3,128,128]{3,2,0,1:T(8,128)(2,1)S(1)} %get-tuple-element.20), channel_id=1, source_target_pairs={{0,3},{1,0},{2,1},{3,2},{4,7},{5,4},{6,5},{7,6},{8,11},{9,8},{10,9... | collective-permute-start | bytes 589832 | tf_op jit(solution)/shard_map/ppermute | solution.py:19
  90.8 20.7 %collective-permute-start.10 = (bf16[2,1,128,128]{3,2,0,1:T(8,128)(2,1)S(1)}, bf16[2,1,128,128]{3,2,0,1:T(8,128)(2,1)S(1)}, u32[]{:S(2)}, u32[]{:S(2)}) collective-permute-start(bf16[2,1,128,128]{3,2,0,1:T(8,128)(2,1)S(1)} %get-tuple-element.17), channel_id=1, source_target_pairs={{0,3},{1,0},{2,1},{3,2},{4,7},{5,4},{6,5},{7,6},{8,11},{9,8},{10,9... | collective-permute-start | bytes 196616 | tf_op jit(solution)/shard_map/ppermute | solution.py:19
  93.5 22.3 %collective-permute-start.9 = (bf16[2,1,128,128]{3,2,0,1:T(8,128)(2,1)S(1)}, bf16[2,1,128,128]{3,2,0,1:T(8,128)(2,1)S(1)}, u32[]{:S(2)}, u32[]{:S(2)}) collective-permute-start(bf16[2,1,128,128]{3,2,0,1:T(8,128)(2,1)S(1)} %get-tuple-element.18), channel_id=1, source_target_pairs={{0,2},{1,3},{2,0},{3,1},{4,6},{5,7},{6,4},{7,5},{8,10},{9,11},{10,... | collective-permute-start | bytes 196616 | tf_op jit(solution)/shard_map/ppermute | solution.py:19
  97.3 18.5 %collective-permute-start.8 = (bf16[2,1,128,128]{3,2,0,1:T(8,128)(2,1)S(1)}, bf16[2,1,128,128]{3,2,0,1:T(8,128)(2,1)S(1)}, u32[]{:S(2)}, u32[]{:S(2)}) collective-permute-start(bf16[2,1,128,128]{3,2,0,1:T(8,128)(2,1)S(1)} %get-tuple-element.16), channel_id=1, source_target_pairs={{0,1},{1,2},{2,3},{3,0},{4,5},{5,6},{6,7},{7,4},{8,9},{9,10},{10,1... | collective-permute-start | bytes 196616 | tf_op jit(solution)/shard_map/ppermute | solution.py:19
  100.0 15.8 %collective-permute-start.16 = (bf16[2,128,128]{2,1,0:T(8,128)(2,1)}, bf16[2,128,128]{2,1,0:T(8,128)(2,1)S(1)}, u32[]{:S(2)}, u32[]{:S(2)}) collective-permute-start(bf16[2,128,128]{2,1,0:T(8,128)(2,1)} %get-tuple-element.25), channel_id=1, source_target_pairs={{96,16},{128,48},{160,80},{192,112},{224,144},{256,176},{288,208},... | collective-permute-start | bytes 196616 | tf_op jit(solution)/shard_map/ppermute | solution.py:34
  105.1 15.4 %collective-permute-start.15 = (bf16[2,128,128]{2,1,0:T(8,128)(2,1)}, bf16[2,128,128]{2,1,0:T(8,128)(2,1)}, u32[]{:S(2)}, u32[]{:S(2)}) collective-permute-start(bf16[2,128,128]{2,1,0:T(8,128)(2,1)} %get-tuple-element.26), channel_id=1, source_target_pairs={{64,16},{96,48},{128,80},{160,112},{192,144},{224,176},{256,208},{... | collective-permute-start | bytes 196616 | tf_op jit(solution)/shard_map/ppermute | solution.py:34
  111.5 14.6 %collective-permute-start.14 = (bf16[2,128,128]{2,1,0:T(8,128)(2,1)}, bf16[2,128,128]{2,1,0:T(8,128)(2,1)}, u32[]{:S(2)}, u32[]{:S(2)}) collective-permute-start(bf16[2,128,128]{2,1,0:T(8,128)(2,1)} %get-tuple-element.24), channel_id=1, source_target_pairs={{32,16},{64,48},{96,80},{128,112},{160,144},{192,176},{224,208},{2... | collective-permute-start | bytes 196616 | tf_op jit(solution)/shard_map/ppermute | solution.py:34
  127.1 15.5 %collective-permute-start.19 = (bf16[2,128,128]{2,1,0:T(8,128)(2,1)S(1)}, bf16[2,128,128]{2,1,0:T(8,128)(2,1)S(1)}, u32[]{:S(2)}, u32[]{:S(2)}) collective-permute-start(bf16[2,128,128]{2,1,0:T(8,128)(2,1)S(1)} %fusion.15), channel_id=1, source_target_pairs={{0,4},{4,8},{8,12},{12,0},{1,5},{5,9},{9,13},{13,1},{2,6},{6,10},{... | collective-permute-start | bytes 196616 | tf_op jit(solution)/shard_map/ppermute | solution.py:19
  129.6 13.0 %collective-permute-start.18 = (bf16[2,128,128]{2,1,0:T(8,128)(2,1)S(1)}, bf16[2,128,128]{2,1,0:T(8,128)(2,1)S(1)}, u32[]{:S(2)}, u32[]{:S(2)}) collective-permute-start(bf16[2,128,128]{2,1,0:T(8,128)(2,1)S(1)} %fusion.15), channel_id=1, source_target_pairs={{0,8},{4,12},{8,0},{12,4},{1,9},{5,13},{9,1},{13,5},{2,10},{6,14},... | collective-permute-start | bytes 196616 | tf_op jit(solution)/shard_map/ppermute | solution.py:19
  137.8 6.7 %collective-permute-start.17 = (bf16[2,128,128]{2,1,0:T(8,128)(2,1)S(1)}, bf16[2,128,128]{2,1,0:T(8,128)(2,1)S(1)}, u32[]{:S(2)}, u32[]{:S(2)}) collective-permute-start(bf16[2,128,128]{2,1,0:T(8,128)(2,1)S(1)} %fusion.15), channel_id=1, source_target_pairs={{0,12},{4,0},{8,4},{12,8},{1,13},{5,1},{9,5},{13,9},{2,14},{6,2},{... | collective-permute-start | bytes 196616 | tf_op jit(solution)/shard_map/ppermute | solution.py:19
  144.5 12.2 %collective-permute-start.22 = (bf16[4,2,128,128]{3,2,1,0:T(8,128)(2,1)S(1)}, bf16[4,2,128,128]{3,2,1,0:T(8,128)(2,1)S(1)}, u32[]{:S(2)}, u32[]{:S(2)}) collective-permute-start(bf16[4,2,128,128]{3,2,1,0:T(8,128)(2,1)S(1)} %get-tuple-element.23), channel_id=1, source_target_pairs={{0,1},{1,2},{2,3},{3,0},{4,5},{5,6},{6,7},{7,4},{8,9},{9,10},{10,1... | collective-permute-start | bytes 786440 | tf_op jit(solution)/shard_map/ppermute | solution.py:19
  148.3 13.2 %collective-permute-start.21 = (bf16[4,2,128,128]{3,2,1,0:T(8,128)(2,1)S(1)}, bf16[4,2,128,128]{3,2,1,0:T(8,128)(2,1)S(1)}, u32[]{:S(2)}, u32[]{:S(2)}) collective-permute-start(bf16[4,2,128,128]{3,2,1,0:T(8,128)(2,1)S(1)} %get-tuple-element.23), channel_id=1, source_target_pairs={{0,2},{1,3},{2,0},{3,1},{4,6},{5,7},{6,4},{7,5},{8,10},{9,11},{10,... | collective-permute-start | bytes 786440 | tf_op jit(solution)/shard_map/ppermute | solution.py:19
  153.0 9.8 %collective-permute-start.20 = (bf16[4,2,128,128]{3,2,1,0:T(8,128)(2,1)S(1)}, bf16[4,2,128,128]{3,2,1,0:T(8,128)(2,1)S(1)}, u32[]{:S(2)}, u32[]{:S(2)}) collective-permute-start(bf16[4,2,128,128]{3,2,1,0:T(8,128)(2,1)S(1)} %get-tuple-element.23), channel_id=1, source_target_pairs={{0,3},{1,0},{2,1},{3,2},{4,7},{5,4},{6,5},{7,6},{8,11},{9,8},{10,9... | collective-permute-start | bytes 786440 | tf_op jit(solution)/shard_map/ppermute | solution.py:19

commit v9 on v8

--- a/solution.py
+++ b/solution.py
@@ -198,10 +198,10 @@
             part = part + cycled(piece, "sub", step).astype(jnp.float32)
         return part
 
-    fetched_parts = reduce_parts(1, half)
-    running = reduce_parts(0, 1)[:, 0]
+    reduced = reduce_parts(0, half)
+    running = reduced[:, 0]
     for step in range(1, half):
-        term = fetched_parts[:, step - 1].astype(jnp.bfloat16)
+        term = reduced[:, step].astype(jnp.bfloat16)
         running = running + chip_return(term, "ctx", step).astype(jnp.float32)
     mine = running.astype(jnp.bfloat16)
     by_group = jnp.stack([mine] + [cycled(mine, "grp", -step) for step in range(1, groups)])

time: 168 us -> 167 us (level)
  waiting for transfers between devices: 32.8 us -> 40.2 us
  starting transfers between devices: 99.5 us -> 94.3 us
    ppermute x15 -> x12, waiting for transfers between devices: 10.2 us -> 23.1 us  [cycled(): lax.ppermute(value, axis, [(source, (source + steps) % count) for source...]
    ppermute x15 -> x12, starting transfers between devices: 58.8 us -> 52.6 us  [cycled(): lax.ppermute(value, axis, [(source, (source + steps) % count) for source...]
    ppermute x3, waiting for transfers between devices: 10.3 us -> 4.79 us  [chip_return(): lax.ppermute(value, axis, [(target, source) for source, target in pairs])]
  transfers between devices with their start and end apart: 23 -> 20, of which waited for: 12 -> 15; matrix products, arithmetic and copies ran while one was open for 4% -> 4% of each run, Pallas kernels for 0% -> 0%
where the time goes in v9:
time: 167 us; the launch traced here: 166 us
  starting transfers between devices  94.3 us (56%)
  waiting for transfers between devices  40.2 us (24%)
  Pallas kernels  16.1 us (10%)
  local copies, waits for them, and re-layouts  8.71 us (5%)
  other arithmetic  5.51 us (3%)
    ppermute x12, starting transfers between devices, cycled(): lax.ppermute(value, axis, [(source, (source + steps) % count) for source...  52.6 us
    ppermute x12, waiting for transfers between devices, cycled(): lax.ppermute(value, axis, [(source, (source + steps) % count) for source...  23.1 us
    ppermute x3, starting transfers between devices, chip_fetch(): return lax.ppermute(value, axis, chip_pairs(lax.axis_size(axis), step))  21 us
    ppermute x3, starting transfers between devices, chip_return(): lax.ppermute(value, axis, [(target, source) for source, target in pairs])  16.6 us
    pallas_call x1, Pallas kernels, local_grads(): pl.pallas_call(kernel, grid_spec=pltpu.PrefetchScalarGridSpec(num_scalar_...  16.1 us
    ppermute x3, waiting for transfers between devices, chip_fetch(): return lax.ppermute(value, axis, chip_pairs(lax.axis_size(axis), step))  9.16 us
    ppermute x3, waiting for transfers between devices, chip_return(): lax.ppermute(value, axis, [(target, source) for source, target in pairs])  4.79 us
    ppermute x2, starting transfers between devices, swap_cores(): lax.ppermute(value, axis, [(source, source ^ 1) for source in range(count)])  4.1 us
  transfers between devices with their start and end apart: 20, of which 15 were waited for; matrix products, arithmetic and copies ran while one was open for 4% of the time, Pallas kernels for 0%

profile of v9, /device:TPU:6, one launch (start us, length us, event | category | flops | bytes accessed | tf_op | source)
XLA Modules:
  0.0 166.0 jit_solution(11106696232069971855)
XLA Ops:
  0.7 1.0 constant_dynamic-slice_fusion
  1.7 0.5 fusion.6
  2.2 12.2 %collective-permute-start.2 = (bf16[2,128,128]{2,1,0:T(8,128)(2,1)S(1)}, bf16[2,128,128]{2,1,0:T(8,128)(2,1)S(1)}, u32[]{:S(2)}, u32[]{:S(2)}) collective-permute-start(bf16[2,128,128]{2,1,0:T(8,128)(2,1)S(1)} %slice.72), channel_id=1, source_target_pairs={{16,96},{48,128},{80,160},{112,192},{144,224},{176,256},{208,288},... | collective-permute-start | bytes 196616 | tf_op jit(solution)/shard_map/ppermute | solution.py:29
  14.3 4.3 %collective-permute-start.1 = (bf16[2,128,128]{2,1,0:T(8,128)(2,1)S(1)}, bf16[2,128,128]{2,1,0:T(8,128)(2,1)S(1)}, u32[]{:S(2)}, u32[]{:S(2)}) collective-permute-start(bf16[2,128,128]{2,1,0:T(8,128)(2,1)S(1)} %slice.72), channel_id=1, source_target_pairs={{16,64},{48,96},{80,128},{112,160},{144,192},{176,224},{208,256},{... | collective-permute-start | bytes 196616 | tf_op jit(solution)/shard_map/ppermute | solution.py:29
  18.6 4.6 %collective-permute-start = (bf16[2,128,128]{2,1,0:T(8,128)(2,1)S(1)}, bf16[2,128,128]{2,1,0:T(8,128)(2,1)S(1)}, u32[]{:S(2)}, u32[]{:S(2)}) collective-permute-start(bf16[2,128,128]{2,1,0:T(8,128)(2,1)S(1)} %slice.72), channel_id=1, source_target_pairs={{16,32},{48,64},{80,96},{112,128},{144,160},{176,192},{208,224},{2... | collective-permute-start | bytes 196616 | tf_op jit(solution)/shard_map/ppermute | solution.py:29
  23.2 0.8 constant_dynamic-slice_fusion.2
  24.0 0.1 reshape.262
  24.1 2.6 %collective-permute-done.2 = bf16[2,128,128]{2,1,0:T(8,128)(2,1)S(1)} collective-permute-done((bf16[2,128,128]{2,1,0:T(8,128)(2,1)S(1)}, bf16[2,128,128]{2,1,0:T(8,128)(2,1)S(1)}, u32[]{:S(2)}, u32[]{:S(2)}) %collective-permute-start.2) | collective-permute-done | bytes 65568 | tf_op jit(solution)/shard_map/ppermute | solution.py:29
  26.7 3.3 %collective-permute-done.1 = bf16[2,128,128]{2,1,0:T(8,128)(2,1)S(1)} collective-permute-done((bf16[2,128,128]{2,1,0:T(8,128)(2,1)S(1)}, bf16[2,128,128]{2,1,0:T(8,128)(2,1)S(1)}, u32[]{:S(2)}, u32[]{:S(2)}) %collective-permute-start.1) | collective-permute-done | bytes 65568 | tf_op jit(solution)/shard_map/ppermute | solution.py:29
  29.9 3.3 %collective-permute-done = bf16[2,128,128]{2,1,0:T(8,128)(2,1)S(1)} collective-permute-done((bf16[2,128,128]{2,1,0:T(8,128)(2,1)S(1)}, bf16[2,128,128]{2,1,0:T(8,128)(2,1)S(1)}, u32[]{:S(2)}, u32[]{:S(2)}) %collective-permute-start) | collective-permute-done | bytes 65568 | tf_op jit(solution)/shard_map/ppermute | solution.py:29
  33.3 3.5 %collective-permute-start.5 = (bf16[3,2,128,128]{3,2,1,0:T(8,128)(2,1)S(1)}, bf16[3,2,128,128]{3,2,1,0:T(8,128)(2,1)S(1)}, u32[]{:S(2)}, u32[]{:S(2)}) collective-permute-start(bf16[3,2,128,128]{3,2,1,0:T(8,128)(2,1)S(1)} %pad_maximum_fusion.4), channel_id=1, source_target_pairs={{0,1},{1,2},{2,3},{3,0},{4,5},{5,6},{6,7},{7,4},{8,9},{9,10},{10,1... | collective-permute-start | bytes 589832 | tf_op jit(solution)/shard_map/ppermute | solution.py:19
  36.8 4.8 %collective-permute-start.4 = (bf16[3,2,128,128]{3,2,1,0:T(8,128)(2,1)S(1)}, bf16[3,2,128,128]{3,2,1,0:T(8,128)(2,1)S(1)}, u32[]{:S(2)}, u32[]{:S(2)}) collective-permute-start(bf16[3,2,128,128]{3,2,1,0:T(8,128)(2,1)S(1)} %pad_maximum_fusion.4), channel_id=1, source_target_pairs={{0,2},{1,3},{2,0},{3,1},{4,6},{5,7},{6,4},{7,5},{8,10},{9,11},{10,... | collective-permute-start | bytes 589832 | tf_op jit(solution)/shard_map/ppermute | solution.py:19
  41.6 3.3 %collective-permute-start.3 = (bf16[3,2,128,128]{3,2,1,0:T(8,128)(2,1)S(1)}, bf16[3,2,128,128]{3,2,1,0:T(8,128)(2,1)S(1)}, u32[]{:S(2)}, u32[]{:S(2)}) collective-permute-start(bf16[3,2,128,128]{3,2,1,0:T(8,128)(2,1)S(1)} %pad_maximum_fusion.4), channel_id=1, source_target_pairs={{0,3},{1,0},{2,1},{3,2},{4,7},{5,4},{6,5},{7,6},{8,11},{9,8},{10,9... | collective-permute-start | bytes 589832 | tf_op jit(solution)/shard_map/ppermute | solution.py:19
  44.9 1.2 gather_fusion
  46.1 1.2 gather_fusion.1
  47.4 0.5 fusion.38
  47.9 0.9 collective-permute-done.4
  48.7 1.3 collective-permute-done.3
  50.1 1.9 %collective-permute-start.6 = (bf16[4,2,512,128]{3,2,1,0:T(8,128)(2,1)S(1)}, bf16[4,2,512,128]{3,2,1,0:T(8,128)(2,1)S(1)}, u32[]{:S(2)}, u32[]{:S(2)}) collective-permute-start(bf16[4,2,512,128]{3,2,1,0:T(8,128)(2,1)S(1)} %maximum_maximum_fusion), channel_id=1, source_target_pairs={{0,16},{16,0},{32,48},{48,32},{64,80},{80,64},{96,112},{112,96},{1... | collective-permute-start | bytes 3145736 | tf_op jit(solution)/shard_map/ppermute | solution.py:39
  52.1 0.1 reshape.289
  52.2 0.1 fusion.21
  52.3 0.1 broadcast_in_dim.47
  52.3 0.1 eq.59
  52.4 0.1 broadcast_in_dim.49
  52.5 0.1 eq.60
  52.6 0.1 broadcast_in_dim.50
  52.7 0.6 fusion.20.slots_ref
  53.3 0.7 select_select_fusion.code_ref
  54.0 0.7 collective-permute-done.6
  54.7 0.2 pad_maximum_fusion.1
  54.9 1.5 fusion.36
  56.3 16.1 %shard_map.103 = (bf16[2048,128]{1,0:T(8,128)(2,1)}, f32[4096,128]{1,0:T(8,128)}, f32[4096,128]{1,0:T(8,128)}) custom-call(s32[8,16]{1,0:T(8,128)} %fusion.20.slots_ref, bf16[2048,128]{1,0:T(8,128)(2,1)} %bitcast.81, bf16[2048,128]{1,0:T(8,128)(2,1)} %bitcast.82, s32[8,1,1024]{2,1,0:T(1,128)} %select_select_fusion.code_ref, bf16[4096,128]{1,0:T(8,128)(2,1)} %bitcast.69, ...), custom_call_target="tpu_custom_call" | custom-call | tf_op jit(solution)/shard_map/pallas_call | solution.py:105
  72.5 1.8 %fusion.2 = bf16[2,4,512,128]{3,2,1,0:T(8,128)(2,1)S(1)} fusion(f32[1,8,512,128]{3,2,1,0:T(8,128)} %bitcast.64, f32[1,8,512,128]{3,2,1,0:T(8,128)} %bitcast.62), kind=kLoop, calls=%fused_computation.8 | loop fusion | flops 524288 | bytes 5242880 | tf_op jit(solution)/shard_map/convert.4
  74.3 2.2 %collective-permute-start.7 = (bf16[2,4,512,128]{3,2,1,0:T(8,128)(2,1)S(1)}, bf16[2,4,512,128]{3,2,1,0:T(8,128)(2,1)S(1)}, u32[]{:S(2)}, u32[]{:S(2)}) collective-permute-start(bf16[2,4,512,128]{3,2,1,0:T(8,128)(2,1)S(1)} %fusion.2), channel_id=1, source_target_pairs={{0,16},{16,0},{32,48},{48,32},{64,80},{80,64},{96,112},{112,96},{1... | collective-permute-start | bytes 3145736 | tf_op jit(solution)/shard_map/ppermute | solution.py:39
  76.5 2.5 %collective-permute-done.7 = bf16[2,4,512,128]{3,2,1,0:T(8,128)(2,1)S(1)} collective-permute-done((bf16[2,4,512,128]{3,2,1,0:T(8,128)(2,1)S(1)}, bf16[2,4,512,128]{3,2,1,0:T(8,128)(2,1)S(1)}, u32[]{:S(2)}, u32[]{:S(2)}) %collective-permute-start.7) | collective-permute-done | bytes 1048608 | tf_op jit(solution)/shard_map/ppermute | solution.py:39
  79.0 0.3 fusion.33
  79.4 4.6 %collective-permute-start.10 = (bf16[2,4,128,128]{3,2,1,0:T(8,128)(2,1)S(1)}, bf16[2,4,128,128]{3,2,1,0:T(8,128)(2,1)S(1)}, u32[]{:S(2)}, u32[]{:S(2)}) collective-permute-start(bf16[2,4,128,128]{3,2,1,0:T(8,128)(2,1)S(1)} %get-tuple-element.21), channel_id=1, source_target_pairs={{0,3},{1,0},{2,1},{3,2},{4,7},{5,4},{6,5},{7,6},{8,11},{9,8},{10,9... | collective-permute-start | bytes 786440 | tf_op jit(solution)/shard_map/ppermute | solution.py:19
  84.0 3.8 %collective-permute-start.9 = (bf16[2,4,128,128]{3,2,1,0:T(8,128)(2,1)S(1)}, bf16[2,4,128,128]{3,2,1,0:T(8,128)(2,1)S(1)}, u32[]{:S(2)}, u32[]{:S(2)}) collective-permute-start(bf16[2,4,128,128]{3,2,1,0:T(8,128)(2,1)S(1)} %get-tuple-element.22), channel_id=1, source_target_pairs={{0,2},{1,3},{2,0},{3,1},{4,6},{5,7},{6,4},{7,5},{8,10},{9,11},{10,... | collective-permute-start | bytes 786440 | tf_op jit(solution)/shard_map/ppermute | solution.py:19
  87.8 1.9 %collective-permute-start.8 = (bf16[2,4,128,128]{3,2,1,0:T(8,128)(2,1)S(1)}, bf16[2,4,128,128]{3,2,1,0:T(8,128)(2,1)S(1)}, u32[]{:S(2)}, u32[]{:S(2)}) collective-permute-start(bf16[2,4,128,128]{3,2,1,0:T(8,128)(2,1)S(1)} %get-tuple-element.20), channel_id=1, source_target_pairs={{0,1},{1,2},{2,3},{3,0},{4,5},{5,6},{6,7},{7,4},{8,9},{9,10},{10,1... | collective-permute-start | bytes 786440 | tf_op jit(solution)/shard_map/ppermute | solution.py:19
  89.8 5.7 %collective-permute-done.10 = bf16[2,4,128,128]{3,2,1,0:T(8,128)(2,1)S(1)} collective-permute-done((bf16[2,4,128,128]{3,2,1,0:T(8,128)(2,1)S(1)}, bf16[2,4,128,128]{3,2,1,0:T(8,128)(2,1)S(1)}, u32[]{:S(2)}, u32[]{:S(2)}) %collective-permute-start.10) | collective-permute-done | bytes 262176 | tf_op jit(solution)/shard_map/ppermute | solution.py:19
  95.5 1.1 collective-permute-done.9
  96.6 4.5 %collective-permute-done.8 = bf16[2,4,128,128]{3,2,1,0:T(8,128)(2,1)S(1)} collective-permute-done((bf16[2,4,128,128]{3,2,1,0:T(8,128)(2,1)S(1)}, bf16[2,4,128,128]{3,2,1,0:T(8,128)(2,1)S(1)}, u32[]{:S(2)}, u32[]{:S(2)}) %collective-permute-start.8) | collective-permute-done | bytes 262176 | tf_op jit(solution)/shard_map/ppermute | solution.py:19
  101.1 0.1 fusion.31
  101.3 6.3 %collective-permute-start.13 = (bf16[2,128,128]{2,1,0:T(8,128)(2,1)S(1)}, bf16[2,128,128]{2,1,0:T(8,128)(2,1)S(1)}, u32[]{:S(2)}, u32[]{:S(2)}) collective-permute-start(bf16[2,128,128]{2,1,0:T(8,128)(2,1)S(1)} %get-tuple-element.26), channel_id=1, source_target_pairs={{96,16},{128,48},{160,80},{192,112},{224,144},{256,176},{288,208},... | collective-permute-start | bytes 196616 | tf_op jit(solution)/shard_map/ppermute | solution.py:34
  107.6 5.2 %collective-permute-start.12 = (bf16[2,128,128]{2,1,0:T(8,128)(2,1)S(1)}, bf16[2,128,128]{2,1,0:T(8,128)(2,1)S(1)}, u32[]{:S(2)}, u32[]{:S(2)}) collective-permute-start(bf16[2,128,128]{2,1,0:T(8,128)(2,1)S(1)} %get-tuple-element.27), channel_id=1, source_target_pairs={{64,16},{96,48},{128,80},{160,112},{192,144},{224,176},{256,208},{... | collective-permute-start | bytes 196616 | tf_op jit(solution)/shard_map/ppermute | solution.py:34
  112.7 5.1 %collective-permute-start.11 = (bf16[2,128,128]{2,1,0:T(8,128)(2,1)S(1)}, bf16[2,128,128]{2,1,0:T(8,128)(2,1)S(1)}, u32[]{:S(2)}, u32[]{:S(2)}) collective-permute-start(bf16[2,128,128]{2,1,0:T(8,128)(2,1)S(1)} %get-tuple-element.25), channel_id=1, source_target_pairs={{32,16},{64,48},{96,80},{128,112},{160,144},{192,176},{224,208},{2... | collective-permute-start | bytes 196616 | tf_op jit(solution)/shard_map/ppermute | solution.py:34
  117.8 0.1 broadcast_add_fusion
  117.9 0.1 add.179
  118.0 4.7 %collective-permute-done.12 = bf16[2,128,128]{2,1,0:T(8,128)(2,1)S(1)} collective-permute-done((bf16[2,128,128]{2,1,0:T(8,128)(2,1)S(1)}, bf16[2,128,128]{2,1,0:T(8,128)(2,1)S(1)}, u32[]{:S(2)}, u32[]{:S(2)}) %collective-permute-start.12) | collective-permute-done | bytes 65568 | tf_op jit(solution)/shard_map/ppermute | solution.py:34
  122.7 0.1 collective-permute-done.11
  122.8 6.4 %collective-permute-start.16 = (bf16[2,128,128]{2,1,0:T(8,128)(2,1)S(1)}, bf16[2,128,128]{2,1,0:T(8,128)(2,1)S(1)}, u32[]{:S(2)}, u32[]{:S(2)}) collective-permute-start(bf16[2,128,128]{2,1,0:T(8,128)(2,1)S(1)} %fusion.11), channel_id=1, source_target_pairs={{0,4},{4,8},{8,12},{12,0},{1,5},{5,9},{9,13},{13,1},{2,6},{6,10},{... | collective-permute-start | bytes 196616 | tf_op jit(solution)/shard_map/ppermute | solution.py:19
  129.2 9.2 %collective-permute-start.15 = (bf16[2,128,128]{2,1,0:T(8,128)(2,1)S(1)}, bf16[2,128,128]{2,1,0:T(8,128)(2,1)S(1)}, u32[]{:S(2)}, u32[]{:S(2)}) collective-permute-start(bf16[2,128,128]{2,1,0:T(8,128)(2,1)S(1)} %fusion.11), channel_id=1, source_target_pairs={{0,8},{4,12},{8,0},{12,4},{1,9},{5,13},{9,1},{13,5},{2,10},{6,14},... | collective-permute-start | bytes 196616 | tf_op jit(solution)/shard_map/ppermute | solution.py:19
  138.5 4.8 %collective-permute-start.14 = (bf16[2,128,128]{2,1,0:T(8,128)(2,1)S(1)}, bf16[2,128,128]{2,1,0:T(8,128)(2,1)S(1)}, u32[]{:S(2)}, u32[]{:S(2)}) collective-permute-start(bf16[2,128,128]{2,1,0:T(8,128)(2,1)S(1)} %fusion.11), channel_id=1, source_target_pairs={{0,12},{4,0},{8,4},{12,8},{1,13},{5,1},{9,5},{13,9},{2,14},{6,2},{... | collective-permute-start | bytes 196616 | tf_op jit(solution)/shard_map/ppermute | solution.py:19
  143.3 1.9 %collective-permute-done.14 = bf16[2,128,128]{2,1,0:T(8,128)(2,1)S(1)} collective-permute-done((bf16[2,128,128]{2,1,0:T(8,128)(2,1)S(1)}, bf16[2,128,128]{2,1,0:T(8,128)(2,1)S(1)}, u32[]{:S(2)}, u32[]{:S(2)}) %collective-permute-start.14) | collective-permute-done | bytes 65568 | tf_op jit(solution)/shard_map/ppermute | solution.py:19
  145.2 1.9 %collective-permute-start.19 = (bf16[4,2,128,128]{3,2,1,0:T(8,128)(2,1)S(1)}, bf16[4,2,128,128]{3,2,1,0:T(8,128)(2,1)S(1)}, u32[]{:S(2)}, u32[]{:S(2)}) collective-permute-start(bf16[4,2,128,128]{3,2,1,0:T(8,128)(2,1)S(1)} %get-tuple-element.24), channel_id=1, source_target_pairs={{0,1},{1,2},{2,3},{3,0},{4,5},{5,6},{6,7},{7,4},{8,9},{9,10},{10,1... | collective-permute-start | bytes 786440 | tf_op jit(solution)/shard_map/ppermute | solution.py:19
  147.1 3.8 %collective-permute-start.18 = (bf16[4,2,128,128]{3,2,1,0:T(8,128)(2,1)S(1)}, bf16[4,2,128,128]{3,2,1,0:T(8,128)(2,1)S(1)}, u32[]{:S(2)}, u32[]{:S(2)}) collective-permute-start(bf16[4,2,128,128]{3,2,1,0:T(8,128)(2,1)S(1)} %get-tuple-element.24), channel_id=1, source_target_pairs={{0,2},{1,3},{2,0},{3,1},{4,6},{5,7},{6,4},{7,5},{8,10},{9,11},{10,... | collective-permute-start | bytes 786440 | tf_op jit(solution)/shard_map/ppermute | solution.py:19
  151.0 4.5 %collective-permute-start.17 = (bf16[4,2,128,128]{3,2,1,0:T(8,128)(2,1)S(1)}, bf16[4,2,128,128]{3,2,1,0:T(8,128)(2,1)S(1)}, u32[]{:S(2)}, u32[]{:S(2)}) collective-permute-start(bf16[4,2,128,128]{3,2,1,0:T(8,128)(2,1)S(1)} %get-tuple-element.24), channel_id=1, source_target_pairs={{0,3},{1,0},{2,1},{3,2},{4,7},{5,4},{6,5},{7,6},{8,11},{9,8},{10,9... | collective-permute-start | bytes 786440 | tf_op jit(solution)/shard_map/ppermute | solution.py:19
  155.5 0.1 compare_and_fusion
  155.6 5.2 %collective-permute-done.19 = bf16[4,2,128,128]{3,2,1,0:T(8,128)(2,1)S(1)} collective-permute-done((bf16[4,2,128,128]{3,2,1,0:T(8,128)(2,1)S(1)}, bf16[4,2,128,128]{3,2,1,0:T(8,128)(2,1)S(1)}, u32[]{:S(2)}, u32[]{:S(2)}) %collective-permute-start.19) | collective-permute-done | bytes 262176 | tf_op jit(solution)/shard_map/ppermute | solution.py:19
  160.9 2.5 %collective-permute-done.17 = bf16[4,2,128,128]{3,2,1,0:T(8,128)(2,1)S(1)} collective-permute-done((bf16[4,2,128,128]{3,2,1,0:T(8,128)(2,1)S(1)}, bf16[4,2,128,128]{3,2,1,0:T(8,128)(2,1)S(1)}, u32[]{:S(2)}, u32[]{:S(2)}) %collective-permute-start.17) | collective-permute-done | bytes 262176 | tf_op jit(solution)/shard_map/ppermute | solution.py:19
  163.3 0.1 pad_maximum_fusion.2
  163.5 0.7 gather_fusion.2
  164.3 0.2 convert_bitcast_fusion
  164.5 1.5 fusion.35
  (30 shorter events, 0.4 us)
Async XLA Ops:
  0.6 44.2 %copy-start.1 = (s32[7]{0:T(128)S(1)}, s32[7]{0:T(128)}, u32[]{:S(2)}) copy-start(s32[7]{0:T(128)} %constant.156.clone) | copy-start | bytes 88
  2.2 24.5 %collective-permute-start.2 = (bf16[2,128,128]{2,1,0:T(8,128)(2,1)S(1)}, bf16[2,128,128]{2,1,0:T(8,128)(2,1)S(1)}, u32[]{:S(2)}, u32[]{:S(2)}) collective-permute-start(bf16[2,128,128]{2,1,0:T(8,128)(2,1)S(1)} %slice.72), channel_id=1, source_target_pairs={{16,96},{48,128},{80,160},{112,192},{144,224},{176,256},{208,288},... | collective-permute-start | bytes 196616 | tf_op jit(solution)/shard_map/ppermute | solution.py:29
  14.3 15.6 %collective-permute-start.1 = (bf16[2,128,128]{2,1,0:T(8,128)(2,1)S(1)}, bf16[2,128,128]{2,1,0:T(8,128)(2,1)S(1)}, u32[]{:S(2)}, u32[]{:S(2)}) collective-permute-start(bf16[2,128,128]{2,1,0:T(8,128)(2,1)S(1)} %slice.72), channel_id=1, source_target_pairs={{16,64},{48,96},{80,128},{112,160},{144,192},{176,224},{208,256},{... | collective-permute-start | bytes 196616 | tf_op jit(solution)/shard_map/ppermute | solution.py:29
  18.6 14.6 %collective-permute-start = (bf16[2,128,128]{2,1,0:T(8,128)(2,1)S(1)}, bf16[2,128,128]{2,1,0:T(8,128)(2,1)S(1)}, u32[]{:S(2)}, u32[]{:S(2)}) collective-permute-start(bf16[2,128,128]{2,1,0:T(8,128)(2,1)S(1)} %slice.72), channel_id=1, source_target_pairs={{16,32},{48,64},{80,96},{112,128},{144,160},{176,192},{208,224},{2... | collective-permute-start | bytes 196616 | tf_op jit(solution)/shard_map/ppermute | solution.py:29
  33.3 14.6 %collective-permute-start.5 = (bf16[3,2,128,128]{3,2,1,0:T(8,128)(2,1)S(1)}, bf16[3,2,128,128]{3,2,1,0:T(8,128)(2,1)S(1)}, u32[]{:S(2)}, u32[]{:S(2)}) collective-permute-start(bf16[3,2,128,128]{3,2,1,0:T(8,128)(2,1)S(1)} %pad_maximum_fusion.4), channel_id=1, source_target_pairs={{0,1},{1,2},{2,3},{3,0},{4,5},{5,6},{6,7},{7,4},{8,9},{9,10},{10,1... | collective-permute-start | bytes 589832 | tf_op jit(solution)/shard_map/ppermute | solution.py:19
  36.8 12.0 %collective-permute-start.4 = (bf16[3,2,128,128]{3,2,1,0:T(8,128)(2,1)S(1)}, bf16[3,2,128,128]{3,2,1,0:T(8,128)(2,1)S(1)}, u32[]{:S(2)}, u32[]{:S(2)}) collective-permute-start(bf16[3,2,128,128]{3,2,1,0:T(8,128)(2,1)S(1)} %pad_maximum_fusion.4), channel_id=1, source_target_pairs={{0,2},{1,3},{2,0},{3,1},{4,6},{5,7},{6,4},{7,5},{8,10},{9,11},{10,... | collective-permute-start | bytes 589832 | tf_op jit(solution)/shard_map/ppermute | solution.py:19
  41.6 8.5 %collective-permute-start.3 = (bf16[3,2,128,128]{3,2,1,0:T(8,128)(2,1)S(1)}, bf16[3,2,128,128]{3,2,1,0:T(8,128)(2,1)S(1)}, u32[]{:S(2)}, u32[]{:S(2)}) collective-permute-start(bf16[3,2,128,128]{3,2,1,0:T(8,128)(2,1)S(1)} %pad_maximum_fusion.4), channel_id=1, source_target_pairs={{0,3},{1,0},{2,1},{3,2},{4,7},{5,4},{6,5},{7,6},{8,11},{9,8},{10,9... | collective-permute-start | bytes 589832 | tf_op jit(solution)/shard_map/ppermute | solution.py:19
  44.9 1.2 copy-start
  50.1 4.6 %collective-permute-start.6 = (bf16[4,2,512,128]{3,2,1,0:T(8,128)(2,1)S(1)}, bf16[4,2,512,128]{3,2,1,0:T(8,128)(2,1)S(1)}, u32[]{:S(2)}, u32[]{:S(2)}) collective-permute-start(bf16[4,2,512,128]{3,2,1,0:T(8,128)(2,1)S(1)} %maximum_maximum_fusion), channel_id=1, source_target_pairs={{0,16},{16,0},{32,48},{48,32},{64,80},{80,64},{96,112},{112,96},{1... | collective-permute-start | bytes 3145736 | tf_op jit(solution)/shard_map/ppermute | solution.py:39
  72.5 6.5 %copy-start.2 = (f32[4096,128]{1,0:T(8,128)S(1)}, f32[4096,128]{1,0:T(8,128)}, u32[]{:S(2)}) copy-start(f32[4096,128]{1,0:T(8,128)} %get-tuple-element.7) | copy-start | bytes 6291460
  72.5 6.5 %copy-start.3 = (f32[4096,128]{1,0:T(8,128)S(1)}, f32[4096,128]{1,0:T(8,128)}, u32[]{:S(2)}) copy-start(f32[4096,128]{1,0:T(8,128)} %get-tuple-element.8) | copy-start | bytes 6291460
  74.3 4.7 %collective-permute-start.7 = (bf16[2,4,512,128]{3,2,1,0:T(8,128)(2,1)S(1)}, bf16[2,4,512,128]{3,2,1,0:T(8,128)(2,1)S(1)}, u32[]{:S(2)}, u32[]{:S(2)}) collective-permute-start(bf16[2,4,512,128]{3,2,1,0:T(8,128)(2,1)S(1)} %fusion.2), channel_id=1, source_target_pairs={{0,16},{16,0},{32,48},{48,32},{64,80},{80,64},{96,112},{112,96},{1... | collective-permute-start | bytes 3145736 | tf_op jit(solution)/shard_map/ppermute | solution.py:39
  79.4 16.1 %collective-permute-start.10 = (bf16[2,4,128,128]{3,2,1,0:T(8,128)(2,1)S(1)}, bf16[2,4,128,128]{3,2,1,0:T(8,128)(2,1)S(1)}, u32[]{:S(2)}, u32[]{:S(2)}) collective-permute-start(bf16[2,4,128,128]{3,2,1,0:T(8,128)(2,1)S(1)} %get-tuple-element.21), channel_id=1, source_target_pairs={{0,3},{1,0},{2,1},{3,2},{4,7},{5,4},{6,5},{7,6},{8,11},{9,8},{10,9... | collective-permute-start | bytes 786440 | tf_op jit(solution)/shard_map/ppermute | solution.py:19
  84.0 12.6 %collective-permute-start.9 = (bf16[2,4,128,128]{3,2,1,0:T(8,128)(2,1)S(1)}, bf16[2,4,128,128]{3,2,1,0:T(8,128)(2,1)S(1)}, u32[]{:S(2)}, u32[]{:S(2)}) collective-permute-start(bf16[2,4,128,128]{3,2,1,0:T(8,128)(2,1)S(1)} %get-tuple-element.22), channel_id=1, source_target_pairs={{0,2},{1,3},{2,0},{3,1},{4,6},{5,7},{6,4},{7,5},{8,10},{9,11},{10,... | collective-permute-start | bytes 786440 | tf_op jit(solution)/shard_map/ppermute | solution.py:19
  87.8 13.3 %collective-permute-start.8 = (bf16[2,4,128,128]{3,2,1,0:T(8,128)(2,1)S(1)}, bf16[2,4,128,128]{3,2,1,0:T(8,128)(2,1)S(1)}, u32[]{:S(2)}, u32[]{:S(2)}) collective-permute-start(bf16[2,4,128,128]{3,2,1,0:T(8,128)(2,1)S(1)} %get-tuple-element.20), channel_id=1, source_target_pairs={{0,1},{1,2},{2,3},{3,0},{4,5},{5,6},{6,7},{7,4},{8,9},{9,10},{10,1... | collective-permute-start | bytes 786440 | tf_op jit(solution)/shard_map/ppermute | solution.py:19
  101.3 16.7 %collective-permute-start.13 = (bf16[2,128,128]{2,1,0:T(8,128)(2,1)S(1)}, bf16[2,128,128]{2,1,0:T(8,128)(2,1)S(1)}, u32[]{:S(2)}, u32[]{:S(2)}) collective-permute-start(bf16[2,128,128]{2,1,0:T(8,128)(2,1)S(1)} %get-tuple-element.26), channel_id=1, source_target_pairs={{96,16},{128,48},{160,80},{192,112},{224,144},{256,176},{288,208},... | collective-permute-start | bytes 196616 | tf_op jit(solution)/shard_map/ppermute | solution.py:34
  107.6 15.1 %collective-permute-start.12 = (bf16[2,128,128]{2,1,0:T(8,128)(2,1)S(1)}, bf16[2,128,128]{2,1,0:T(8,128)(2,1)S(1)}, u32[]{:S(2)}, u32[]{:S(2)}) collective-permute-start(bf16[2,128,128]{2,1,0:T(8,128)(2,1)S(1)} %get-tuple-element.27), channel_id=1, source_target_pairs={{64,16},{96,48},{128,80},{160,112},{192,144},{224,176},{256,208},{... | collective-permute-start | bytes 196616 | tf_op jit(solution)/shard_map/ppermute | solution.py:34
  112.7 10.1 %collective-permute-start.11 = (bf16[2,128,128]{2,1,0:T(8,128)(2,1)S(1)}, bf16[2,128,128]{2,1,0:T(8,128)(2,1)S(1)}, u32[]{:S(2)}, u32[]{:S(2)}) collective-permute-start(bf16[2,128,128]{2,1,0:T(8,128)(2,1)S(1)} %get-tuple-element.25), channel_id=1, source_target_pairs={{32,16},{64,48},{96,80},{128,112},{160,144},{192,176},{224,208},{2... | collective-permute-start | bytes 196616 | tf_op jit(solution)/shard_map/ppermute | solution.py:34
  122.8 20.5 %collective-permute-start.16 = (bf16[2,128,128]{2,1,0:T(8,128)(2,1)S(1)}, bf16[2,128,128]{2,1,0:T(8,128)(2,1)S(1)}, u32[]{:S(2)}, u32[]{:S(2)}) collective-permute-start(bf16[2,128,128]{2,1,0:T(8,128)(2,1)S(1)} %fusion.11), channel_id=1, source_target_pairs={{0,4},{4,8},{8,12},{12,0},{1,5},{5,9},{9,13},{13,1},{2,6},{6,10},{... | collective-permute-start | bytes 196616 | tf_op jit(solution)/shard_map/ppermute | solution.py:19
  129.2 14.1 %collective-permute-start.15 = (bf16[2,128,128]{2,1,0:T(8,128)(2,1)S(1)}, bf16[2,128,128]{2,1,0:T(8,128)(2,1)S(1)}, u32[]{:S(2)}, u32[]{:S(2)}) collective-permute-start(bf16[2,128,128]{2,1,0:T(8,128)(2,1)S(1)} %fusion.11), channel_id=1, source_target_pairs={{0,8},{4,12},{8,0},{12,4},{1,9},{5,13},{9,1},{13,5},{2,10},{6,14},... | collective-permute-start | bytes 196616 | tf_op jit(solution)/shard_map/ppermute | solution.py:19
  138.5 6.7 %collective-permute-start.14 = (bf16[2,128,128]{2,1,0:T(8,128)(2,1)S(1)}, bf16[2,128,128]{2,1,0:T(8,128)(2,1)S(1)}, u32[]{:S(2)}, u32[]{:S(2)}) collective-permute-start(bf16[2,128,128]{2,1,0:T(8,128)(2,1)S(1)} %fusion.11), channel_id=1, source_target_pairs={{0,12},{4,0},{8,4},{12,8},{1,13},{5,1},{9,5},{13,9},{2,14},{6,2},{... | collective-permute-start | bytes 196616 | tf_op jit(solution)/shard_map/ppermute | solution.py:19
  145.2 15.6 %collective-permute-start.19 = (bf16[4,2,128,128]{3,2,1,0:T(8,128)(2,1)S(1)}, bf16[4,2,128,128]{3,2,1,0:T(8,128)(2,1)S(1)}, u32[]{:S(2)}, u32[]{:S(2)}) collective-permute-start(bf16[4,2,128,128]{3,2,1,0:T(8,128)(2,1)S(1)} %get-tuple-element.24), channel_id=1, source_target_pairs={{0,1},{1,2},{2,3},{3,0},{4,5},{5,6},{6,7},{7,4},{8,9},{9,10},{10,1... | collective-permute-start | bytes 786440 | tf_op jit(solution)/shard_map/ppermute | solution.py:19
  147.1 13.7 %collective-permute-start.18 = (bf16[4,2,128,128]{3,2,1,0:T(8,128)(2,1)S(1)}, bf16[4,2,128,128]{3,2,1,0:T(8,128)(2,1)S(1)}, u32[]{:S(2)}, u32[]{:S(2)}) collective-permute-start(bf16[4,2,128,128]{3,2,1,0:T(8,128)(2,1)S(1)} %get-tuple-element.24), channel_id=1, source_target_pairs={{0,2},{1,3},{2,0},{3,1},{4,6},{5,7},{6,4},{7,5},{8,10},{9,11},{10,... | collective-permute-start | bytes 786440 | tf_op jit(solution)/shard_map/ppermute | solution.py:19
  151.0 12.4 %collective-permute-start.17 = (bf16[4,2,128,128]{3,2,1,0:T(8,128)(2,1)S(1)}, bf16[4,2,128,128]{3,2,1,0:T(8,128)(2,1)S(1)}, u32[]{:S(2)}, u32[]{:S(2)}) collective-permute-start(bf16[4,2,128,128]{3,2,1,0:T(8,128)(2,1)S(1)} %get-tuple-element.24), channel_id=1, source_target_pairs={{0,3},{1,0},{2,1},{3,2},{4,7},{5,4},{6,5},{7,6},{8,11},{9,8},{10,9... | collective-permute-start | bytes 786440 | tf_op jit(solution)/shard_map/ppermute | solution.py:19

commit v10 on v9

--- a/solution.py
+++ b/solution.py
@@ -162,7 +162,10 @@
     rolled = jnp.roll(own_tiles, -part_index * quarter, axis=1)
     own_part = rolled[:, :quarter]
     even = ctx_index % 2 == 0
-    took = jnp.stack([chip_fetch(own_part, "ctx", step) for step in range(1, 4)])
+    took = [chip_fetch(own_part, "ctx", 1)]
+    for step in range(2, 4):
+        took.append(chip_fetch(took[-1], "ctx", 1))
+    took = jnp.stack(took)
     pieces = [took] + [cycled(took, "sub", -step) for step in range(1, parts_count)]
     took = jnp.concatenate(pieces, axis=2)
     mine = jnp.concatenate([rolled[None], took], axis=0)
@@ -178,7 +181,7 @@
     rolled_block = (local_block // per_part - part_index) % parts_count * per_part + local_block % per_part
     offset = jnp.clip(ctx_index - chosen // blocks_here, 0, REACH)
     placed = jnp.where(
-        even, jnp.array([0, 1, 5, 2, 6, 3, 7], jnp.int32)[offset], jnp.array([0, 4, 5, 1, 6, 2, 7], jnp.int32)[offset]
+        even, jnp.array([0, 1, 5, 6, 2, 3, 7], jnp.int32)[offset], jnp.array([0, 4, 5, 1, 2, 6, 7], jnp.int32)[offset]
     )
     slot_index = placed * blocks_here + rolled_block
     code = jnp.where(live_mask == 1, jnp.where(chosen < block_ids[:, None], 2, 1), 0)
@@ -199,10 +202,10 @@
         return part
 
     reduced = reduce_parts(0, half)
-    running = reduced[:, 0]
-    for step in range(1, half):
-        term = reduced[:, step].astype(jnp.bfloat16)
-        running = running + chip_return(term, "ctx", step).astype(jnp.float32)
+    running = reduced[:, half - 1]
+    for step in range(half - 2, -1, -1):
+        returned = chip_return(running.astype(jnp.bfloat16), "ctx", 1)
+        running = reduced[:, step] + returned.astype(jnp.float32)
     mine = running.astype(jnp.bfloat16)
     by_group = jnp.stack([mine] + [cycled(mine, "grp", -step) for step in range(1, groups)])
     by_part = jnp.stack([by_group] + [cycled(by_group, "sub", -step) for step in range(1, parts_count)])

time: 167 us -> 184 us (1.10)
  waiting for transfers between devices: 40.2 us -> 50.4 us
  starting transfers between devices: 94.3 us -> 102 us
    ppermute x3, starting transfers between devices: 16.6 us -> 30.4 us  [chip_return(): lax.ppermute(value, axis, [(target, source) for source, target in pairs])]
    ppermute x12, starting transfers between devices: 52.6 us -> 40.9 us  [cycled(): lax.ppermute(value, axis, [(source, (source + steps) % count) for source...]
    ppermute x3, waiting for transfers between devices: 4.79 us -> 11.4 us  [chip_return(): lax.ppermute(value, axis, [(target, source) for source, target in pairs])]
    ppermute x3, starting transfers between devices: 21 us -> 26.3 us  [chip_fetch(): return lax.ppermute(value, axis, chip_pairs(lax.axis_size(axis), step))]
    ppermute x12, waiting for transfers between devices: 23.1 us -> 25.1 us  [cycled(): lax.ppermute(value, axis, [(source, (source + steps) % count) for source...]
  transfers between devices with their start and end apart: 20 -> 20, of which waited for: 15 -> 17; matrix products, arithmetic and copies ran while one was open for 4% -> 3% of each run, Pallas kernels for 0% -> 0%
where the time goes in v10:
time: 184 us
  starting transfers between devices  102 us (55%)
  waiting for transfers between devices  50.4 us (27%)
  Pallas kernels  16.1 us (9%)
  local copies, waits for them, and re-layouts  8.71 us (5%)
  other arithmetic  5.52 us (3%)
    ppermute x12, starting transfers between devices, cycled(): lax.ppermute(value, axis, [(source, (source + steps) % count) for source...  40.9 us
    ppermute x3, starting transfers between devices, chip_return(): lax.ppermute(value, axis, [(target, source) for source, target in pairs])  30.4 us
    ppermute x3, starting transfers between devices, chip_fetch(): return lax.ppermute(value, axis, chip_pairs(lax.axis_size(axis), step))  26.3 us
    ppermute x12, waiting for transfers between devices, cycled(): lax.ppermute(value, axis, [(source, (source + steps) % count) for source...  25.1 us
    pallas_call x1, Pallas kernels, local_grads(): pl.pallas_call(kernel, grid_spec=pltpu.PrefetchScalarGridSpec(num_scalar_...  16.1 us
    ppermute x3, waiting for transfers between devices, chip_return(): lax.ppermute(value, axis, [(target, source) for source, target in pairs])  11.4 us
    ppermute x3, waiting for transfers between devices, chip_fetch(): return lax.ppermute(value, axis, chip_pairs(lax.axis_size(axis), step))  10.7 us
    ppermute x2, starting transfers between devices, swap_cores(): lax.ppermute(value, axis, [(source, source ^ 1) for source in range(count)])  4.1 us
  transfers between devices with their start and end apart: 20, of which 17 were waited for; matrix products, arithmetic and copies ran while one was open for 3% of the time, Pallas kernels for 0%

profile of v10, /device:TPU:6, one launch (start us, length us, event | category | flops | bytes accessed | tf_op | source)
XLA Modules:
  0.0 183.5 jit_solution(5251338633176765778)
XLA Ops:
  0.7 1.0 constant_dynamic-slice_fusion
  1.7 0.5 fusion.6
  2.2 8.5 %collective-permute-start = (bf16[2,128,128]{2,1,0:T(8,128)(2,1)S(1)}, bf16[2,128,128]{2,1,0:T(8,128)(2,1)S(1)}, u32[]{:S(2)}, u32[]{:S(2)}) collective-permute-start(bf16[2,128,128]{2,1,0:T(8,128)(2,1)S(1)} %slice.70), channel_id=1, source_target_pairs={{16,32},{48,64},{80,96},{112,128},{144,160},{176,192},{208,224},{2... | collective-permute-start | bytes 196616 | tf_op jit(solution)/shard_map/ppermute | solution.py:29
  10.7 6.1 %collective-permute-done = bf16[2,128,128]{2,1,0:T(8,128)(2,1)S(1)} collective-permute-done((bf16[2,128,128]{2,1,0:T(8,128)(2,1)S(1)}, bf16[2,128,128]{2,1,0:T(8,128)(2,1)S(1)}, u32[]{:S(2)}, u32[]{:S(2)}) %collective-permute-start) | collective-permute-done | bytes 65568 | tf_op jit(solution)/shard_map/ppermute | solution.py:29
  16.8 8.9 %collective-permute-start.1 = (bf16[2,128,128]{2,1,0:T(8,128)(2,1)S(1)}, bf16[2,128,128]{2,1,0:T(8,128)(2,1)S(1)}, u32[]{:S(2)}, u32[]{:S(2)}) collective-permute-start(bf16[2,128,128]{2,1,0:T(8,128)(2,1)S(1)} %collective-permute-done), channel_id=1, source_target_pairs={{16,32},{48,64},{80,96},{112,128},{144,160},{176,192},{208,224},{2... | collective-permute-start | bytes 196616 | tf_op jit(solution)/shard_map/ppermute | solution.py:29
  25.8 0.8 constant_dynamic-slice_fusion.2
  26.5 1.4 collective-permute-done.1
  27.9 8.9 %collective-permute-start.2 = (bf16[2,128,128]{2,1,0:T(8,128)(2,1)S(1)}, bf16[2,128,128]{2,1,0:T(8,128)(2,1)S(1)}, u32[]{:S(2)}, u32[]{:S(2)}) collective-permute-start(bf16[2,128,128]{2,1,0:T(8,128)(2,1)S(1)} %collective-permute-done.1), channel_id=1, source_target_pairs={{16,32},{48,64},{80,96},{112,128},{144,160},{176,192},{208,224},{2... | collective-permute-start | bytes 196616 | tf_op jit(solution)/shard_map/ppermute | solution.py:29
  36.9 0.1 reshape.260
  36.9 3.2 %collective-permute-done.2 = bf16[2,128,128]{2,1,0:T(8,128)(2,1)S(1)} collective-permute-done((bf16[2,128,128]{2,1,0:T(8,128)(2,1)S(1)}, bf16[2,128,128]{2,1,0:T(8,128)(2,1)S(1)}, u32[]{:S(2)}, u32[]{:S(2)}) %collective-permute-start.2) | collective-permute-done | bytes 65568 | tf_op jit(solution)/shard_map/ppermute | solution.py:29
  40.1 3.5 %collective-permute-start.5 = (bf16[3,2,128,128]{3,2,1,0:T(8,128)(2,1)S(1)}, bf16[3,2,128,128]{3,2,1,0:T(8,128)(2,1)S(1)}, u32[]{:S(2)}, u32[]{:S(2)}) collective-permute-start(bf16[3,2,128,128]{3,2,1,0:T(8,128)(2,1)S(1)} %pad_maximum_fusion.4), channel_id=1, source_target_pairs={{0,1},{1,2},{2,3},{3,0},{4,5},{5,6},{6,7},{7,4},{8,9},{9,10},{10,1... | collective-permute-start | bytes 589832 | tf_op jit(solution)/shard_map/ppermute | solution.py:19
  43.6 4.8 %collective-permute-start.4 = (bf16[3,2,128,128]{3,2,1,0:T(8,128)(2,1)S(1)}, bf16[3,2,128,128]{3,2,1,0:T(8,128)(2,1)S(1)}, u32[]{:S(2)}, u32[]{:S(2)}) collective-permute-start(bf16[3,2,128,128]{3,2,1,0:T(8,128)(2,1)S(1)} %pad_maximum_fusion.4), channel_id=1, source_target_pairs={{0,2},{1,3},{2,0},{3,1},{4,6},{5,7},{6,4},{7,5},{8,10},{9,11},{10,... | collective-permute-start | bytes 589832 | tf_op jit(solution)/shard_map/ppermute | solution.py:19
  48.4 3.3 %collective-permute-start.3 = (bf16[3,2,128,128]{3,2,1,0:T(8,128)(2,1)S(1)}, bf16[3,2,128,128]{3,2,1,0:T(8,128)(2,1)S(1)}, u32[]{:S(2)}, u32[]{:S(2)}) collective-permute-start(bf16[3,2,128,128]{3,2,1,0:T(8,128)(2,1)S(1)} %pad_maximum_fusion.4), channel_id=1, source_target_pairs={{0,3},{1,0},{2,1},{3,2},{4,7},{5,4},{6,5},{7,6},{8,11},{9,8},{10,9... | collective-permute-start | bytes 589832 | tf_op jit(solution)/shard_map/ppermute | solution.py:19
  51.7 1.2 gather_fusion
  53.0 1.2 gather_fusion.1
  54.2 0.5 fusion.39
  54.7 0.9 collective-permute-done.4
  55.6 1.3 collective-permute-done.3
  57.0 1.9 %collective-permute-start.6 = (bf16[4,2,512,128]{3,2,1,0:T(8,128)(2,1)S(1)}, bf16[4,2,512,128]{3,2,1,0:T(8,128)(2,1)S(1)}, u32[]{:S(2)}, u32[]{:S(2)}) collective-permute-start(bf16[4,2,512,128]{3,2,1,0:T(8,128)(2,1)S(1)} %maximum_maximum_fusion), channel_id=1, source_target_pairs={{0,16},{16,0},{32,48},{48,32},{64,80},{80,64},{96,112},{112,96},{1... | collective-permute-start | bytes 3145736 | tf_op jit(solution)/shard_map/ppermute | solution.py:39
  58.9 0.1 reshape.287
  59.0 0.1 fusion.24
  59.1 0.1 broadcast_in_dim.47
  59.2 0.1 eq.59
  59.3 0.1 broadcast_in_dim.49
  59.4 0.1 eq.60
  59.6 0.6 fusion.23.slots_ref
  60.2 0.7 select_select_fusion.code_ref
  60.9 0.7 collective-permute-done.6
  61.5 0.2 pad_maximum_fusion.1
  61.7 1.5 fusion.37
  63.2 16.1 %shard_map.103 = (bf16[2048,128]{1,0:T(8,128)(2,1)}, f32[4096,128]{1,0:T(8,128)}, f32[4096,128]{1,0:T(8,128)}) custom-call(s32[8,16]{1,0:T(8,128)} %fusion.23.slots_ref, bf16[2048,128]{1,0:T(8,128)(2,1)} %bitcast.85, bf16[2048,128]{1,0:T(8,128)(2,1)} %bitcast.86, s32[8,1,1024]{2,1,0:T(1,128)} %select_select_fusion.code_ref, bf16[4096,128]{1,0:T(8,128)(2,1)} %bitcast.73, ...), custom_call_target="tpu_custom_call" | custom-call | tf_op jit(solution)/shard_map/pallas_call | solution.py:105
  79.3 1.8 %fusion.2 = bf16[2,4,512,128]{3,2,1,0:T(8,128)(2,1)S(1)} fusion(f32[1,8,512,128]{3,2,1,0:T(8,128)} %bitcast.68, f32[1,8,512,128]{3,2,1,0:T(8,128)} %bitcast.66), kind=kLoop, calls=%fused_computation.8 | loop fusion | flops 524288 | bytes 5242880 | tf_op jit(solution)/shard_map/convert.2
  81.2 2.2 %collective-permute-start.7 = (bf16[2,4,512,128]{3,2,1,0:T(8,128)(2,1)S(1)}, bf16[2,4,512,128]{3,2,1,0:T(8,128)(2,1)S(1)}, u32[]{:S(2)}, u32[]{:S(2)}) collective-permute-start(bf16[2,4,512,128]{3,2,1,0:T(8,128)(2,1)S(1)} %fusion.2), channel_id=1, source_target_pairs={{0,16},{16,0},{32,48},{48,32},{64,80},{80,64},{96,112},{112,96},{1... | collective-permute-start | bytes 3145736 | tf_op jit(solution)/shard_map/ppermute | solution.py:39
  83.4 2.5 %collective-permute-done.7 = bf16[2,4,512,128]{3,2,1,0:T(8,128)(2,1)S(1)} collective-permute-done((bf16[2,4,512,128]{3,2,1,0:T(8,128)(2,1)S(1)}, bf16[2,4,512,128]{3,2,1,0:T(8,128)(2,1)S(1)}, u32[]{:S(2)}, u32[]{:S(2)}) %collective-permute-start.7) | collective-permute-done | bytes 1048608 | tf_op jit(solution)/shard_map/ppermute | solution.py:39
  85.9 0.3 fusion.34
  86.3 4.6 %collective-permute-start.10 = (bf16[2,4,128,128]{3,2,1,0:T(8,128)(2,1)S(1)}, bf16[2,4,128,128]{3,2,1,0:T(8,128)(2,1)S(1)}, u32[]{:S(2)}, u32[]{:S(2)}) collective-permute-start(bf16[2,4,128,128]{3,2,1,0:T(8,128)(2,1)S(1)} %get-tuple-element.19), channel_id=1, source_target_pairs={{0,3},{1,0},{2,1},{3,2},{4,7},{5,4},{6,5},{7,6},{8,11},{9,8},{10,9... | collective-permute-start | bytes 786440 | tf_op jit(solution)/shard_map/ppermute | solution.py:19
  90.8 3.8 %collective-permute-start.9 = (bf16[2,4,128,128]{3,2,1,0:T(8,128)(2,1)S(1)}, bf16[2,4,128,128]{3,2,1,0:T(8,128)(2,1)S(1)}, u32[]{:S(2)}, u32[]{:S(2)}) collective-permute-start(bf16[2,4,128,128]{3,2,1,0:T(8,128)(2,1)S(1)} %get-tuple-element.20), channel_id=1, source_target_pairs={{0,2},{1,3},{2,0},{3,1},{4,6},{5,7},{6,4},{7,5},{8,10},{9,11},{10,... | collective-permute-start | bytes 786440 | tf_op jit(solution)/shard_map/ppermute | solution.py:19
  94.7 1.9 %collective-permute-start.8 = (bf16[2,4,128,128]{3,2,1,0:T(8,128)(2,1)S(1)}, bf16[2,4,128,128]{3,2,1,0:T(8,128)(2,1)S(1)}, u32[]{:S(2)}, u32[]{:S(2)}) collective-permute-start(bf16[2,4,128,128]{3,2,1,0:T(8,128)(2,1)S(1)} %get-tuple-element.18), channel_id=1, source_target_pairs={{0,1},{1,2},{2,3},{3,0},{4,5},{5,6},{6,7},{7,4},{8,9},{9,10},{10,1... | collective-permute-start | bytes 786440 | tf_op jit(solution)/shard_map/ppermute | solution.py:19
  96.6 5.7 %collective-permute-done.10 = bf16[2,4,128,128]{3,2,1,0:T(8,128)(2,1)S(1)} collective-permute-done((bf16[2,4,128,128]{3,2,1,0:T(8,128)(2,1)S(1)}, bf16[2,4,128,128]{3,2,1,0:T(8,128)(2,1)S(1)}, u32[]{:S(2)}, u32[]{:S(2)}) %collective-permute-start.10) | collective-permute-done | bytes 262176 | tf_op jit(solution)/shard_map/ppermute | solution.py:19
  102.3 1.1 collective-permute-done.9
  103.4 4.5 %collective-permute-done.8 = bf16[2,4,128,128]{3,2,1,0:T(8,128)(2,1)S(1)} collective-permute-done((bf16[2,4,128,128]{3,2,1,0:T(8,128)(2,1)S(1)}, bf16[2,4,128,128]{3,2,1,0:T(8,128)(2,1)S(1)}, u32[]{:S(2)}, u32[]{:S(2)}) %collective-permute-start.8) | collective-permute-done | bytes 262176 | tf_op jit(solution)/shard_map/ppermute | solution.py:19
  107.9 0.1 fusion.4
  108.1 12.8 %collective-permute-start.11 = (bf16[2,128,128]{2,1,0:T(8,128)(2,1)S(1)}, bf16[2,128,128]{2,1,0:T(8,128)(2,1)S(1)}, u32[]{:S(2)}, u32[]{:S(2)}) collective-permute-start(bf16[2,128,128]{2,1,0:T(8,128)(2,1)S(1)} %fusion.14), channel_id=1, source_target_pairs={{32,16},{64,48},{96,80},{128,112},{160,144},{192,176},{224,208},{2... | collective-permute-start | bytes 196616 | tf_op jit(solution)/shard_map/ppermute | solution.py:34
  120.9 3.8 %collective-permute-done.11 = bf16[2,128,128]{2,1,0:T(8,128)(2,1)S(1)} collective-permute-done((bf16[2,128,128]{2,1,0:T(8,128)(2,1)S(1)}, bf16[2,128,128]{2,1,0:T(8,128)(2,1)S(1)}, u32[]{:S(2)}, u32[]{:S(2)}) %collective-permute-start.11) | collective-permute-done | bytes 65568 | tf_op jit(solution)/shard_map/ppermute | solution.py:34
  124.7 8.7 %collective-permute-start.12 = (bf16[2,128,128]{2,1,0:T(8,128)(2,1)S(1)}, bf16[2,128,128]{2,1,0:T(8,128)(2,1)S(1)}, u32[]{:S(2)}, u32[]{:S(2)}) collective-permute-start(bf16[2,128,128]{2,1,0:T(8,128)(2,1)S(1)} %fusion.9), channel_id=1, source_target_pairs={{32,16},{64,48},{96,80},{128,112},{160,144},{192,176},{224,208},{2... | collective-permute-start | bytes 196616 | tf_op jit(solution)/shard_map/ppermute | solution.py:34
  133.5 3.6 %collective-permute-done.12 = bf16[2,128,128]{2,1,0:T(8,128)(2,1)S(1)} collective-permute-done((bf16[2,128,128]{2,1,0:T(8,128)(2,1)S(1)}, bf16[2,128,128]{2,1,0:T(8,128)(2,1)S(1)}, u32[]{:S(2)}, u32[]{:S(2)}) %collective-permute-start.12) | collective-permute-done | bytes 65568 | tf_op jit(solution)/shard_map/ppermute | solution.py:34
  137.1 8.9 %collective-permute-start.13 = (bf16[2,128,128]{2,1,0:T(8,128)(2,1)S(1)}, bf16[2,128,128]{2,1,0:T(8,128)(2,1)S(1)}, u32[]{:S(2)}, u32[]{:S(2)}) collective-permute-start(bf16[2,128,128]{2,1,0:T(8,128)(2,1)S(1)} %fusion.11), channel_id=1, source_target_pairs={{32,16},{64,48},{96,80},{128,112},{160,144},{192,176},{224,208},{2... | collective-permute-start | bytes 196616 | tf_op jit(solution)/shard_map/ppermute | solution.py:34
  146.0 0.1 add.179
  146.1 4.0 %collective-permute-done.13 = bf16[2,128,128]{2,1,0:T(8,128)(2,1)S(1)} collective-permute-done((bf16[2,128,128]{2,1,0:T(8,128)(2,1)S(1)}, bf16[2,128,128]{2,1,0:T(8,128)(2,1)S(1)}, u32[]{:S(2)}, u32[]{:S(2)}) %collective-permute-start.13) | collective-permute-done | bytes 65568 | tf_op jit(solution)/shard_map/ppermute | solution.py:34
  150.1 1.9 %collective-permute-start.16 = (bf16[2,128,128]{2,1,0:T(8,128)(2,1)S(1)}, bf16[2,128,128]{2,1,0:T(8,128)(2,1)S(1)}, u32[]{:S(2)}, u32[]{:S(2)}) collective-permute-start(bf16[2,128,128]{2,1,0:T(8,128)(2,1)S(1)} %fusion.13), channel_id=1, source_target_pairs={{0,4},{4,8},{8,12},{12,0},{1,5},{5,9},{9,13},{13,1},{2,6},{6,10},{... | collective-permute-start | bytes 196616 | tf_op jit(solution)/shard_map/ppermute | solution.py:19
  152.1 1.9 %collective-permute-start.15 = (bf16[2,128,128]{2,1,0:T(8,128)(2,1)S(1)}, bf16[2,128,128]{2,1,0:T(8,128)(2,1)S(1)}, u32[]{:S(2)}, u32[]{:S(2)}) collective-permute-start(bf16[2,128,128]{2,1,0:T(8,128)(2,1)S(1)} %fusion.13), channel_id=1, source_target_pairs={{0,8},{4,12},{8,0},{12,4},{1,9},{5,13},{9,1},{13,5},{2,10},{6,14},... | collective-permute-start | bytes 196616 | tf_op jit(solution)/shard_map/ppermute | solution.py:19
  154.0 5.7 %collective-permute-start.14 = (bf16[2,128,128]{2,1,0:T(8,128)(2,1)S(1)}, bf16[2,128,128]{2,1,0:T(8,128)(2,1)S(1)}, u32[]{:S(2)}, u32[]{:S(2)}) collective-permute-start(bf16[2,128,128]{2,1,0:T(8,128)(2,1)S(1)} %fusion.13), channel_id=1, source_target_pairs={{0,12},{4,0},{8,4},{12,8},{1,13},{5,1},{9,5},{13,9},{2,14},{6,2},{... | collective-permute-start | bytes 196616 | tf_op jit(solution)/shard_map/ppermute | solution.py:19
  159.7 1.2 collective-permute-done.15
  160.9 1.6 collective-permute-done.14
  162.6 1.9 %collective-permute-start.19 = (bf16[4,2,128,128]{3,2,1,0:T(8,128)(2,1)S(1)}, bf16[4,2,128,128]{3,2,1,0:T(8,128)(2,1)S(1)}, u32[]{:S(2)}, u32[]{:S(2)}) collective-permute-start(bf16[4,2,128,128]{3,2,1,0:T(8,128)(2,1)S(1)} %get-tuple-element.22), channel_id=1, source_target_pairs={{0,1},{1,2},{2,3},{3,0},{4,5},{5,6},{6,7},{7,4},{8,9},{9,10},{10,1... | collective-permute-start | bytes 786440 | tf_op jit(solution)/shard_map/ppermute | solution.py:19
  164.5 3.0 %collective-permute-start.18 = (bf16[4,2,128,128]{3,2,1,0:T(8,128)(2,1)S(1)}, bf16[4,2,128,128]{3,2,1,0:T(8,128)(2,1)S(1)}, u32[]{:S(2)}, u32[]{:S(2)}) collective-permute-start(bf16[4,2,128,128]{3,2,1,0:T(8,128)(2,1)S(1)} %get-tuple-element.22), channel_id=1, source_target_pairs={{0,2},{1,3},{2,0},{3,1},{4,6},{5,7},{6,4},{7,5},{8,10},{9,11},{10,... | collective-permute-start | bytes 786440 | tf_op jit(solution)/shard_map/ppermute | solution.py:19
  167.5 4.5 %collective-permute-start.17 = (bf16[4,2,128,128]{3,2,1,0:T(8,128)(2,1)S(1)}, bf16[4,2,128,128]{3,2,1,0:T(8,128)(2,1)S(1)}, u32[]{:S(2)}, u32[]{:S(2)}) collective-permute-start(bf16[4,2,128,128]{3,2,1,0:T(8,128)(2,1)S(1)} %get-tuple-element.22), channel_id=1, source_target_pairs={{0,3},{1,0},{2,1},{3,2},{4,7},{5,4},{6,5},{7,6},{8,11},{9,8},{10,9... | collective-permute-start | bytes 786440 | tf_op jit(solution)/shard_map/ppermute | solution.py:19
  172.0 0.1 compare_and_fusion
  172.1 6.3 %collective-permute-done.19 = bf16[4,2,128,128]{3,2,1,0:T(8,128)(2,1)S(1)} collective-permute-done((bf16[4,2,128,128]{3,2,1,0:T(8,128)(2,1)S(1)}, bf16[4,2,128,128]{3,2,1,0:T(8,128)(2,1)S(1)}, u32[]{:S(2)}, u32[]{:S(2)}) %collective-permute-start.19) | collective-permute-done | bytes 262176 | tf_op jit(solution)/shard_map/ppermute | solution.py:19
  178.4 2.5 %collective-permute-done.17 = bf16[4,2,128,128]{3,2,1,0:T(8,128)(2,1)S(1)} collective-permute-done((bf16[4,2,128,128]{3,2,1,0:T(8,128)(2,1)S(1)}, bf16[4,2,128,128]{3,2,1,0:T(8,128)(2,1)S(1)}, u32[]{:S(2)}, u32[]{:S(2)}) %collective-permute-start.17) | collective-permute-done | bytes 262176 | tf_op jit(solution)/shard_map/ppermute | solution.py:19
  180.9 0.1 pad_maximum_fusion.2
  181.0 0.7 gather_fusion.2
  181.9 0.2 convert_bitcast_fusion
  182.1 1.5 fusion.36
  (32 shorter events, 0.6 us)
Async XLA Ops:
  0.6 51.1 %copy-start.1 = (s32[7]{0:T(128)S(1)}, s32[7]{0:T(128)}, u32[]{:S(2)}) copy-start(s32[7]{0:T(128)} %constant.156.clone) | copy-start | bytes 88
  2.2 14.7 %collective-permute-start = (bf16[2,128,128]{2,1,0:T(8,128)(2,1)S(1)}, bf16[2,128,128]{2,1,0:T(8,128)(2,1)S(1)}, u32[]{:S(2)}, u32[]{:S(2)}) collective-permute-start(bf16[2,128,128]{2,1,0:T(8,128)(2,1)S(1)} %slice.70), channel_id=1, source_target_pairs={{16,32},{48,64},{80,96},{112,128},{144,160},{176,192},{208,224},{2... | collective-permute-start | bytes 196616 | tf_op jit(solution)/shard_map/ppermute | solution.py:29
  16.8 11.1 %collective-permute-start.1 = (bf16[2,128,128]{2,1,0:T(8,128)(2,1)S(1)}, bf16[2,128,128]{2,1,0:T(8,128)(2,1)S(1)}, u32[]{:S(2)}, u32[]{:S(2)}) collective-permute-start(bf16[2,128,128]{2,1,0:T(8,128)(2,1)S(1)} %collective-permute-done), channel_id=1, source_target_pairs={{16,32},{48,64},{80,96},{112,128},{144,160},{176,192},{208,224},{2... | collective-permute-start | bytes 196616 | tf_op jit(solution)/shard_map/ppermute | solution.py:29
  27.9 12.2 %collective-permute-start.2 = (bf16[2,128,128]{2,1,0:T(8,128)(2,1)S(1)}, bf16[2,128,128]{2,1,0:T(8,128)(2,1)S(1)}, u32[]{:S(2)}, u32[]{:S(2)}) collective-permute-start(bf16[2,128,128]{2,1,0:T(8,128)(2,1)S(1)} %collective-permute-done.1), channel_id=1, source_target_pairs={{16,32},{48,64},{80,96},{112,128},{144,160},{176,192},{208,224},{2... | collective-permute-start | bytes 196616 | tf_op jit(solution)/shard_map/ppermute | solution.py:29
  40.1 14.6 %collective-permute-start.5 = (bf16[3,2,128,128]{3,2,1,0:T(8,128)(2,1)S(1)}, bf16[3,2,128,128]{3,2,1,0:T(8,128)(2,1)S(1)}, u32[]{:S(2)}, u32[]{:S(2)}) collective-permute-start(bf16[3,2,128,128]{3,2,1,0:T(8,128)(2,1)S(1)} %pad_maximum_fusion.4), channel_id=1, source_target_pairs={{0,1},{1,2},{2,3},{3,0},{4,5},{5,6},{6,7},{7,4},{8,9},{9,10},{10,1... | collective-permute-start | bytes 589832 | tf_op jit(solution)/shard_map/ppermute | solution.py:19
  43.6 12.0 %collective-permute-start.4 = (bf16[3,2,128,128]{3,2,1,0:T(8,128)(2,1)S(1)}, bf16[3,2,128,128]{3,2,1,0:T(8,128)(2,1)S(1)}, u32[]{:S(2)}, u32[]{:S(2)}) collective-permute-start(bf16[3,2,128,128]{3,2,1,0:T(8,128)(2,1)S(1)} %pad_maximum_fusion.4), channel_id=1, source_target_pairs={{0,2},{1,3},{2,0},{3,1},{4,6},{5,7},{6,4},{7,5},{8,10},{9,11},{10,... | collective-permute-start | bytes 589832 | tf_op jit(solution)/shard_map/ppermute | solution.py:19
  48.4 8.5 %collective-permute-start.3 = (bf16[3,2,128,128]{3,2,1,0:T(8,128)(2,1)S(1)}, bf16[3,2,128,128]{3,2,1,0:T(8,128)(2,1)S(1)}, u32[]{:S(2)}, u32[]{:S(2)}) collective-permute-start(bf16[3,2,128,128]{3,2,1,0:T(8,128)(2,1)S(1)} %pad_maximum_fusion.4), channel_id=1, source_target_pairs={{0,3},{1,0},{2,1},{3,2},{4,7},{5,4},{6,5},{7,6},{8,11},{9,8},{10,9... | collective-permute-start | bytes 589832 | tf_op jit(solution)/shard_map/ppermute | solution.py:19
  51.7 1.2 copy-start
  57.0 4.6 %collective-permute-start.6 = (bf16[4,2,512,128]{3,2,1,0:T(8,128)(2,1)S(1)}, bf16[4,2,512,128]{3,2,1,0:T(8,128)(2,1)S(1)}, u32[]{:S(2)}, u32[]{:S(2)}) collective-permute-start(bf16[4,2,512,128]{3,2,1,0:T(8,128)(2,1)S(1)} %maximum_maximum_fusion), channel_id=1, source_target_pairs={{0,16},{16,0},{32,48},{48,32},{64,80},{80,64},{96,112},{112,96},{1... | collective-permute-start | bytes 3145736 | tf_op jit(solution)/shard_map/ppermute | solution.py:39
  79.3 6.5 %copy-start.2 = (f32[4096,128]{1,0:T(8,128)S(1)}, f32[4096,128]{1,0:T(8,128)}, u32[]{:S(2)}) copy-start(f32[4096,128]{1,0:T(8,128)} %get-tuple-element.7) | copy-start | bytes 6291460
  79.3 6.5 %copy-start.3 = (f32[4096,128]{1,0:T(8,128)S(1)}, f32[4096,128]{1,0:T(8,128)}, u32[]{:S(2)}) copy-start(f32[4096,128]{1,0:T(8,128)} %get-tuple-element.8) | copy-start | bytes 6291460
  81.2 4.7 %collective-permute-start.7 = (bf16[2,4,512,128]{3,2,1,0:T(8,128)(2,1)S(1)}, bf16[2,4,512,128]{3,2,1,0:T(8,128)(2,1)S(1)}, u32[]{:S(2)}, u32[]{:S(2)}) collective-permute-start(bf16[2,4,512,128]{3,2,1,0:T(8,128)(2,1)S(1)} %fusion.2), channel_id=1, source_target_pairs={{0,16},{16,0},{32,48},{48,32},{64,80},{80,64},{96,112},{112,96},{1... | collective-permute-start | bytes 3145736 | tf_op jit(solution)/shard_map/ppermute | solution.py:39
  86.3 16.1 %collective-permute-start.10 = (bf16[2,4,128,128]{3,2,1,0:T(8,128)(2,1)S(1)}, bf16[2,4,128,128]{3,2,1,0:T(8,128)(2,1)S(1)}, u32[]{:S(2)}, u32[]{:S(2)}) collective-permute-start(bf16[2,4,128,128]{3,2,1,0:T(8,128)(2,1)S(1)} %get-tuple-element.19), channel_id=1, source_target_pairs={{0,3},{1,0},{2,1},{3,2},{4,7},{5,4},{6,5},{7,6},{8,11},{9,8},{10,9... | collective-permute-start | bytes 786440 | tf_op jit(solution)/shard_map/ppermute | solution.py:19
  90.8 12.6 %collective-permute-start.9 = (bf16[2,4,128,128]{3,2,1,0:T(8,128)(2,1)S(1)}, bf16[2,4,128,128]{3,2,1,0:T(8,128)(2,1)S(1)}, u32[]{:S(2)}, u32[]{:S(2)}) collective-permute-start(bf16[2,4,128,128]{3,2,1,0:T(8,128)(2,1)S(1)} %get-tuple-element.20), channel_id=1, source_target_pairs={{0,2},{1,3},{2,0},{3,1},{4,6},{5,7},{6,4},{7,5},{8,10},{9,11},{10,... | collective-permute-start | bytes 786440 | tf_op jit(solution)/shard_map/ppermute | solution.py:19
  94.7 13.3 %collective-permute-start.8 = (bf16[2,4,128,128]{3,2,1,0:T(8,128)(2,1)S(1)}, bf16[2,4,128,128]{3,2,1,0:T(8,128)(2,1)S(1)}, u32[]{:S(2)}, u32[]{:S(2)}) collective-permute-start(bf16[2,4,128,128]{3,2,1,0:T(8,128)(2,1)S(1)} %get-tuple-element.18), channel_id=1, source_target_pairs={{0,1},{1,2},{2,3},{3,0},{4,5},{5,6},{6,7},{7,4},{8,9},{9,10},{10,1... | collective-permute-start | bytes 786440 | tf_op jit(solution)/shard_map/ppermute | solution.py:19
  108.1 16.6 %collective-permute-start.11 = (bf16[2,128,128]{2,1,0:T(8,128)(2,1)S(1)}, bf16[2,128,128]{2,1,0:T(8,128)(2,1)S(1)}, u32[]{:S(2)}, u32[]{:S(2)}) collective-permute-start(bf16[2,128,128]{2,1,0:T(8,128)(2,1)S(1)} %fusion.14), channel_id=1, source_target_pairs={{32,16},{64,48},{96,80},{128,112},{160,144},{192,176},{224,208},{2... | collective-permute-start | bytes 196616 | tf_op jit(solution)/shard_map/ppermute | solution.py:34
  124.7 12.3 %collective-permute-start.12 = (bf16[2,128,128]{2,1,0:T(8,128)(2,1)S(1)}, bf16[2,128,128]{2,1,0:T(8,128)(2,1)S(1)}, u32[]{:S(2)}, u32[]{:S(2)}) collective-permute-start(bf16[2,128,128]{2,1,0:T(8,128)(2,1)S(1)} %fusion.9), channel_id=1, source_target_pairs={{32,16},{64,48},{96,80},{128,112},{160,144},{192,176},{224,208},{2... | collective-permute-start | bytes 196616 | tf_op jit(solution)/shard_map/ppermute | solution.py:34
  137.1 13.1 %collective-permute-start.13 = (bf16[2,128,128]{2,1,0:T(8,128)(2,1)S(1)}, bf16[2,128,128]{2,1,0:T(8,128)(2,1)S(1)}, u32[]{:S(2)}, u32[]{:S(2)}) collective-permute-start(bf16[2,128,128]{2,1,0:T(8,128)(2,1)S(1)} %fusion.11), channel_id=1, source_target_pairs={{32,16},{64,48},{96,80},{128,112},{160,144},{192,176},{224,208},{2... | collective-permute-start | bytes 196616 | tf_op jit(solution)/shard_map/ppermute | solution.py:34
  150.1 9.6 %collective-permute-start.16 = (bf16[2,128,128]{2,1,0:T(8,128)(2,1)S(1)}, bf16[2,128,128]{2,1,0:T(8,128)(2,1)S(1)}, u32[]{:S(2)}, u32[]{:S(2)}) collective-permute-start(bf16[2,128,128]{2,1,0:T(8,128)(2,1)S(1)} %fusion.13), channel_id=1, source_target_pairs={{0,4},{4,8},{8,12},{12,0},{1,5},{5,9},{9,13},{13,1},{2,6},{6,10},{... | collective-permute-start | bytes 196616 | tf_op jit(solution)/shard_map/ppermute | solution.py:19
  152.1 8.9 %collective-permute-start.15 = (bf16[2,128,128]{2,1,0:T(8,128)(2,1)S(1)}, bf16[2,128,128]{2,1,0:T(8,128)(2,1)S(1)}, u32[]{:S(2)}, u32[]{:S(2)}) collective-permute-start(bf16[2,128,128]{2,1,0:T(8,128)(2,1)S(1)} %fusion.13), channel_id=1, source_target_pairs={{0,8},{4,12},{8,0},{12,4},{1,9},{5,13},{9,1},{13,5},{2,10},{6,14},... | collective-permute-start | bytes 196616 | tf_op jit(solution)/shard_map/ppermute | solution.py:19
  154.0 8.5 %collective-permute-start.14 = (bf16[2,128,128]{2,1,0:T(8,128)(2,1)S(1)}, bf16[2,128,128]{2,1,0:T(8,128)(2,1)S(1)}, u32[]{:S(2)}, u32[]{:S(2)}) collective-permute-start(bf16[2,128,128]{2,1,0:T(8,128)(2,1)S(1)} %fusion.13), channel_id=1, source_target_pairs={{0,12},{4,0},{8,4},{12,8},{1,13},{5,1},{9,5},{13,9},{2,14},{6,2},{... | collective-permute-start | bytes 196616 | tf_op jit(solution)/shard_map/ppermute | solution.py:19
  162.6 15.8 %collective-permute-start.19 = (bf16[4,2,128,128]{3,2,1,0:T(8,128)(2,1)S(1)}, bf16[4,2,128,128]{3,2,1,0:T(8,128)(2,1)S(1)}, u32[]{:S(2)}, u32[]{:S(2)}) collective-permute-start(bf16[4,2,128,128]{3,2,1,0:T(8,128)(2,1)S(1)} %get-tuple-element.22), channel_id=1, source_target_pairs={{0,1},{1,2},{2,3},{3,0},{4,5},{5,6},{6,7},{7,4},{8,9},{9,10},{10,1... | collective-permute-start | bytes 786440 | tf_op jit(solution)/shard_map/ppermute | solution.py:19
  164.5 13.9 %collective-permute-start.18 = (bf16[4,2,128,128]{3,2,1,0:T(8,128)(2,1)S(1)}, bf16[4,2,128,128]{3,2,1,0:T(8,128)(2,1)S(1)}, u32[]{:S(2)}, u32[]{:S(2)}) collective-permute-start(bf16[4,2,128,128]{3,2,1,0:T(8,128)(2,1)S(1)} %get-tuple-element.22), channel_id=1, source_target_pairs={{0,2},{1,3},{2,0},{3,1},{4,6},{5,7},{6,4},{7,5},{8,10},{9,11},{10,... | collective-permute-start | bytes 786440 | tf_op jit(solution)/shard_map/ppermute | solution.py:19
  167.5 13.4 %collective-permute-start.17 = (bf16[4,2,128,128]{3,2,1,0:T(8,128)(2,1)S(1)}, bf16[4,2,128,128]{3,2,1,0:T(8,128)(2,1)S(1)}, u32[]{:S(2)}, u32[]{:S(2)}) collective-permute-start(bf16[4,2,128,128]{3,2,1,0:T(8,128)(2,1)S(1)} %get-tuple-element.22), channel_id=1, source_target_pairs={{0,3},{1,0},{2,1},{3,2},{4,7},{5,4},{6,5},{7,6},{8,11},{9,8},{10,9... | collective-permute-start | bytes 786440 | tf_op jit(solution)/shard_map/ppermute | solution.py:19

commit v11 on v9

--- a/solution.py
+++ b/solution.py
@@ -39,20 +39,32 @@
     return lax.ppermute(value, axis, [(source, source ^ 1) for source in range(count)])
 
 
-def block_kernel(slots_ref, q_ref, do_ref, code_ref, k_ref, v_ref, dq_ref, dk_ref, dv_ref,
+def block_kernel(slots_ref, q_ref, do_ref, code_ref, near_ref, far_ref, dq_ref, dkv_ref,
                  k_sel, v_sel, *, inv_root, heads_here):
     step = pl.program_id(0)
     slots = k_sel.shape[0] // BLOCK
+    half, per_tile = near_ref.shape[0], near_ref.shape[2] // BLOCK
 
     @pl.when(step == 0)
     def _():
-        dk_ref[...] = jnp.zeros_like(dk_ref)
-        dv_ref[...] = jnp.zeros_like(dv_ref)
+        dkv_ref[...] = jnp.zeros_like(dkv_ref)
 
     for slot in range(slots):
-        start = pl.multiple_of(slots_ref[step, slot] * BLOCK, BLOCK)
-        k_sel[slot * BLOCK:(slot + 1) * BLOCK, :] = k_ref[pl.ds(start, BLOCK), :]
-        v_sel[slot * BLOCK:(slot + 1) * BLOCK, :] = v_ref[pl.ds(start, BLOCK), :]
+        tile = slots_ref[step, slot] // per_tile
+        row = pl.multiple_of(slots_ref[step, slot] % per_tile * BLOCK, BLOCK)
+        target = slice(slot * BLOCK, (slot + 1) * BLOCK)
+
+        @pl.when(tile < half)
+        def _():
+            here = jnp.minimum(tile, half - 1)
+            k_sel[target, :] = near_ref[here, 0, pl.ds(row, BLOCK), :]
+            v_sel[target, :] = near_ref[here, 1, pl.ds(row, BLOCK), :]
+
+        @pl.when(tile >= half)
+        def _():
+            there = jnp.maximum(tile - half, 0)
+            k_sel[target, :] = far_ref[there, 0, pl.ds(row, BLOCK), :]
+            v_sel[target, :] = far_ref[there, 1, pl.ds(row, BLOCK), :]
     q = q_ref[...]
     do = do_ref[...]
     keys = k_sel[...]
@@ -84,16 +96,15 @@
     )
     for slot in range(slots):
         start = pl.multiple_of(slots_ref[step, slot] * BLOCK, BLOCK)
-        dk_ref[pl.ds(start, BLOCK), :] += key_part[slot * BLOCK:(slot + 1) * BLOCK]
-        dv_ref[pl.ds(start, BLOCK), :] += value_part[slot * BLOCK:(slot + 1) * BLOCK]
-
-
-def local_grads(queries, out_grad, key_tiles, value_tiles, slot_index, code, inv_root,
-                interpret=False):
+        dkv_ref[0, pl.ds(start, BLOCK), :] += key_part[slot * BLOCK:(slot + 1) * BLOCK]
+        dkv_ref[1, pl.ds(start, BLOCK), :] += value_part[slot * BLOCK:(slot + 1) * BLOCK]
+
+
+def local_grads(queries, out_grad, near, far, slot_index, code, inv_root, interpret=False):
     tokens_here, heads_here, width = queries.shape
     blocks_here, slots = slot_index.shape
     rows = BLOCK * heads_here
-    store = key_tiles.shape[0] * BLOCK
+    store = (near.shape[0] + far.shape[0]) * near.shape[2]
     cols = slots * BLOCK
     key_pos = jnp.tile(jnp.arange(BLOCK, dtype=jnp.int32), slots)[None, :]
     code_cols = jnp.repeat(code.astype(jnp.int32), BLOCK, axis=1)
@@ -102,7 +113,7 @@
     kernel = functools.partial(block_kernel, inv_root=inv_root, heads_here=heads_here)
     whole = lambda step, slots_ref: (0, 0)
     per_block = lambda step, slots_ref: (step, 0)
-    query_grad, key_grad, value_grad = pl.pallas_call(
+    query_grad, grads = pl.pallas_call(
         kernel,
         grid_spec=pltpu.PrefetchScalarGridSpec(
             num_scalar_prefetch=1,
@@ -111,13 +122,12 @@
                 pl.BlockSpec((rows, width), per_block),
                 pl.BlockSpec((rows, width), per_block),
                 pl.BlockSpec((None, 1, cols), lambda step, slots_ref: (step, 0, 0)),
-                pl.BlockSpec((store, width), whole),
-                pl.BlockSpec((store, width), whole),
+                pl.BlockSpec(near.shape, lambda step, slots_ref: (0, 0, 0, 0)),
+                pl.BlockSpec(far.shape, lambda step, slots_ref: (0, 0, 0, 0)),
             ],
             out_specs=[
                 pl.BlockSpec((rows, width), per_block),
-                pl.BlockSpec((store, width), whole),
-                pl.BlockSpec((store, width), whole),
+                pl.BlockSpec((2, store, width), lambda step, slots_ref: (0, 0, 0)),
             ],
             scratch_shapes=[
                 pltpu.VMEM((cols, width), jnp.bfloat16),
@@ -126,8 +136,7 @@
         ),
         out_shape=[
             jax.ShapeDtypeStruct((tokens_here * heads_here, width), jnp.bfloat16),
-            jax.ShapeDtypeStruct((store, width), jnp.float32),
-            jax.ShapeDtypeStruct((store, width), jnp.float32),
+            jax.ShapeDtypeStruct((2, store, width), jnp.float32),
         ],
         compiler_params=pltpu.CompilerParams(dimension_semantics=("arbitrary",)),
         interpret=interpret,
@@ -136,10 +145,10 @@
         queries.reshape(tokens_here * heads_here, width),
         out_grad.reshape(tokens_here * heads_here, width),
         code_cols,
-        key_tiles.reshape(store, width),
-        value_tiles.reshape(store, width),
-    )
-    return query_grad.reshape(tokens_here, heads_here, width), key_grad, value_grad
+        near,
+        far,
+    )
+    return query_grad.reshape(tokens_here, heads_here, width), grads
 
 
 def per_device(queries, key_rows, value_rows, out_grad, selected, live_slots):
@@ -166,10 +175,8 @@
     pieces = [took] + [cycled(took, "sub", -step) for step in range(1, parts_count)]
     took = jnp.concatenate(pieces, axis=2)
     mine = jnp.concatenate([rolled[None], took], axis=0)
-    tile_store = jnp.concatenate([mine, swap_cores(mine, "ctx")], axis=0)
-    store_span = tile_store.shape[0]
-    key_tiles = tile_store[:, 0].reshape(store_span * blocks_here, BLOCK, width)
-    value_tiles = tile_store[:, 1].reshape(store_span * blocks_here, BLOCK, width)
+    partner_tiles = swap_cores(mine, "ctx")
+    store_span = 2 * mine.shape[0]
     chosen = lax.dynamic_index_in_dim(selected, group_index, 1, keepdims=False)
     live_mask = lax.dynamic_index_in_dim(live_slots, group_index, 1, keepdims=False)
     block_ids = ctx_index * blocks_here + jnp.arange(blocks_here, dtype=jnp.int32)
@@ -182,10 +189,10 @@
     )
     slot_index = placed * blocks_here + rolled_block
     code = jnp.where(live_mask == 1, jnp.where(chosen < block_ids[:, None], 2, 1), 0)
-    query_grad, key_grad, value_grad = local_grads(
-        queries, out_grad, key_tiles, value_tiles, slot_index, code, inv_root
-    )
-    grads = jnp.stack([key_grad, value_grad]).reshape(2, store_span, tokens_here, width)
+    query_grad, grads = local_grads(
+        queries, out_grad, mine, partner_tiles, slot_index, code, inv_root
+    )
+    grads = grads.reshape(2, store_span, tokens_here, width)
     half = store_span // 2
     back = swap_cores(grads[:, half:].astype(jnp.bfloat16), "ctx").astype(jnp.float32)
     totals = grads[:, :half] + back

time: 167 us -> 170 us (1.018)
  Pallas kernels: 16.1 us -> 18.6 us
    pallas_call x1, Pallas kernels: 16.1 us -> 18.6 us  [local_grads(): pl.pallas_call(kernel, grid_spec=pltpu.PrefetchScalarGridSpec(num_scalar_...]
    another operation x2 -> x1, other arithmetic: 1.98 us -> 0.14 us
where the time goes in v11:
time: 170 us; the launch traced here: 169 us
  starting transfers between devices  94.1 us (55%)
  waiting for transfers between devices  40.2 us (24%)
  Pallas kernels  18.6 us (11%)
  local copies, waits for them, and re-layouts  9.96 us (6%)
  other arithmetic  5.14 us (3%)
    ppermute x12, starting transfers between devices, cycled(): lax.ppermute(value, axis, [(source, (source + steps) % count) for source...  52.6 us
    ppermute x12, waiting for transfers between devices, cycled(): lax.ppermute(value, axis, [(source, (source + steps) % count) for source...  23.1 us
    ppermute x3, starting transfers between devices, chip_fetch(): return lax.ppermute(value, axis, chip_pairs(lax.axis_size(axis), step))  21 us
    pallas_call x1, Pallas kernels, local_grads(): pl.pallas_call(kernel, grid_spec=pltpu.PrefetchScalarGridSpec(num_scalar_...  18.6 us
    ppermute x3, starting transfers between devices, chip_return(): lax.ppermute(value, axis, [(target, source) for source, target in pairs])  16.6 us
    ppermute x3, waiting for transfers between devices, chip_fetch(): return lax.ppermute(value, axis, chip_pairs(lax.axis_size(axis), step))  9.16 us
    ppermute x3, waiting for transfers between devices, chip_return(): lax.ppermute(value, axis, [(target, source) for source, target in pairs])  4.79 us
    ppermute x2, starting transfers between devices, swap_cores(): lax.ppermute(value, axis, [(source, source ^ 1) for source in range(count)])  3.96 us
  transfers between devices with their start and end apart: 20, of which 15 were waited for; matrix products, arithmetic and copies ran while one was open for 4% of the time, Pallas kernels for 0%

profile of v11, /device:TPU:6, one launch (start us, length us, event | category | flops | bytes accessed | tf_op | source)
XLA Modules:
  0.0 169.2 jit_solution(1963204281440146830)
XLA Ops:
  0.7 1.0 constant_dynamic-slice_fusion
  1.7 0.5 fusion.3
  2.2 12.2 %collective-permute-start.2 = (bf16[2,128,128]{2,1,0:T(8,128)(2,1)S(1)}, bf16[2,128,128]{2,1,0:T(8,128)(2,1)S(1)}, u32[]{:S(2)}, u32[]{:S(2)}) collective-permute-start(bf16[2,128,128]{2,1,0:T(8,128)(2,1)S(1)} %slice.64), channel_id=1, source_target_pairs={{16,96},{48,128},{80,160},{112,192},{144,224},{176,256},{208,288},... | collective-permute-start | bytes 196616 | tf_op jit(solution)/shard_map/ppermute | solution.py:29
  14.3 4.3 %collective-permute-start.1 = (bf16[2,128,128]{2,1,0:T(8,128)(2,1)S(1)}, bf16[2,128,128]{2,1,0:T(8,128)(2,1)S(1)}, u32[]{:S(2)}, u32[]{:S(2)}) collective-permute-start(bf16[2,128,128]{2,1,0:T(8,128)(2,1)S(1)} %slice.64), channel_id=1, source_target_pairs={{16,64},{48,96},{80,128},{112,160},{144,192},{176,224},{208,256},{... | collective-permute-start | bytes 196616 | tf_op jit(solution)/shard_map/ppermute | solution.py:29
  18.6 4.6 %collective-permute-start = (bf16[2,128,128]{2,1,0:T(8,128)(2,1)S(1)}, bf16[2,128,128]{2,1,0:T(8,128)(2,1)S(1)}, u32[]{:S(2)}, u32[]{:S(2)}) collective-permute-start(bf16[2,128,128]{2,1,0:T(8,128)(2,1)S(1)} %slice.64), channel_id=1, source_target_pairs={{16,32},{48,64},{80,96},{112,128},{144,160},{176,192},{208,224},{2... | collective-permute-start | bytes 196616 | tf_op jit(solution)/shard_map/ppermute | solution.py:29
  23.2 0.8 constant_dynamic-slice_fusion.2
  24.0 0.1 reshape.261
  24.1 2.6 %collective-permute-done.2 = bf16[2,128,128]{2,1,0:T(8,128)(2,1)S(1)} collective-permute-done((bf16[2,128,128]{2,1,0:T(8,128)(2,1)S(1)}, bf16[2,128,128]{2,1,0:T(8,128)(2,1)S(1)}, u32[]{:S(2)}, u32[]{:S(2)}) %collective-permute-start.2) | collective-permute-done | bytes 65568 | tf_op jit(solution)/shard_map/ppermute | solution.py:29
  26.7 3.3 %collective-permute-done.1 = bf16[2,128,128]{2,1,0:T(8,128)(2,1)S(1)} collective-permute-done((bf16[2,128,128]{2,1,0:T(8,128)(2,1)S(1)}, bf16[2,128,128]{2,1,0:T(8,128)(2,1)S(1)}, u32[]{:S(2)}, u32[]{:S(2)}) %collective-permute-start.1) | collective-permute-done | bytes 65568 | tf_op jit(solution)/shard_map/ppermute | solution.py:29
  29.9 3.3 %collective-permute-done = bf16[2,128,128]{2,1,0:T(8,128)(2,1)S(1)} collective-permute-done((bf16[2,128,128]{2,1,0:T(8,128)(2,1)S(1)}, bf16[2,128,128]{2,1,0:T(8,128)(2,1)S(1)}, u32[]{:S(2)}, u32[]{:S(2)}) %collective-permute-start) | collective-permute-done | bytes 65568 | tf_op jit(solution)/shard_map/ppermute | solution.py:29
  33.3 3.5 %collective-permute-start.5 = (bf16[3,2,128,128]{3,2,1,0:T(8,128)(2,1)S(1)}, bf16[3,2,128,128]{3,2,1,0:T(8,128)(2,1)S(1)}, u32[]{:S(2)}, u32[]{:S(2)}) collective-permute-start(bf16[3,2,128,128]{3,2,1,0:T(8,128)(2,1)S(1)} %pad_maximum_fusion.2), channel_id=1, source_target_pairs={{0,1},{1,2},{2,3},{3,0},{4,5},{5,6},{6,7},{7,4},{8,9},{9,10},{10,1... | collective-permute-start | bytes 589832 | tf_op jit(solution)/shard_map/ppermute | solution.py:19
  36.8 4.8 %collective-permute-start.4 = (bf16[3,2,128,128]{3,2,1,0:T(8,128)(2,1)S(1)}, bf16[3,2,128,128]{3,2,1,0:T(8,128)(2,1)S(1)}, u32[]{:S(2)}, u32[]{:S(2)}) collective-permute-start(bf16[3,2,128,128]{3,2,1,0:T(8,128)(2,1)S(1)} %pad_maximum_fusion.2), channel_id=1, source_target_pairs={{0,2},{1,3},{2,0},{3,1},{4,6},{5,7},{6,4},{7,5},{8,10},{9,11},{10,... | collective-permute-start | bytes 589832 | tf_op jit(solution)/shard_map/ppermute | solution.py:19
  41.6 3.3 %collective-permute-start.3 = (bf16[3,2,128,128]{3,2,1,0:T(8,128)(2,1)S(1)}, bf16[3,2,128,128]{3,2,1,0:T(8,128)(2,1)S(1)}, u32[]{:S(2)}, u32[]{:S(2)}) collective-permute-start(bf16[3,2,128,128]{3,2,1,0:T(8,128)(2,1)S(1)} %pad_maximum_fusion.2), channel_id=1, source_target_pairs={{0,3},{1,0},{2,1},{3,2},{4,7},{5,4},{6,5},{7,6},{8,11},{9,8},{10,9... | collective-permute-start | bytes 589832 | tf_op jit(solution)/shard_map/ppermute | solution.py:19
  44.9 1.2 gather_fusion
  46.1 1.2 gather_fusion.1
  47.4 0.5 fusion.33
  47.9 0.9 collective-permute-done.4
  48.7 1.3 collective-permute-done.3
  50.1 1.9 %collective-permute-start.6 = (bf16[4,2,512,128]{3,2,1,0:T(8,128)(2,1)S(1)}, bf16[4,2,512,128]{3,2,1,0:T(8,128)(2,1)S(1)}, u32[]{:S(2)}, u32[]{:S(2)}) collective-permute-start(bf16[4,2,512,128]{3,2,1,0:T(8,128)(2,1)S(1)} %maximum_maximum_fusion.near_ref), channel_id=1, source_target_pairs={{0,16},{16,0},{32,48},{48,32},{64,80},{80,64},{96,112},{112,96},{1... | collective-permute-start | bytes 3145736 | tf_op jit(solution)/shard_map/ppermute | solution.py:39
  52.1 0.1 reshape.288
  52.2 0.1 fusion.18
  52.3 0.1 broadcast_in_dim.47
  52.4 0.1 eq.59
  52.5 0.1 broadcast_in_dim.49
  52.5 0.1 eq.60
  52.7 0.1 broadcast_in_dim.50
  52.7 0.6 fusion.17.slots_ref
  53.3 0.7 select_select_fusion.code_ref
  54.0 0.7 collective-permute-done.6.far_ref
  54.7 1.0 copy-done.3
  55.7 18.6 %shard_map.103 = (bf16[2048,128]{1,0:T(8,128)(2,1)}, f32[2,4096,128]{2,1,0:T(8,128)}) custom-call(s32[8,16]{1,0:T(8,128)} %fusion.17.slots_ref, bf16[2048,128]{1,0:T(8,128)(2,1)} %bitcast.65, bf16[2048,128]{1,0:T(8,128)(2,1)} %bitcast.66, s32[8,1,1024]{2,1,0:T(1,128)} %select_select_fusion.code_ref, bf16[4,2,512,128]{3,2,1,0:T(8,128)(2,1)} %copy-done.2, ...), custom_call_target="tpu_custom_call" | custom-call | tf_op jit(solution)/shard_map/pallas_call | solution.py:116
  74.3 1.8 %slice.96 = bf16[2,4,512,128]{3,2,1,0:T(8,128)(2,1)S(1)} slice(f32[2,8,512,128]{3,2,1,0:T(8,128)} %bitcast.61), slice={[0:2], [4:8], [0:512], [0:128]} | slice | bytes 2097152 | tf_op jit(solution)/shard_map/slice | solution.py:197
  76.0 2.0 %collective-permute-start.7 = (bf16[2,4,512,128]{3,2,1,0:T(8,128)(2,1)S(1)}, bf16[2,4,512,128]{3,2,1,0:T(8,128)(2,1)S(1)}, u32[]{:S(2)}, u32[]{:S(2)}) collective-permute-start(bf16[2,4,512,128]{3,2,1,0:T(8,128)(2,1)S(1)} %slice.96), channel_id=1, source_target_pairs={{0,16},{16,0},{32,48},{48,32},{64,80},{80,64},{96,112},{112,96},{1... | collective-permute-start | bytes 3145736 | tf_op jit(solution)/shard_map/ppermute | solution.py:39
  78.1 2.5 %collective-permute-done.7 = bf16[2,4,512,128]{3,2,1,0:T(8,128)(2,1)S(1)} collective-permute-done((bf16[2,4,512,128]{3,2,1,0:T(8,128)(2,1)S(1)}, bf16[2,4,512,128]{3,2,1,0:T(8,128)(2,1)S(1)}, u32[]{:S(2)}, u32[]{:S(2)}) %collective-permute-start.7) | collective-permute-done | bytes 1048608 | tf_op jit(solution)/shard_map/ppermute | solution.py:39
  80.6 1.9 %fusion.30 = (bf16[2,4,512,128]{3,2,1,0:T(8,128)(2,1)S(1)}, f32[2,4,512,128]{3,2,1,0:T(8,128)S(1)}) fusion(bf16[2,4,512,128]{3,2,1,0:T(8,128)(2,1)S(1)} %collective-permute-done.7, f32[2,8,512,128]{3,2,1,0:T(8,128)} %bitcast.62), kind=kLoop, calls=%fused_computation.88 | loop fusion | flops 1572864 | bytes 6291456 | tf_op jit(solution)/shard_map/convert_element_type | solution.py:199
  82.6 4.6 %collective-permute-start.10 = (bf16[2,4,128,128]{3,2,1,0:T(8,128)(2,1)S(1)}, bf16[2,4,128,128]{3,2,1,0:T(8,128)(2,1)S(1)}, u32[]{:S(2)}, u32[]{:S(2)}) collective-permute-start(bf16[2,4,128,128]{3,2,1,0:T(8,128)(2,1)S(1)} %get-tuple-element.17), channel_id=1, source_target_pairs={{0,3},{1,0},{2,1},{3,2},{4,7},{5,4},{6,5},{7,6},{8,11},{9,8},{10,9... | collective-permute-start | bytes 786440 | tf_op jit(solution)/shard_map/ppermute | solution.py:19
  87.2 3.8 %collective-permute-start.9 = (bf16[2,4,128,128]{3,2,1,0:T(8,128)(2,1)S(1)}, bf16[2,4,128,128]{3,2,1,0:T(8,128)(2,1)S(1)}, u32[]{:S(2)}, u32[]{:S(2)}) collective-permute-start(bf16[2,4,128,128]{3,2,1,0:T(8,128)(2,1)S(1)} %get-tuple-element.18), channel_id=1, source_target_pairs={{0,2},{1,3},{2,0},{3,1},{4,6},{5,7},{6,4},{7,5},{8,10},{9,11},{10,... | collective-permute-start | bytes 786440 | tf_op jit(solution)/shard_map/ppermute | solution.py:19
  91.0 1.9 %collective-permute-start.8 = (bf16[2,4,128,128]{3,2,1,0:T(8,128)(2,1)S(1)}, bf16[2,4,128,128]{3,2,1,0:T(8,128)(2,1)S(1)}, u32[]{:S(2)}, u32[]{:S(2)}) collective-permute-start(bf16[2,4,128,128]{3,2,1,0:T(8,128)(2,1)S(1)} %get-tuple-element.16), channel_id=1, source_target_pairs={{0,1},{1,2},{2,3},{3,0},{4,5},{5,6},{6,7},{7,4},{8,9},{9,10},{10,1... | collective-permute-start | bytes 786440 | tf_op jit(solution)/shard_map/ppermute | solution.py:19
  93.0 5.7 %collective-permute-done.10 = bf16[2,4,128,128]{3,2,1,0:T(8,128)(2,1)S(1)} collective-permute-done((bf16[2,4,128,128]{3,2,1,0:T(8,128)(2,1)S(1)}, bf16[2,4,128,128]{3,2,1,0:T(8,128)(2,1)S(1)}, u32[]{:S(2)}, u32[]{:S(2)}) %collective-permute-start.10) | collective-permute-done | bytes 262176 | tf_op jit(solution)/shard_map/ppermute | solution.py:19
  98.7 1.1 collective-permute-done.9
  99.8 4.5 %collective-permute-done.8 = bf16[2,4,128,128]{3,2,1,0:T(8,128)(2,1)S(1)} collective-permute-done((bf16[2,4,128,128]{3,2,1,0:T(8,128)(2,1)S(1)}, bf16[2,4,128,128]{3,2,1,0:T(8,128)(2,1)S(1)}, u32[]{:S(2)}, u32[]{:S(2)}) %collective-permute-start.8) | collective-permute-done | bytes 262176 | tf_op jit(solution)/shard_map/ppermute | solution.py:19
  104.3 0.1 fusion.28
  104.4 6.3 %collective-permute-start.13 = (bf16[2,128,128]{2,1,0:T(8,128)(2,1)S(1)}, bf16[2,128,128]{2,1,0:T(8,128)(2,1)S(1)}, u32[]{:S(2)}, u32[]{:S(2)}) collective-permute-start(bf16[2,128,128]{2,1,0:T(8,128)(2,1)S(1)} %get-tuple-element.22), channel_id=1, source_target_pairs={{96,16},{128,48},{160,80},{192,112},{224,144},{256,176},{288,208},... | collective-permute-start | bytes 196616 | tf_op jit(solution)/shard_map/ppermute | solution.py:34
  110.8 5.1 %collective-permute-start.12 = (bf16[2,128,128]{2,1,0:T(8,128)(2,1)S(1)}, bf16[2,128,128]{2,1,0:T(8,128)(2,1)S(1)}, u32[]{:S(2)}, u32[]{:S(2)}) collective-permute-start(bf16[2,128,128]{2,1,0:T(8,128)(2,1)S(1)} %get-tuple-element.23), channel_id=1, source_target_pairs={{64,16},{96,48},{128,80},{160,112},{192,144},{224,176},{256,208},{... | collective-permute-start | bytes 196616 | tf_op jit(solution)/shard_map/ppermute | solution.py:34
  115.9 5.1 %collective-permute-start.11 = (bf16[2,128,128]{2,1,0:T(8,128)(2,1)S(1)}, bf16[2,128,128]{2,1,0:T(8,128)(2,1)S(1)}, u32[]{:S(2)}, u32[]{:S(2)}) collective-permute-start(bf16[2,128,128]{2,1,0:T(8,128)(2,1)S(1)} %get-tuple-element.21), channel_id=1, source_target_pairs={{32,16},{64,48},{96,80},{128,112},{160,144},{192,176},{224,208},{2... | collective-permute-start | bytes 196616 | tf_op jit(solution)/shard_map/ppermute | solution.py:34
  121.0 0.1 broadcast_add_fusion
  121.1 0.1 add.179
  121.2 4.7 %collective-permute-done.12 = bf16[2,128,128]{2,1,0:T(8,128)(2,1)S(1)} collective-permute-done((bf16[2,128,128]{2,1,0:T(8,128)(2,1)S(1)}, bf16[2,128,128]{2,1,0:T(8,128)(2,1)S(1)}, u32[]{:S(2)}, u32[]{:S(2)}) %collective-permute-start.12) | collective-permute-done | bytes 65568 | tf_op jit(solution)/shard_map/ppermute | solution.py:34
  125.9 0.1 collective-permute-done.11
  126.0 6.4 %collective-permute-start.16 = (bf16[2,128,128]{2,1,0:T(8,128)(2,1)S(1)}, bf16[2,128,128]{2,1,0:T(8,128)(2,1)S(1)}, u32[]{:S(2)}, u32[]{:S(2)}) collective-permute-start(bf16[2,128,128]{2,1,0:T(8,128)(2,1)S(1)} %fusion.8), channel_id=1, source_target_pairs={{0,4},{4,8},{8,12},{12,0},{1,5},{5,9},{9,13},{13,1},{2,6},{6,10},{... | collective-permute-start | bytes 196616 | tf_op jit(solution)/shard_map/ppermute | solution.py:19
  132.4 9.2 %collective-permute-start.15 = (bf16[2,128,128]{2,1,0:T(8,128)(2,1)S(1)}, bf16[2,128,128]{2,1,0:T(8,128)(2,1)S(1)}, u32[]{:S(2)}, u32[]{:S(2)}) collective-permute-start(bf16[2,128,128]{2,1,0:T(8,128)(2,1)S(1)} %fusion.8), channel_id=1, source_target_pairs={{0,8},{4,12},{8,0},{12,4},{1,9},{5,13},{9,1},{13,5},{2,10},{6,14},... | collective-permute-start | bytes 196616 | tf_op jit(solution)/shard_map/ppermute | solution.py:19
  141.7 4.8 %collective-permute-start.14 = (bf16[2,128,128]{2,1,0:T(8,128)(2,1)S(1)}, bf16[2,128,128]{2,1,0:T(8,128)(2,1)S(1)}, u32[]{:S(2)}, u32[]{:S(2)}) collective-permute-start(bf16[2,128,128]{2,1,0:T(8,128)(2,1)S(1)} %fusion.8), channel_id=1, source_target_pairs={{0,12},{4,0},{8,4},{12,8},{1,13},{5,1},{9,5},{13,9},{2,14},{6,2},{... | collective-permute-start | bytes 196616 | tf_op jit(solution)/shard_map/ppermute | solution.py:19
  146.5 1.9 %collective-permute-done.14 = bf16[2,128,128]{2,1,0:T(8,128)(2,1)S(1)} collective-permute-done((bf16[2,128,128]{2,1,0:T(8,128)(2,1)S(1)}, bf16[2,128,128]{2,1,0:T(8,128)(2,1)S(1)}, u32[]{:S(2)}, u32[]{:S(2)}) %collective-permute-start.14) | collective-permute-done | bytes 65568 | tf_op jit(solution)/shard_map/ppermute | solution.py:19
  148.4 1.9 %collective-permute-start.19 = (bf16[4,2,128,128]{3,2,1,0:T(8,128)(2,1)S(1)}, bf16[4,2,128,128]{3,2,1,0:T(8,128)(2,1)S(1)}, u32[]{:S(2)}, u32[]{:S(2)}) collective-permute-start(bf16[4,2,128,128]{3,2,1,0:T(8,128)(2,1)S(1)} %get-tuple-element.20), channel_id=1, source_target_pairs={{0,1},{1,2},{2,3},{3,0},{4,5},{5,6},{6,7},{7,4},{8,9},{9,10},{10,1... | collective-permute-start | bytes 786440 | tf_op jit(solution)/shard_map/ppermute | solution.py:19
  150.3 3.8 %collective-permute-start.18 = (bf16[4,2,128,128]{3,2,1,0:T(8,128)(2,1)S(1)}, bf16[4,2,128,128]{3,2,1,0:T(8,128)(2,1)S(1)}, u32[]{:S(2)}, u32[]{:S(2)}) collective-permute-start(bf16[4,2,128,128]{3,2,1,0:T(8,128)(2,1)S(1)} %get-tuple-element.20), channel_id=1, source_target_pairs={{0,2},{1,3},{2,0},{3,1},{4,6},{5,7},{6,4},{7,5},{8,10},{9,11},{10,... | collective-permute-start | bytes 786440 | tf_op jit(solution)/shard_map/ppermute | solution.py:19
  154.2 4.5 %collective-permute-start.17 = (bf16[4,2,128,128]{3,2,1,0:T(8,128)(2,1)S(1)}, bf16[4,2,128,128]{3,2,1,0:T(8,128)(2,1)S(1)}, u32[]{:S(2)}, u32[]{:S(2)}) collective-permute-start(bf16[4,2,128,128]{3,2,1,0:T(8,128)(2,1)S(1)} %get-tuple-element.20), channel_id=1, source_target_pairs={{0,3},{1,0},{2,1},{3,2},{4,7},{5,4},{6,5},{7,6},{8,11},{9,8},{10,9... | collective-permute-start | bytes 786440 | tf_op jit(solution)/shard_map/ppermute | solution.py:19
  158.7 0.1 compare_and_fusion
  158.8 5.2 %collective-permute-done.19 = bf16[4,2,128,128]{3,2,1,0:T(8,128)(2,1)S(1)} collective-permute-done((bf16[4,2,128,128]{3,2,1,0:T(8,128)(2,1)S(1)}, bf16[4,2,128,128]{3,2,1,0:T(8,128)(2,1)S(1)}, u32[]{:S(2)}, u32[]{:S(2)}) %collective-permute-start.19) | collective-permute-done | bytes 262176 | tf_op jit(solution)/shard_map/ppermute | solution.py:19
  164.1 2.5 %collective-permute-done.17 = bf16[4,2,128,128]{3,2,1,0:T(8,128)(2,1)S(1)} collective-permute-done((bf16[4,2,128,128]{3,2,1,0:T(8,128)(2,1)S(1)}, bf16[4,2,128,128]{3,2,1,0:T(8,128)(2,1)S(1)}, u32[]{:S(2)}, u32[]{:S(2)}) %collective-permute-start.17) | collective-permute-done | bytes 262176 | tf_op jit(solution)/shard_map/ppermute | solution.py:19
  166.5 0.1 pad_maximum_fusion
  166.7 0.7 gather_fusion.2
  167.4 0.1 copy.24
  167.5 0.2 convert_bitcast_fusion
  167.7 1.5 fusion.31
  (28 shorter events, 0.3 us)
Async XLA Ops:
  0.6 44.2 %copy-start.1 = (s32[7]{0:T(128)S(1)}, s32[7]{0:T(128)}, u32[]{:S(2)}) copy-start(s32[7]{0:T(128)} %constant.156.clone) | copy-start | bytes 88
  2.2 24.5 %collective-permute-start.2 = (bf16[2,128,128]{2,1,0:T(8,128)(2,1)S(1)}, bf16[2,128,128]{2,1,0:T(8,128)(2,1)S(1)}, u32[]{:S(2)}, u32[]{:S(2)}) collective-permute-start(bf16[2,128,128]{2,1,0:T(8,128)(2,1)S(1)} %slice.64), channel_id=1, source_target_pairs={{16,96},{48,128},{80,160},{112,192},{144,224},{176,256},{208,288},... | collective-permute-start | bytes 196616 | tf_op jit(solution)/shard_map/ppermute | solution.py:29
  14.3 15.6 %collective-permute-start.1 = (bf16[2,128,128]{2,1,0:T(8,128)(2,1)S(1)}, bf16[2,128,128]{2,1,0:T(8,128)(2,1)S(1)}, u32[]{:S(2)}, u32[]{:S(2)}) collective-permute-start(bf16[2,128,128]{2,1,0:T(8,128)(2,1)S(1)} %slice.64), channel_id=1, source_target_pairs={{16,64},{48,96},{80,128},{112,160},{144,192},{176,224},{208,256},{... | collective-permute-start | bytes 196616 | tf_op jit(solution)/shard_map/ppermute | solution.py:29
  18.6 14.6 %collective-permute-start = (bf16[2,128,128]{2,1,0:T(8,128)(2,1)S(1)}, bf16[2,128,128]{2,1,0:T(8,128)(2,1)S(1)}, u32[]{:S(2)}, u32[]{:S(2)}) collective-permute-start(bf16[2,128,128]{2,1,0:T(8,128)(2,1)S(1)} %slice.64), channel_id=1, source_target_pairs={{16,32},{48,64},{80,96},{112,128},{144,160},{176,192},{208,224},{2... | collective-permute-start | bytes 196616 | tf_op jit(solution)/shard_map/ppermute | solution.py:29
  33.3 14.6 %collective-permute-start.5 = (bf16[3,2,128,128]{3,2,1,0:T(8,128)(2,1)S(1)}, bf16[3,2,128,128]{3,2,1,0:T(8,128)(2,1)S(1)}, u32[]{:S(2)}, u32[]{:S(2)}) collective-permute-start(bf16[3,2,128,128]{3,2,1,0:T(8,128)(2,1)S(1)} %pad_maximum_fusion.2), channel_id=1, source_target_pairs={{0,1},{1,2},{2,3},{3,0},{4,5},{5,6},{6,7},{7,4},{8,9},{9,10},{10,1... | collective-permute-start | bytes 589832 | tf_op jit(solution)/shard_map/ppermute | solution.py:19
  36.8 12.0 %collective-permute-start.4 = (bf16[3,2,128,128]{3,2,1,0:T(8,128)(2,1)S(1)}, bf16[3,2,128,128]{3,2,1,0:T(8,128)(2,1)S(1)}, u32[]{:S(2)}, u32[]{:S(2)}) collective-permute-start(bf16[3,2,128,128]{3,2,1,0:T(8,128)(2,1)S(1)} %pad_maximum_fusion.2), channel_id=1, source_target_pairs={{0,2},{1,3},{2,0},{3,1},{4,6},{5,7},{6,4},{7,5},{8,10},{9,11},{10,... | collective-permute-start | bytes 589832 | tf_op jit(solution)/shard_map/ppermute | solution.py:19
  41.6 8.5 %collective-permute-start.3 = (bf16[3,2,128,128]{3,2,1,0:T(8,128)(2,1)S(1)}, bf16[3,2,128,128]{3,2,1,0:T(8,128)(2,1)S(1)}, u32[]{:S(2)}, u32[]{:S(2)}) collective-permute-start(bf16[3,2,128,128]{3,2,1,0:T(8,128)(2,1)S(1)} %pad_maximum_fusion.2), channel_id=1, source_target_pairs={{0,3},{1,0},{2,1},{3,2},{4,7},{5,4},{6,5},{7,6},{8,11},{9,8},{10,9... | collective-permute-start | bytes 589832 | tf_op jit(solution)/shard_map/ppermute | solution.py:19
  44.9 1.2 copy-start
  50.1 4.6 %copy-start.2 = (bf16[4,2,512,128]{3,2,1,0:T(8,128)(2,1)}, bf16[4,2,512,128]{3,2,1,0:T(8,128)(2,1)S(1)}, u32[]{:S(2)}) copy-start(bf16[4,2,512,128]{3,2,1,0:T(8,128)(2,1)S(1)} %maximum_maximum_fusion.near_ref) | copy-start | bytes 3145732
  50.1 4.6 %collective-permute-start.6 = (bf16[4,2,512,128]{3,2,1,0:T(8,128)(2,1)S(1)}, bf16[4,2,512,128]{3,2,1,0:T(8,128)(2,1)S(1)}, u32[]{:S(2)}, u32[]{:S(2)}) collective-permute-start(bf16[4,2,512,128]{3,2,1,0:T(8,128)(2,1)S(1)} %maximum_maximum_fusion.near_ref), channel_id=1, source_target_pairs={{0,16},{16,0},{32,48},{48,32},{64,80},{80,64},{96,112},{112,96},{1... | collective-permute-start | bytes 3145736 | tf_op jit(solution)/shard_map/ppermute | solution.py:39
  54.7 1.0 copy-start.3
  76.0 4.6 %collective-permute-start.7 = (bf16[2,4,512,128]{3,2,1,0:T(8,128)(2,1)S(1)}, bf16[2,4,512,128]{3,2,1,0:T(8,128)(2,1)S(1)}, u32[]{:S(2)}, u32[]{:S(2)}) collective-permute-start(bf16[2,4,512,128]{3,2,1,0:T(8,128)(2,1)S(1)} %slice.96), channel_id=1, source_target_pairs={{0,16},{16,0},{32,48},{48,32},{64,80},{80,64},{96,112},{112,96},{1... | collective-permute-start | bytes 3145736 | tf_op jit(solution)/shard_map/ppermute | solution.py:39
  82.6 16.1 %collective-permute-start.10 = (bf16[2,4,128,128]{3,2,1,0:T(8,128)(2,1)S(1)}, bf16[2,4,128,128]{3,2,1,0:T(8,128)(2,1)S(1)}, u32[]{:S(2)}, u32[]{:S(2)}) collective-permute-start(bf16[2,4,128,128]{3,2,1,0:T(8,128)(2,1)S(1)} %get-tuple-element.17), channel_id=1, source_target_pairs={{0,3},{1,0},{2,1},{3,2},{4,7},{5,4},{6,5},{7,6},{8,11},{9,8},{10,9... | collective-permute-start | bytes 786440 | tf_op jit(solution)/shard_map/ppermute | solution.py:19
  87.2 12.6 %collective-permute-start.9 = (bf16[2,4,128,128]{3,2,1,0:T(8,128)(2,1)S(1)}, bf16[2,4,128,128]{3,2,1,0:T(8,128)(2,1)S(1)}, u32[]{:S(2)}, u32[]{:S(2)}) collective-permute-start(bf16[2,4,128,128]{3,2,1,0:T(8,128)(2,1)S(1)} %get-tuple-element.18), channel_id=1, source_target_pairs={{0,2},{1,3},{2,0},{3,1},{4,6},{5,7},{6,4},{7,5},{8,10},{9,11},{10,... | collective-permute-start | bytes 786440 | tf_op jit(solution)/shard_map/ppermute | solution.py:19
  91.0 13.3 %collective-permute-start.8 = (bf16[2,4,128,128]{3,2,1,0:T(8,128)(2,1)S(1)}, bf16[2,4,128,128]{3,2,1,0:T(8,128)(2,1)S(1)}, u32[]{:S(2)}, u32[]{:S(2)}) collective-permute-start(bf16[2,4,128,128]{3,2,1,0:T(8,128)(2,1)S(1)} %get-tuple-element.16), channel_id=1, source_target_pairs={{0,1},{1,2},{2,3},{3,0},{4,5},{5,6},{6,7},{7,4},{8,9},{9,10},{10,1... | collective-permute-start | bytes 786440 | tf_op jit(solution)/shard_map/ppermute | solution.py:19
  104.4 16.7 %collective-permute-start.13 = (bf16[2,128,128]{2,1,0:T(8,128)(2,1)S(1)}, bf16[2,128,128]{2,1,0:T(8,128)(2,1)S(1)}, u32[]{:S(2)}, u32[]{:S(2)}) collective-permute-start(bf16[2,128,128]{2,1,0:T(8,128)(2,1)S(1)} %get-tuple-element.22), channel_id=1, source_target_pairs={{96,16},{128,48},{160,80},{192,112},{224,144},{256,176},{288,208},... | collective-permute-start | bytes 196616 | tf_op jit(solution)/shard_map/ppermute | solution.py:34
  110.8 15.1 %collective-permute-start.12 = (bf16[2,128,128]{2,1,0:T(8,128)(2,1)S(1)}, bf16[2,128,128]{2,1,0:T(8,128)(2,1)S(1)}, u32[]{:S(2)}, u32[]{:S(2)}) collective-permute-start(bf16[2,128,128]{2,1,0:T(8,128)(2,1)S(1)} %get-tuple-element.23), channel_id=1, source_target_pairs={{64,16},{96,48},{128,80},{160,112},{192,144},{224,176},{256,208},{... | collective-permute-start | bytes 196616 | tf_op jit(solution)/shard_map/ppermute | solution.py:34
  115.9 10.1 %collective-permute-start.11 = (bf16[2,128,128]{2,1,0:T(8,128)(2,1)S(1)}, bf16[2,128,128]{2,1,0:T(8,128)(2,1)S(1)}, u32[]{:S(2)}, u32[]{:S(2)}) collective-permute-start(bf16[2,128,128]{2,1,0:T(8,128)(2,1)S(1)} %get-tuple-element.21), channel_id=1, source_target_pairs={{32,16},{64,48},{96,80},{128,112},{160,144},{192,176},{224,208},{2... | collective-permute-start | bytes 196616 | tf_op jit(solution)/shard_map/ppermute | solution.py:34
  126.0 20.5 %collective-permute-start.16 = (bf16[2,128,128]{2,1,0:T(8,128)(2,1)S(1)}, bf16[2,128,128]{2,1,0:T(8,128)(2,1)S(1)}, u32[]{:S(2)}, u32[]{:S(2)}) collective-permute-start(bf16[2,128,128]{2,1,0:T(8,128)(2,1)S(1)} %fusion.8), channel_id=1, source_target_pairs={{0,4},{4,8},{8,12},{12,0},{1,5},{5,9},{9,13},{13,1},{2,6},{6,10},{... | collective-permute-start | bytes 196616 | tf_op jit(solution)/shard_map/ppermute | solution.py:19
  132.4 14.1 %collective-permute-start.15 = (bf16[2,128,128]{2,1,0:T(8,128)(2,1)S(1)}, bf16[2,128,128]{2,1,0:T(8,128)(2,1)S(1)}, u32[]{:S(2)}, u32[]{:S(2)}) collective-permute-start(bf16[2,128,128]{2,1,0:T(8,128)(2,1)S(1)} %fusion.8), channel_id=1, source_target_pairs={{0,8},{4,12},{8,0},{12,4},{1,9},{5,13},{9,1},{13,5},{2,10},{6,14},... | collective-permute-start | bytes 196616 | tf_op jit(solution)/shard_map/ppermute | solution.py:19
  141.7 6.7 %collective-permute-start.14 = (bf16[2,128,128]{2,1,0:T(8,128)(2,1)S(1)}, bf16[2,128,128]{2,1,0:T(8,128)(2,1)S(1)}, u32[]{:S(2)}, u32[]{:S(2)}) collective-permute-start(bf16[2,128,128]{2,1,0:T(8,128)(2,1)S(1)} %fusion.8), channel_id=1, source_target_pairs={{0,12},{4,0},{8,4},{12,8},{1,13},{5,1},{9,5},{13,9},{2,14},{6,2},{... | collective-permute-start | bytes 196616 | tf_op jit(solution)/shard_map/ppermute | solution.py:19
  148.4 15.6 %collective-permute-start.19 = (bf16[4,2,128,128]{3,2,1,0:T(8,128)(2,1)S(1)}, bf16[4,2,128,128]{3,2,1,0:T(8,128)(2,1)S(1)}, u32[]{:S(2)}, u32[]{:S(2)}) collective-permute-start(bf16[4,2,128,128]{3,2,1,0:T(8,128)(2,1)S(1)} %get-tuple-element.20), channel_id=1, source_target_pairs={{0,1},{1,2},{2,3},{3,0},{4,5},{5,6},{6,7},{7,4},{8,9},{9,10},{10,1... | collective-permute-start | bytes 786440 | tf_op jit(solution)/shard_map/ppermute | solution.py:19
  150.3 13.7 %collective-permute-start.18 = (bf16[4,2,128,128]{3,2,1,0:T(8,128)(2,1)S(1)}, bf16[4,2,128,128]{3,2,1,0:T(8,128)(2,1)S(1)}, u32[]{:S(2)}, u32[]{:S(2)}) collective-permute-start(bf16[4,2,128,128]{3,2,1,0:T(8,128)(2,1)S(1)} %get-tuple-element.20), channel_id=1, source_target_pairs={{0,2},{1,3},{2,0},{3,1},{4,6},{5,7},{6,4},{7,5},{8,10},{9,11},{10,... | collective-permute-start | bytes 786440 | tf_op jit(solution)/shard_map/ppermute | solution.py:19
  154.2 12.4 %collective-permute-start.17 = (bf16[4,2,128,128]{3,2,1,0:T(8,128)(2,1)S(1)}, bf16[4,2,128,128]{3,2,1,0:T(8,128)(2,1)S(1)}, u32[]{:S(2)}, u32[]{:S(2)}) collective-permute-start(bf16[4,2,128,128]{3,2,1,0:T(8,128)(2,1)S(1)} %get-tuple-element.20), channel_id=1, source_target_pairs={{0,3},{1,0},{2,1},{3,2},{4,7},{5,4},{6,5},{7,6},{8,11},{9,8},{10,9... | collective-permute-start | bytes 786440 | tf_op jit(solution)/shard_map/ppermute | solution.py:19

commit v12 on v11

--- a/solution.py
+++ b/solution.py
@@ -54,17 +54,15 @@
         row = pl.multiple_of(slots_ref[step, slot] % per_tile * BLOCK, BLOCK)
         target = slice(slot * BLOCK, (slot + 1) * BLOCK)
 
-        @pl.when(tile < half)
-        def _():
-            here = jnp.minimum(tile, half - 1)
-            k_sel[target, :] = near_ref[here, 0, pl.ds(row, BLOCK), :]
-            v_sel[target, :] = near_ref[here, 1, pl.ds(row, BLOCK), :]
-
-        @pl.when(tile >= half)
-        def _():
-            there = jnp.maximum(tile - half, 0)
-            k_sel[target, :] = far_ref[there, 0, pl.ds(row, BLOCK), :]
-            v_sel[target, :] = far_ref[there, 1, pl.ds(row, BLOCK), :]
+        inside = tile < half
+        here = jnp.minimum(tile, half - 1)
+        there = jnp.maximum(tile - half, 0)
+        k_sel[target, :] = jnp.where(
+            inside, near_ref[here, 0, pl.ds(row, BLOCK), :], far_ref[there, 0, pl.ds(row, BLOCK), :]
+        )
+        v_sel[target, :] = jnp.where(
+            inside, near_ref[here, 1, pl.ds(row, BLOCK), :], far_ref[there, 1, pl.ds(row, BLOCK), :]
+        )
     q = q_ref[...]
     do = do_ref[...]
     keys = k_sel[...]

time: 170 us -> 169 us (level)
  no operation moved by 1% of the time
where the time goes in v12:
time: 169 us; the launch traced here: 168 us
  starting transfers between devices  94.1 us (56%)
  waiting for transfers between devices  40.2 us (24%)
  Pallas kernels  17.5 us (10%)
  local copies, waits for them, and re-layouts  9.96 us (6%)
  other arithmetic  5.14 us (3%)
    ppermute x12, starting transfers between devices, cycled(): lax.ppermute(value, axis, [(source, (source + steps) % count) for source...  52.6 us
    ppermute x12, waiting for transfers between devices, cycled(): lax.ppermute(value, axis, [(source, (source + steps) % count) for source...  23.1 us
    ppermute x3, starting transfers between devices, chip_fetch(): return lax.ppermute(value, axis, chip_pairs(lax.axis_size(axis), step))  21 us
    pallas_call x1, Pallas kernels, local_grads(): pl.pallas_call(kernel, grid_spec=pltpu.PrefetchScalarGridSpec(num_scalar_...  17.5 us
    ppermute x3, starting transfers between devices, chip_return(): lax.ppermute(value, axis, [(target, source) for source, target in pairs])  16.6 us
    ppermute x3, waiting for transfers between devices, chip_fetch(): return lax.ppermute(value, axis, chip_pairs(lax.axis_size(axis), step))  9.16 us
    ppermute x3, waiting for transfers between devices, chip_return(): lax.ppermute(value, axis, [(target, source) for source, target in pairs])  4.8 us
    ppermute x2, starting transfers between devices, swap_cores(): lax.ppermute(value, axis, [(source, source ^ 1) for source in range(count)])  3.96 us
  transfers between devices with their start and end apart: 20, of which 15 were waited for; matrix products, arithmetic and copies ran while one was open for 4% of the time, Pallas kernels for 0%

profile of v12, /device:TPU:6, one launch (start us, length us, event | category | flops | bytes accessed | tf_op | source)
XLA Modules:
  0.0 168.1 jit_solution(11359836957493877239)
XLA Ops:
  0.7 1.0 constant_dynamic-slice_fusion
  1.7 0.5 fusion.3
  2.2 12.2 %collective-permute-start.2 = (bf16[2,128,128]{2,1,0:T(8,128)(2,1)S(1)}, bf16[2,128,128]{2,1,0:T(8,128)(2,1)S(1)}, u32[]{:S(2)}, u32[]{:S(2)}) collective-permute-start(bf16[2,128,128]{2,1,0:T(8,128)(2,1)S(1)} %slice.64), channel_id=1, source_target_pairs={{16,96},{48,128},{80,160},{112,192},{144,224},{176,256},{208,288},... | collective-permute-start | bytes 196616 | tf_op jit(solution)/shard_map/ppermute | solution.py:29
  14.3 4.3 %collective-permute-start.1 = (bf16[2,128,128]{2,1,0:T(8,128)(2,1)S(1)}, bf16[2,128,128]{2,1,0:T(8,128)(2,1)S(1)}, u32[]{:S(2)}, u32[]{:S(2)}) collective-permute-start(bf16[2,128,128]{2,1,0:T(8,128)(2,1)S(1)} %slice.64), channel_id=1, source_target_pairs={{16,64},{48,96},{80,128},{112,160},{144,192},{176,224},{208,256},{... | collective-permute-start | bytes 196616 | tf_op jit(solution)/shard_map/ppermute | solution.py:29
  18.6 4.6 %collective-permute-start = (bf16[2,128,128]{2,1,0:T(8,128)(2,1)S(1)}, bf16[2,128,128]{2,1,0:T(8,128)(2,1)S(1)}, u32[]{:S(2)}, u32[]{:S(2)}) collective-permute-start(bf16[2,128,128]{2,1,0:T(8,128)(2,1)S(1)} %slice.64), channel_id=1, source_target_pairs={{16,32},{48,64},{80,96},{112,128},{144,160},{176,192},{208,224},{2... | collective-permute-start | bytes 196616 | tf_op jit(solution)/shard_map/ppermute | solution.py:29
  23.2 0.8 constant_dynamic-slice_fusion.2
  24.0 0.1 reshape.261
  24.1 2.6 %collective-permute-done.2 = bf16[2,128,128]{2,1,0:T(8,128)(2,1)S(1)} collective-permute-done((bf16[2,128,128]{2,1,0:T(8,128)(2,1)S(1)}, bf16[2,128,128]{2,1,0:T(8,128)(2,1)S(1)}, u32[]{:S(2)}, u32[]{:S(2)}) %collective-permute-start.2) | collective-permute-done | bytes 65568 | tf_op jit(solution)/shard_map/ppermute | solution.py:29
  26.7 3.3 %collective-permute-done.1 = bf16[2,128,128]{2,1,0:T(8,128)(2,1)S(1)} collective-permute-done((bf16[2,128,128]{2,1,0:T(8,128)(2,1)S(1)}, bf16[2,128,128]{2,1,0:T(8,128)(2,1)S(1)}, u32[]{:S(2)}, u32[]{:S(2)}) %collective-permute-start.1) | collective-permute-done | bytes 65568 | tf_op jit(solution)/shard_map/ppermute | solution.py:29
  29.9 3.3 %collective-permute-done = bf16[2,128,128]{2,1,0:T(8,128)(2,1)S(1)} collective-permute-done((bf16[2,128,128]{2,1,0:T(8,128)(2,1)S(1)}, bf16[2,128,128]{2,1,0:T(8,128)(2,1)S(1)}, u32[]{:S(2)}, u32[]{:S(2)}) %collective-permute-start) | collective-permute-done | bytes 65568 | tf_op jit(solution)/shard_map/ppermute | solution.py:29
  33.3 3.5 %collective-permute-start.5 = (bf16[3,2,128,128]{3,2,1,0:T(8,128)(2,1)S(1)}, bf16[3,2,128,128]{3,2,1,0:T(8,128)(2,1)S(1)}, u32[]{:S(2)}, u32[]{:S(2)}) collective-permute-start(bf16[3,2,128,128]{3,2,1,0:T(8,128)(2,1)S(1)} %pad_maximum_fusion.2), channel_id=1, source_target_pairs={{0,1},{1,2},{2,3},{3,0},{4,5},{5,6},{6,7},{7,4},{8,9},{9,10},{10,1... | collective-permute-start | bytes 589832 | tf_op jit(solution)/shard_map/ppermute | solution.py:19
  36.8 4.8 %collective-permute-start.4 = (bf16[3,2,128,128]{3,2,1,0:T(8,128)(2,1)S(1)}, bf16[3,2,128,128]{3,2,1,0:T(8,128)(2,1)S(1)}, u32[]{:S(2)}, u32[]{:S(2)}) collective-permute-start(bf16[3,2,128,128]{3,2,1,0:T(8,128)(2,1)S(1)} %pad_maximum_fusion.2), channel_id=1, source_target_pairs={{0,2},{1,3},{2,0},{3,1},{4,6},{5,7},{6,4},{7,5},{8,10},{9,11},{10,... | collective-permute-start | bytes 589832 | tf_op jit(solution)/shard_map/ppermute | solution.py:19
  41.6 3.3 %collective-permute-start.3 = (bf16[3,2,128,128]{3,2,1,0:T(8,128)(2,1)S(1)}, bf16[3,2,128,128]{3,2,1,0:T(8,128)(2,1)S(1)}, u32[]{:S(2)}, u32[]{:S(2)}) collective-permute-start(bf16[3,2,128,128]{3,2,1,0:T(8,128)(2,1)S(1)} %pad_maximum_fusion.2), channel_id=1, source_target_pairs={{0,3},{1,0},{2,1},{3,2},{4,7},{5,4},{6,5},{7,6},{8,11},{9,8},{10,9... | collective-permute-start | bytes 589832 | tf_op jit(solution)/shard_map/ppermute | solution.py:19
  44.9 1.2 gather_fusion
  46.1 1.2 gather_fusion.1
  47.4 0.5 fusion.33
  47.9 0.9 collective-permute-done.4
  48.7 1.3 collective-permute-done.3
  50.1 1.9 %collective-permute-start.6 = (bf16[4,2,512,128]{3,2,1,0:T(8,128)(2,1)S(1)}, bf16[4,2,512,128]{3,2,1,0:T(8,128)(2,1)S(1)}, u32[]{:S(2)}, u32[]{:S(2)}) collective-permute-start(bf16[4,2,512,128]{3,2,1,0:T(8,128)(2,1)S(1)} %maximum_maximum_fusion.near_ref), channel_id=1, source_target_pairs={{0,16},{16,0},{32,48},{48,32},{64,80},{80,64},{96,112},{112,96},{1... | collective-permute-start | bytes 3145736 | tf_op jit(solution)/shard_map/ppermute | solution.py:39
  52.1 0.1 reshape.288
  52.2 0.1 fusion.18
  52.3 0.1 broadcast_in_dim.47
  52.4 0.1 eq.59
  52.5 0.1 broadcast_in_dim.49
  52.5 0.1 eq.60
  52.7 0.1 broadcast_in_dim.50
  52.7 0.6 fusion.17.slots_ref
  53.3 0.7 select_select_fusion.code_ref
  54.0 0.7 collective-permute-done.6.far_ref
  54.7 1.0 copy-done.3
  55.7 17.5 %shard_map.103 = (bf16[2048,128]{1,0:T(8,128)(2,1)}, f32[2,4096,128]{2,1,0:T(8,128)}) custom-call(s32[8,16]{1,0:T(8,128)} %fusion.17.slots_ref, bf16[2048,128]{1,0:T(8,128)(2,1)} %bitcast.65, bf16[2048,128]{1,0:T(8,128)(2,1)} %bitcast.66, s32[8,1,1024]{2,1,0:T(1,128)} %select_select_fusion.code_ref, bf16[4,2,512,128]{3,2,1,0:T(8,128)(2,1)} %copy-done.2, ...), custom_call_target="tpu_custom_call" | custom-call | tf_op jit(solution)/shard_map/pallas_call | solution.py:114
  73.2 1.8 %slice.96 = bf16[2,4,512,128]{3,2,1,0:T(8,128)(2,1)S(1)} slice(f32[2,8,512,128]{3,2,1,0:T(8,128)} %bitcast.61), slice={[0:2], [4:8], [0:512], [0:128]} | slice | bytes 2097152 | tf_op jit(solution)/shard_map/slice | solution.py:195
  74.9 2.0 %collective-permute-start.7 = (bf16[2,4,512,128]{3,2,1,0:T(8,128)(2,1)S(1)}, bf16[2,4,512,128]{3,2,1,0:T(8,128)(2,1)S(1)}, u32[]{:S(2)}, u32[]{:S(2)}) collective-permute-start(bf16[2,4,512,128]{3,2,1,0:T(8,128)(2,1)S(1)} %slice.96), channel_id=1, source_target_pairs={{0,16},{16,0},{32,48},{48,32},{64,80},{80,64},{96,112},{112,96},{1... | collective-permute-start | bytes 3145736 | tf_op jit(solution)/shard_map/ppermute | solution.py:39
  77.0 2.5 %collective-permute-done.7 = bf16[2,4,512,128]{3,2,1,0:T(8,128)(2,1)S(1)} collective-permute-done((bf16[2,4,512,128]{3,2,1,0:T(8,128)(2,1)S(1)}, bf16[2,4,512,128]{3,2,1,0:T(8,128)(2,1)S(1)}, u32[]{:S(2)}, u32[]{:S(2)}) %collective-permute-start.7) | collective-permute-done | bytes 1048608 | tf_op jit(solution)/shard_map/ppermute | solution.py:39
  79.5 1.9 %fusion.30 = (bf16[2,4,512,128]{3,2,1,0:T(8,128)(2,1)S(1)}, f32[2,4,512,128]{3,2,1,0:T(8,128)S(1)}) fusion(bf16[2,4,512,128]{3,2,1,0:T(8,128)(2,1)S(1)} %collective-permute-done.7, f32[2,8,512,128]{3,2,1,0:T(8,128)} %bitcast.62), kind=kLoop, calls=%fused_computation.88 | loop fusion | flops 1572864 | bytes 6291456 | tf_op jit(solution)/shard_map/convert_element_type | solution.py:197
  81.5 4.6 %collective-permute-start.10 = (bf16[2,4,128,128]{3,2,1,0:T(8,128)(2,1)S(1)}, bf16[2,4,128,128]{3,2,1,0:T(8,128)(2,1)S(1)}, u32[]{:S(2)}, u32[]{:S(2)}) collective-permute-start(bf16[2,4,128,128]{3,2,1,0:T(8,128)(2,1)S(1)} %get-tuple-element.17), channel_id=1, source_target_pairs={{0,3},{1,0},{2,1},{3,2},{4,7},{5,4},{6,5},{7,6},{8,11},{9,8},{10,9... | collective-permute-start | bytes 786440 | tf_op jit(solution)/shard_map/ppermute | solution.py:19
  86.1 3.8 %collective-permute-start.9 = (bf16[2,4,128,128]{3,2,1,0:T(8,128)(2,1)S(1)}, bf16[2,4,128,128]{3,2,1,0:T(8,128)(2,1)S(1)}, u32[]{:S(2)}, u32[]{:S(2)}) collective-permute-start(bf16[2,4,128,128]{3,2,1,0:T(8,128)(2,1)S(1)} %get-tuple-element.18), channel_id=1, source_target_pairs={{0,2},{1,3},{2,0},{3,1},{4,6},{5,7},{6,4},{7,5},{8,10},{9,11},{10,... | collective-permute-start | bytes 786440 | tf_op jit(solution)/shard_map/ppermute | solution.py:19
  89.9 1.9 %collective-permute-start.8 = (bf16[2,4,128,128]{3,2,1,0:T(8,128)(2,1)S(1)}, bf16[2,4,128,128]{3,2,1,0:T(8,128)(2,1)S(1)}, u32[]{:S(2)}, u32[]{:S(2)}) collective-permute-start(bf16[2,4,128,128]{3,2,1,0:T(8,128)(2,1)S(1)} %get-tuple-element.16), channel_id=1, source_target_pairs={{0,1},{1,2},{2,3},{3,0},{4,5},{5,6},{6,7},{7,4},{8,9},{9,10},{10,1... | collective-permute-start | bytes 786440 | tf_op jit(solution)/shard_map/ppermute | solution.py:19
  91.8 5.7 %collective-permute-done.10 = bf16[2,4,128,128]{3,2,1,0:T(8,128)(2,1)S(1)} collective-permute-done((bf16[2,4,128,128]{3,2,1,0:T(8,128)(2,1)S(1)}, bf16[2,4,128,128]{3,2,1,0:T(8,128)(2,1)S(1)}, u32[]{:S(2)}, u32[]{:S(2)}) %collective-permute-start.10) | collective-permute-done | bytes 262176 | tf_op jit(solution)/shard_map/ppermute | solution.py:19
  97.6 1.1 collective-permute-done.9
  98.7 4.5 %collective-permute-done.8 = bf16[2,4,128,128]{3,2,1,0:T(8,128)(2,1)S(1)} collective-permute-done((bf16[2,4,128,128]{3,2,1,0:T(8,128)(2,1)S(1)}, bf16[2,4,128,128]{3,2,1,0:T(8,128)(2,1)S(1)}, u32[]{:S(2)}, u32[]{:S(2)}) %collective-permute-start.8) | collective-permute-done | bytes 262176 | tf_op jit(solution)/shard_map/ppermute | solution.py:19
  103.2 0.1 fusion.28
  103.3 6.3 %collective-permute-start.13 = (bf16[2,128,128]{2,1,0:T(8,128)(2,1)S(1)}, bf16[2,128,128]{2,1,0:T(8,128)(2,1)S(1)}, u32[]{:S(2)}, u32[]{:S(2)}) collective-permute-start(bf16[2,128,128]{2,1,0:T(8,128)(2,1)S(1)} %get-tuple-element.22), channel_id=1, source_target_pairs={{96,16},{128,48},{160,80},{192,112},{224,144},{256,176},{288,208},... | collective-permute-start | bytes 196616 | tf_op jit(solution)/shard_map/ppermute | solution.py:34
  109.7 5.1 %collective-permute-start.12 = (bf16[2,128,128]{2,1,0:T(8,128)(2,1)S(1)}, bf16[2,128,128]{2,1,0:T(8,128)(2,1)S(1)}, u32[]{:S(2)}, u32[]{:S(2)}) collective-permute-start(bf16[2,128,128]{2,1,0:T(8,128)(2,1)S(1)} %get-tuple-element.23), channel_id=1, source_target_pairs={{64,16},{96,48},{128,80},{160,112},{192,144},{224,176},{256,208},{... | collective-permute-start | bytes 196616 | tf_op jit(solution)/shard_map/ppermute | solution.py:34
  114.8 5.1 %collective-permute-start.11 = (bf16[2,128,128]{2,1,0:T(8,128)(2,1)S(1)}, bf16[2,128,128]{2,1,0:T(8,128)(2,1)S(1)}, u32[]{:S(2)}, u32[]{:S(2)}) collective-permute-start(bf16[2,128,128]{2,1,0:T(8,128)(2,1)S(1)} %get-tuple-element.21), channel_id=1, source_target_pairs={{32,16},{64,48},{96,80},{128,112},{160,144},{192,176},{224,208},{2... | collective-permute-start | bytes 196616 | tf_op jit(solution)/shard_map/ppermute | solution.py:34
  119.9 0.1 broadcast_add_fusion
  120.0 0.1 add.179
  120.1 4.7 %collective-permute-done.12 = bf16[2,128,128]{2,1,0:T(8,128)(2,1)S(1)} collective-permute-done((bf16[2,128,128]{2,1,0:T(8,128)(2,1)S(1)}, bf16[2,128,128]{2,1,0:T(8,128)(2,1)S(1)}, u32[]{:S(2)}, u32[]{:S(2)}) %collective-permute-start.12) | collective-permute-done | bytes 65568 | tf_op jit(solution)/shard_map/ppermute | solution.py:34
  124.8 0.1 collective-permute-done.11
  124.9 6.4 %collective-permute-start.16 = (bf16[2,128,128]{2,1,0:T(8,128)(2,1)S(1)}, bf16[2,128,128]{2,1,0:T(8,128)(2,1)S(1)}, u32[]{:S(2)}, u32[]{:S(2)}) collective-permute-start(bf16[2,128,128]{2,1,0:T(8,128)(2,1)S(1)} %fusion.8), channel_id=1, source_target_pairs={{0,4},{4,8},{8,12},{12,0},{1,5},{5,9},{9,13},{13,1},{2,6},{6,10},{... | collective-permute-start | bytes 196616 | tf_op jit(solution)/shard_map/ppermute | solution.py:19
  131.3 9.2 %collective-permute-start.15 = (bf16[2,128,128]{2,1,0:T(8,128)(2,1)S(1)}, bf16[2,128,128]{2,1,0:T(8,128)(2,1)S(1)}, u32[]{:S(2)}, u32[]{:S(2)}) collective-permute-start(bf16[2,128,128]{2,1,0:T(8,128)(2,1)S(1)} %fusion.8), channel_id=1, source_target_pairs={{0,8},{4,12},{8,0},{12,4},{1,9},{5,13},{9,1},{13,5},{2,10},{6,14},... | collective-permute-start | bytes 196616 | tf_op jit(solution)/shard_map/ppermute | solution.py:19
  140.5 4.8 %collective-permute-start.14 = (bf16[2,128,128]{2,1,0:T(8,128)(2,1)S(1)}, bf16[2,128,128]{2,1,0:T(8,128)(2,1)S(1)}, u32[]{:S(2)}, u32[]{:S(2)}) collective-permute-start(bf16[2,128,128]{2,1,0:T(8,128)(2,1)S(1)} %fusion.8), channel_id=1, source_target_pairs={{0,12},{4,0},{8,4},{12,8},{1,13},{5,1},{9,5},{13,9},{2,14},{6,2},{... | collective-permute-start | bytes 196616 | tf_op jit(solution)/shard_map/ppermute | solution.py:19
  145.4 1.9 %collective-permute-done.14 = bf16[2,128,128]{2,1,0:T(8,128)(2,1)S(1)} collective-permute-done((bf16[2,128,128]{2,1,0:T(8,128)(2,1)S(1)}, bf16[2,128,128]{2,1,0:T(8,128)(2,1)S(1)}, u32[]{:S(2)}, u32[]{:S(2)}) %collective-permute-start.14) | collective-permute-done | bytes 65568 | tf_op jit(solution)/shard_map/ppermute | solution.py:19
  147.3 1.9 %collective-permute-start.19 = (bf16[4,2,128,128]{3,2,1,0:T(8,128)(2,1)S(1)}, bf16[4,2,128,128]{3,2,1,0:T(8,128)(2,1)S(1)}, u32[]{:S(2)}, u32[]{:S(2)}) collective-permute-start(bf16[4,2,128,128]{3,2,1,0:T(8,128)(2,1)S(1)} %get-tuple-element.20), channel_id=1, source_target_pairs={{0,1},{1,2},{2,3},{3,0},{4,5},{5,6},{6,7},{7,4},{8,9},{9,10},{10,1... | collective-permute-start | bytes 786440 | tf_op jit(solution)/shard_map/ppermute | solution.py:19
  149.2 3.8 %collective-permute-start.18 = (bf16[4,2,128,128]{3,2,1,0:T(8,128)(2,1)S(1)}, bf16[4,2,128,128]{3,2,1,0:T(8,128)(2,1)S(1)}, u32[]{:S(2)}, u32[]{:S(2)}) collective-permute-start(bf16[4,2,128,128]{3,2,1,0:T(8,128)(2,1)S(1)} %get-tuple-element.20), channel_id=1, source_target_pairs={{0,2},{1,3},{2,0},{3,1},{4,6},{5,7},{6,4},{7,5},{8,10},{9,11},{10,... | collective-permute-start | bytes 786440 | tf_op jit(solution)/shard_map/ppermute | solution.py:19
  153.1 4.5 %collective-permute-start.17 = (bf16[4,2,128,128]{3,2,1,0:T(8,128)(2,1)S(1)}, bf16[4,2,128,128]{3,2,1,0:T(8,128)(2,1)S(1)}, u32[]{:S(2)}, u32[]{:S(2)}) collective-permute-start(bf16[4,2,128,128]{3,2,1,0:T(8,128)(2,1)S(1)} %get-tuple-element.20), channel_id=1, source_target_pairs={{0,3},{1,0},{2,1},{3,2},{4,7},{5,4},{6,5},{7,6},{8,11},{9,8},{10,9... | collective-permute-start | bytes 786440 | tf_op jit(solution)/shard_map/ppermute | solution.py:19
  157.6 0.1 compare_and_fusion
  157.7 5.2 %collective-permute-done.19 = bf16[4,2,128,128]{3,2,1,0:T(8,128)(2,1)S(1)} collective-permute-done((bf16[4,2,128,128]{3,2,1,0:T(8,128)(2,1)S(1)}, bf16[4,2,128,128]{3,2,1,0:T(8,128)(2,1)S(1)}, u32[]{:S(2)}, u32[]{:S(2)}) %collective-permute-start.19) | collective-permute-done | bytes 262176 | tf_op jit(solution)/shard_map/ppermute | solution.py:19
  162.9 2.5 %collective-permute-done.17 = bf16[4,2,128,128]{3,2,1,0:T(8,128)(2,1)S(1)} collective-permute-done((bf16[4,2,128,128]{3,2,1,0:T(8,128)(2,1)S(1)}, bf16[4,2,128,128]{3,2,1,0:T(8,128)(2,1)S(1)}, u32[]{:S(2)}, u32[]{:S(2)}) %collective-permute-start.17) | collective-permute-done | bytes 262176 | tf_op jit(solution)/shard_map/ppermute | solution.py:19
  165.4 0.1 pad_maximum_fusion
  165.6 0.7 gather_fusion.2
  166.3 0.1 copy.24
  166.4 0.2 convert_bitcast_fusion
  166.6 1.5 fusion.31
  (28 shorter events, 0.3 us)
Async XLA Ops:
  0.6 44.2 %copy-start.1 = (s32[7]{0:T(128)S(1)}, s32[7]{0:T(128)}, u32[]{:S(2)}) copy-start(s32[7]{0:T(128)} %constant.156.clone) | copy-start | bytes 88
  2.2 24.5 %collective-permute-start.2 = (bf16[2,128,128]{2,1,0:T(8,128)(2,1)S(1)}, bf16[2,128,128]{2,1,0:T(8,128)(2,1)S(1)}, u32[]{:S(2)}, u32[]{:S(2)}) collective-permute-start(bf16[2,128,128]{2,1,0:T(8,128)(2,1)S(1)} %slice.64), channel_id=1, source_target_pairs={{16,96},{48,128},{80,160},{112,192},{144,224},{176,256},{208,288},... | collective-permute-start | bytes 196616 | tf_op jit(solution)/shard_map/ppermute | solution.py:29
  14.3 15.6 %collective-permute-start.1 = (bf16[2,128,128]{2,1,0:T(8,128)(2,1)S(1)}, bf16[2,128,128]{2,1,0:T(8,128)(2,1)S(1)}, u32[]{:S(2)}, u32[]{:S(2)}) collective-permute-start(bf16[2,128,128]{2,1,0:T(8,128)(2,1)S(1)} %slice.64), channel_id=1, source_target_pairs={{16,64},{48,96},{80,128},{112,160},{144,192},{176,224},{208,256},{... | collective-permute-start | bytes 196616 | tf_op jit(solution)/shard_map/ppermute | solution.py:29
  18.6 14.6 %collective-permute-start = (bf16[2,128,128]{2,1,0:T(8,128)(2,1)S(1)}, bf16[2,128,128]{2,1,0:T(8,128)(2,1)S(1)}, u32[]{:S(2)}, u32[]{:S(2)}) collective-permute-start(bf16[2,128,128]{2,1,0:T(8,128)(2,1)S(1)} %slice.64), channel_id=1, source_target_pairs={{16,32},{48,64},{80,96},{112,128},{144,160},{176,192},{208,224},{2... | collective-permute-start | bytes 196616 | tf_op jit(solution)/shard_map/ppermute | solution.py:29
  33.3 14.6 %collective-permute-start.5 = (bf16[3,2,128,128]{3,2,1,0:T(8,128)(2,1)S(1)}, bf16[3,2,128,128]{3,2,1,0:T(8,128)(2,1)S(1)}, u32[]{:S(2)}, u32[]{:S(2)}) collective-permute-start(bf16[3,2,128,128]{3,2,1,0:T(8,128)(2,1)S(1)} %pad_maximum_fusion.2), channel_id=1, source_target_pairs={{0,1},{1,2},{2,3},{3,0},{4,5},{5,6},{6,7},{7,4},{8,9},{9,10},{10,1... | collective-permute-start | bytes 589832 | tf_op jit(solution)/shard_map/ppermute | solution.py:19
  36.8 12.0 %collective-permute-start.4 = (bf16[3,2,128,128]{3,2,1,0:T(8,128)(2,1)S(1)}, bf16[3,2,128,128]{3,2,1,0:T(8,128)(2,1)S(1)}, u32[]{:S(2)}, u32[]{:S(2)}) collective-permute-start(bf16[3,2,128,128]{3,2,1,0:T(8,128)(2,1)S(1)} %pad_maximum_fusion.2), channel_id=1, source_target_pairs={{0,2},{1,3},{2,0},{3,1},{4,6},{5,7},{6,4},{7,5},{8,10},{9,11},{10,... | collective-permute-start | bytes 589832 | tf_op jit(solution)/shard_map/ppermute | solution.py:19
  41.6 8.5 %collective-permute-start.3 = (bf16[3,2,128,128]{3,2,1,0:T(8,128)(2,1)S(1)}, bf16[3,2,128,128]{3,2,1,0:T(8,128)(2,1)S(1)}, u32[]{:S(2)}, u32[]{:S(2)}) collective-permute-start(bf16[3,2,128,128]{3,2,1,0:T(8,128)(2,1)S(1)} %pad_maximum_fusion.2), channel_id=1, source_target_pairs={{0,3},{1,0},{2,1},{3,2},{4,7},{5,4},{6,5},{7,6},{8,11},{9,8},{10,9... | collective-permute-start | bytes 589832 | tf_op jit(solution)/shard_map/ppermute | solution.py:19
  44.9 1.2 copy-start
  50.1 4.6 %copy-start.2 = (bf16[4,2,512,128]{3,2,1,0:T(8,128)(2,1)}, bf16[4,2,512,128]{3,2,1,0:T(8,128)(2,1)S(1)}, u32[]{:S(2)}) copy-start(bf16[4,2,512,128]{3,2,1,0:T(8,128)(2,1)S(1)} %maximum_maximum_fusion.near_ref) | copy-start | bytes 3145732
  50.1 4.6 %collective-permute-start.6 = (bf16[4,2,512,128]{3,2,1,0:T(8,128)(2,1)S(1)}, bf16[4,2,512,128]{3,2,1,0:T(8,128)(2,1)S(1)}, u32[]{:S(2)}, u32[]{:S(2)}) collective-permute-start(bf16[4,2,512,128]{3,2,1,0:T(8,128)(2,1)S(1)} %maximum_maximum_fusion.near_ref), channel_id=1, source_target_pairs={{0,16},{16,0},{32,48},{48,32},{64,80},{80,64},{96,112},{112,96},{1... | collective-permute-start | bytes 3145736 | tf_op jit(solution)/shard_map/ppermute | solution.py:39
  54.7 1.0 copy-start.3
  74.9 4.6 %collective-permute-start.7 = (bf16[2,4,512,128]{3,2,1,0:T(8,128)(2,1)S(1)}, bf16[2,4,512,128]{3,2,1,0:T(8,128)(2,1)S(1)}, u32[]{:S(2)}, u32[]{:S(2)}) collective-permute-start(bf16[2,4,512,128]{3,2,1,0:T(8,128)(2,1)S(1)} %slice.96), channel_id=1, source_target_pairs={{0,16},{16,0},{32,48},{48,32},{64,80},{80,64},{96,112},{112,96},{1... | collective-permute-start | bytes 3145736 | tf_op jit(solution)/shard_map/ppermute | solution.py:39
  81.5 16.1 %collective-permute-start.10 = (bf16[2,4,128,128]{3,2,1,0:T(8,128)(2,1)S(1)}, bf16[2,4,128,128]{3,2,1,0:T(8,128)(2,1)S(1)}, u32[]{:S(2)}, u32[]{:S(2)}) collective-permute-start(bf16[2,4,128,128]{3,2,1,0:T(8,128)(2,1)S(1)} %get-tuple-element.17), channel_id=1, source_target_pairs={{0,3},{1,0},{2,1},{3,2},{4,7},{5,4},{6,5},{7,6},{8,11},{9,8},{10,9... | collective-permute-start | bytes 786440 | tf_op jit(solution)/shard_map/ppermute | solution.py:19
  86.1 12.6 %collective-permute-start.9 = (bf16[2,4,128,128]{3,2,1,0:T(8,128)(2,1)S(1)}, bf16[2,4,128,128]{3,2,1,0:T(8,128)(2,1)S(1)}, u32[]{:S(2)}, u32[]{:S(2)}) collective-permute-start(bf16[2,4,128,128]{3,2,1,0:T(8,128)(2,1)S(1)} %get-tuple-element.18), channel_id=1, source_target_pairs={{0,2},{1,3},{2,0},{3,1},{4,6},{5,7},{6,4},{7,5},{8,10},{9,11},{10,... | collective-permute-start | bytes 786440 | tf_op jit(solution)/shard_map/ppermute | solution.py:19
  89.9 13.3 %collective-permute-start.8 = (bf16[2,4,128,128]{3,2,1,0:T(8,128)(2,1)S(1)}, bf16[2,4,128,128]{3,2,1,0:T(8,128)(2,1)S(1)}, u32[]{:S(2)}, u32[]{:S(2)}) collective-permute-start(bf16[2,4,128,128]{3,2,1,0:T(8,128)(2,1)S(1)} %get-tuple-element.16), channel_id=1, source_target_pairs={{0,1},{1,2},{2,3},{3,0},{4,5},{5,6},{6,7},{7,4},{8,9},{9,10},{10,1... | collective-permute-start | bytes 786440 | tf_op jit(solution)/shard_map/ppermute | solution.py:19
  103.3 16.7 %collective-permute-start.13 = (bf16[2,128,128]{2,1,0:T(8,128)(2,1)S(1)}, bf16[2,128,128]{2,1,0:T(8,128)(2,1)S(1)}, u32[]{:S(2)}, u32[]{:S(2)}) collective-permute-start(bf16[2,128,128]{2,1,0:T(8,128)(2,1)S(1)} %get-tuple-element.22), channel_id=1, source_target_pairs={{96,16},{128,48},{160,80},{192,112},{224,144},{256,176},{288,208},... | collective-permute-start | bytes 196616 | tf_op jit(solution)/shard_map/ppermute | solution.py:34
  109.7 15.1 %collective-permute-start.12 = (bf16[2,128,128]{2,1,0:T(8,128)(2,1)S(1)}, bf16[2,128,128]{2,1,0:T(8,128)(2,1)S(1)}, u32[]{:S(2)}, u32[]{:S(2)}) collective-permute-start(bf16[2,128,128]{2,1,0:T(8,128)(2,1)S(1)} %get-tuple-element.23), channel_id=1, source_target_pairs={{64,16},{96,48},{128,80},{160,112},{192,144},{224,176},{256,208},{... | collective-permute-start | bytes 196616 | tf_op jit(solution)/shard_map/ppermute | solution.py:34
  114.8 10.1 %collective-permute-start.11 = (bf16[2,128,128]{2,1,0:T(8,128)(2,1)S(1)}, bf16[2,128,128]{2,1,0:T(8,128)(2,1)S(1)}, u32[]{:S(2)}, u32[]{:S(2)}) collective-permute-start(bf16[2,128,128]{2,1,0:T(8,128)(2,1)S(1)} %get-tuple-element.21), channel_id=1, source_target_pairs={{32,16},{64,48},{96,80},{128,112},{160,144},{192,176},{224,208},{2... | collective-permute-start | bytes 196616 | tf_op jit(solution)/shard_map/ppermute | solution.py:34
  124.9 20.5 %collective-permute-start.16 = (bf16[2,128,128]{2,1,0:T(8,128)(2,1)S(1)}, bf16[2,128,128]{2,1,0:T(8,128)(2,1)S(1)}, u32[]{:S(2)}, u32[]{:S(2)}) collective-permute-start(bf16[2,128,128]{2,1,0:T(8,128)(2,1)S(1)} %fusion.8), channel_id=1, source_target_pairs={{0,4},{4,8},{8,12},{12,0},{1,5},{5,9},{9,13},{13,1},{2,6},{6,10},{... | collective-permute-start | bytes 196616 | tf_op jit(solution)/shard_map/ppermute | solution.py:19
  131.3 14.1 %collective-permute-start.15 = (bf16[2,128,128]{2,1,0:T(8,128)(2,1)S(1)}, bf16[2,128,128]{2,1,0:T(8,128)(2,1)S(1)}, u32[]{:S(2)}, u32[]{:S(2)}) collective-permute-start(bf16[2,128,128]{2,1,0:T(8,128)(2,1)S(1)} %fusion.8), channel_id=1, source_target_pairs={{0,8},{4,12},{8,0},{12,4},{1,9},{5,13},{9,1},{13,5},{2,10},{6,14},... | collective-permute-start | bytes 196616 | tf_op jit(solution)/shard_map/ppermute | solution.py:19
  140.5 6.7 %collective-permute-start.14 = (bf16[2,128,128]{2,1,0:T(8,128)(2,1)S(1)}, bf16[2,128,128]{2,1,0:T(8,128)(2,1)S(1)}, u32[]{:S(2)}, u32[]{:S(2)}) collective-permute-start(bf16[2,128,128]{2,1,0:T(8,128)(2,1)S(1)} %fusion.8), channel_id=1, source_target_pairs={{0,12},{4,0},{8,4},{12,8},{1,13},{5,1},{9,5},{13,9},{2,14},{6,2},{... | collective-permute-start | bytes 196616 | tf_op jit(solution)/shard_map/ppermute | solution.py:19
  147.3 15.6 %collective-permute-start.19 = (bf16[4,2,128,128]{3,2,1,0:T(8,128)(2,1)S(1)}, bf16[4,2,128,128]{3,2,1,0:T(8,128)(2,1)S(1)}, u32[]{:S(2)}, u32[]{:S(2)}) collective-permute-start(bf16[4,2,128,128]{3,2,1,0:T(8,128)(2,1)S(1)} %get-tuple-element.20), channel_id=1, source_target_pairs={{0,1},{1,2},{2,3},{3,0},{4,5},{5,6},{6,7},{7,4},{8,9},{9,10},{10,1... | collective-permute-start | bytes 786440 | tf_op jit(solution)/shard_map/ppermute | solution.py:19
  149.2 13.7 %collective-permute-start.18 = (bf16[4,2,128,128]{3,2,1,0:T(8,128)(2,1)S(1)}, bf16[4,2,128,128]{3,2,1,0:T(8,128)(2,1)S(1)}, u32[]{:S(2)}, u32[]{:S(2)}) collective-permute-start(bf16[4,2,128,128]{3,2,1,0:T(8,128)(2,1)S(1)} %get-tuple-element.20), channel_id=1, source_target_pairs={{0,2},{1,3},{2,0},{3,1},{4,6},{5,7},{6,4},{7,5},{8,10},{9,11},{10,... | collective-permute-start | bytes 786440 | tf_op jit(solution)/shard_map/ppermute | solution.py:19
  153.1 12.4 %collective-permute-start.17 = (bf16[4,2,128,128]{3,2,1,0:T(8,128)(2,1)S(1)}, bf16[4,2,128,128]{3,2,1,0:T(8,128)(2,1)S(1)}, u32[]{:S(2)}, u32[]{:S(2)}) collective-permute-start(bf16[4,2,128,128]{3,2,1,0:T(8,128)(2,1)S(1)} %get-tuple-element.20), channel_id=1, source_target_pairs={{0,3},{1,0},{2,1},{3,2},{4,7},{5,4},{6,5},{7,6},{8,11},{9,8},{10,9... | collective-permute-start | bytes 786440 | tf_op jit(solution)/shard_map/ppermute | solution.py:19

commit v13 on v9

--- a/solution.py
+++ b/solution.py
@@ -187,7 +187,7 @@
     )
     grads = jnp.stack([key_grad, value_grad]).reshape(2, store_span, tokens_here, width)
     half = store_span // 2
-    back = swap_cores(grads[:, half:].astype(jnp.bfloat16), "ctx").astype(jnp.float32)
+    back = swap_cores(grads[:, half:], "ctx")
     totals = grads[:, :half] + back
     sent = totals.astype(jnp.bfloat16)
 

time: 167 us -> 168 us (level)
  no operation moved by 1% of the time
where the time goes in v13:
time: 168 us
  starting transfers between devices  94.3 us (56%)
  waiting for transfers between devices  41.7 us (25%)
  Pallas kernels  16.1 us (10%)
  local copies, waits for them, and re-layouts  8.73 us (5%)
  other arithmetic  5.51 us (3%)
    ppermute x12, starting transfers between devices, cycled(): lax.ppermute(value, axis, [(source, (source + steps) % count) for source...  52.6 us
    ppermute x12, waiting for transfers between devices, cycled(): lax.ppermute(value, axis, [(source, (source + steps) % count) for source...  23.1 us
    ppermute x3, starting transfers between devices, chip_fetch(): return lax.ppermute(value, axis, chip_pairs(lax.axis_size(axis), step))  21 us
    ppermute x3, starting transfers between devices, chip_return(): lax.ppermute(value, axis, [(target, source) for source, target in pairs])  16.6 us
    pallas_call x1, Pallas kernels, local_grads(): pl.pallas_call(kernel, grid_spec=pltpu.PrefetchScalarGridSpec(num_scalar_...  16.1 us
    ppermute x3, waiting for transfers between devices, chip_fetch(): return lax.ppermute(value, axis, chip_pairs(lax.axis_size(axis), step))  9.16 us
    ppermute x3, waiting for transfers between devices, chip_return(): lax.ppermute(value, axis, [(target, source) for source, target in pairs])  4.78 us
    ppermute x2, waiting for transfers between devices, swap_cores(): lax.ppermute(value, axis, [(source, source ^ 1) for source in range(count)])  4.67 us
  transfers between devices with their start and end apart: 20, of which 15 were waited for; matrix products, arithmetic and copies ran while one was open for 4% of the time, Pallas kernels for 0%

profile of v13, /device:TPU:6, one launch (start us, length us, event | category | flops | bytes accessed | tf_op | source)
XLA Modules:
  0.0 167.5 jit_solution(8695333301542684041)
XLA Ops:
  0.7 1.0 constant_dynamic-slice_fusion
  1.7 0.5 fusion.5
  2.2 12.2 %collective-permute-start.2 = (bf16[2,128,128]{2,1,0:T(8,128)(2,1)S(1)}, bf16[2,128,128]{2,1,0:T(8,128)(2,1)S(1)}, u32[]{:S(2)}, u32[]{:S(2)}) collective-permute-start(bf16[2,128,128]{2,1,0:T(8,128)(2,1)S(1)} %slice.71), channel_id=1, source_target_pairs={{16,96},{48,128},{80,160},{112,192},{144,224},{176,256},{208,288},... | collective-permute-start | bytes 196616 | tf_op jit(solution)/shard_map/ppermute | solution.py:29
  14.3 4.3 %collective-permute-start.1 = (bf16[2,128,128]{2,1,0:T(8,128)(2,1)S(1)}, bf16[2,128,128]{2,1,0:T(8,128)(2,1)S(1)}, u32[]{:S(2)}, u32[]{:S(2)}) collective-permute-start(bf16[2,128,128]{2,1,0:T(8,128)(2,1)S(1)} %slice.71), channel_id=1, source_target_pairs={{16,64},{48,96},{80,128},{112,160},{144,192},{176,224},{208,256},{... | collective-permute-start | bytes 196616 | tf_op jit(solution)/shard_map/ppermute | solution.py:29
  18.6 4.6 %collective-permute-start = (bf16[2,128,128]{2,1,0:T(8,128)(2,1)S(1)}, bf16[2,128,128]{2,1,0:T(8,128)(2,1)S(1)}, u32[]{:S(2)}, u32[]{:S(2)}) collective-permute-start(bf16[2,128,128]{2,1,0:T(8,128)(2,1)S(1)} %slice.71), channel_id=1, source_target_pairs={{16,32},{48,64},{80,96},{112,128},{144,160},{176,192},{208,224},{2... | collective-permute-start | bytes 196616 | tf_op jit(solution)/shard_map/ppermute | solution.py:29
  23.2 0.8 constant_dynamic-slice_fusion.2
  24.0 0.1 reshape.262
  24.1 2.6 %collective-permute-done.2 = bf16[2,128,128]{2,1,0:T(8,128)(2,1)S(1)} collective-permute-done((bf16[2,128,128]{2,1,0:T(8,128)(2,1)S(1)}, bf16[2,128,128]{2,1,0:T(8,128)(2,1)S(1)}, u32[]{:S(2)}, u32[]{:S(2)}) %collective-permute-start.2) | collective-permute-done | bytes 65568 | tf_op jit(solution)/shard_map/ppermute | solution.py:29
  26.7 3.3 %collective-permute-done.1 = bf16[2,128,128]{2,1,0:T(8,128)(2,1)S(1)} collective-permute-done((bf16[2,128,128]{2,1,0:T(8,128)(2,1)S(1)}, bf16[2,128,128]{2,1,0:T(8,128)(2,1)S(1)}, u32[]{:S(2)}, u32[]{:S(2)}) %collective-permute-start.1) | collective-permute-done | bytes 65568 | tf_op jit(solution)/shard_map/ppermute | solution.py:29
  29.9 3.3 %collective-permute-done = bf16[2,128,128]{2,1,0:T(8,128)(2,1)S(1)} collective-permute-done((bf16[2,128,128]{2,1,0:T(8,128)(2,1)S(1)}, bf16[2,128,128]{2,1,0:T(8,128)(2,1)S(1)}, u32[]{:S(2)}, u32[]{:S(2)}) %collective-permute-start) | collective-permute-done | bytes 65568 | tf_op jit(solution)/shard_map/ppermute | solution.py:29
  33.3 3.5 %collective-permute-start.5 = (bf16[3,2,128,128]{3,2,1,0:T(8,128)(2,1)S(1)}, bf16[3,2,128,128]{3,2,1,0:T(8,128)(2,1)S(1)}, u32[]{:S(2)}, u32[]{:S(2)}) collective-permute-start(bf16[3,2,128,128]{3,2,1,0:T(8,128)(2,1)S(1)} %pad_maximum_fusion.4), channel_id=1, source_target_pairs={{0,1},{1,2},{2,3},{3,0},{4,5},{5,6},{6,7},{7,4},{8,9},{9,10},{10,1... | collective-permute-start | bytes 589832 | tf_op jit(solution)/shard_map/ppermute | solution.py:19
  36.8 4.8 %collective-permute-start.4 = (bf16[3,2,128,128]{3,2,1,0:T(8,128)(2,1)S(1)}, bf16[3,2,128,128]{3,2,1,0:T(8,128)(2,1)S(1)}, u32[]{:S(2)}, u32[]{:S(2)}) collective-permute-start(bf16[3,2,128,128]{3,2,1,0:T(8,128)(2,1)S(1)} %pad_maximum_fusion.4), channel_id=1, source_target_pairs={{0,2},{1,3},{2,0},{3,1},{4,6},{5,7},{6,4},{7,5},{8,10},{9,11},{10,... | collective-permute-start | bytes 589832 | tf_op jit(solution)/shard_map/ppermute | solution.py:19
  41.6 3.3 %collective-permute-start.3 = (bf16[3,2,128,128]{3,2,1,0:T(8,128)(2,1)S(1)}, bf16[3,2,128,128]{3,2,1,0:T(8,128)(2,1)S(1)}, u32[]{:S(2)}, u32[]{:S(2)}) collective-permute-start(bf16[3,2,128,128]{3,2,1,0:T(8,128)(2,1)S(1)} %pad_maximum_fusion.4), channel_id=1, source_target_pairs={{0,3},{1,0},{2,1},{3,2},{4,7},{5,4},{6,5},{7,6},{8,11},{9,8},{10,9... | collective-permute-start | bytes 589832 | tf_op jit(solution)/shard_map/ppermute | solution.py:19
  44.9 1.2 gather_fusion
  46.1 1.2 gather_fusion.1
  47.4 0.5 fusion.37
  47.9 0.9 collective-permute-done.4
  48.7 1.3 collective-permute-done.3
  50.1 1.9 %collective-permute-start.6 = (bf16[4,2,512,128]{3,2,1,0:T(8,128)(2,1)S(1)}, bf16[4,2,512,128]{3,2,1,0:T(8,128)(2,1)S(1)}, u32[]{:S(2)}, u32[]{:S(2)}) collective-permute-start(bf16[4,2,512,128]{3,2,1,0:T(8,128)(2,1)S(1)} %maximum_maximum_fusion), channel_id=1, source_target_pairs={{0,16},{16,0},{32,48},{48,32},{64,80},{80,64},{96,112},{112,96},{1... | collective-permute-start | bytes 3145736 | tf_op jit(solution)/shard_map/ppermute | solution.py:39
  52.1 0.1 reshape.289
  52.2 0.1 fusion.20
  52.3 0.1 broadcast_in_dim.47
  52.3 0.1 eq.59
  52.4 0.1 broadcast_in_dim.49
  52.5 0.1 eq.60
  52.6 0.1 broadcast_in_dim.50
  52.7 0.6 fusion.19.slots_ref
  53.3 0.7 select_select_fusion.code_ref
  54.0 0.7 collective-permute-done.6
  54.7 0.2 pad_maximum_fusion.1
  54.9 1.5 fusion.35
  56.3 16.1 %shard_map.103 = (bf16[2048,128]{1,0:T(8,128)(2,1)}, f32[4096,128]{1,0:T(8,128)}, f32[4096,128]{1,0:T(8,128)}) custom-call(s32[8,16]{1,0:T(8,128)} %fusion.19.slots_ref, bf16[2048,128]{1,0:T(8,128)(2,1)} %bitcast.81, bf16[2048,128]{1,0:T(8,128)(2,1)} %bitcast.82, s32[8,1,1024]{2,1,0:T(1,128)} %select_select_fusion.code_ref, bf16[4096,128]{1,0:T(8,128)(2,1)} %bitcast.69, ...), custom_call_target="tpu_custom_call" | custom-call | tf_op jit(solution)/shard_map/pallas_call | solution.py:105
  72.5 1.8 %pad_maximum_fusion = f32[2,4,512,128]{3,2,1,0:T(8,128)S(1)} fusion(f32[1,8,512,128]{3,2,1,0:T(8,128)} %bitcast.64, f32[1,8,512,128]{3,2,1,0:T(8,128)} %bitcast.62), kind=kLoop, calls=%fused_computation.7 | loop fusion | flops 524288 | bytes 6291456 | tf_op jit(solution)/shard_map/stack | solution.py:188
  74.3 2.2 %collective-permute-start.7 = (f32[2,4,512,128]{3,2,1,0:T(8,128)S(1)}, f32[2,4,512,128]{3,2,1,0:T(8,128)S(1)}, u32[]{:S(2)}, u32[]{:S(2)}) collective-permute-start(f32[2,4,512,128]{3,2,1,0:T(8,128)S(1)} %pad_maximum_fusion), channel_id=1, source_target_pairs={{0,16},{16,0},{32,48},{48,32},{64,80},{80,64},{96,112},{112,96},{1... | collective-permute-start | bytes 6291464 | tf_op jit(solution)/shard_map/ppermute | solution.py:39
  76.5 4.0 %collective-permute-done.7 = f32[2,4,512,128]{3,2,1,0:T(8,128)S(1)} collective-permute-done((f32[2,4,512,128]{3,2,1,0:T(8,128)S(1)}, f32[2,4,512,128]{3,2,1,0:T(8,128)S(1)}, u32[]{:S(2)}, u32[]{:S(2)}) %collective-permute-start.7) | collective-permute-done | bytes 2097184 | tf_op jit(solution)/shard_map/ppermute | solution.py:39
  80.5 0.3 fusion.32
  80.9 4.6 %collective-permute-start.10 = (bf16[2,4,128,128]{3,2,1,0:T(8,128)(2,1)S(1)}, bf16[2,4,128,128]{3,2,1,0:T(8,128)(2,1)S(1)}, u32[]{:S(2)}, u32[]{:S(2)}) collective-permute-start(bf16[2,4,128,128]{3,2,1,0:T(8,128)(2,1)S(1)} %get-tuple-element.21), channel_id=1, source_target_pairs={{0,3},{1,0},{2,1},{3,2},{4,7},{5,4},{6,5},{7,6},{8,11},{9,8},{10,9... | collective-permute-start | bytes 786440 | tf_op jit(solution)/shard_map/ppermute | solution.py:19
  85.5 3.8 %collective-permute-start.9 = (bf16[2,4,128,128]{3,2,1,0:T(8,128)(2,1)S(1)}, bf16[2,4,128,128]{3,2,1,0:T(8,128)(2,1)S(1)}, u32[]{:S(2)}, u32[]{:S(2)}) collective-permute-start(bf16[2,4,128,128]{3,2,1,0:T(8,128)(2,1)S(1)} %get-tuple-element.22), channel_id=1, source_target_pairs={{0,2},{1,3},{2,0},{3,1},{4,6},{5,7},{6,4},{7,5},{8,10},{9,11},{10,... | collective-permute-start | bytes 786440 | tf_op jit(solution)/shard_map/ppermute | solution.py:19
  89.3 1.9 %collective-permute-start.8 = (bf16[2,4,128,128]{3,2,1,0:T(8,128)(2,1)S(1)}, bf16[2,4,128,128]{3,2,1,0:T(8,128)(2,1)S(1)}, u32[]{:S(2)}, u32[]{:S(2)}) collective-permute-start(bf16[2,4,128,128]{3,2,1,0:T(8,128)(2,1)S(1)} %get-tuple-element.20), channel_id=1, source_target_pairs={{0,1},{1,2},{2,3},{3,0},{4,5},{5,6},{6,7},{7,4},{8,9},{9,10},{10,1... | collective-permute-start | bytes 786440 | tf_op jit(solution)/shard_map/ppermute | solution.py:19
  91.3 5.7 %collective-permute-done.10 = bf16[2,4,128,128]{3,2,1,0:T(8,128)(2,1)S(1)} collective-permute-done((bf16[2,4,128,128]{3,2,1,0:T(8,128)(2,1)S(1)}, bf16[2,4,128,128]{3,2,1,0:T(8,128)(2,1)S(1)}, u32[]{:S(2)}, u32[]{:S(2)}) %collective-permute-start.10) | collective-permute-done | bytes 262176 | tf_op jit(solution)/shard_map/ppermute | solution.py:19
  97.0 1.1 collective-permute-done.9
  98.1 4.5 %collective-permute-done.8 = bf16[2,4,128,128]{3,2,1,0:T(8,128)(2,1)S(1)} collective-permute-done((bf16[2,4,128,128]{3,2,1,0:T(8,128)(2,1)S(1)}, bf16[2,4,128,128]{3,2,1,0:T(8,128)(2,1)S(1)}, u32[]{:S(2)}, u32[]{:S(2)}) %collective-permute-start.8) | collective-permute-done | bytes 262176 | tf_op jit(solution)/shard_map/ppermute | solution.py:19
  102.6 0.1 fusion.30
  102.8 6.3 %collective-permute-start.13 = (bf16[2,128,128]{2,1,0:T(8,128)(2,1)S(1)}, bf16[2,128,128]{2,1,0:T(8,128)(2,1)S(1)}, u32[]{:S(2)}, u32[]{:S(2)}) collective-permute-start(bf16[2,128,128]{2,1,0:T(8,128)(2,1)S(1)} %get-tuple-element.26), channel_id=1, source_target_pairs={{96,16},{128,48},{160,80},{192,112},{224,144},{256,176},{288,208},... | collective-permute-start | bytes 196616 | tf_op jit(solution)/shard_map/ppermute | solution.py:34
  109.1 5.1 %collective-permute-start.12 = (bf16[2,128,128]{2,1,0:T(8,128)(2,1)S(1)}, bf16[2,128,128]{2,1,0:T(8,128)(2,1)S(1)}, u32[]{:S(2)}, u32[]{:S(2)}) collective-permute-start(bf16[2,128,128]{2,1,0:T(8,128)(2,1)S(1)} %get-tuple-element.27), channel_id=1, source_target_pairs={{64,16},{96,48},{128,80},{160,112},{192,144},{224,176},{256,208},{... | collective-permute-start | bytes 196616 | tf_op jit(solution)/shard_map/ppermute | solution.py:34
  114.3 5.1 %collective-permute-start.11 = (bf16[2,128,128]{2,1,0:T(8,128)(2,1)S(1)}, bf16[2,128,128]{2,1,0:T(8,128)(2,1)S(1)}, u32[]{:S(2)}, u32[]{:S(2)}) collective-permute-start(bf16[2,128,128]{2,1,0:T(8,128)(2,1)S(1)} %get-tuple-element.25), channel_id=1, source_target_pairs={{32,16},{64,48},{96,80},{128,112},{160,144},{192,176},{224,208},{2... | collective-permute-start | bytes 196616 | tf_op jit(solution)/shard_map/ppermute | solution.py:34
  119.4 0.1 broadcast_add_fusion
  119.4 0.1 add.179
  119.5 4.7 %collective-permute-done.12 = bf16[2,128,128]{2,1,0:T(8,128)(2,1)S(1)} collective-permute-done((bf16[2,128,128]{2,1,0:T(8,128)(2,1)S(1)}, bf16[2,128,128]{2,1,0:T(8,128)(2,1)S(1)}, u32[]{:S(2)}, u32[]{:S(2)}) %collective-permute-start.12) | collective-permute-done | bytes 65568 | tf_op jit(solution)/shard_map/ppermute | solution.py:34
  124.2 0.1 collective-permute-done.11
  124.3 6.4 %collective-permute-start.16 = (bf16[2,128,128]{2,1,0:T(8,128)(2,1)S(1)}, bf16[2,128,128]{2,1,0:T(8,128)(2,1)S(1)}, u32[]{:S(2)}, u32[]{:S(2)}) collective-permute-start(bf16[2,128,128]{2,1,0:T(8,128)(2,1)S(1)} %fusion.10), channel_id=1, source_target_pairs={{0,4},{4,8},{8,12},{12,0},{1,5},{5,9},{9,13},{13,1},{2,6},{6,10},{... | collective-permute-start | bytes 196616 | tf_op jit(solution)/shard_map/ppermute | solution.py:19
  130.8 9.2 %collective-permute-start.15 = (bf16[2,128,128]{2,1,0:T(8,128)(2,1)S(1)}, bf16[2,128,128]{2,1,0:T(8,128)(2,1)S(1)}, u32[]{:S(2)}, u32[]{:S(2)}) collective-permute-start(bf16[2,128,128]{2,1,0:T(8,128)(2,1)S(1)} %fusion.10), channel_id=1, source_target_pairs={{0,8},{4,12},{8,0},{12,4},{1,9},{5,13},{9,1},{13,5},{2,10},{6,14},... | collective-permute-start | bytes 196616 | tf_op jit(solution)/shard_map/ppermute | solution.py:19
  140.0 4.8 %collective-permute-start.14 = (bf16[2,128,128]{2,1,0:T(8,128)(2,1)S(1)}, bf16[2,128,128]{2,1,0:T(8,128)(2,1)S(1)}, u32[]{:S(2)}, u32[]{:S(2)}) collective-permute-start(bf16[2,128,128]{2,1,0:T(8,128)(2,1)S(1)} %fusion.10), channel_id=1, source_target_pairs={{0,12},{4,0},{8,4},{12,8},{1,13},{5,1},{9,5},{13,9},{2,14},{6,2},{... | collective-permute-start | bytes 196616 | tf_op jit(solution)/shard_map/ppermute | solution.py:19
  144.8 1.9 %collective-permute-done.14 = bf16[2,128,128]{2,1,0:T(8,128)(2,1)S(1)} collective-permute-done((bf16[2,128,128]{2,1,0:T(8,128)(2,1)S(1)}, bf16[2,128,128]{2,1,0:T(8,128)(2,1)S(1)}, u32[]{:S(2)}, u32[]{:S(2)}) %collective-permute-start.14) | collective-permute-done | bytes 65568 | tf_op jit(solution)/shard_map/ppermute | solution.py:19
  146.7 1.9 %collective-permute-start.19 = (bf16[4,2,128,128]{3,2,1,0:T(8,128)(2,1)S(1)}, bf16[4,2,128,128]{3,2,1,0:T(8,128)(2,1)S(1)}, u32[]{:S(2)}, u32[]{:S(2)}) collective-permute-start(bf16[4,2,128,128]{3,2,1,0:T(8,128)(2,1)S(1)} %get-tuple-element.24), channel_id=1, source_target_pairs={{0,1},{1,2},{2,3},{3,0},{4,5},{5,6},{6,7},{7,4},{8,9},{9,10},{10,1... | collective-permute-start | bytes 786440 | tf_op jit(solution)/shard_map/ppermute | solution.py:19
  148.7 3.8 %collective-permute-start.18 = (bf16[4,2,128,128]{3,2,1,0:T(8,128)(2,1)S(1)}, bf16[4,2,128,128]{3,2,1,0:T(8,128)(2,1)S(1)}, u32[]{:S(2)}, u32[]{:S(2)}) collective-permute-start(bf16[4,2,128,128]{3,2,1,0:T(8,128)(2,1)S(1)} %get-tuple-element.24), channel_id=1, source_target_pairs={{0,2},{1,3},{2,0},{3,1},{4,6},{5,7},{6,4},{7,5},{8,10},{9,11},{10,... | collective-permute-start | bytes 786440 | tf_op jit(solution)/shard_map/ppermute | solution.py:19
  152.5 4.5 %collective-permute-start.17 = (bf16[4,2,128,128]{3,2,1,0:T(8,128)(2,1)S(1)}, bf16[4,2,128,128]{3,2,1,0:T(8,128)(2,1)S(1)}, u32[]{:S(2)}, u32[]{:S(2)}) collective-permute-start(bf16[4,2,128,128]{3,2,1,0:T(8,128)(2,1)S(1)} %get-tuple-element.24), channel_id=1, source_target_pairs={{0,3},{1,0},{2,1},{3,2},{4,7},{5,4},{6,5},{7,6},{8,11},{9,8},{10,9... | collective-permute-start | bytes 786440 | tf_op jit(solution)/shard_map/ppermute | solution.py:19
  157.0 0.1 compare_and_fusion
  157.1 5.2 %collective-permute-done.19 = bf16[4,2,128,128]{3,2,1,0:T(8,128)(2,1)S(1)} collective-permute-done((bf16[4,2,128,128]{3,2,1,0:T(8,128)(2,1)S(1)}, bf16[4,2,128,128]{3,2,1,0:T(8,128)(2,1)S(1)}, u32[]{:S(2)}, u32[]{:S(2)}) %collective-permute-start.19) | collective-permute-done | bytes 262176 | tf_op jit(solution)/shard_map/ppermute | solution.py:19
  162.4 2.5 %collective-permute-done.17 = bf16[4,2,128,128]{3,2,1,0:T(8,128)(2,1)S(1)} collective-permute-done((bf16[4,2,128,128]{3,2,1,0:T(8,128)(2,1)S(1)}, bf16[4,2,128,128]{3,2,1,0:T(8,128)(2,1)S(1)}, u32[]{:S(2)}, u32[]{:S(2)}) %collective-permute-start.17) | collective-permute-done | bytes 262176 | tf_op jit(solution)/shard_map/ppermute | solution.py:19
  164.9 0.1 pad_maximum_fusion.2
  165.0 0.7 gather_fusion.2
  165.8 0.2 convert_bitcast_fusion
  166.0 1.5 fusion.34
  (30 shorter events, 0.4 us)
Async XLA Ops:
  0.6 44.2 %copy-start.1 = (s32[7]{0:T(128)S(1)}, s32[7]{0:T(128)}, u32[]{:S(2)}) copy-start(s32[7]{0:T(128)} %constant.156.clone) | copy-start | bytes 88
  2.2 24.5 %collective-permute-start.2 = (bf16[2,128,128]{2,1,0:T(8,128)(2,1)S(1)}, bf16[2,128,128]{2,1,0:T(8,128)(2,1)S(1)}, u32[]{:S(2)}, u32[]{:S(2)}) collective-permute-start(bf16[2,128,128]{2,1,0:T(8,128)(2,1)S(1)} %slice.71), channel_id=1, source_target_pairs={{16,96},{48,128},{80,160},{112,192},{144,224},{176,256},{208,288},... | collective-permute-start | bytes 196616 | tf_op jit(solution)/shard_map/ppermute | solution.py:29
  14.3 15.6 %collective-permute-start.1 = (bf16[2,128,128]{2,1,0:T(8,128)(2,1)S(1)}, bf16[2,128,128]{2,1,0:T(8,128)(2,1)S(1)}, u32[]{:S(2)}, u32[]{:S(2)}) collective-permute-start(bf16[2,128,128]{2,1,0:T(8,128)(2,1)S(1)} %slice.71), channel_id=1, source_target_pairs={{16,64},{48,96},{80,128},{112,160},{144,192},{176,224},{208,256},{... | collective-permute-start | bytes 196616 | tf_op jit(solution)/shard_map/ppermute | solution.py:29
  18.6 14.6 %collective-permute-start = (bf16[2,128,128]{2,1,0:T(8,128)(2,1)S(1)}, bf16[2,128,128]{2,1,0:T(8,128)(2,1)S(1)}, u32[]{:S(2)}, u32[]{:S(2)}) collective-permute-start(bf16[2,128,128]{2,1,0:T(8,128)(2,1)S(1)} %slice.71), channel_id=1, source_target_pairs={{16,32},{48,64},{80,96},{112,128},{144,160},{176,192},{208,224},{2... | collective-permute-start | bytes 196616 | tf_op jit(solution)/shard_map/ppermute | solution.py:29
  33.3 14.6 %collective-permute-start.5 = (bf16[3,2,128,128]{3,2,1,0:T(8,128)(2,1)S(1)}, bf16[3,2,128,128]{3,2,1,0:T(8,128)(2,1)S(1)}, u32[]{:S(2)}, u32[]{:S(2)}) collective-permute-start(bf16[3,2,128,128]{3,2,1,0:T(8,128)(2,1)S(1)} %pad_maximum_fusion.4), channel_id=1, source_target_pairs={{0,1},{1,2},{2,3},{3,0},{4,5},{5,6},{6,7},{7,4},{8,9},{9,10},{10,1... | collective-permute-start | bytes 589832 | tf_op jit(solution)/shard_map/ppermute | solution.py:19
  36.8 12.0 %collective-permute-start.4 = (bf16[3,2,128,128]{3,2,1,0:T(8,128)(2,1)S(1)}, bf16[3,2,128,128]{3,2,1,0:T(8,128)(2,1)S(1)}, u32[]{:S(2)}, u32[]{:S(2)}) collective-permute-start(bf16[3,2,128,128]{3,2,1,0:T(8,128)(2,1)S(1)} %pad_maximum_fusion.4), channel_id=1, source_target_pairs={{0,2},{1,3},{2,0},{3,1},{4,6},{5,7},{6,4},{7,5},{8,10},{9,11},{10,... | collective-permute-start | bytes 589832 | tf_op jit(solution)/shard_map/ppermute | solution.py:19
  41.6 8.5 %collective-permute-start.3 = (bf16[3,2,128,128]{3,2,1,0:T(8,128)(2,1)S(1)}, bf16[3,2,128,128]{3,2,1,0:T(8,128)(2,1)S(1)}, u32[]{:S(2)}, u32[]{:S(2)}) collective-permute-start(bf16[3,2,128,128]{3,2,1,0:T(8,128)(2,1)S(1)} %pad_maximum_fusion.4), channel_id=1, source_target_pairs={{0,3},{1,0},{2,1},{3,2},{4,7},{5,4},{6,5},{7,6},{8,11},{9,8},{10,9... | collective-permute-start | bytes 589832 | tf_op jit(solution)/shard_map/ppermute | solution.py:19
  44.9 1.2 copy-start
  50.1 4.6 %collective-permute-start.6 = (bf16[4,2,512,128]{3,2,1,0:T(8,128)(2,1)S(1)}, bf16[4,2,512,128]{3,2,1,0:T(8,128)(2,1)S(1)}, u32[]{:S(2)}, u32[]{:S(2)}) collective-permute-start(bf16[4,2,512,128]{3,2,1,0:T(8,128)(2,1)S(1)} %maximum_maximum_fusion), channel_id=1, source_target_pairs={{0,16},{16,0},{32,48},{48,32},{64,80},{80,64},{96,112},{112,96},{1... | collective-permute-start | bytes 3145736 | tf_op jit(solution)/shard_map/ppermute | solution.py:39
  72.5 8.1 %copy-start.2 = (f32[4096,128]{1,0:T(8,128)S(1)}, f32[4096,128]{1,0:T(8,128)}, u32[]{:S(2)}) copy-start(f32[4096,128]{1,0:T(8,128)} %get-tuple-element.7) | copy-start | bytes 6291460
  72.5 8.0 %copy-start.3 = (f32[4096,128]{1,0:T(8,128)S(1)}, f32[4096,128]{1,0:T(8,128)}, u32[]{:S(2)}) copy-start(f32[4096,128]{1,0:T(8,128)} %get-tuple-element.8) | copy-start | bytes 6291460
  74.3 6.2 %collective-permute-start.7 = (f32[2,4,512,128]{3,2,1,0:T(8,128)S(1)}, f32[2,4,512,128]{3,2,1,0:T(8,128)S(1)}, u32[]{:S(2)}, u32[]{:S(2)}) collective-permute-start(f32[2,4,512,128]{3,2,1,0:T(8,128)S(1)} %pad_maximum_fusion), channel_id=1, source_target_pairs={{0,16},{16,0},{32,48},{48,32},{64,80},{80,64},{96,112},{112,96},{1... | collective-permute-start | bytes 6291464 | tf_op jit(solution)/shard_map/ppermute | solution.py:39
  80.9 16.1 %collective-permute-start.10 = (bf16[2,4,128,128]{3,2,1,0:T(8,128)(2,1)S(1)}, bf16[2,4,128,128]{3,2,1,0:T(8,128)(2,1)S(1)}, u32[]{:S(2)}, u32[]{:S(2)}) collective-permute-start(bf16[2,4,128,128]{3,2,1,0:T(8,128)(2,1)S(1)} %get-tuple-element.21), channel_id=1, source_target_pairs={{0,3},{1,0},{2,1},{3,2},{4,7},{5,4},{6,5},{7,6},{8,11},{9,8},{10,9... | collective-permute-start | bytes 786440 | tf_op jit(solution)/shard_map/ppermute | solution.py:19
  85.5 12.6 %collective-permute-start.9 = (bf16[2,4,128,128]{3,2,1,0:T(8,128)(2,1)S(1)}, bf16[2,4,128,128]{3,2,1,0:T(8,128)(2,1)S(1)}, u32[]{:S(2)}, u32[]{:S(2)}) collective-permute-start(bf16[2,4,128,128]{3,2,1,0:T(8,128)(2,1)S(1)} %get-tuple-element.22), channel_id=1, source_target_pairs={{0,2},{1,3},{2,0},{3,1},{4,6},{5,7},{6,4},{7,5},{8,10},{9,11},{10,... | collective-permute-start | bytes 786440 | tf_op jit(solution)/shard_map/ppermute | solution.py:19
  89.3 13.3 %collective-permute-start.8 = (bf16[2,4,128,128]{3,2,1,0:T(8,128)(2,1)S(1)}, bf16[2,4,128,128]{3,2,1,0:T(8,128)(2,1)S(1)}, u32[]{:S(2)}, u32[]{:S(2)}) collective-permute-start(bf16[2,4,128,128]{3,2,1,0:T(8,128)(2,1)S(1)} %get-tuple-element.20), channel_id=1, source_target_pairs={{0,1},{1,2},{2,3},{3,0},{4,5},{5,6},{6,7},{7,4},{8,9},{9,10},{10,1... | collective-permute-start | bytes 786440 | tf_op jit(solution)/shard_map/ppermute | solution.py:19
  102.8 16.7 %collective-permute-start.13 = (bf16[2,128,128]{2,1,0:T(8,128)(2,1)S(1)}, bf16[2,128,128]{2,1,0:T(8,128)(2,1)S(1)}, u32[]{:S(2)}, u32[]{:S(2)}) collective-permute-start(bf16[2,128,128]{2,1,0:T(8,128)(2,1)S(1)} %get-tuple-element.26), channel_id=1, source_target_pairs={{96,16},{128,48},{160,80},{192,112},{224,144},{256,176},{288,208},... | collective-permute-start | bytes 196616 | tf_op jit(solution)/shard_map/ppermute | solution.py:34
  109.1 15.1 %collective-permute-start.12 = (bf16[2,128,128]{2,1,0:T(8,128)(2,1)S(1)}, bf16[2,128,128]{2,1,0:T(8,128)(2,1)S(1)}, u32[]{:S(2)}, u32[]{:S(2)}) collective-permute-start(bf16[2,128,128]{2,1,0:T(8,128)(2,1)S(1)} %get-tuple-element.27), channel_id=1, source_target_pairs={{64,16},{96,48},{128,80},{160,112},{192,144},{224,176},{256,208},{... | collective-permute-start | bytes 196616 | tf_op jit(solution)/shard_map/ppermute | solution.py:34
  114.3 10.0 %collective-permute-start.11 = (bf16[2,128,128]{2,1,0:T(8,128)(2,1)S(1)}, bf16[2,128,128]{2,1,0:T(8,128)(2,1)S(1)}, u32[]{:S(2)}, u32[]{:S(2)}) collective-permute-start(bf16[2,128,128]{2,1,0:T(8,128)(2,1)S(1)} %get-tuple-element.25), channel_id=1, source_target_pairs={{32,16},{64,48},{96,80},{128,112},{160,144},{192,176},{224,208},{2... | collective-permute-start | bytes 196616 | tf_op jit(solution)/shard_map/ppermute | solution.py:34
  124.3 20.5 %collective-permute-start.16 = (bf16[2,128,128]{2,1,0:T(8,128)(2,1)S(1)}, bf16[2,128,128]{2,1,0:T(8,128)(2,1)S(1)}, u32[]{:S(2)}, u32[]{:S(2)}) collective-permute-start(bf16[2,128,128]{2,1,0:T(8,128)(2,1)S(1)} %fusion.10), channel_id=1, source_target_pairs={{0,4},{4,8},{8,12},{12,0},{1,5},{5,9},{9,13},{13,1},{2,6},{6,10},{... | collective-permute-start | bytes 196616 | tf_op jit(solution)/shard_map/ppermute | solution.py:19
  130.8 14.1 %collective-permute-start.15 = (bf16[2,128,128]{2,1,0:T(8,128)(2,1)S(1)}, bf16[2,128,128]{2,1,0:T(8,128)(2,1)S(1)}, u32[]{:S(2)}, u32[]{:S(2)}) collective-permute-start(bf16[2,128,128]{2,1,0:T(8,128)(2,1)S(1)} %fusion.10), channel_id=1, source_target_pairs={{0,8},{4,12},{8,0},{12,4},{1,9},{5,13},{9,1},{13,5},{2,10},{6,14},... | collective-permute-start | bytes 196616 | tf_op jit(solution)/shard_map/ppermute | solution.py:19
  140.0 6.7 %collective-permute-start.14 = (bf16[2,128,128]{2,1,0:T(8,128)(2,1)S(1)}, bf16[2,128,128]{2,1,0:T(8,128)(2,1)S(1)}, u32[]{:S(2)}, u32[]{:S(2)}) collective-permute-start(bf16[2,128,128]{2,1,0:T(8,128)(2,1)S(1)} %fusion.10), channel_id=1, source_target_pairs={{0,12},{4,0},{8,4},{12,8},{1,13},{5,1},{9,5},{13,9},{2,14},{6,2},{... | collective-permute-start | bytes 196616 | tf_op jit(solution)/shard_map/ppermute | solution.py:19
  146.7 15.6 %collective-permute-start.19 = (bf16[4,2,128,128]{3,2,1,0:T(8,128)(2,1)S(1)}, bf16[4,2,128,128]{3,2,1,0:T(8,128)(2,1)S(1)}, u32[]{:S(2)}, u32[]{:S(2)}) collective-permute-start(bf16[4,2,128,128]{3,2,1,0:T(8,128)(2,1)S(1)} %get-tuple-element.24), channel_id=1, source_target_pairs={{0,1},{1,2},{2,3},{3,0},{4,5},{5,6},{6,7},{7,4},{8,9},{9,10},{10,1... | collective-permute-start | bytes 786440 | tf_op jit(solution)/shard_map/ppermute | solution.py:19
  148.7 13.7 %collective-permute-start.18 = (bf16[4,2,128,128]{3,2,1,0:T(8,128)(2,1)S(1)}, bf16[4,2,128,128]{3,2,1,0:T(8,128)(2,1)S(1)}, u32[]{:S(2)}, u32[]{:S(2)}) collective-permute-start(bf16[4,2,128,128]{3,2,1,0:T(8,128)(2,1)S(1)} %get-tuple-element.24), channel_id=1, source_target_pairs={{0,2},{1,3},{2,0},{3,1},{4,6},{5,7},{6,4},{7,5},{8,10},{9,11},{10,... | collective-permute-start | bytes 786440 | tf_op jit(solution)/shard_map/ppermute | solution.py:19
  152.5 12.4 %collective-permute-start.17 = (bf16[4,2,128,128]{3,2,1,0:T(8,128)(2,1)S(1)}, bf16[4,2,128,128]{3,2,1,0:T(8,128)(2,1)S(1)}, u32[]{:S(2)}, u32[]{:S(2)}) collective-permute-start(bf16[4,2,128,128]{3,2,1,0:T(8,128)(2,1)S(1)} %get-tuple-element.24), channel_id=1, source_target_pairs={{0,3},{1,0},{2,1},{3,2},{4,7},{5,4},{6,5},{7,6},{8,11},{9,8},{10,9... | collective-permute-start | bytes 786440 | tf_op jit(solution)/shard_map/ppermute | solution.py:19

commit v14 on v9

--- a/solution.py
+++ b/solution.py
@@ -162,7 +162,8 @@
     rolled = jnp.roll(own_tiles, -part_index * quarter, axis=1)
     own_part = rolled[:, :quarter]
     even = ctx_index % 2 == 0
-    took = jnp.stack([chip_fetch(own_part, "ctx", step) for step in range(1, 4)])
+    took = [chip_fetch(own_part, "ctx", step) for step in range(1, 3)]
+    took = jnp.stack(took + [chip_fetch(took[1], "ctx", 1)])
     pieces = [took] + [cycled(took, "sub", -step) for step in range(1, parts_count)]
     took = jnp.concatenate(pieces, axis=2)
     mine = jnp.concatenate([rolled[None], took], axis=0)
@@ -178,7 +179,7 @@
     rolled_block = (local_block // per_part - part_index) % parts_count * per_part + local_block % per_part
     offset = jnp.clip(ctx_index - chosen // blocks_here, 0, REACH)
     placed = jnp.where(
-        even, jnp.array([0, 1, 5, 2, 6, 3, 7], jnp.int32)[offset], jnp.array([0, 4, 5, 1, 6, 2, 7], jnp.int32)[offset]
+        even, jnp.array([0, 1, 5, 2, 6, 7, 3], jnp.int32)[offset], jnp.array([0, 4, 5, 1, 6, 2, 3], jnp.int32)[offset]
     )
     slot_index = placed * blocks_here + rolled_block
     code = jnp.where(live_mask == 1, jnp.where(chosen < block_ids[:, None], 2, 1), 0)
@@ -200,9 +201,15 @@
 
     reduced = reduce_parts(0, half)
     running = reduced[:, 0]
-    for step in range(1, half):
+    for step in range(1, half - 1):
         term = reduced[:, step].astype(jnp.bfloat16)
         running = running + chip_return(term, "ctx", step).astype(jnp.float32)
+    count = lax.axis_size("ctx")
+    farthest = lax.ppermute(
+        reduced[:, half - 1].astype(jnp.bfloat16), "ctx",
+        [(source, source - REACH) for source in range(REACH, count)],
+    )
+    running = running + farthest.astype(jnp.float32)
     mine = running.astype(jnp.bfloat16)
     by_group = jnp.stack([mine] + [cycled(mine, "grp", -step) for step in range(1, groups)])
     by_part = jnp.stack([by_group] + [cycled(by_group, "sub", -step) for step in range(1, parts_count)])

time: 167 us -> 169 us (1.012)
    ppermute x12, starting transfers between devices: 52.6 us -> 43 us  [cycled(): lax.ppermute(value, axis, [(source, (source + steps) % count) for source...]
    ppermute x0 -> x1, starting transfers between devices: none -> 7.94 us  [per_device(): lax.ppermute(reduced[:, half - 1].astype(jnp.bfloat16), 'ctx', [(source,...]
    ppermute x3, starting transfers between devices: 21 us -> 26.2 us  [chip_fetch(): return lax.ppermute(value, axis, chip_pairs(lax.axis_size(axis), step))]
    ppermute x3, waiting for transfers between devices: 9.16 us -> 5.88 us  [chip_fetch(): return lax.ppermute(value, axis, chip_pairs(lax.axis_size(axis), step))]
    ppermute x3 -> x2, starting transfers between devices: 16.6 us -> 14.2 us  [chip_return(): lax.ppermute(value, axis, [(target, source) for source, target in pairs])]
    ppermute x3 -> x2, waiting for transfers between devices: 4.79 us -> 7.04 us  [chip_return(): lax.ppermute(value, axis, [(target, source) for source, target in pairs])]
  transfers between devices with their start and end apart: 20 -> 20, of which waited for: 15 -> 13; matrix products, arithmetic and copies ran while one was open for 4% -> 4% of each run, Pallas kernels for 0% -> 0%
where the time goes in v14:
time: 169 us; the launch traced here: 167 us
  starting transfers between devices  95.4 us (56%)
  waiting for transfers between devices  39.8 us (24%)
  Pallas kernels  16.1 us (10%)
  local copies, waits for them, and re-layouts  8.71 us (5%)
  other arithmetic  5.51 us (3%)
    ppermute x12, starting transfers between devices, cycled(): lax.ppermute(value, axis, [(source, (source + steps) % count) for source...  43 us
    ppermute x3, starting transfers between devices, chip_fetch(): return lax.ppermute(value, axis, chip_pairs(lax.axis_size(axis), step))  26.2 us
    ppermute x12, waiting for transfers between devices, cycled(): lax.ppermute(value, axis, [(source, (source + steps) % count) for source...  23.7 us
    pallas_call x1, Pallas kernels, local_grads(): pl.pallas_call(kernel, grid_spec=pltpu.PrefetchScalarGridSpec(num_scalar_...  16.1 us
    ppermute x2, starting transfers between devices, chip_return(): lax.ppermute(value, axis, [(target, source) for source, target in pairs])  14.2 us
    ppermute x1, starting transfers between devices, per_device(): lax.ppermute(reduced[:, half - 1].astype(jnp.bfloat16), 'ctx', [(source,...  7.94 us
    ppermute x2, waiting for transfers between devices, chip_return(): lax.ppermute(value, axis, [(target, source) for source, target in pairs])  7.04 us
    ppermute x3, waiting for transfers between devices, chip_fetch(): return lax.ppermute(value, axis, chip_pairs(lax.axis_size(axis), step))  5.88 us
  transfers between devices with their start and end apart: 20, of which 13 were waited for; matrix products, arithmetic and copies ran while one was open for 4% of the time, Pallas kernels for 0%

profile of v14, /device:TPU:6, one launch (start us, length us, event | category | flops | bytes accessed | tf_op | source)
XLA Modules:
  0.0 166.8 jit_solution(480088923912183991)
XLA Ops:
  0.7 1.0 constant_dynamic-slice_fusion
  1.7 0.5 fusion.6
  2.2 15.2 %collective-permute-start.1 = (bf16[2,128,128]{2,1,0:T(8,128)(2,1)S(1)}, bf16[2,128,128]{2,1,0:T(8,128)(2,1)S(1)}, u32[]{:S(2)}, u32[]{:S(2)}) collective-permute-start(bf16[2,128,128]{2,1,0:T(8,128)(2,1)S(1)} %slice.72), channel_id=1, source_target_pairs={{16,64},{48,96},{80,128},{112,160},{144,192},{176,224},{208,256},{... | collective-permute-start | bytes 196616 | tf_op jit(solution)/shard_map/ppermute | solution.py:29
  17.3 4.6 %collective-permute-start = (bf16[2,128,128]{2,1,0:T(8,128)(2,1)S(1)}, bf16[2,128,128]{2,1,0:T(8,128)(2,1)S(1)}, u32[]{:S(2)}, u32[]{:S(2)}) collective-permute-start(bf16[2,128,128]{2,1,0:T(8,128)(2,1)S(1)} %slice.72), channel_id=1, source_target_pairs={{16,32},{48,64},{80,96},{112,128},{144,160},{176,192},{208,224},{2... | collective-permute-start | bytes 196616 | tf_op jit(solution)/shard_map/ppermute | solution.py:29
  21.9 0.8 constant_dynamic-slice_fusion.2
  22.7 6.5 %collective-permute-start.2 = (bf16[2,128,128]{2,1,0:T(8,128)(2,1)S(1)}, bf16[2,128,128]{2,1,0:T(8,128)(2,1)S(1)}, u32[]{:S(2)}, u32[]{:S(2)}) collective-permute-start(bf16[2,128,128]{2,1,0:T(8,128)(2,1)S(1)} %collective-permute-done.1), channel_id=1, source_target_pairs={{16,32},{48,64},{80,96},{112,128},{144,160},{176,192},{208,224},{2... | collective-permute-start | bytes 196616 | tf_op jit(solution)/shard_map/ppermute | solution.py:29
  29.2 0.1 reshape.262
  29.3 5.9 %collective-permute-done.2 = bf16[2,128,128]{2,1,0:T(8,128)(2,1)S(1)} collective-permute-done((bf16[2,128,128]{2,1,0:T(8,128)(2,1)S(1)}, bf16[2,128,128]{2,1,0:T(8,128)(2,1)S(1)}, u32[]{:S(2)}, u32[]{:S(2)}) %collective-permute-start.2) | collective-permute-done | bytes 65568 | tf_op jit(solution)/shard_map/ppermute | solution.py:29
  35.2 3.5 %collective-permute-start.5 = (bf16[3,2,128,128]{3,2,1,0:T(8,128)(2,1)S(1)}, bf16[3,2,128,128]{3,2,1,0:T(8,128)(2,1)S(1)}, u32[]{:S(2)}, u32[]{:S(2)}) collective-permute-start(bf16[3,2,128,128]{3,2,1,0:T(8,128)(2,1)S(1)} %pad_maximum_fusion.4), channel_id=1, source_target_pairs={{0,1},{1,2},{2,3},{3,0},{4,5},{5,6},{6,7},{7,4},{8,9},{9,10},{10,1... | collective-permute-start | bytes 589832 | tf_op jit(solution)/shard_map/ppermute | solution.py:19
  38.7 4.8 %collective-permute-start.4 = (bf16[3,2,128,128]{3,2,1,0:T(8,128)(2,1)S(1)}, bf16[3,2,128,128]{3,2,1,0:T(8,128)(2,1)S(1)}, u32[]{:S(2)}, u32[]{:S(2)}) collective-permute-start(bf16[3,2,128,128]{3,2,1,0:T(8,128)(2,1)S(1)} %pad_maximum_fusion.4), channel_id=1, source_target_pairs={{0,2},{1,3},{2,0},{3,1},{4,6},{5,7},{6,4},{7,5},{8,10},{9,11},{10,... | collective-permute-start | bytes 589832 | tf_op jit(solution)/shard_map/ppermute | solution.py:19
  43.5 3.3 %collective-permute-start.3 = (bf16[3,2,128,128]{3,2,1,0:T(8,128)(2,1)S(1)}, bf16[3,2,128,128]{3,2,1,0:T(8,128)(2,1)S(1)}, u32[]{:S(2)}, u32[]{:S(2)}) collective-permute-start(bf16[3,2,128,128]{3,2,1,0:T(8,128)(2,1)S(1)} %pad_maximum_fusion.4), channel_id=1, source_target_pairs={{0,3},{1,0},{2,1},{3,2},{4,7},{5,4},{6,5},{7,6},{8,11},{9,8},{10,9... | collective-permute-start | bytes 589832 | tf_op jit(solution)/shard_map/ppermute | solution.py:19
  46.8 1.2 gather_fusion
  48.0 1.2 gather_fusion.1
  49.3 0.5 fusion.38
  49.8 0.8 collective-permute-done.4
  50.6 1.3 collective-permute-done.3
  51.9 0.1 maximum_maximum_fusion
  52.0 1.9 %collective-permute-start.6 = (bf16[4,2,512,128]{3,2,1,0:T(8,128)(2,1)S(1)}, bf16[4,2,512,128]{3,2,1,0:T(8,128)(2,1)S(1)}, u32[]{:S(2)}, u32[]{:S(2)}) collective-permute-start(bf16[4,2,512,128]{3,2,1,0:T(8,128)(2,1)S(1)} %maximum_maximum_fusion), channel_id=1, source_target_pairs={{0,16},{16,0},{32,48},{48,32},{64,80},{80,64},{96,112},{112,96},{1... | collective-permute-start | bytes 3145736 | tf_op jit(solution)/shard_map/ppermute | solution.py:39
  53.9 0.1 reshape.289
  54.0 0.1 fusion.21
  54.1 0.1 broadcast_in_dim.47
  54.2 0.1 eq.59
  54.3 0.1 broadcast_in_dim.49
  54.4 0.1 eq.60
  54.5 0.1 broadcast_in_dim.50
  54.5 0.6 fusion.20.slots_ref
  55.2 0.7 select_select_fusion.code_ref
  55.8 0.7 collective-permute-done.6
  56.5 0.2 pad_maximum_fusion.1
  56.7 1.5 fusion.36
  58.2 16.1 %shard_map.103 = (bf16[2048,128]{1,0:T(8,128)(2,1)}, f32[4096,128]{1,0:T(8,128)}, f32[4096,128]{1,0:T(8,128)}) custom-call(s32[8,16]{1,0:T(8,128)} %fusion.20.slots_ref, bf16[2048,128]{1,0:T(8,128)(2,1)} %bitcast.81, bf16[2048,128]{1,0:T(8,128)(2,1)} %bitcast.82, s32[8,1,1024]{2,1,0:T(1,128)} %select_select_fusion.code_ref, bf16[4096,128]{1,0:T(8,128)(2,1)} %bitcast.69, ...), custom_call_target="tpu_custom_call" | custom-call | tf_op jit(solution)/shard_map/pallas_call | solution.py:105
  74.3 1.8 %fusion.2 = bf16[2,4,512,128]{3,2,1,0:T(8,128)(2,1)S(1)} fusion(f32[1,8,512,128]{3,2,1,0:T(8,128)} %bitcast.64, f32[1,8,512,128]{3,2,1,0:T(8,128)} %bitcast.62), kind=kLoop, calls=%fused_computation.8 | loop fusion | flops 524288 | bytes 5242880 | tf_op jit(solution)/shard_map/convert.4
  76.2 2.2 %collective-permute-start.7 = (bf16[2,4,512,128]{3,2,1,0:T(8,128)(2,1)S(1)}, bf16[2,4,512,128]{3,2,1,0:T(8,128)(2,1)S(1)}, u32[]{:S(2)}, u32[]{:S(2)}) collective-permute-start(bf16[2,4,512,128]{3,2,1,0:T(8,128)(2,1)S(1)} %fusion.2), channel_id=1, source_target_pairs={{0,16},{16,0},{32,48},{48,32},{64,80},{80,64},{96,112},{112,96},{1... | collective-permute-start | bytes 3145736 | tf_op jit(solution)/shard_map/ppermute | solution.py:39
  78.3 2.5 %collective-permute-done.7 = bf16[2,4,512,128]{3,2,1,0:T(8,128)(2,1)S(1)} collective-permute-done((bf16[2,4,512,128]{3,2,1,0:T(8,128)(2,1)S(1)}, bf16[2,4,512,128]{3,2,1,0:T(8,128)(2,1)S(1)}, u32[]{:S(2)}, u32[]{:S(2)}) %collective-permute-start.7) | collective-permute-done | bytes 1048608 | tf_op jit(solution)/shard_map/ppermute | solution.py:39
  80.8 0.3 fusion.33
  81.2 4.6 %collective-permute-start.10 = (bf16[2,4,128,128]{3,2,1,0:T(8,128)(2,1)S(1)}, bf16[2,4,128,128]{3,2,1,0:T(8,128)(2,1)S(1)}, u32[]{:S(2)}, u32[]{:S(2)}) collective-permute-start(bf16[2,4,128,128]{3,2,1,0:T(8,128)(2,1)S(1)} %get-tuple-element.21), channel_id=1, source_target_pairs={{0,3},{1,0},{2,1},{3,2},{4,7},{5,4},{6,5},{7,6},{8,11},{9,8},{10,9... | collective-permute-start | bytes 786440 | tf_op jit(solution)/shard_map/ppermute | solution.py:19
  85.8 3.8 %collective-permute-start.9 = (bf16[2,4,128,128]{3,2,1,0:T(8,128)(2,1)S(1)}, bf16[2,4,128,128]{3,2,1,0:T(8,128)(2,1)S(1)}, u32[]{:S(2)}, u32[]{:S(2)}) collective-permute-start(bf16[2,4,128,128]{3,2,1,0:T(8,128)(2,1)S(1)} %get-tuple-element.22), channel_id=1, source_target_pairs={{0,2},{1,3},{2,0},{3,1},{4,6},{5,7},{6,4},{7,5},{8,10},{9,11},{10,... | collective-permute-start | bytes 786440 | tf_op jit(solution)/shard_map/ppermute | solution.py:19
  89.6 1.9 %collective-permute-start.8 = (bf16[2,4,128,128]{3,2,1,0:T(8,128)(2,1)S(1)}, bf16[2,4,128,128]{3,2,1,0:T(8,128)(2,1)S(1)}, u32[]{:S(2)}, u32[]{:S(2)}) collective-permute-start(bf16[2,4,128,128]{3,2,1,0:T(8,128)(2,1)S(1)} %get-tuple-element.20), channel_id=1, source_target_pairs={{0,1},{1,2},{2,3},{3,0},{4,5},{5,6},{6,7},{7,4},{8,9},{9,10},{10,1... | collective-permute-start | bytes 786440 | tf_op jit(solution)/shard_map/ppermute | solution.py:19
  91.6 5.7 %collective-permute-done.10 = bf16[2,4,128,128]{3,2,1,0:T(8,128)(2,1)S(1)} collective-permute-done((bf16[2,4,128,128]{3,2,1,0:T(8,128)(2,1)S(1)}, bf16[2,4,128,128]{3,2,1,0:T(8,128)(2,1)S(1)}, u32[]{:S(2)}, u32[]{:S(2)}) %collective-permute-start.10) | collective-permute-done | bytes 262176 | tf_op jit(solution)/shard_map/ppermute | solution.py:19
  97.3 1.1 collective-permute-done.9
  98.4 4.5 %collective-permute-done.8 = bf16[2,4,128,128]{3,2,1,0:T(8,128)(2,1)S(1)} collective-permute-done((bf16[2,4,128,128]{3,2,1,0:T(8,128)(2,1)S(1)}, bf16[2,4,128,128]{3,2,1,0:T(8,128)(2,1)S(1)}, u32[]{:S(2)}, u32[]{:S(2)}) %collective-permute-start.8) | collective-permute-done | bytes 262176 | tf_op jit(solution)/shard_map/ppermute | solution.py:19
  102.9 0.1 fusion.31
  103.1 7.9 %collective-permute-start.13 = (bf16[2,128,128]{2,1,0:T(8,128)(2,1)S(1)}, bf16[2,128,128]{2,1,0:T(8,128)(2,1)S(1)}, u32[]{:S(2)}, u32[]{:S(2)}) collective-permute-start(bf16[2,128,128]{2,1,0:T(8,128)(2,1)S(1)} %get-tuple-element.26), channel_id=1, source_target_pairs={{96,0},{112,16},{128,32},{144,48},{160,64},{176,80},{192,96},{208,... | collective-permute-start | bytes 196616 | tf_op jit(solution)/shard_map/ppermute | solution.py:208
  111.0 7.5 %collective-permute-start.12 = (bf16[2,128,128]{2,1,0:T(8,128)(2,1)S(1)}, bf16[2,128,128]{2,1,0:T(8,128)(2,1)S(1)}, u32[]{:S(2)}, u32[]{:S(2)}) collective-permute-start(bf16[2,128,128]{2,1,0:T(8,128)(2,1)S(1)} %get-tuple-element.27), channel_id=1, source_target_pairs={{64,16},{96,48},{128,80},{160,112},{192,144},{224,176},{256,208},{... | collective-permute-start | bytes 196616 | tf_op jit(solution)/shard_map/ppermute | solution.py:34
  118.5 6.7 %collective-permute-start.11 = (bf16[2,128,128]{2,1,0:T(8,128)(2,1)S(1)}, bf16[2,128,128]{2,1,0:T(8,128)(2,1)S(1)}, u32[]{:S(2)}, u32[]{:S(2)}) collective-permute-start(bf16[2,128,128]{2,1,0:T(8,128)(2,1)S(1)} %get-tuple-element.25), channel_id=1, source_target_pairs={{32,16},{64,48},{96,80},{128,112},{160,144},{192,176},{224,208},{2... | collective-permute-start | bytes 196616 | tf_op jit(solution)/shard_map/ppermute | solution.py:34
  125.3 0.1 broadcast_add_fusion
  125.3 0.1 add.179
  125.4 1.2 collective-permute-done.12
  126.6 5.9 %collective-permute-done.11 = bf16[2,128,128]{2,1,0:T(8,128)(2,1)S(1)} collective-permute-done((bf16[2,128,128]{2,1,0:T(8,128)(2,1)S(1)}, bf16[2,128,128]{2,1,0:T(8,128)(2,1)S(1)}, u32[]{:S(2)}, u32[]{:S(2)}) %collective-permute-start.11) | collective-permute-done | bytes 65568 | tf_op jit(solution)/shard_map/ppermute | solution.py:34
  132.5 1.9 %collective-permute-start.16 = (bf16[2,128,128]{2,1,0:T(8,128)(2,1)S(1)}, bf16[2,128,128]{2,1,0:T(8,128)(2,1)S(1)}, u32[]{:S(2)}, u32[]{:S(2)}) collective-permute-start(bf16[2,128,128]{2,1,0:T(8,128)(2,1)S(1)} %fusion.11), channel_id=1, source_target_pairs={{0,4},{4,8},{8,12},{12,0},{1,5},{5,9},{9,13},{13,1},{2,6},{6,10},{... | collective-permute-start | bytes 196616 | tf_op jit(solution)/shard_map/ppermute | solution.py:19
  134.4 4.8 %collective-permute-start.15 = (bf16[2,128,128]{2,1,0:T(8,128)(2,1)S(1)}, bf16[2,128,128]{2,1,0:T(8,128)(2,1)S(1)}, u32[]{:S(2)}, u32[]{:S(2)}) collective-permute-start(bf16[2,128,128]{2,1,0:T(8,128)(2,1)S(1)} %fusion.11), channel_id=1, source_target_pairs={{0,8},{4,12},{8,0},{12,4},{1,9},{5,13},{9,1},{13,5},{2,10},{6,14},... | collective-permute-start | bytes 196616 | tf_op jit(solution)/shard_map/ppermute | solution.py:19
  139.2 4.8 %collective-permute-start.14 = (bf16[2,128,128]{2,1,0:T(8,128)(2,1)S(1)}, bf16[2,128,128]{2,1,0:T(8,128)(2,1)S(1)}, u32[]{:S(2)}, u32[]{:S(2)}) collective-permute-start(bf16[2,128,128]{2,1,0:T(8,128)(2,1)S(1)} %fusion.11), channel_id=1, source_target_pairs={{0,12},{4,0},{8,4},{12,8},{1,13},{5,1},{9,5},{13,9},{2,14},{6,2},{... | collective-permute-start | bytes 196616 | tf_op jit(solution)/shard_map/ppermute | solution.py:19
  144.1 1.9 %collective-permute-done.14 = bf16[2,128,128]{2,1,0:T(8,128)(2,1)S(1)} collective-permute-done((bf16[2,128,128]{2,1,0:T(8,128)(2,1)S(1)}, bf16[2,128,128]{2,1,0:T(8,128)(2,1)S(1)}, u32[]{:S(2)}, u32[]{:S(2)}) %collective-permute-start.14) | collective-permute-done | bytes 65568 | tf_op jit(solution)/shard_map/ppermute | solution.py:19
  146.0 1.9 %collective-permute-start.19 = (bf16[4,2,128,128]{3,2,1,0:T(8,128)(2,1)S(1)}, bf16[4,2,128,128]{3,2,1,0:T(8,128)(2,1)S(1)}, u32[]{:S(2)}, u32[]{:S(2)}) collective-permute-start(bf16[4,2,128,128]{3,2,1,0:T(8,128)(2,1)S(1)} %get-tuple-element.24), channel_id=1, source_target_pairs={{0,1},{1,2},{2,3},{3,0},{4,5},{5,6},{6,7},{7,4},{8,9},{9,10},{10,1... | collective-permute-start | bytes 786440 | tf_op jit(solution)/shard_map/ppermute | solution.py:19
  147.9 3.1 %collective-permute-start.18 = (bf16[4,2,128,128]{3,2,1,0:T(8,128)(2,1)S(1)}, bf16[4,2,128,128]{3,2,1,0:T(8,128)(2,1)S(1)}, u32[]{:S(2)}, u32[]{:S(2)}) collective-permute-start(bf16[4,2,128,128]{3,2,1,0:T(8,128)(2,1)S(1)} %get-tuple-element.24), channel_id=1, source_target_pairs={{0,2},{1,3},{2,0},{3,1},{4,6},{5,7},{6,4},{7,5},{8,10},{9,11},{10,... | collective-permute-start | bytes 786440 | tf_op jit(solution)/shard_map/ppermute | solution.py:19
  151.1 4.5 %collective-permute-start.17 = (bf16[4,2,128,128]{3,2,1,0:T(8,128)(2,1)S(1)}, bf16[4,2,128,128]{3,2,1,0:T(8,128)(2,1)S(1)}, u32[]{:S(2)}, u32[]{:S(2)}) collective-permute-start(bf16[4,2,128,128]{3,2,1,0:T(8,128)(2,1)S(1)} %get-tuple-element.24), channel_id=1, source_target_pairs={{0,3},{1,0},{2,1},{3,2},{4,7},{5,4},{6,5},{7,6},{8,11},{9,8},{10,9... | collective-permute-start | bytes 786440 | tf_op jit(solution)/shard_map/ppermute | solution.py:19
  155.6 0.1 compare_and_fusion
  155.7 5.9 %collective-permute-done.19 = bf16[4,2,128,128]{3,2,1,0:T(8,128)(2,1)S(1)} collective-permute-done((bf16[4,2,128,128]{3,2,1,0:T(8,128)(2,1)S(1)}, bf16[4,2,128,128]{3,2,1,0:T(8,128)(2,1)S(1)}, u32[]{:S(2)}, u32[]{:S(2)}) %collective-permute-start.19) | collective-permute-done | bytes 262176 | tf_op jit(solution)/shard_map/ppermute | solution.py:19
  161.6 2.5 %collective-permute-done.17 = bf16[4,2,128,128]{3,2,1,0:T(8,128)(2,1)S(1)} collective-permute-done((bf16[4,2,128,128]{3,2,1,0:T(8,128)(2,1)S(1)}, bf16[4,2,128,128]{3,2,1,0:T(8,128)(2,1)S(1)}, u32[]{:S(2)}, u32[]{:S(2)}) %collective-permute-start.17) | collective-permute-done | bytes 262176 | tf_op jit(solution)/shard_map/ppermute | solution.py:19
  164.1 0.1 pad_maximum_fusion.2
  164.2 0.7 gather_fusion.2
  165.0 0.1 copy.24
  165.1 0.2 convert_bitcast_fusion
  165.3 1.5 fusion.35
  (30 shorter events, 0.3 us)
Async XLA Ops:
  0.6 46.1 %copy-start.1 = (s32[7]{0:T(128)S(1)}, s32[7]{0:T(128)}, u32[]{:S(2)}) copy-start(s32[7]{0:T(128)} %constant.156.clone) | copy-start | bytes 88
  2.2 20.5 %collective-permute-start.1 = (bf16[2,128,128]{2,1,0:T(8,128)(2,1)S(1)}, bf16[2,128,128]{2,1,0:T(8,128)(2,1)S(1)}, u32[]{:S(2)}, u32[]{:S(2)}) collective-permute-start(bf16[2,128,128]{2,1,0:T(8,128)(2,1)S(1)} %slice.72), channel_id=1, source_target_pairs={{16,64},{48,96},{80,128},{112,160},{144,192},{176,224},{208,256},{... | collective-permute-start | bytes 196616 | tf_op jit(solution)/shard_map/ppermute | solution.py:29
  17.3 11.9 %collective-permute-start = (bf16[2,128,128]{2,1,0:T(8,128)(2,1)S(1)}, bf16[2,128,128]{2,1,0:T(8,128)(2,1)S(1)}, u32[]{:S(2)}, u32[]{:S(2)}) collective-permute-start(bf16[2,128,128]{2,1,0:T(8,128)(2,1)S(1)} %slice.72), channel_id=1, source_target_pairs={{16,32},{48,64},{80,96},{112,128},{144,160},{176,192},{208,224},{2... | collective-permute-start | bytes 196616 | tf_op jit(solution)/shard_map/ppermute | solution.py:29
  22.7 12.4 %collective-permute-start.2 = (bf16[2,128,128]{2,1,0:T(8,128)(2,1)S(1)}, bf16[2,128,128]{2,1,0:T(8,128)(2,1)S(1)}, u32[]{:S(2)}, u32[]{:S(2)}) collective-permute-start(bf16[2,128,128]{2,1,0:T(8,128)(2,1)S(1)} %collective-permute-done.1), channel_id=1, source_target_pairs={{16,32},{48,64},{80,96},{112,128},{144,160},{176,192},{208,224},{2... | collective-permute-start | bytes 196616 | tf_op jit(solution)/shard_map/ppermute | solution.py:29
  35.2 14.6 %collective-permute-start.5 = (bf16[3,2,128,128]{3,2,1,0:T(8,128)(2,1)S(1)}, bf16[3,2,128,128]{3,2,1,0:T(8,128)(2,1)S(1)}, u32[]{:S(2)}, u32[]{:S(2)}) collective-permute-start(bf16[3,2,128,128]{3,2,1,0:T(8,128)(2,1)S(1)} %pad_maximum_fusion.4), channel_id=1, source_target_pairs={{0,1},{1,2},{2,3},{3,0},{4,5},{5,6},{6,7},{7,4},{8,9},{9,10},{10,1... | collective-permute-start | bytes 589832 | tf_op jit(solution)/shard_map/ppermute | solution.py:19
  38.7 11.9 %collective-permute-start.4 = (bf16[3,2,128,128]{3,2,1,0:T(8,128)(2,1)S(1)}, bf16[3,2,128,128]{3,2,1,0:T(8,128)(2,1)S(1)}, u32[]{:S(2)}, u32[]{:S(2)}) collective-permute-start(bf16[3,2,128,128]{3,2,1,0:T(8,128)(2,1)S(1)} %pad_maximum_fusion.4), channel_id=1, source_target_pairs={{0,2},{1,3},{2,0},{3,1},{4,6},{5,7},{6,4},{7,5},{8,10},{9,11},{10,... | collective-permute-start | bytes 589832 | tf_op jit(solution)/shard_map/ppermute | solution.py:19
  43.5 8.4 %collective-permute-start.3 = (bf16[3,2,128,128]{3,2,1,0:T(8,128)(2,1)S(1)}, bf16[3,2,128,128]{3,2,1,0:T(8,128)(2,1)S(1)}, u32[]{:S(2)}, u32[]{:S(2)}) collective-permute-start(bf16[3,2,128,128]{3,2,1,0:T(8,128)(2,1)S(1)} %pad_maximum_fusion.4), channel_id=1, source_target_pairs={{0,3},{1,0},{2,1},{3,2},{4,7},{5,4},{6,5},{7,6},{8,11},{9,8},{10,9... | collective-permute-start | bytes 589832 | tf_op jit(solution)/shard_map/ppermute | solution.py:19
  46.8 1.2 copy-start
  52.0 4.6 %collective-permute-start.6 = (bf16[4,2,512,128]{3,2,1,0:T(8,128)(2,1)S(1)}, bf16[4,2,512,128]{3,2,1,0:T(8,128)(2,1)S(1)}, u32[]{:S(2)}, u32[]{:S(2)}) collective-permute-start(bf16[4,2,512,128]{3,2,1,0:T(8,128)(2,1)S(1)} %maximum_maximum_fusion), channel_id=1, source_target_pairs={{0,16},{16,0},{32,48},{48,32},{64,80},{80,64},{96,112},{112,96},{1... | collective-permute-start | bytes 3145736 | tf_op jit(solution)/shard_map/ppermute | solution.py:39
  74.3 6.5 %copy-start.2 = (f32[4096,128]{1,0:T(8,128)S(1)}, f32[4096,128]{1,0:T(8,128)}, u32[]{:S(2)}) copy-start(f32[4096,128]{1,0:T(8,128)} %get-tuple-element.7) | copy-start | bytes 6291460
  74.3 6.5 %copy-start.3 = (f32[4096,128]{1,0:T(8,128)S(1)}, f32[4096,128]{1,0:T(8,128)}, u32[]{:S(2)}) copy-start(f32[4096,128]{1,0:T(8,128)} %get-tuple-element.8) | copy-start | bytes 6291460
  76.2 4.7 %collective-permute-start.7 = (bf16[2,4,512,128]{3,2,1,0:T(8,128)(2,1)S(1)}, bf16[2,4,512,128]{3,2,1,0:T(8,128)(2,1)S(1)}, u32[]{:S(2)}, u32[]{:S(2)}) collective-permute-start(bf16[2,4,512,128]{3,2,1,0:T(8,128)(2,1)S(1)} %fusion.2), channel_id=1, source_target_pairs={{0,16},{16,0},{32,48},{48,32},{64,80},{80,64},{96,112},{112,96},{1... | collective-permute-start | bytes 3145736 | tf_op jit(solution)/shard_map/ppermute | solution.py:39
  81.2 16.1 %collective-permute-start.10 = (bf16[2,4,128,128]{3,2,1,0:T(8,128)(2,1)S(1)}, bf16[2,4,128,128]{3,2,1,0:T(8,128)(2,1)S(1)}, u32[]{:S(2)}, u32[]{:S(2)}) collective-permute-start(bf16[2,4,128,128]{3,2,1,0:T(8,128)(2,1)S(1)} %get-tuple-element.21), channel_id=1, source_target_pairs={{0,3},{1,0},{2,1},{3,2},{4,7},{5,4},{6,5},{7,6},{8,11},{9,8},{10,9... | collective-permute-start | bytes 786440 | tf_op jit(solution)/shard_map/ppermute | solution.py:19
  85.8 12.6 %collective-permute-start.9 = (bf16[2,4,128,128]{3,2,1,0:T(8,128)(2,1)S(1)}, bf16[2,4,128,128]{3,2,1,0:T(8,128)(2,1)S(1)}, u32[]{:S(2)}, u32[]{:S(2)}) collective-permute-start(bf16[2,4,128,128]{3,2,1,0:T(8,128)(2,1)S(1)} %get-tuple-element.22), channel_id=1, source_target_pairs={{0,2},{1,3},{2,0},{3,1},{4,6},{5,7},{6,4},{7,5},{8,10},{9,11},{10,... | collective-permute-start | bytes 786440 | tf_op jit(solution)/shard_map/ppermute | solution.py:19
  89.6 13.3 %collective-permute-start.8 = (bf16[2,4,128,128]{3,2,1,0:T(8,128)(2,1)S(1)}, bf16[2,4,128,128]{3,2,1,0:T(8,128)(2,1)S(1)}, u32[]{:S(2)}, u32[]{:S(2)}) collective-permute-start(bf16[2,4,128,128]{3,2,1,0:T(8,128)(2,1)S(1)} %get-tuple-element.20), channel_id=1, source_target_pairs={{0,1},{1,2},{2,3},{3,0},{4,5},{5,6},{6,7},{7,4},{8,9},{9,10},{10,1... | collective-permute-start | bytes 786440 | tf_op jit(solution)/shard_map/ppermute | solution.py:19
  103.1 22.3 %collective-permute-start.13 = (bf16[2,128,128]{2,1,0:T(8,128)(2,1)S(1)}, bf16[2,128,128]{2,1,0:T(8,128)(2,1)S(1)}, u32[]{:S(2)}, u32[]{:S(2)}) collective-permute-start(bf16[2,128,128]{2,1,0:T(8,128)(2,1)S(1)} %get-tuple-element.26), channel_id=1, source_target_pairs={{96,0},{112,16},{128,32},{144,48},{160,64},{176,80},{192,96},{208,... | collective-permute-start | bytes 196616 | tf_op jit(solution)/shard_map/ppermute | solution.py:208
  111.0 15.6 %collective-permute-start.12 = (bf16[2,128,128]{2,1,0:T(8,128)(2,1)S(1)}, bf16[2,128,128]{2,1,0:T(8,128)(2,1)S(1)}, u32[]{:S(2)}, u32[]{:S(2)}) collective-permute-start(bf16[2,128,128]{2,1,0:T(8,128)(2,1)S(1)} %get-tuple-element.27), channel_id=1, source_target_pairs={{64,16},{96,48},{128,80},{160,112},{192,144},{224,176},{256,208},{... | collective-permute-start | bytes 196616 | tf_op jit(solution)/shard_map/ppermute | solution.py:34
  118.5 13.9 %collective-permute-start.11 = (bf16[2,128,128]{2,1,0:T(8,128)(2,1)S(1)}, bf16[2,128,128]{2,1,0:T(8,128)(2,1)S(1)}, u32[]{:S(2)}, u32[]{:S(2)}) collective-permute-start(bf16[2,128,128]{2,1,0:T(8,128)(2,1)S(1)} %get-tuple-element.25), channel_id=1, source_target_pairs={{32,16},{64,48},{96,80},{128,112},{160,144},{192,176},{224,208},{2... | collective-permute-start | bytes 196616 | tf_op jit(solution)/shard_map/ppermute | solution.py:34
  132.5 11.6 %collective-permute-start.16 = (bf16[2,128,128]{2,1,0:T(8,128)(2,1)S(1)}, bf16[2,128,128]{2,1,0:T(8,128)(2,1)S(1)}, u32[]{:S(2)}, u32[]{:S(2)}) collective-permute-start(bf16[2,128,128]{2,1,0:T(8,128)(2,1)S(1)} %fusion.11), channel_id=1, source_target_pairs={{0,4},{4,8},{8,12},{12,0},{1,5},{5,9},{9,13},{13,1},{2,6},{6,10},{... | collective-permute-start | bytes 196616 | tf_op jit(solution)/shard_map/ppermute | solution.py:19
  134.4 9.7 %collective-permute-start.15 = (bf16[2,128,128]{2,1,0:T(8,128)(2,1)S(1)}, bf16[2,128,128]{2,1,0:T(8,128)(2,1)S(1)}, u32[]{:S(2)}, u32[]{:S(2)}) collective-permute-start(bf16[2,128,128]{2,1,0:T(8,128)(2,1)S(1)} %fusion.11), channel_id=1, source_target_pairs={{0,8},{4,12},{8,0},{12,4},{1,9},{5,13},{9,1},{13,5},{2,10},{6,14},... | collective-permute-start | bytes 196616 | tf_op jit(solution)/shard_map/ppermute | solution.py:19
  139.2 6.7 %collective-permute-start.14 = (bf16[2,128,128]{2,1,0:T(8,128)(2,1)S(1)}, bf16[2,128,128]{2,1,0:T(8,128)(2,1)S(1)}, u32[]{:S(2)}, u32[]{:S(2)}) collective-permute-start(bf16[2,128,128]{2,1,0:T(8,128)(2,1)S(1)} %fusion.11), channel_id=1, source_target_pairs={{0,12},{4,0},{8,4},{12,8},{1,13},{5,1},{9,5},{13,9},{2,14},{6,2},{... | collective-permute-start | bytes 196616 | tf_op jit(solution)/shard_map/ppermute | solution.py:19
  146.0 15.6 %collective-permute-start.19 = (bf16[4,2,128,128]{3,2,1,0:T(8,128)(2,1)S(1)}, bf16[4,2,128,128]{3,2,1,0:T(8,128)(2,1)S(1)}, u32[]{:S(2)}, u32[]{:S(2)}) collective-permute-start(bf16[4,2,128,128]{3,2,1,0:T(8,128)(2,1)S(1)} %get-tuple-element.24), channel_id=1, source_target_pairs={{0,1},{1,2},{2,3},{3,0},{4,5},{5,6},{6,7},{7,4},{8,9},{9,10},{10,1... | collective-permute-start | bytes 786440 | tf_op jit(solution)/shard_map/ppermute | solution.py:19
  147.9 13.7 %collective-permute-start.18 = (bf16[4,2,128,128]{3,2,1,0:T(8,128)(2,1)S(1)}, bf16[4,2,128,128]{3,2,1,0:T(8,128)(2,1)S(1)}, u32[]{:S(2)}, u32[]{:S(2)}) collective-permute-start(bf16[4,2,128,128]{3,2,1,0:T(8,128)(2,1)S(1)} %get-tuple-element.24), channel_id=1, source_target_pairs={{0,2},{1,3},{2,0},{3,1},{4,6},{5,7},{6,4},{7,5},{8,10},{9,11},{10,... | collective-permute-start | bytes 786440 | tf_op jit(solution)/shard_map/ppermute | solution.py:19
  151.1 13.1 %collective-permute-start.17 = (bf16[4,2,128,128]{3,2,1,0:T(8,128)(2,1)S(1)}, bf16[4,2,128,128]{3,2,1,0:T(8,128)(2,1)S(1)}, u32[]{:S(2)}, u32[]{:S(2)}) collective-permute-start(bf16[4,2,128,128]{3,2,1,0:T(8,128)(2,1)S(1)} %get-tuple-element.24), channel_id=1, source_target_pairs={{0,3},{1,0},{2,1},{3,2},{4,7},{5,4},{6,5},{7,6},{8,11},{9,8},{10,9... | collective-permute-start | bytes 786440 | tf_op jit(solution)/shard_map/ppermute | solution.py:19

commit v15 on v9

--- a/solution.py
+++ b/solution.py
@@ -160,7 +160,12 @@
         ]
     )
     rolled = jnp.roll(own_tiles, -part_index * quarter, axis=1)
-    own_part = rolled[:, :quarter]
+    own_part = jnp.stack(
+        [
+            lax.dynamic_slice(rows, (group_index, part_index * quarter, 0), (1, quarter, width))[0]
+            for rows in (key_rows, value_rows)
+        ]
+    )
     even = ctx_index % 2 == 0
     took = jnp.stack([chip_fetch(own_part, "ctx", step) for step in range(1, 4)])
     pieces = [took] + [cycled(took, "sub", -step) for step in range(1, parts_count)]

time: 167 us -> 166 us (level)
    ppermute x3, waiting for transfers between devices: 9.16 us -> 6.61 us  [chip_fetch(): return lax.ppermute(value, axis, chip_pairs(lax.axis_size(axis), step))]
  transfers between devices with their start and end apart: 20 -> 20, of which waited for: 15 -> 14; matrix products, arithmetic and copies ran while one was open for 4% -> 4% of each run, Pallas kernels for 0% -> 0%
where the time goes in v15:
time: 166 us; the launch traced here: 165 us
  starting transfers between devices  94.3 us (57%)
  waiting for transfers between devices  39.2 us (24%)
  Pallas kernels  16.1 us (10%)
  local copies, waits for them, and re-layouts  9.5 us (6%)
  other arithmetic  5.06 us (3%)
    ppermute x12, starting transfers between devices, cycled(): lax.ppermute(value, axis, [(source, (source + steps) % count) for source...  52.6 us
    ppermute x12, waiting for transfers between devices, cycled(): lax.ppermute(value, axis, [(source, (source + steps) % count) for source...  24.6 us
    ppermute x3, starting transfers between devices, chip_fetch(): return lax.ppermute(value, axis, chip_pairs(lax.axis_size(axis), step))  21 us
    ppermute x3, starting transfers between devices, chip_return(): lax.ppermute(value, axis, [(target, source) for source, target in pairs])  16.6 us
    pallas_call x1, Pallas kernels, local_grads(): pl.pallas_call(kernel, grid_spec=pltpu.PrefetchScalarGridSpec(num_scalar_...  16.1 us
    ppermute x3, waiting for transfers between devices, chip_fetch(): return lax.ppermute(value, axis, chip_pairs(lax.axis_size(axis), step))  6.61 us
    ppermute x3, waiting for transfers between devices, chip_return(): lax.ppermute(value, axis, [(target, source) for source, target in pairs])  4.79 us
    ppermute x2, starting transfers between devices, swap_cores(): lax.ppermute(value, axis, [(source, source ^ 1) for source in range(count)])  4.1 us
  transfers between devices with their start and end apart: 20, of which 14 were waited for; matrix products, arithmetic and copies ran while one was open for 4% of the time, Pallas kernels for 0%

profile of v15, /device:TPU:6, one launch (start us, length us, event | category | flops | bytes accessed | tf_op | source)
XLA Modules:
  0.0 165.3 jit_solution(10449398298422872230)
XLA Ops:
  0.6 0.8 constant_dynamic-slice_fusion
  1.4 12.2 %collective-permute-start.2 = (bf16[2,128,128]{2,1,0:T(8,128)(2,1)S(1)}, bf16[2,128,128]{2,1,0:T(8,128)(2,1)S(1)}, u32[]{:S(2)}, u32[]{:S(2)}) collective-permute-start(bf16[2,128,128]{2,1,0:T(8,128)(2,1)S(1)} %pad_maximum_fusion.5), channel_id=1, source_target_pairs={{16,96},{48,128},{80,160},{112,192},{144,224},{176,256},{208,288},... | collective-permute-start | bytes 196616 | tf_op jit(solution)/shard_map/ppermute | solution.py:29
  13.6 4.3 %collective-permute-start.1 = (bf16[2,128,128]{2,1,0:T(8,128)(2,1)S(1)}, bf16[2,128,128]{2,1,0:T(8,128)(2,1)S(1)}, u32[]{:S(2)}, u32[]{:S(2)}) collective-permute-start(bf16[2,128,128]{2,1,0:T(8,128)(2,1)S(1)} %pad_maximum_fusion.5), channel_id=1, source_target_pairs={{16,64},{48,96},{80,128},{112,160},{144,192},{176,224},{208,256},{... | collective-permute-start | bytes 196616 | tf_op jit(solution)/shard_map/ppermute | solution.py:29
  17.9 4.6 %collective-permute-start = (bf16[2,128,128]{2,1,0:T(8,128)(2,1)S(1)}, bf16[2,128,128]{2,1,0:T(8,128)(2,1)S(1)}, u32[]{:S(2)}, u32[]{:S(2)}) collective-permute-start(bf16[2,128,128]{2,1,0:T(8,128)(2,1)S(1)} %pad_maximum_fusion.5), channel_id=1, source_target_pairs={{16,32},{48,64},{80,96},{112,128},{144,160},{176,192},{208,224},{2... | collective-permute-start | bytes 196616 | tf_op jit(solution)/shard_map/ppermute | solution.py:29
  22.5 0.8 constant_dynamic-slice_fusion.4
  23.3 0.1 reshape.262
  23.4 1.2 gather_fusion
  24.6 1.2 gather_fusion.1
  25.9 3.3 %collective-permute-done.1 = bf16[2,128,128]{2,1,0:T(8,128)(2,1)S(1)} collective-permute-done((bf16[2,128,128]{2,1,0:T(8,128)(2,1)S(1)}, bf16[2,128,128]{2,1,0:T(8,128)(2,1)S(1)}, u32[]{:S(2)}, u32[]{:S(2)}) %collective-permute-start.1) | collective-permute-done | bytes 65568 | tf_op jit(solution)/shard_map/ppermute | solution.py:29
  29.2 3.3 %collective-permute-done = bf16[2,128,128]{2,1,0:T(8,128)(2,1)S(1)} collective-permute-done((bf16[2,128,128]{2,1,0:T(8,128)(2,1)S(1)}, bf16[2,128,128]{2,1,0:T(8,128)(2,1)S(1)}, u32[]{:S(2)}, u32[]{:S(2)}) %collective-permute-start) | collective-permute-done | bytes 65568 | tf_op jit(solution)/shard_map/ppermute | solution.py:29
  32.5 3.5 %collective-permute-start.5 = (bf16[3,2,128,128]{3,2,1,0:T(8,128)(2,1)S(1)}, bf16[3,2,128,128]{3,2,1,0:T(8,128)(2,1)S(1)}, u32[]{:S(2)}, u32[]{:S(2)}) collective-permute-start(bf16[3,2,128,128]{3,2,1,0:T(8,128)(2,1)S(1)} %pad_maximum_fusion.4), channel_id=1, source_target_pairs={{0,1},{1,2},{2,3},{3,0},{4,5},{5,6},{6,7},{7,4},{8,9},{9,10},{10,1... | collective-permute-start | bytes 589832 | tf_op jit(solution)/shard_map/ppermute | solution.py:19
  36.0 4.8 %collective-permute-start.4 = (bf16[3,2,128,128]{3,2,1,0:T(8,128)(2,1)S(1)}, bf16[3,2,128,128]{3,2,1,0:T(8,128)(2,1)S(1)}, u32[]{:S(2)}, u32[]{:S(2)}) collective-permute-start(bf16[3,2,128,128]{3,2,1,0:T(8,128)(2,1)S(1)} %pad_maximum_fusion.4), channel_id=1, source_target_pairs={{0,2},{1,3},{2,0},{3,1},{4,6},{5,7},{6,4},{7,5},{8,10},{9,11},{10,... | collective-permute-start | bytes 589832 | tf_op jit(solution)/shard_map/ppermute | solution.py:19
  40.9 3.3 %collective-permute-start.3 = (bf16[3,2,128,128]{3,2,1,0:T(8,128)(2,1)S(1)}, bf16[3,2,128,128]{3,2,1,0:T(8,128)(2,1)S(1)}, u32[]{:S(2)}, u32[]{:S(2)}) collective-permute-start(bf16[3,2,128,128]{3,2,1,0:T(8,128)(2,1)S(1)} %pad_maximum_fusion.4), channel_id=1, source_target_pairs={{0,3},{1,0},{2,1},{3,2},{4,7},{5,4},{6,5},{7,6},{8,11},{9,8},{10,9... | collective-permute-start | bytes 589832 | tf_op jit(solution)/shard_map/ppermute | solution.py:19
  44.1 1.0 constant_dynamic-slice_fusion.2
  45.1 0.5 fusion.7
  45.6 2.4 %collective-permute-done.4 = bf16[3,2,128,128]{3,2,1,0:T(8,128)(2,1)S(1)} collective-permute-done((bf16[3,2,128,128]{3,2,1,0:T(8,128)(2,1)S(1)}, bf16[3,2,128,128]{3,2,1,0:T(8,128)(2,1)S(1)}, u32[]{:S(2)}, u32[]{:S(2)}) %collective-permute-start.4) | collective-permute-done | bytes 196640 | tf_op jit(solution)/shard_map/ppermute | solution.py:19
  48.0 1.3 collective-permute-done.3
  49.4 1.9 %collective-permute-start.6 = (bf16[4,2,512,128]{3,2,1,0:T(8,128)(2,1)S(1)}, bf16[4,2,512,128]{3,2,1,0:T(8,128)(2,1)S(1)}, u32[]{:S(2)}, u32[]{:S(2)}) collective-permute-start(bf16[4,2,512,128]{3,2,1,0:T(8,128)(2,1)S(1)} %maximum_maximum_fusion), channel_id=1, source_target_pairs={{0,16},{16,0},{32,48},{48,32},{64,80},{80,64},{96,112},{112,96},{1... | collective-permute-start | bytes 3145736 | tf_op jit(solution)/shard_map/ppermute | solution.py:39
  51.4 0.1 reshape.289
  51.4 0.1 fusion.22
  51.5 0.1 broadcast_in_dim.47
  51.6 0.1 eq.59
  51.7 0.1 broadcast_in_dim.49
  51.8 0.1 eq.60
  51.9 0.1 broadcast_in_dim.50
  52.0 0.6 fusion.21.slots_ref
  52.6 0.7 select_select_fusion.code_ref
  53.3 0.7 collective-permute-done.6
  54.0 0.2 pad_maximum_fusion.1
  54.2 1.5 fusion.37
  55.6 16.1 %shard_map.103 = (bf16[2048,128]{1,0:T(8,128)(2,1)}, f32[4096,128]{1,0:T(8,128)}, f32[4096,128]{1,0:T(8,128)}) custom-call(s32[8,16]{1,0:T(8,128)} %fusion.21.slots_ref, bf16[2048,128]{1,0:T(8,128)(2,1)} %bitcast.81, bf16[2048,128]{1,0:T(8,128)(2,1)} %bitcast.82, s32[8,1,1024]{2,1,0:T(1,128)} %select_select_fusion.code_ref, bf16[4096,128]{1,0:T(8,128)(2,1)} %bitcast.69, ...), custom_call_target="tpu_custom_call" | custom-call | tf_op jit(solution)/shard_map/pallas_call | solution.py:105
  71.8 1.8 %fusion.2 = bf16[2,4,512,128]{3,2,1,0:T(8,128)(2,1)S(1)} fusion(f32[1,8,512,128]{3,2,1,0:T(8,128)} %bitcast.64, f32[1,8,512,128]{3,2,1,0:T(8,128)} %bitcast.62), kind=kLoop, calls=%fused_computation.8 | loop fusion | flops 524288 | bytes 5242880 | tf_op jit(solution)/shard_map/convert.4
  73.6 2.2 %collective-permute-start.7 = (bf16[2,4,512,128]{3,2,1,0:T(8,128)(2,1)S(1)}, bf16[2,4,512,128]{3,2,1,0:T(8,128)(2,1)S(1)}, u32[]{:S(2)}, u32[]{:S(2)}) collective-permute-start(bf16[2,4,512,128]{3,2,1,0:T(8,128)(2,1)S(1)} %fusion.2), channel_id=1, source_target_pairs={{0,16},{16,0},{32,48},{48,32},{64,80},{80,64},{96,112},{112,96},{1... | collective-permute-start | bytes 3145736 | tf_op jit(solution)/shard_map/ppermute | solution.py:39
  75.8 2.5 %collective-permute-done.7 = bf16[2,4,512,128]{3,2,1,0:T(8,128)(2,1)S(1)} collective-permute-done((bf16[2,4,512,128]{3,2,1,0:T(8,128)(2,1)S(1)}, bf16[2,4,512,128]{3,2,1,0:T(8,128)(2,1)S(1)}, u32[]{:S(2)}, u32[]{:S(2)}) %collective-permute-start.7) | collective-permute-done | bytes 1048608 | tf_op jit(solution)/shard_map/ppermute | solution.py:39
  78.3 0.3 fusion.34
  78.7 4.6 %collective-permute-start.10 = (bf16[2,4,128,128]{3,2,1,0:T(8,128)(2,1)S(1)}, bf16[2,4,128,128]{3,2,1,0:T(8,128)(2,1)S(1)}, u32[]{:S(2)}, u32[]{:S(2)}) collective-permute-start(bf16[2,4,128,128]{3,2,1,0:T(8,128)(2,1)S(1)} %get-tuple-element.21), channel_id=1, source_target_pairs={{0,3},{1,0},{2,1},{3,2},{4,7},{5,4},{6,5},{7,6},{8,11},{9,8},{10,9... | collective-permute-start | bytes 786440 | tf_op jit(solution)/shard_map/ppermute | solution.py:19
  83.3 3.8 %collective-permute-start.9 = (bf16[2,4,128,128]{3,2,1,0:T(8,128)(2,1)S(1)}, bf16[2,4,128,128]{3,2,1,0:T(8,128)(2,1)S(1)}, u32[]{:S(2)}, u32[]{:S(2)}) collective-permute-start(bf16[2,4,128,128]{3,2,1,0:T(8,128)(2,1)S(1)} %get-tuple-element.22), channel_id=1, source_target_pairs={{0,2},{1,3},{2,0},{3,1},{4,6},{5,7},{6,4},{7,5},{8,10},{9,11},{10,... | collective-permute-start | bytes 786440 | tf_op jit(solution)/shard_map/ppermute | solution.py:19
  87.1 1.9 %collective-permute-start.8 = (bf16[2,4,128,128]{3,2,1,0:T(8,128)(2,1)S(1)}, bf16[2,4,128,128]{3,2,1,0:T(8,128)(2,1)S(1)}, u32[]{:S(2)}, u32[]{:S(2)}) collective-permute-start(bf16[2,4,128,128]{3,2,1,0:T(8,128)(2,1)S(1)} %get-tuple-element.20), channel_id=1, source_target_pairs={{0,1},{1,2},{2,3},{3,0},{4,5},{5,6},{6,7},{7,4},{8,9},{9,10},{10,1... | collective-permute-start | bytes 786440 | tf_op jit(solution)/shard_map/ppermute | solution.py:19
  89.1 5.7 %collective-permute-done.10 = bf16[2,4,128,128]{3,2,1,0:T(8,128)(2,1)S(1)} collective-permute-done((bf16[2,4,128,128]{3,2,1,0:T(8,128)(2,1)S(1)}, bf16[2,4,128,128]{3,2,1,0:T(8,128)(2,1)S(1)}, u32[]{:S(2)}, u32[]{:S(2)}) %collective-permute-start.10) | collective-permute-done | bytes 262176 | tf_op jit(solution)/shard_map/ppermute | solution.py:19
  94.8 1.1 collective-permute-done.9
  95.9 4.5 %collective-permute-done.8 = bf16[2,4,128,128]{3,2,1,0:T(8,128)(2,1)S(1)} collective-permute-done((bf16[2,4,128,128]{3,2,1,0:T(8,128)(2,1)S(1)}, bf16[2,4,128,128]{3,2,1,0:T(8,128)(2,1)S(1)}, u32[]{:S(2)}, u32[]{:S(2)}) %collective-permute-start.8) | collective-permute-done | bytes 262176 | tf_op jit(solution)/shard_map/ppermute | solution.py:19
  100.4 0.1 fusion.32
  100.5 6.3 %collective-permute-start.13 = (bf16[2,128,128]{2,1,0:T(8,128)(2,1)S(1)}, bf16[2,128,128]{2,1,0:T(8,128)(2,1)S(1)}, u32[]{:S(2)}, u32[]{:S(2)}) collective-permute-start(bf16[2,128,128]{2,1,0:T(8,128)(2,1)S(1)} %get-tuple-element.26), channel_id=1, source_target_pairs={{96,16},{128,48},{160,80},{192,112},{224,144},{256,176},{288,208},... | collective-permute-start | bytes 196616 | tf_op jit(solution)/shard_map/ppermute | solution.py:34
  106.9 5.1 %collective-permute-start.12 = (bf16[2,128,128]{2,1,0:T(8,128)(2,1)S(1)}, bf16[2,128,128]{2,1,0:T(8,128)(2,1)S(1)}, u32[]{:S(2)}, u32[]{:S(2)}) collective-permute-start(bf16[2,128,128]{2,1,0:T(8,128)(2,1)S(1)} %get-tuple-element.27), channel_id=1, source_target_pairs={{64,16},{96,48},{128,80},{160,112},{192,144},{224,176},{256,208},{... | collective-permute-start | bytes 196616 | tf_op jit(solution)/shard_map/ppermute | solution.py:34
  112.0 5.1 %collective-permute-start.11 = (bf16[2,128,128]{2,1,0:T(8,128)(2,1)S(1)}, bf16[2,128,128]{2,1,0:T(8,128)(2,1)S(1)}, u32[]{:S(2)}, u32[]{:S(2)}) collective-permute-start(bf16[2,128,128]{2,1,0:T(8,128)(2,1)S(1)} %get-tuple-element.25), channel_id=1, source_target_pairs={{32,16},{64,48},{96,80},{128,112},{160,144},{192,176},{224,208},{2... | collective-permute-start | bytes 196616 | tf_op jit(solution)/shard_map/ppermute | solution.py:34
  117.1 0.1 broadcast_add_fusion
  117.2 0.1 add.186
  117.3 4.7 %collective-permute-done.12 = bf16[2,128,128]{2,1,0:T(8,128)(2,1)S(1)} collective-permute-done((bf16[2,128,128]{2,1,0:T(8,128)(2,1)S(1)}, bf16[2,128,128]{2,1,0:T(8,128)(2,1)S(1)}, u32[]{:S(2)}, u32[]{:S(2)}) %collective-permute-start.12) | collective-permute-done | bytes 65568 | tf_op jit(solution)/shard_map/ppermute | solution.py:34
  122.0 0.1 collective-permute-done.11
  122.1 6.4 %collective-permute-start.16 = (bf16[2,128,128]{2,1,0:T(8,128)(2,1)S(1)}, bf16[2,128,128]{2,1,0:T(8,128)(2,1)S(1)}, u32[]{:S(2)}, u32[]{:S(2)}) collective-permute-start(bf16[2,128,128]{2,1,0:T(8,128)(2,1)S(1)} %fusion.12), channel_id=1, source_target_pairs={{0,4},{4,8},{8,12},{12,0},{1,5},{5,9},{9,13},{13,1},{2,6},{6,10},{... | collective-permute-start | bytes 196616 | tf_op jit(solution)/shard_map/ppermute | solution.py:19
  128.5 9.2 %collective-permute-start.15 = (bf16[2,128,128]{2,1,0:T(8,128)(2,1)S(1)}, bf16[2,128,128]{2,1,0:T(8,128)(2,1)S(1)}, u32[]{:S(2)}, u32[]{:S(2)}) collective-permute-start(bf16[2,128,128]{2,1,0:T(8,128)(2,1)S(1)} %fusion.12), channel_id=1, source_target_pairs={{0,8},{4,12},{8,0},{12,4},{1,9},{5,13},{9,1},{13,5},{2,10},{6,14},... | collective-permute-start | bytes 196616 | tf_op jit(solution)/shard_map/ppermute | solution.py:19
  137.7 4.8 %collective-permute-start.14 = (bf16[2,128,128]{2,1,0:T(8,128)(2,1)S(1)}, bf16[2,128,128]{2,1,0:T(8,128)(2,1)S(1)}, u32[]{:S(2)}, u32[]{:S(2)}) collective-permute-start(bf16[2,128,128]{2,1,0:T(8,128)(2,1)S(1)} %fusion.12), channel_id=1, source_target_pairs={{0,12},{4,0},{8,4},{12,8},{1,13},{5,1},{9,5},{13,9},{2,14},{6,2},{... | collective-permute-start | bytes 196616 | tf_op jit(solution)/shard_map/ppermute | solution.py:19
  142.6 1.9 %collective-permute-done.14 = bf16[2,128,128]{2,1,0:T(8,128)(2,1)S(1)} collective-permute-done((bf16[2,128,128]{2,1,0:T(8,128)(2,1)S(1)}, bf16[2,128,128]{2,1,0:T(8,128)(2,1)S(1)}, u32[]{:S(2)}, u32[]{:S(2)}) %collective-permute-start.14) | collective-permute-done | bytes 65568 | tf_op jit(solution)/shard_map/ppermute | solution.py:19
  144.5 1.9 %collective-permute-start.19 = (bf16[4,2,128,128]{3,2,1,0:T(8,128)(2,1)S(1)}, bf16[4,2,128,128]{3,2,1,0:T(8,128)(2,1)S(1)}, u32[]{:S(2)}, u32[]{:S(2)}) collective-permute-start(bf16[4,2,128,128]{3,2,1,0:T(8,128)(2,1)S(1)} %get-tuple-element.24), channel_id=1, source_target_pairs={{0,1},{1,2},{2,3},{3,0},{4,5},{5,6},{6,7},{7,4},{8,9},{9,10},{10,1... | collective-permute-start | bytes 786440 | tf_op jit(solution)/shard_map/ppermute | solution.py:19
  146.4 3.8 %collective-permute-start.18 = (bf16[4,2,128,128]{3,2,1,0:T(8,128)(2,1)S(1)}, bf16[4,2,128,128]{3,2,1,0:T(8,128)(2,1)S(1)}, u32[]{:S(2)}, u32[]{:S(2)}) collective-permute-start(bf16[4,2,128,128]{3,2,1,0:T(8,128)(2,1)S(1)} %get-tuple-element.24), channel_id=1, source_target_pairs={{0,2},{1,3},{2,0},{3,1},{4,6},{5,7},{6,4},{7,5},{8,10},{9,11},{10,... | collective-permute-start | bytes 786440 | tf_op jit(solution)/shard_map/ppermute | solution.py:19
  150.3 4.5 %collective-permute-start.17 = (bf16[4,2,128,128]{3,2,1,0:T(8,128)(2,1)S(1)}, bf16[4,2,128,128]{3,2,1,0:T(8,128)(2,1)S(1)}, u32[]{:S(2)}, u32[]{:S(2)}) collective-permute-start(bf16[4,2,128,128]{3,2,1,0:T(8,128)(2,1)S(1)} %get-tuple-element.24), channel_id=1, source_target_pairs={{0,3},{1,0},{2,1},{3,2},{4,7},{5,4},{6,5},{7,6},{8,11},{9,8},{10,9... | collective-permute-start | bytes 786440 | tf_op jit(solution)/shard_map/ppermute | solution.py:19
  154.8 0.1 compare_and_fusion
  154.9 5.2 %collective-permute-done.19 = bf16[4,2,128,128]{3,2,1,0:T(8,128)(2,1)S(1)} collective-permute-done((bf16[4,2,128,128]{3,2,1,0:T(8,128)(2,1)S(1)}, bf16[4,2,128,128]{3,2,1,0:T(8,128)(2,1)S(1)}, u32[]{:S(2)}, u32[]{:S(2)}) %collective-permute-start.19) | collective-permute-done | bytes 262176 | tf_op jit(solution)/shard_map/ppermute | solution.py:19
  160.1 2.5 %collective-permute-done.17 = bf16[4,2,128,128]{3,2,1,0:T(8,128)(2,1)S(1)} collective-permute-done((bf16[4,2,128,128]{3,2,1,0:T(8,128)(2,1)S(1)}, bf16[4,2,128,128]{3,2,1,0:T(8,128)(2,1)S(1)}, u32[]{:S(2)}, u32[]{:S(2)}) %collective-permute-start.17) | collective-permute-done | bytes 262176 | tf_op jit(solution)/shard_map/ppermute | solution.py:19
  162.6 0.1 pad_maximum_fusion.2
  162.7 0.7 gather_fusion.2
  163.5 0.1 copy.24
  163.6 0.2 convert_bitcast_fusion
  163.8 1.5 fusion.36
  (30 shorter events, 0.4 us)
Async XLA Ops:
  0.6 22.8 %copy-start.1 = (s32[7]{0:T(128)S(1)}, s32[7]{0:T(128)}, u32[]{:S(2)}) copy-start(s32[7]{0:T(128)} %constant.157.clone) | copy-start | bytes 88
  1.4 24.5 %collective-permute-start.2 = (bf16[2,128,128]{2,1,0:T(8,128)(2,1)S(1)}, bf16[2,128,128]{2,1,0:T(8,128)(2,1)S(1)}, u32[]{:S(2)}, u32[]{:S(2)}) collective-permute-start(bf16[2,128,128]{2,1,0:T(8,128)(2,1)S(1)} %pad_maximum_fusion.5), channel_id=1, source_target_pairs={{16,96},{48,128},{80,160},{112,192},{144,224},{176,256},{208,288},... | collective-permute-start | bytes 196616 | tf_op jit(solution)/shard_map/ppermute | solution.py:29
  13.6 15.6 %collective-permute-start.1 = (bf16[2,128,128]{2,1,0:T(8,128)(2,1)S(1)}, bf16[2,128,128]{2,1,0:T(8,128)(2,1)S(1)}, u32[]{:S(2)}, u32[]{:S(2)}) collective-permute-start(bf16[2,128,128]{2,1,0:T(8,128)(2,1)S(1)} %pad_maximum_fusion.5), channel_id=1, source_target_pairs={{16,64},{48,96},{80,128},{112,160},{144,192},{176,224},{208,256},{... | collective-permute-start | bytes 196616 | tf_op jit(solution)/shard_map/ppermute | solution.py:29
  17.9 14.6 %collective-permute-start = (bf16[2,128,128]{2,1,0:T(8,128)(2,1)S(1)}, bf16[2,128,128]{2,1,0:T(8,128)(2,1)S(1)}, u32[]{:S(2)}, u32[]{:S(2)}) collective-permute-start(bf16[2,128,128]{2,1,0:T(8,128)(2,1)S(1)} %pad_maximum_fusion.5), channel_id=1, source_target_pairs={{16,32},{48,64},{80,96},{112,128},{144,160},{176,192},{208,224},{2... | collective-permute-start | bytes 196616 | tf_op jit(solution)/shard_map/ppermute | solution.py:29
  23.4 1.2 copy-start
  32.5 13.1 %collective-permute-start.5 = (bf16[3,2,128,128]{3,2,1,0:T(8,128)(2,1)S(1)}, bf16[3,2,128,128]{3,2,1,0:T(8,128)(2,1)S(1)}, u32[]{:S(2)}, u32[]{:S(2)}) collective-permute-start(bf16[3,2,128,128]{3,2,1,0:T(8,128)(2,1)S(1)} %pad_maximum_fusion.4), channel_id=1, source_target_pairs={{0,1},{1,2},{2,3},{3,0},{4,5},{5,6},{6,7},{7,4},{8,9},{9,10},{10,1... | collective-permute-start | bytes 589832 | tf_op jit(solution)/shard_map/ppermute | solution.py:19
  36.0 12.0 %collective-permute-start.4 = (bf16[3,2,128,128]{3,2,1,0:T(8,128)(2,1)S(1)}, bf16[3,2,128,128]{3,2,1,0:T(8,128)(2,1)S(1)}, u32[]{:S(2)}, u32[]{:S(2)}) collective-permute-start(bf16[3,2,128,128]{3,2,1,0:T(8,128)(2,1)S(1)} %pad_maximum_fusion.4), channel_id=1, source_target_pairs={{0,2},{1,3},{2,0},{3,1},{4,6},{5,7},{6,4},{7,5},{8,10},{9,11},{10,... | collective-permute-start | bytes 589832 | tf_op jit(solution)/shard_map/ppermute | solution.py:19
  40.9 8.5 %collective-permute-start.3 = (bf16[3,2,128,128]{3,2,1,0:T(8,128)(2,1)S(1)}, bf16[3,2,128,128]{3,2,1,0:T(8,128)(2,1)S(1)}, u32[]{:S(2)}, u32[]{:S(2)}) collective-permute-start(bf16[3,2,128,128]{3,2,1,0:T(8,128)(2,1)S(1)} %pad_maximum_fusion.4), channel_id=1, source_target_pairs={{0,3},{1,0},{2,1},{3,2},{4,7},{5,4},{6,5},{7,6},{8,11},{9,8},{10,9... | collective-permute-start | bytes 589832 | tf_op jit(solution)/shard_map/ppermute | solution.py:19
  49.4 4.6 %collective-permute-start.6 = (bf16[4,2,512,128]{3,2,1,0:T(8,128)(2,1)S(1)}, bf16[4,2,512,128]{3,2,1,0:T(8,128)(2,1)S(1)}, u32[]{:S(2)}, u32[]{:S(2)}) collective-permute-start(bf16[4,2,512,128]{3,2,1,0:T(8,128)(2,1)S(1)} %maximum_maximum_fusion), channel_id=1, source_target_pairs={{0,16},{16,0},{32,48},{48,32},{64,80},{80,64},{96,112},{112,96},{1... | collective-permute-start | bytes 3145736 | tf_op jit(solution)/shard_map/ppermute | solution.py:39
  71.7 6.5 %copy-start.2 = (f32[4096,128]{1,0:T(8,128)S(1)}, f32[4096,128]{1,0:T(8,128)}, u32[]{:S(2)}) copy-start(f32[4096,128]{1,0:T(8,128)} %get-tuple-element.7) | copy-start | bytes 6291460
  71.8 6.5 %copy-start.3 = (f32[4096,128]{1,0:T(8,128)S(1)}, f32[4096,128]{1,0:T(8,128)}, u32[]{:S(2)}) copy-start(f32[4096,128]{1,0:T(8,128)} %get-tuple-element.8) | copy-start | bytes 6291460
  73.6 4.7 %collective-permute-start.7 = (bf16[2,4,512,128]{3,2,1,0:T(8,128)(2,1)S(1)}, bf16[2,4,512,128]{3,2,1,0:T(8,128)(2,1)S(1)}, u32[]{:S(2)}, u32[]{:S(2)}) collective-permute-start(bf16[2,4,512,128]{3,2,1,0:T(8,128)(2,1)S(1)} %fusion.2), channel_id=1, source_target_pairs={{0,16},{16,0},{32,48},{48,32},{64,80},{80,64},{96,112},{112,96},{1... | collective-permute-start | bytes 3145736 | tf_op jit(solution)/shard_map/ppermute | solution.py:39
  78.7 16.1 %collective-permute-start.10 = (bf16[2,4,128,128]{3,2,1,0:T(8,128)(2,1)S(1)}, bf16[2,4,128,128]{3,2,1,0:T(8,128)(2,1)S(1)}, u32[]{:S(2)}, u32[]{:S(2)}) collective-permute-start(bf16[2,4,128,128]{3,2,1,0:T(8,128)(2,1)S(1)} %get-tuple-element.21), channel_id=1, source_target_pairs={{0,3},{1,0},{2,1},{3,2},{4,7},{5,4},{6,5},{7,6},{8,11},{9,8},{10,9... | collective-permute-start | bytes 786440 | tf_op jit(solution)/shard_map/ppermute | solution.py:19
  83.3 12.6 %collective-permute-start.9 = (bf16[2,4,128,128]{3,2,1,0:T(8,128)(2,1)S(1)}, bf16[2,4,128,128]{3,2,1,0:T(8,128)(2,1)S(1)}, u32[]{:S(2)}, u32[]{:S(2)}) collective-permute-start(bf16[2,4,128,128]{3,2,1,0:T(8,128)(2,1)S(1)} %get-tuple-element.22), channel_id=1, source_target_pairs={{0,2},{1,3},{2,0},{3,1},{4,6},{5,7},{6,4},{7,5},{8,10},{9,11},{10,... | collective-permute-start | bytes 786440 | tf_op jit(solution)/shard_map/ppermute | solution.py:19
  87.1 13.3 %collective-permute-start.8 = (bf16[2,4,128,128]{3,2,1,0:T(8,128)(2,1)S(1)}, bf16[2,4,128,128]{3,2,1,0:T(8,128)(2,1)S(1)}, u32[]{:S(2)}, u32[]{:S(2)}) collective-permute-start(bf16[2,4,128,128]{3,2,1,0:T(8,128)(2,1)S(1)} %get-tuple-element.20), channel_id=1, source_target_pairs={{0,1},{1,2},{2,3},{3,0},{4,5},{5,6},{6,7},{7,4},{8,9},{9,10},{10,1... | collective-permute-start | bytes 786440 | tf_op jit(solution)/shard_map/ppermute | solution.py:19
  100.5 16.7 %collective-permute-start.13 = (bf16[2,128,128]{2,1,0:T(8,128)(2,1)S(1)}, bf16[2,128,128]{2,1,0:T(8,128)(2,1)S(1)}, u32[]{:S(2)}, u32[]{:S(2)}) collective-permute-start(bf16[2,128,128]{2,1,0:T(8,128)(2,1)S(1)} %get-tuple-element.26), channel_id=1, source_target_pairs={{96,16},{128,48},{160,80},{192,112},{224,144},{256,176},{288,208},... | collective-permute-start | bytes 196616 | tf_op jit(solution)/shard_map/ppermute | solution.py:34
  106.9 15.1 %collective-permute-start.12 = (bf16[2,128,128]{2,1,0:T(8,128)(2,1)S(1)}, bf16[2,128,128]{2,1,0:T(8,128)(2,1)S(1)}, u32[]{:S(2)}, u32[]{:S(2)}) collective-permute-start(bf16[2,128,128]{2,1,0:T(8,128)(2,1)S(1)} %get-tuple-element.27), channel_id=1, source_target_pairs={{64,16},{96,48},{128,80},{160,112},{192,144},{224,176},{256,208},{... | collective-permute-start | bytes 196616 | tf_op jit(solution)/shard_map/ppermute | solution.py:34
  112.0 10.1 %collective-permute-start.11 = (bf16[2,128,128]{2,1,0:T(8,128)(2,1)S(1)}, bf16[2,128,128]{2,1,0:T(8,128)(2,1)S(1)}, u32[]{:S(2)}, u32[]{:S(2)}) collective-permute-start(bf16[2,128,128]{2,1,0:T(8,128)(2,1)S(1)} %get-tuple-element.25), channel_id=1, source_target_pairs={{32,16},{64,48},{96,80},{128,112},{160,144},{192,176},{224,208},{2... | collective-permute-start | bytes 196616 | tf_op jit(solution)/shard_map/ppermute | solution.py:34
  122.1 20.5 %collective-permute-start.16 = (bf16[2,128,128]{2,1,0:T(8,128)(2,1)S(1)}, bf16[2,128,128]{2,1,0:T(8,128)(2,1)S(1)}, u32[]{:S(2)}, u32[]{:S(2)}) collective-permute-start(bf16[2,128,128]{2,1,0:T(8,128)(2,1)S(1)} %fusion.12), channel_id=1, source_target_pairs={{0,4},{4,8},{8,12},{12,0},{1,5},{5,9},{9,13},{13,1},{2,6},{6,10},{... | collective-permute-start | bytes 196616 | tf_op jit(solution)/shard_map/ppermute | solution.py:19
  128.5 14.1 %collective-permute-start.15 = (bf16[2,128,128]{2,1,0:T(8,128)(2,1)S(1)}, bf16[2,128,128]{2,1,0:T(8,128)(2,1)S(1)}, u32[]{:S(2)}, u32[]{:S(2)}) collective-permute-start(bf16[2,128,128]{2,1,0:T(8,128)(2,1)S(1)} %fusion.12), channel_id=1, source_target_pairs={{0,8},{4,12},{8,0},{12,4},{1,9},{5,13},{9,1},{13,5},{2,10},{6,14},... | collective-permute-start | bytes 196616 | tf_op jit(solution)/shard_map/ppermute | solution.py:19
  137.7 6.7 %collective-permute-start.14 = (bf16[2,128,128]{2,1,0:T(8,128)(2,1)S(1)}, bf16[2,128,128]{2,1,0:T(8,128)(2,1)S(1)}, u32[]{:S(2)}, u32[]{:S(2)}) collective-permute-start(bf16[2,128,128]{2,1,0:T(8,128)(2,1)S(1)} %fusion.12), channel_id=1, source_target_pairs={{0,12},{4,0},{8,4},{12,8},{1,13},{5,1},{9,5},{13,9},{2,14},{6,2},{... | collective-permute-start | bytes 196616 | tf_op jit(solution)/shard_map/ppermute | solution.py:19
  144.5 15.6 %collective-permute-start.19 = (bf16[4,2,128,128]{3,2,1,0:T(8,128)(2,1)S(1)}, bf16[4,2,128,128]{3,2,1,0:T(8,128)(2,1)S(1)}, u32[]{:S(2)}, u32[]{:S(2)}) collective-permute-start(bf16[4,2,128,128]{3,2,1,0:T(8,128)(2,1)S(1)} %get-tuple-element.24), channel_id=1, source_target_pairs={{0,1},{1,2},{2,3},{3,0},{4,5},{5,6},{6,7},{7,4},{8,9},{9,10},{10,1... | collective-permute-start | bytes 786440 | tf_op jit(solution)/shard_map/ppermute | solution.py:19
  146.4 13.7 %collective-permute-start.18 = (bf16[4,2,128,128]{3,2,1,0:T(8,128)(2,1)S(1)}, bf16[4,2,128,128]{3,2,1,0:T(8,128)(2,1)S(1)}, u32[]{:S(2)}, u32[]{:S(2)}) collective-permute-start(bf16[4,2,128,128]{3,2,1,0:T(8,128)(2,1)S(1)} %get-tuple-element.24), channel_id=1, source_target_pairs={{0,2},{1,3},{2,0},{3,1},{4,6},{5,7},{6,4},{7,5},{8,10},{9,11},{10,... | collective-permute-start | bytes 786440 | tf_op jit(solution)/shard_map/ppermute | solution.py:19
  150.3 12.4 %collective-permute-start.17 = (bf16[4,2,128,128]{3,2,1,0:T(8,128)(2,1)S(1)}, bf16[4,2,128,128]{3,2,1,0:T(8,128)(2,1)S(1)}, u32[]{:S(2)}, u32[]{:S(2)}) collective-permute-start(bf16[4,2,128,128]{3,2,1,0:T(8,128)(2,1)S(1)} %get-tuple-element.24), channel_id=1, source_target_pairs={{0,3},{1,0},{2,1},{3,2},{4,7},{5,4},{6,5},{7,6},{8,11},{9,8},{10,9... | collective-permute-start | bytes 786440 | tf_op jit(solution)/shard_map/ppermute | solution.py:19

commit v16 on v15

--- a/solution.py
+++ b/solution.py
@@ -49,50 +49,53 @@
         dk_ref[...] = jnp.zeros_like(dk_ref)
         dv_ref[...] = jnp.zeros_like(dv_ref)
 
-    for slot in range(slots):
-        start = pl.multiple_of(slots_ref[step, slot] * BLOCK, BLOCK)
-        k_sel[slot * BLOCK:(slot + 1) * BLOCK, :] = k_ref[pl.ds(start, BLOCK), :]
-        v_sel[slot * BLOCK:(slot + 1) * BLOCK, :] = v_ref[pl.ds(start, BLOCK), :]
-    q = q_ref[...]
-    do = do_ref[...]
-    keys = k_sel[...]
-    values = v_sel[...]
-    rows, cols = q.shape[0], keys.shape[0]
-    scores = lax.dot_general(
-        q, keys, (((1,), (1,)), ((), ())), preferred_element_type=jnp.float32
-    ) * inv_root
-    query_pos = lax.broadcasted_iota(jnp.int32, (rows, 1), 0) // heads_here
-    allowed = query_pos >= code_ref[...]
-    scores = jnp.where(allowed, scores, -1e30)
-    row_max = jnp.max(scores, axis=1, keepdims=True)
-    shifted = jnp.exp(scores - row_max)
-    weights = shifted * (1.0 / jnp.sum(shifted, axis=1, keepdims=True))
-    weights_b = weights.astype(jnp.bfloat16)
-    output = jnp.dot(weights_b, values, preferred_element_type=jnp.float32)
-    row_delta = jnp.sum(do.astype(jnp.float32) * output, axis=1, keepdims=True)
-    prob_grad = lax.dot_general(
-        do, values, (((1,), (1,)), ((), ())), preferred_element_type=jnp.float32
-    )
-    score_b = (weights * (prob_grad - row_delta)).astype(jnp.bfloat16)
-    query_part = jnp.dot(score_b, keys, preferred_element_type=jnp.float32) * inv_root
-    dq_ref[...] = query_part.astype(jnp.bfloat16)
-    key_part = lax.dot_general(
-        score_b, q, (((0,), (0,)), ((), ())), preferred_element_type=jnp.float32
-    ) * inv_root
-    value_part = lax.dot_general(
-        weights_b, do, (((0,), (0,)), ((), ())), preferred_element_type=jnp.float32
-    )
-    for slot in range(slots):
-        start = pl.multiple_of(slots_ref[step, slot] * BLOCK, BLOCK)
-        dk_ref[pl.ds(start, BLOCK), :] += key_part[slot * BLOCK:(slot + 1) * BLOCK]
-        dv_ref[pl.ds(start, BLOCK), :] += value_part[slot * BLOCK:(slot + 1) * BLOCK]
+    pair = code_ref.shape[0]
+    rows_each = q_ref.shape[0] // pair
+    for part in range(pair):
+        for slot in range(slots):
+            start = pl.multiple_of(slots_ref[pair * step + part, slot] * BLOCK, BLOCK)
+            k_sel[slot * BLOCK:(slot + 1) * BLOCK, :] = k_ref[pl.ds(start, BLOCK), :]
+            v_sel[slot * BLOCK:(slot + 1) * BLOCK, :] = v_ref[pl.ds(start, BLOCK), :]
+        q = q_ref[part * rows_each:(part + 1) * rows_each, :]
+        do = do_ref[part * rows_each:(part + 1) * rows_each, :]
+        keys = k_sel[...]
+        values = v_sel[...]
+        rows, cols = q.shape[0], keys.shape[0]
+        scores = lax.dot_general(
+            q, keys, (((1,), (1,)), ((), ())), preferred_element_type=jnp.float32
+        ) * inv_root
+        query_pos = lax.broadcasted_iota(jnp.int32, (rows, 1), 0) // heads_here
+        allowed = query_pos >= code_ref[part]
+        scores = jnp.where(allowed, scores, -1e30)
+        row_max = jnp.max(scores, axis=1, keepdims=True)
+        shifted = jnp.exp(scores - row_max)
+        weights = shifted * (1.0 / jnp.sum(shifted, axis=1, keepdims=True))
+        weights_b = weights.astype(jnp.bfloat16)
+        output = jnp.dot(weights_b, values, preferred_element_type=jnp.float32)
+        row_delta = jnp.sum(do.astype(jnp.float32) * output, axis=1, keepdims=True)
+        prob_grad = lax.dot_general(
+            do, values, (((1,), (1,)), ((), ())), preferred_element_type=jnp.float32
+        )
+        score_b = (weights * (prob_grad - row_delta)).astype(jnp.bfloat16)
+        query_part = jnp.dot(score_b, keys, preferred_element_type=jnp.float32) * inv_root
+        dq_ref[part * rows_each:(part + 1) * rows_each, :] = query_part.astype(jnp.bfloat16)
+        key_part = lax.dot_general(
+            score_b, q, (((0,), (0,)), ((), ())), preferred_element_type=jnp.float32
+        ) * inv_root
+        value_part = lax.dot_general(
+            weights_b, do, (((0,), (0,)), ((), ())), preferred_element_type=jnp.float32
+        )
+        for slot in range(slots):
+            start = pl.multiple_of(slots_ref[pair * step + part, slot] * BLOCK, BLOCK)
+            dk_ref[pl.ds(start, BLOCK), :] += key_part[slot * BLOCK:(slot + 1) * BLOCK]
+            dv_ref[pl.ds(start, BLOCK), :] += value_part[slot * BLOCK:(slot + 1) * BLOCK]
 
 
 def local_grads(queries, out_grad, key_tiles, value_tiles, slot_index, code, inv_root,
                 interpret=False):
     tokens_here, heads_here, width = queries.shape
     blocks_here, slots = slot_index.shape
-    rows = BLOCK * heads_here
+    rows = 2 * BLOCK * heads_here
     store = key_tiles.shape[0] * BLOCK
     cols = slots * BLOCK
     key_pos = jnp.tile(jnp.arange(BLOCK, dtype=jnp.int32), slots)[None, :]
@@ -106,11 +109,11 @@
         kernel,
         grid_spec=pltpu.PrefetchScalarGridSpec(
             num_scalar_prefetch=1,
-            grid=(blocks_here,),
+            grid=(blocks_here // 2,),
             in_specs=[
                 pl.BlockSpec((rows, width), per_block),
                 pl.BlockSpec((rows, width), per_block),
-                pl.BlockSpec((None, 1, cols), lambda step, slots_ref: (step, 0, 0)),
+                pl.BlockSpec((2, 1, cols), lambda step, slots_ref: (step, 0, 0)),
                 pl.BlockSpec((store, width), whole),
                 pl.BlockSpec((store, width), whole),
             ],

time: 166 us -> 165 us (level)
  no operation moved by 1% of the time
where the time goes in v16:
time: 165 us
  starting transfers between devices  94.3 us (57%)
  waiting for transfers between devices  39.2 us (24%)
  Pallas kernels  15.4 us (9%)
  local copies, waits for them, and re-layouts  9.5 us (6%)
  other arithmetic  5.06 us (3%)
    ppermute x12, starting transfers between devices, cycled(): lax.ppermute(value, axis, [(source, (source + steps) % count) for source...  52.6 us
    ppermute x12, waiting for transfers between devices, cycled(): lax.ppermute(value, axis, [(source, (source + steps) % count) for source...  24.6 us
    ppermute x3, starting transfers between devices, chip_fetch(): return lax.ppermute(value, axis, chip_pairs(lax.axis_size(axis), step))  21 us
    ppermute x3, starting transfers between devices, chip_return(): lax.ppermute(value, axis, [(target, source) for source, target in pairs])  16.6 us
    pallas_call x1, Pallas kernels, local_grads(): pl.pallas_call(kernel, grid_spec=pltpu.PrefetchScalarGridSpec(num_scalar_...  15.4 us
    ppermute x3, waiting for transfers between devices, chip_fetch(): return lax.ppermute(value, axis, chip_pairs(lax.axis_size(axis), step))  6.61 us
    ppermute x3, waiting for transfers between devices, chip_return(): lax.ppermute(value, axis, [(target, source) for source, target in pairs])  4.79 us
    ppermute x2, starting transfers between devices, swap_cores(): lax.ppermute(value, axis, [(source, source ^ 1) for source in range(count)])  4.08 us
  transfers between devices with their start and end apart: 20, of which 14 were waited for; matrix products, arithmetic and copies ran while one was open for 4% of the time, Pallas kernels for 0%

profile of v16, /device:TPU:6, one launch (start us, length us, event | category | flops | bytes accessed | tf_op | source)
XLA Modules:
  0.0 164.5 jit_solution(6397080687647406586)
XLA Ops:
  0.6 0.8 constant_dynamic-slice_fusion
  1.4 12.2 %collective-permute-start.2 = (bf16[2,128,128]{2,1,0:T(8,128)(2,1)S(1)}, bf16[2,128,128]{2,1,0:T(8,128)(2,1)S(1)}, u32[]{:S(2)}, u32[]{:S(2)}) collective-permute-start(bf16[2,128,128]{2,1,0:T(8,128)(2,1)S(1)} %pad_maximum_fusion.5), channel_id=1, source_target_pairs={{16,96},{48,128},{80,160},{112,192},{144,224},{176,256},{208,288},... | collective-permute-start | bytes 196616 | tf_op jit(solution)/shard_map/ppermute | solution.py:29
  13.6 4.3 %collective-permute-start.1 = (bf16[2,128,128]{2,1,0:T(8,128)(2,1)S(1)}, bf16[2,128,128]{2,1,0:T(8,128)(2,1)S(1)}, u32[]{:S(2)}, u32[]{:S(2)}) collective-permute-start(bf16[2,128,128]{2,1,0:T(8,128)(2,1)S(1)} %pad_maximum_fusion.5), channel_id=1, source_target_pairs={{16,64},{48,96},{80,128},{112,160},{144,192},{176,224},{208,256},{... | collective-permute-start | bytes 196616 | tf_op jit(solution)/shard_map/ppermute | solution.py:29
  17.9 4.6 %collective-permute-start = (bf16[2,128,128]{2,1,0:T(8,128)(2,1)S(1)}, bf16[2,128,128]{2,1,0:T(8,128)(2,1)S(1)}, u32[]{:S(2)}, u32[]{:S(2)}) collective-permute-start(bf16[2,128,128]{2,1,0:T(8,128)(2,1)S(1)} %pad_maximum_fusion.5), channel_id=1, source_target_pairs={{16,32},{48,64},{80,96},{112,128},{144,160},{176,192},{208,224},{2... | collective-permute-start | bytes 196616 | tf_op jit(solution)/shard_map/ppermute | solution.py:29
  22.5 0.8 constant_dynamic-slice_fusion.4
  23.3 0.1 reshape.262
  23.4 1.2 gather_fusion
  24.6 1.2 gather_fusion.1
  25.9 3.3 %collective-permute-done.1 = bf16[2,128,128]{2,1,0:T(8,128)(2,1)S(1)} collective-permute-done((bf16[2,128,128]{2,1,0:T(8,128)(2,1)S(1)}, bf16[2,128,128]{2,1,0:T(8,128)(2,1)S(1)}, u32[]{:S(2)}, u32[]{:S(2)}) %collective-permute-start.1) | collective-permute-done | bytes 65568 | tf_op jit(solution)/shard_map/ppermute | solution.py:29
  29.2 3.3 %collective-permute-done = bf16[2,128,128]{2,1,0:T(8,128)(2,1)S(1)} collective-permute-done((bf16[2,128,128]{2,1,0:T(8,128)(2,1)S(1)}, bf16[2,128,128]{2,1,0:T(8,128)(2,1)S(1)}, u32[]{:S(2)}, u32[]{:S(2)}) %collective-permute-start) | collective-permute-done | bytes 65568 | tf_op jit(solution)/shard_map/ppermute | solution.py:29
  32.5 3.5 %collective-permute-start.5 = (bf16[3,2,128,128]{3,2,1,0:T(8,128)(2,1)S(1)}, bf16[3,2,128,128]{3,2,1,0:T(8,128)(2,1)S(1)}, u32[]{:S(2)}, u32[]{:S(2)}) collective-permute-start(bf16[3,2,128,128]{3,2,1,0:T(8,128)(2,1)S(1)} %pad_maximum_fusion.4), channel_id=1, source_target_pairs={{0,1},{1,2},{2,3},{3,0},{4,5},{5,6},{6,7},{7,4},{8,9},{9,10},{10,1... | collective-permute-start | bytes 589832 | tf_op jit(solution)/shard_map/ppermute | solution.py:19
  36.0 4.8 %collective-permute-start.4 = (bf16[3,2,128,128]{3,2,1,0:T(8,128)(2,1)S(1)}, bf16[3,2,128,128]{3,2,1,0:T(8,128)(2,1)S(1)}, u32[]{:S(2)}, u32[]{:S(2)}) collective-permute-start(bf16[3,2,128,128]{3,2,1,0:T(8,128)(2,1)S(1)} %pad_maximum_fusion.4), channel_id=1, source_target_pairs={{0,2},{1,3},{2,0},{3,1},{4,6},{5,7},{6,4},{7,5},{8,10},{9,11},{10,... | collective-permute-start | bytes 589832 | tf_op jit(solution)/shard_map/ppermute | solution.py:19
  40.9 3.3 %collective-permute-start.3 = (bf16[3,2,128,128]{3,2,1,0:T(8,128)(2,1)S(1)}, bf16[3,2,128,128]{3,2,1,0:T(8,128)(2,1)S(1)}, u32[]{:S(2)}, u32[]{:S(2)}) collective-permute-start(bf16[3,2,128,128]{3,2,1,0:T(8,128)(2,1)S(1)} %pad_maximum_fusion.4), channel_id=1, source_target_pairs={{0,3},{1,0},{2,1},{3,2},{4,7},{5,4},{6,5},{7,6},{8,11},{9,8},{10,9... | collective-permute-start | bytes 589832 | tf_op jit(solution)/shard_map/ppermute | solution.py:19
  44.1 1.0 constant_dynamic-slice_fusion.2
  45.1 0.5 fusion.7
  45.6 2.4 %collective-permute-done.4 = bf16[3,2,128,128]{3,2,1,0:T(8,128)(2,1)S(1)} collective-permute-done((bf16[3,2,128,128]{3,2,1,0:T(8,128)(2,1)S(1)}, bf16[3,2,128,128]{3,2,1,0:T(8,128)(2,1)S(1)}, u32[]{:S(2)}, u32[]{:S(2)}) %collective-permute-start.4) | collective-permute-done | bytes 196640 | tf_op jit(solution)/shard_map/ppermute | solution.py:19
  48.0 1.3 collective-permute-done.3
  49.4 1.9 %collective-permute-start.6 = (bf16[4,2,512,128]{3,2,1,0:T(8,128)(2,1)S(1)}, bf16[4,2,512,128]{3,2,1,0:T(8,128)(2,1)S(1)}, u32[]{:S(2)}, u32[]{:S(2)}) collective-permute-start(bf16[4,2,512,128]{3,2,1,0:T(8,128)(2,1)S(1)} %maximum_maximum_fusion), channel_id=1, source_target_pairs={{0,16},{16,0},{32,48},{48,32},{64,80},{80,64},{96,112},{112,96},{1... | collective-permute-start | bytes 3145736 | tf_op jit(solution)/shard_map/ppermute | solution.py:39
  51.4 0.1 reshape.289
  51.4 0.1 fusion.22
  51.5 0.1 broadcast_in_dim.47
  51.6 0.1 eq.59
  51.7 0.1 broadcast_in_dim.49
  51.8 0.1 eq.60
  51.9 0.1 broadcast_in_dim.50
  52.0 0.6 fusion.21.slots_ref
  52.6 0.7 select_select_fusion.code_ref
  53.3 0.7 collective-permute-done.6
  54.0 0.2 pad_maximum_fusion.1
  54.2 1.5 fusion.37
  55.6 15.4 %shard_map.103 = (bf16[2048,128]{1,0:T(8,128)(2,1)}, f32[4096,128]{1,0:T(8,128)}, f32[4096,128]{1,0:T(8,128)}) custom-call(s32[8,16]{1,0:T(8,128)} %fusion.21.slots_ref, bf16[2048,128]{1,0:T(8,128)(2,1)} %bitcast.81, bf16[2048,128]{1,0:T(8,128)(2,1)} %bitcast.82, s32[8,1,1024]{2,1,0:T(1,128)} %select_select_fusion.code_ref, bf16[4096,128]{1,0:T(8,128)(2,1)} %bitcast.69, ...), custom_call_target="tpu_custom_call" | custom-call | tf_op jit(solution)/shard_map/pallas_call | solution.py:108
  71.0 1.8 %fusion.2 = bf16[2,4,512,128]{3,2,1,0:T(8,128)(2,1)S(1)} fusion(f32[1,8,512,128]{3,2,1,0:T(8,128)} %bitcast.64, f32[1,8,512,128]{3,2,1,0:T(8,128)} %bitcast.62), kind=kLoop, calls=%fused_computation.8 | loop fusion | flops 524288 | bytes 5242880 | tf_op jit(solution)/shard_map/convert.4
  72.9 2.2 %collective-permute-start.7 = (bf16[2,4,512,128]{3,2,1,0:T(8,128)(2,1)S(1)}, bf16[2,4,512,128]{3,2,1,0:T(8,128)(2,1)S(1)}, u32[]{:S(2)}, u32[]{:S(2)}) collective-permute-start(bf16[2,4,512,128]{3,2,1,0:T(8,128)(2,1)S(1)} %fusion.2), channel_id=1, source_target_pairs={{0,16},{16,0},{32,48},{48,32},{64,80},{80,64},{96,112},{112,96},{1... | collective-permute-start | bytes 3145736 | tf_op jit(solution)/shard_map/ppermute | solution.py:39
  75.1 2.5 %collective-permute-done.7 = bf16[2,4,512,128]{3,2,1,0:T(8,128)(2,1)S(1)} collective-permute-done((bf16[2,4,512,128]{3,2,1,0:T(8,128)(2,1)S(1)}, bf16[2,4,512,128]{3,2,1,0:T(8,128)(2,1)S(1)}, u32[]{:S(2)}, u32[]{:S(2)}) %collective-permute-start.7) | collective-permute-done | bytes 1048608 | tf_op jit(solution)/shard_map/ppermute | solution.py:39
  77.6 0.3 fusion.34
  78.0 4.6 %collective-permute-start.10 = (bf16[2,4,128,128]{3,2,1,0:T(8,128)(2,1)S(1)}, bf16[2,4,128,128]{3,2,1,0:T(8,128)(2,1)S(1)}, u32[]{:S(2)}, u32[]{:S(2)}) collective-permute-start(bf16[2,4,128,128]{3,2,1,0:T(8,128)(2,1)S(1)} %get-tuple-element.21), channel_id=1, source_target_pairs={{0,3},{1,0},{2,1},{3,2},{4,7},{5,4},{6,5},{7,6},{8,11},{9,8},{10,9... | collective-permute-start | bytes 786440 | tf_op jit(solution)/shard_map/ppermute | solution.py:19
  82.5 3.8 %collective-permute-start.9 = (bf16[2,4,128,128]{3,2,1,0:T(8,128)(2,1)S(1)}, bf16[2,4,128,128]{3,2,1,0:T(8,128)(2,1)S(1)}, u32[]{:S(2)}, u32[]{:S(2)}) collective-permute-start(bf16[2,4,128,128]{3,2,1,0:T(8,128)(2,1)S(1)} %get-tuple-element.22), channel_id=1, source_target_pairs={{0,2},{1,3},{2,0},{3,1},{4,6},{5,7},{6,4},{7,5},{8,10},{9,11},{10,... | collective-permute-start | bytes 786440 | tf_op jit(solution)/shard_map/ppermute | solution.py:19
  86.4 1.9 %collective-permute-start.8 = (bf16[2,4,128,128]{3,2,1,0:T(8,128)(2,1)S(1)}, bf16[2,4,128,128]{3,2,1,0:T(8,128)(2,1)S(1)}, u32[]{:S(2)}, u32[]{:S(2)}) collective-permute-start(bf16[2,4,128,128]{3,2,1,0:T(8,128)(2,1)S(1)} %get-tuple-element.20), channel_id=1, source_target_pairs={{0,1},{1,2},{2,3},{3,0},{4,5},{5,6},{6,7},{7,4},{8,9},{9,10},{10,1... | collective-permute-start | bytes 786440 | tf_op jit(solution)/shard_map/ppermute | solution.py:19
  88.3 5.7 %collective-permute-done.10 = bf16[2,4,128,128]{3,2,1,0:T(8,128)(2,1)S(1)} collective-permute-done((bf16[2,4,128,128]{3,2,1,0:T(8,128)(2,1)S(1)}, bf16[2,4,128,128]{3,2,1,0:T(8,128)(2,1)S(1)}, u32[]{:S(2)}, u32[]{:S(2)}) %collective-permute-start.10) | collective-permute-done | bytes 262176 | tf_op jit(solution)/shard_map/ppermute | solution.py:19
  94.0 1.1 collective-permute-done.9
  95.1 4.5 %collective-permute-done.8 = bf16[2,4,128,128]{3,2,1,0:T(8,128)(2,1)S(1)} collective-permute-done((bf16[2,4,128,128]{3,2,1,0:T(8,128)(2,1)S(1)}, bf16[2,4,128,128]{3,2,1,0:T(8,128)(2,1)S(1)}, u32[]{:S(2)}, u32[]{:S(2)}) %collective-permute-start.8) | collective-permute-done | bytes 262176 | tf_op jit(solution)/shard_map/ppermute | solution.py:19
  99.6 0.1 fusion.32
  99.8 6.3 %collective-permute-start.13 = (bf16[2,128,128]{2,1,0:T(8,128)(2,1)S(1)}, bf16[2,128,128]{2,1,0:T(8,128)(2,1)S(1)}, u32[]{:S(2)}, u32[]{:S(2)}) collective-permute-start(bf16[2,128,128]{2,1,0:T(8,128)(2,1)S(1)} %get-tuple-element.26), channel_id=1, source_target_pairs={{96,16},{128,48},{160,80},{192,112},{224,144},{256,176},{288,208},... | collective-permute-start | bytes 196616 | tf_op jit(solution)/shard_map/ppermute | solution.py:34
  106.1 5.1 %collective-permute-start.12 = (bf16[2,128,128]{2,1,0:T(8,128)(2,1)S(1)}, bf16[2,128,128]{2,1,0:T(8,128)(2,1)S(1)}, u32[]{:S(2)}, u32[]{:S(2)}) collective-permute-start(bf16[2,128,128]{2,1,0:T(8,128)(2,1)S(1)} %get-tuple-element.27), channel_id=1, source_target_pairs={{64,16},{96,48},{128,80},{160,112},{192,144},{224,176},{256,208},{... | collective-permute-start | bytes 196616 | tf_op jit(solution)/shard_map/ppermute | solution.py:34
  111.3 5.1 %collective-permute-start.11 = (bf16[2,128,128]{2,1,0:T(8,128)(2,1)S(1)}, bf16[2,128,128]{2,1,0:T(8,128)(2,1)S(1)}, u32[]{:S(2)}, u32[]{:S(2)}) collective-permute-start(bf16[2,128,128]{2,1,0:T(8,128)(2,1)S(1)} %get-tuple-element.25), channel_id=1, source_target_pairs={{32,16},{64,48},{96,80},{128,112},{160,144},{192,176},{224,208},{2... | collective-permute-start | bytes 196616 | tf_op jit(solution)/shard_map/ppermute | solution.py:34
  116.4 0.1 broadcast_add_fusion
  116.4 0.1 add.186
  116.5 4.6 %collective-permute-done.12 = bf16[2,128,128]{2,1,0:T(8,128)(2,1)S(1)} collective-permute-done((bf16[2,128,128]{2,1,0:T(8,128)(2,1)S(1)}, bf16[2,128,128]{2,1,0:T(8,128)(2,1)S(1)}, u32[]{:S(2)}, u32[]{:S(2)}) %collective-permute-start.12) | collective-permute-done | bytes 65568 | tf_op jit(solution)/shard_map/ppermute | solution.py:34
  121.2 0.2 collective-permute-done.11
  121.4 6.4 %collective-permute-start.16 = (bf16[2,128,128]{2,1,0:T(8,128)(2,1)S(1)}, bf16[2,128,128]{2,1,0:T(8,128)(2,1)S(1)}, u32[]{:S(2)}, u32[]{:S(2)}) collective-permute-start(bf16[2,128,128]{2,1,0:T(8,128)(2,1)S(1)} %fusion.12), channel_id=1, source_target_pairs={{0,4},{4,8},{8,12},{12,0},{1,5},{5,9},{9,13},{13,1},{2,6},{6,10},{... | collective-permute-start | bytes 196616 | tf_op jit(solution)/shard_map/ppermute | solution.py:19
  127.8 9.2 %collective-permute-start.15 = (bf16[2,128,128]{2,1,0:T(8,128)(2,1)S(1)}, bf16[2,128,128]{2,1,0:T(8,128)(2,1)S(1)}, u32[]{:S(2)}, u32[]{:S(2)}) collective-permute-start(bf16[2,128,128]{2,1,0:T(8,128)(2,1)S(1)} %fusion.12), channel_id=1, source_target_pairs={{0,8},{4,12},{8,0},{12,4},{1,9},{5,13},{9,1},{13,5},{2,10},{6,14},... | collective-permute-start | bytes 196616 | tf_op jit(solution)/shard_map/ppermute | solution.py:19
  137.0 4.8 %collective-permute-start.14 = (bf16[2,128,128]{2,1,0:T(8,128)(2,1)S(1)}, bf16[2,128,128]{2,1,0:T(8,128)(2,1)S(1)}, u32[]{:S(2)}, u32[]{:S(2)}) collective-permute-start(bf16[2,128,128]{2,1,0:T(8,128)(2,1)S(1)} %fusion.12), channel_id=1, source_target_pairs={{0,12},{4,0},{8,4},{12,8},{1,13},{5,1},{9,5},{13,9},{2,14},{6,2},{... | collective-permute-start | bytes 196616 | tf_op jit(solution)/shard_map/ppermute | solution.py:19
  141.9 1.9 %collective-permute-done.14 = bf16[2,128,128]{2,1,0:T(8,128)(2,1)S(1)} collective-permute-done((bf16[2,128,128]{2,1,0:T(8,128)(2,1)S(1)}, bf16[2,128,128]{2,1,0:T(8,128)(2,1)S(1)}, u32[]{:S(2)}, u32[]{:S(2)}) %collective-permute-start.14) | collective-permute-done | bytes 65568 | tf_op jit(solution)/shard_map/ppermute | solution.py:19
  143.8 1.9 %collective-permute-start.19 = (bf16[4,2,128,128]{3,2,1,0:T(8,128)(2,1)S(1)}, bf16[4,2,128,128]{3,2,1,0:T(8,128)(2,1)S(1)}, u32[]{:S(2)}, u32[]{:S(2)}) collective-permute-start(bf16[4,2,128,128]{3,2,1,0:T(8,128)(2,1)S(1)} %get-tuple-element.24), channel_id=1, source_target_pairs={{0,1},{1,2},{2,3},{3,0},{4,5},{5,6},{6,7},{7,4},{8,9},{9,10},{10,1... | collective-permute-start | bytes 786440 | tf_op jit(solution)/shard_map/ppermute | solution.py:19
  145.7 3.8 %collective-permute-start.18 = (bf16[4,2,128,128]{3,2,1,0:T(8,128)(2,1)S(1)}, bf16[4,2,128,128]{3,2,1,0:T(8,128)(2,1)S(1)}, u32[]{:S(2)}, u32[]{:S(2)}) collective-permute-start(bf16[4,2,128,128]{3,2,1,0:T(8,128)(2,1)S(1)} %get-tuple-element.24), channel_id=1, source_target_pairs={{0,2},{1,3},{2,0},{3,1},{4,6},{5,7},{6,4},{7,5},{8,10},{9,11},{10,... | collective-permute-start | bytes 786440 | tf_op jit(solution)/shard_map/ppermute | solution.py:19
  149.5 4.5 %collective-permute-start.17 = (bf16[4,2,128,128]{3,2,1,0:T(8,128)(2,1)S(1)}, bf16[4,2,128,128]{3,2,1,0:T(8,128)(2,1)S(1)}, u32[]{:S(2)}, u32[]{:S(2)}) collective-permute-start(bf16[4,2,128,128]{3,2,1,0:T(8,128)(2,1)S(1)} %get-tuple-element.24), channel_id=1, source_target_pairs={{0,3},{1,0},{2,1},{3,2},{4,7},{5,4},{6,5},{7,6},{8,11},{9,8},{10,9... | collective-permute-start | bytes 786440 | tf_op jit(solution)/shard_map/ppermute | solution.py:19
  154.1 0.1 compare_and_fusion
  154.2 5.2 %collective-permute-done.19 = bf16[4,2,128,128]{3,2,1,0:T(8,128)(2,1)S(1)} collective-permute-done((bf16[4,2,128,128]{3,2,1,0:T(8,128)(2,1)S(1)}, bf16[4,2,128,128]{3,2,1,0:T(8,128)(2,1)S(1)}, u32[]{:S(2)}, u32[]{:S(2)}) %collective-permute-start.19) | collective-permute-done | bytes 262176 | tf_op jit(solution)/shard_map/ppermute | solution.py:19
  159.4 2.5 %collective-permute-done.17 = bf16[4,2,128,128]{3,2,1,0:T(8,128)(2,1)S(1)} collective-permute-done((bf16[4,2,128,128]{3,2,1,0:T(8,128)(2,1)S(1)}, bf16[4,2,128,128]{3,2,1,0:T(8,128)(2,1)S(1)}, u32[]{:S(2)}, u32[]{:S(2)}) %collective-permute-start.17) | collective-permute-done | bytes 262176 | tf_op jit(solution)/shard_map/ppermute | solution.py:19
  161.9 0.1 pad_maximum_fusion.2
  162.0 0.7 gather_fusion.2
  162.8 0.1 copy.24
  162.9 0.2 convert_bitcast_fusion
  163.1 1.5 fusion.36
  (30 shorter events, 0.4 us)
Async XLA Ops:
  0.6 22.8 %copy-start.1 = (s32[7]{0:T(128)S(1)}, s32[7]{0:T(128)}, u32[]{:S(2)}) copy-start(s32[7]{0:T(128)} %constant.157.clone) | copy-start | bytes 88
  1.4 24.5 %collective-permute-start.2 = (bf16[2,128,128]{2,1,0:T(8,128)(2,1)S(1)}, bf16[2,128,128]{2,1,0:T(8,128)(2,1)S(1)}, u32[]{:S(2)}, u32[]{:S(2)}) collective-permute-start(bf16[2,128,128]{2,1,0:T(8,128)(2,1)S(1)} %pad_maximum_fusion.5), channel_id=1, source_target_pairs={{16,96},{48,128},{80,160},{112,192},{144,224},{176,256},{208,288},... | collective-permute-start | bytes 196616 | tf_op jit(solution)/shard_map/ppermute | solution.py:29
  13.6 15.6 %collective-permute-start.1 = (bf16[2,128,128]{2,1,0:T(8,128)(2,1)S(1)}, bf16[2,128,128]{2,1,0:T(8,128)(2,1)S(1)}, u32[]{:S(2)}, u32[]{:S(2)}) collective-permute-start(bf16[2,128,128]{2,1,0:T(8,128)(2,1)S(1)} %pad_maximum_fusion.5), channel_id=1, source_target_pairs={{16,64},{48,96},{80,128},{112,160},{144,192},{176,224},{208,256},{... | collective-permute-start | bytes 196616 | tf_op jit(solution)/shard_map/ppermute | solution.py:29
  17.9 14.6 %collective-permute-start = (bf16[2,128,128]{2,1,0:T(8,128)(2,1)S(1)}, bf16[2,128,128]{2,1,0:T(8,128)(2,1)S(1)}, u32[]{:S(2)}, u32[]{:S(2)}) collective-permute-start(bf16[2,128,128]{2,1,0:T(8,128)(2,1)S(1)} %pad_maximum_fusion.5), channel_id=1, source_target_pairs={{16,32},{48,64},{80,96},{112,128},{144,160},{176,192},{208,224},{2... | collective-permute-start | bytes 196616 | tf_op jit(solution)/shard_map/ppermute | solution.py:29
  23.4 1.2 copy-start
  32.5 13.1 %collective-permute-start.5 = (bf16[3,2,128,128]{3,2,1,0:T(8,128)(2,1)S(1)}, bf16[3,2,128,128]{3,2,1,0:T(8,128)(2,1)S(1)}, u32[]{:S(2)}, u32[]{:S(2)}) collective-permute-start(bf16[3,2,128,128]{3,2,1,0:T(8,128)(2,1)S(1)} %pad_maximum_fusion.4), channel_id=1, source_target_pairs={{0,1},{1,2},{2,3},{3,0},{4,5},{5,6},{6,7},{7,4},{8,9},{9,10},{10,1... | collective-permute-start | bytes 589832 | tf_op jit(solution)/shard_map/ppermute | solution.py:19
  36.0 12.0 %collective-permute-start.4 = (bf16[3,2,128,128]{3,2,1,0:T(8,128)(2,1)S(1)}, bf16[3,2,128,128]{3,2,1,0:T(8,128)(2,1)S(1)}, u32[]{:S(2)}, u32[]{:S(2)}) collective-permute-start(bf16[3,2,128,128]{3,2,1,0:T(8,128)(2,1)S(1)} %pad_maximum_fusion.4), channel_id=1, source_target_pairs={{0,2},{1,3},{2,0},{3,1},{4,6},{5,7},{6,4},{7,5},{8,10},{9,11},{10,... | collective-permute-start | bytes 589832 | tf_op jit(solution)/shard_map/ppermute | solution.py:19
  40.9 8.5 %collective-permute-start.3 = (bf16[3,2,128,128]{3,2,1,0:T(8,128)(2,1)S(1)}, bf16[3,2,128,128]{3,2,1,0:T(8,128)(2,1)S(1)}, u32[]{:S(2)}, u32[]{:S(2)}) collective-permute-start(bf16[3,2,128,128]{3,2,1,0:T(8,128)(2,1)S(1)} %pad_maximum_fusion.4), channel_id=1, source_target_pairs={{0,3},{1,0},{2,1},{3,2},{4,7},{5,4},{6,5},{7,6},{8,11},{9,8},{10,9... | collective-permute-start | bytes 589832 | tf_op jit(solution)/shard_map/ppermute | solution.py:19
  49.4 4.6 %collective-permute-start.6 = (bf16[4,2,512,128]{3,2,1,0:T(8,128)(2,1)S(1)}, bf16[4,2,512,128]{3,2,1,0:T(8,128)(2,1)S(1)}, u32[]{:S(2)}, u32[]{:S(2)}) collective-permute-start(bf16[4,2,512,128]{3,2,1,0:T(8,128)(2,1)S(1)} %maximum_maximum_fusion), channel_id=1, source_target_pairs={{0,16},{16,0},{32,48},{48,32},{64,80},{80,64},{96,112},{112,96},{1... | collective-permute-start | bytes 3145736 | tf_op jit(solution)/shard_map/ppermute | solution.py:39
  71.0 6.5 %copy-start.2 = (f32[4096,128]{1,0:T(8,128)S(1)}, f32[4096,128]{1,0:T(8,128)}, u32[]{:S(2)}) copy-start(f32[4096,128]{1,0:T(8,128)} %get-tuple-element.7) | copy-start | bytes 6291460
  71.0 6.5 %copy-start.3 = (f32[4096,128]{1,0:T(8,128)S(1)}, f32[4096,128]{1,0:T(8,128)}, u32[]{:S(2)}) copy-start(f32[4096,128]{1,0:T(8,128)} %get-tuple-element.8) | copy-start | bytes 6291460
  72.9 4.7 %collective-permute-start.7 = (bf16[2,4,512,128]{3,2,1,0:T(8,128)(2,1)S(1)}, bf16[2,4,512,128]{3,2,1,0:T(8,128)(2,1)S(1)}, u32[]{:S(2)}, u32[]{:S(2)}) collective-permute-start(bf16[2,4,512,128]{3,2,1,0:T(8,128)(2,1)S(1)} %fusion.2), channel_id=1, source_target_pairs={{0,16},{16,0},{32,48},{48,32},{64,80},{80,64},{96,112},{112,96},{1... | collective-permute-start | bytes 3145736 | tf_op jit(solution)/shard_map/ppermute | solution.py:39
  78.0 16.1 %collective-permute-start.10 = (bf16[2,4,128,128]{3,2,1,0:T(8,128)(2,1)S(1)}, bf16[2,4,128,128]{3,2,1,0:T(8,128)(2,1)S(1)}, u32[]{:S(2)}, u32[]{:S(2)}) collective-permute-start(bf16[2,4,128,128]{3,2,1,0:T(8,128)(2,1)S(1)} %get-tuple-element.21), channel_id=1, source_target_pairs={{0,3},{1,0},{2,1},{3,2},{4,7},{5,4},{6,5},{7,6},{8,11},{9,8},{10,9... | collective-permute-start | bytes 786440 | tf_op jit(solution)/shard_map/ppermute | solution.py:19
  82.5 12.6 %collective-permute-start.9 = (bf16[2,4,128,128]{3,2,1,0:T(8,128)(2,1)S(1)}, bf16[2,4,128,128]{3,2,1,0:T(8,128)(2,1)S(1)}, u32[]{:S(2)}, u32[]{:S(2)}) collective-permute-start(bf16[2,4,128,128]{3,2,1,0:T(8,128)(2,1)S(1)} %get-tuple-element.22), channel_id=1, source_target_pairs={{0,2},{1,3},{2,0},{3,1},{4,6},{5,7},{6,4},{7,5},{8,10},{9,11},{10,... | collective-permute-start | bytes 786440 | tf_op jit(solution)/shard_map/ppermute | solution.py:19
  86.4 13.3 %collective-permute-start.8 = (bf16[2,4,128,128]{3,2,1,0:T(8,128)(2,1)S(1)}, bf16[2,4,128,128]{3,2,1,0:T(8,128)(2,1)S(1)}, u32[]{:S(2)}, u32[]{:S(2)}) collective-permute-start(bf16[2,4,128,128]{3,2,1,0:T(8,128)(2,1)S(1)} %get-tuple-element.20), channel_id=1, source_target_pairs={{0,1},{1,2},{2,3},{3,0},{4,5},{5,6},{6,7},{7,4},{8,9},{9,10},{10,1... | collective-permute-start | bytes 786440 | tf_op jit(solution)/shard_map/ppermute | solution.py:19
  99.8 16.7 %collective-permute-start.13 = (bf16[2,128,128]{2,1,0:T(8,128)(2,1)S(1)}, bf16[2,128,128]{2,1,0:T(8,128)(2,1)S(1)}, u32[]{:S(2)}, u32[]{:S(2)}) collective-permute-start(bf16[2,128,128]{2,1,0:T(8,128)(2,1)S(1)} %get-tuple-element.26), channel_id=1, source_target_pairs={{96,16},{128,48},{160,80},{192,112},{224,144},{256,176},{288,208},... | collective-permute-start | bytes 196616 | tf_op jit(solution)/shard_map/ppermute | solution.py:34
  106.1 15.0 %collective-permute-start.12 = (bf16[2,128,128]{2,1,0:T(8,128)(2,1)S(1)}, bf16[2,128,128]{2,1,0:T(8,128)(2,1)S(1)}, u32[]{:S(2)}, u32[]{:S(2)}) collective-permute-start(bf16[2,128,128]{2,1,0:T(8,128)(2,1)S(1)} %get-tuple-element.27), channel_id=1, source_target_pairs={{64,16},{96,48},{128,80},{160,112},{192,144},{224,176},{256,208},{... | collective-permute-start | bytes 196616 | tf_op jit(solution)/shard_map/ppermute | solution.py:34
  111.3 10.0 %collective-permute-start.11 = (bf16[2,128,128]{2,1,0:T(8,128)(2,1)S(1)}, bf16[2,128,128]{2,1,0:T(8,128)(2,1)S(1)}, u32[]{:S(2)}, u32[]{:S(2)}) collective-permute-start(bf16[2,128,128]{2,1,0:T(8,128)(2,1)S(1)} %get-tuple-element.25), channel_id=1, source_target_pairs={{32,16},{64,48},{96,80},{128,112},{160,144},{192,176},{224,208},{2... | collective-permute-start | bytes 196616 | tf_op jit(solution)/shard_map/ppermute | solution.py:34
  121.4 20.5 %collective-permute-start.16 = (bf16[2,128,128]{2,1,0:T(8,128)(2,1)S(1)}, bf16[2,128,128]{2,1,0:T(8,128)(2,1)S(1)}, u32[]{:S(2)}, u32[]{:S(2)}) collective-permute-start(bf16[2,128,128]{2,1,0:T(8,128)(2,1)S(1)} %fusion.12), channel_id=1, source_target_pairs={{0,4},{4,8},{8,12},{12,0},{1,5},{5,9},{9,13},{13,1},{2,6},{6,10},{... | collective-permute-start | bytes 196616 | tf_op jit(solution)/shard_map/ppermute | solution.py:19
  127.8 14.1 %collective-permute-start.15 = (bf16[2,128,128]{2,1,0:T(8,128)(2,1)S(1)}, bf16[2,128,128]{2,1,0:T(8,128)(2,1)S(1)}, u32[]{:S(2)}, u32[]{:S(2)}) collective-permute-start(bf16[2,128,128]{2,1,0:T(8,128)(2,1)S(1)} %fusion.12), channel_id=1, source_target_pairs={{0,8},{4,12},{8,0},{12,4},{1,9},{5,13},{9,1},{13,5},{2,10},{6,14},... | collective-permute-start | bytes 196616 | tf_op jit(solution)/shard_map/ppermute | solution.py:19
  137.0 6.7 %collective-permute-start.14 = (bf16[2,128,128]{2,1,0:T(8,128)(2,1)S(1)}, bf16[2,128,128]{2,1,0:T(8,128)(2,1)S(1)}, u32[]{:S(2)}, u32[]{:S(2)}) collective-permute-start(bf16[2,128,128]{2,1,0:T(8,128)(2,1)S(1)} %fusion.12), channel_id=1, source_target_pairs={{0,12},{4,0},{8,4},{12,8},{1,13},{5,1},{9,5},{13,9},{2,14},{6,2},{... | collective-permute-start | bytes 196616 | tf_op jit(solution)/shard_map/ppermute | solution.py:19
  143.8 15.6 %collective-permute-start.19 = (bf16[4,2,128,128]{3,2,1,0:T(8,128)(2,1)S(1)}, bf16[4,2,128,128]{3,2,1,0:T(8,128)(2,1)S(1)}, u32[]{:S(2)}, u32[]{:S(2)}) collective-permute-start(bf16[4,2,128,128]{3,2,1,0:T(8,128)(2,1)S(1)} %get-tuple-element.24), channel_id=1, source_target_pairs={{0,1},{1,2},{2,3},{3,0},{4,5},{5,6},{6,7},{7,4},{8,9},{9,10},{10,1... | collective-permute-start | bytes 786440 | tf_op jit(solution)/shard_map/ppermute | solution.py:19
  145.7 13.7 %collective-permute-start.18 = (bf16[4,2,128,128]{3,2,1,0:T(8,128)(2,1)S(1)}, bf16[4,2,128,128]{3,2,1,0:T(8,128)(2,1)S(1)}, u32[]{:S(2)}, u32[]{:S(2)}) collective-permute-start(bf16[4,2,128,128]{3,2,1,0:T(8,128)(2,1)S(1)} %get-tuple-element.24), channel_id=1, source_target_pairs={{0,2},{1,3},{2,0},{3,1},{4,6},{5,7},{6,4},{7,5},{8,10},{9,11},{10,... | collective-permute-start | bytes 786440 | tf_op jit(solution)/shard_map/ppermute | solution.py:19
  149.5 12.4 %collective-permute-start.17 = (bf16[4,2,128,128]{3,2,1,0:T(8,128)(2,1)S(1)}, bf16[4,2,128,128]{3,2,1,0:T(8,128)(2,1)S(1)}, u32[]{:S(2)}, u32[]{:S(2)}) collective-permute-start(bf16[4,2,128,128]{3,2,1,0:T(8,128)(2,1)S(1)} %get-tuple-element.24), channel_id=1, source_target_pairs={{0,3},{1,0},{2,1},{3,2},{4,7},{5,4},{6,5},{7,6},{8,11},{9,8},{10,9... | collective-permute-start | bytes 786440 | tf_op jit(solution)/shard_map/ppermute | solution.py:19
